TPU v7x, 32 devices: a whole 2x2x4 slice. The times are simulated.
32 devices in a mesh: row: 4 (over z), col: 8 (over y, x, core).
Axes of the slice: x: 2, y: 2, z: 4, core: 2. Of those that a mesh axis runs over, the one named last changes fastest.
Arguments:
- points: bfloat16 [196608, 128], P(('row', 'col')), may hold values from -6 to 6
- weights: bfloat16 [196608, 256], P(('row', 'col')), may hold values from -6 to 6
- leaf_basis: bfloat16 [196608, 128], P(('row', 'col')), may hold values from -0.75 to 0.75
- leaf_rank: int32 [768], P(('row', 'col')), may hold values from 64 to 128
- leaf_skeleton: int32 [768, 128], P(('row', 'col')), may hold values from 0 to 255, as said below
- near_list: int32 [768, 5], P(('row', 'col')), may hold values from 0 to 767, as said below
- far_list: int32 [768, 4], P(('row', 'col')), may hold values from 0 to 767, as said below
- node_basis: bfloat16 [98304, 128], P(('row', 'col')), may hold values from -0.15625 to 0.15625
- node_rank: int32 [32], P(('row', 'col')), may hold values from 64 to 128
- node_skeleton: int32 [32, 128], P(('row', 'col')), may hold values from 0 to 3071, as said below
- node_far: int32 [32, 4], P(('row', 'col')), may hold values from 0 to 31, as said below
- group_basis: bfloat16 [4096, 128], P(('row', 'col')), may hold values from -0.375 to 0.375
- group_rank: int32 [4], P('row'), may hold values from 32 to 128
- group_skeleton: int32 [4, 128], P('row'), may hold values from 0 to 1023, as said below
- group_far: int32 [4, 2], P('row'), may hold values from 0 to 3, as said below
Outputs:
- potentials: bfloat16 [196608, 256], P(('row', 'col'))
Inputs may be any that keep to these rules, and one draw needn't show every extreme that they name: `near_list`: each row lists distinct leaves within 8 leaves of its own leaf; the first entry is the leaf itself. `far_list`: each row lists distinct leaves within 8 leaves of its own leaf, none of them in the same row of near_list. `leaf_skeleton`: distinct within a row. `node_skeleton`: distinct within a row. `group_skeleton`: distinct within a row. `node_far`: distinct nodes of the same group as the listing node, never itself. `group_far`: distinct groups, never the listing group itself.
All inputs are finite; a program needn't handle non-finite values.
Results may differ from a plain program's by a relative error of at most 0.0095.
Values may be sent and summed in bfloat16 or wider, within the bound.
No kernel may reach another device: no remote copies, remote signals or barrier semaphores. Data moves between devices by JAX's collectives and lax.ppermute only.
A program may use at most 192 MiB of HBM per device.

v0:
```python
import functools

import jax
import jax.numpy as jnp
from jax import lax
from jax.experimental import pallas as pl
from jax.experimental.pallas import tpu as pltpu
from jax.sharding import PartitionSpec as P

REACH = 8


def padded(cells, sides, width):
    for axis, dim in sides:
        count = lax.axis_size(axis)
        ends = count - 1
        head = lax.slice_in_dim(cells, 0, width, axis=dim)
        tail = lax.slice_in_dim(cells, cells.shape[dim] - width, cells.shape[dim], axis=dim)
        cells = jnp.concatenate(
            [
                lax.ppermute(tail, axis, [(i, (i + 1) % count) for i in range(ends)]),
                cells,
                lax.ppermute(head, axis, [((i + 1) % count, i) for i in range(ends)]),
            ],
            axis=dim,
        )
    return cells


def kernel_block(left, right):
    left_square = jnp.sum(jnp.square(left.astype(jnp.float32)), axis=-1)
    right_square = jnp.sum(jnp.square(right.astype(jnp.float32)), axis=-1)
    inner = jnp.einsum("...md,...nd->...mn", left, right, preferred_element_type=jnp.float32)
    distance = left_square[..., :, None] + right_square[..., None, :] - 2.0 * inner
    return jnp.exp(distance * (-2.0 / left.shape[-1])).astype(jnp.bfloat16)


def near_kernel(index_ref, target_ref, *refs):
    count = (len(refs) - 1) // 3
    point_refs = refs[:count]
    weight_refs = refs[count : 2 * count]
    norm_refs = refs[2 * count : 3 * count]
    out_ref = refs[-1]
    target = target_ref[0]
    target_wide = target.astype(jnp.float32)
    target_square = jnp.sum(target_wide * target_wide, axis=-1, keepdims=True)
    scale = -2.0 / target.shape[-1]
    total = None
    for position in range(count):
        inner = lax.dot_general(
            target,
            point_refs[position][0],
            (((1,), (1,)), ((), ())),
            preferred_element_type=jnp.float32,
        )
        distance = target_square + norm_refs[position][0] - 2.0 * inner
        kernel = jnp.exp(distance * scale).astype(jnp.bfloat16)
        part = jnp.dot(kernel, weight_refs[position][0], preferred_element_type=jnp.float32)
        total = part if total is None else total + part
    out_ref[0] = total


def near_field(local_points, ext_points, ext_weights, ext_norms, near_local):
    leaves, size, dims = local_points.shape
    rhs = ext_weights.shape[-1]
    count = near_local.shape[1]
    flat_index = near_local.reshape(-1)

    def source_map(position):
        return lambda l, index: (index[l * count + position], 0, 0)

    in_specs = [pl.BlockSpec((1, size, dims), lambda l, index: (l, 0, 0))]
    in_specs += [pl.BlockSpec((1, size, dims), source_map(p)) for p in range(count)]
    in_specs += [pl.BlockSpec((1, size, rhs), source_map(p)) for p in range(count)]
    in_specs += [pl.BlockSpec((1, 1, size), source_map(p)) for p in range(count)]
    return pl.pallas_call(
        near_kernel,
        grid_spec=pltpu.PrefetchScalarGridSpec(
            num_scalar_prefetch=1,
            grid=(leaves,),
            in_specs=in_specs,
            out_specs=pl.BlockSpec((1, size, rhs), lambda l, index: (l, 0, 0)),
        ),
        out_shape=jax.ShapeDtypeStruct((leaves, size, rhs), jnp.float32),
    )(flat_index, local_points, *([ext_points] * count), *([ext_weights] * count), *([ext_norms] * count))


def select_rows(table, index):
    count = table.shape[0]
    onehot = (index[:, None] == jnp.arange(count, dtype=jnp.int32)[None, :]).astype(table.dtype)
    picked = jnp.dot(onehot, table.reshape(count, -1), preferred_element_type=jnp.float32).astype(
        table.dtype
    )
    return picked.reshape(index.shape + table.shape[1:])


def select_within(table, index):
    count = table.shape[1]
    onehot = (index[:, :, None] == jnp.arange(count, dtype=jnp.int32)[None, None, :]).astype(
        table.dtype
    )
    return jnp.einsum("bkp,bpc->bkc", onehot, table, preferred_element_type=jnp.float32).astype(
        table.dtype
    )


def body(
    points,
    weights,
    leaf_basis,
    leaf_rank,
    leaf_skeleton,
    near_list,
    far_list,
    node_basis,
    node_rank,
    node_skeleton,
    node_far,
    group_basis,
    group_rank,
    group_skeleton,
    group_far,
):
    leaf_count = leaf_rank.shape[0]
    leaf_size = points.shape[0] // leaf_count
    dim_count = points.shape[1]
    rhs_count = weights.shape[1]
    rank_count = leaf_basis.shape[1]
    node_width = node_basis.shape[1]
    group_width = group_basis.shape[1]
    local_points = points.reshape(leaf_count, leaf_size, dim_count)
    local_bases = leaf_basis.reshape(leaf_count, leaf_size, rank_count)
    local_weights = weights.reshape(leaf_count, leaf_size, rhs_count)
    leaf_mask = (
        lax.broadcasted_iota(jnp.int32, (leaf_count, rank_count), 1) < leaf_rank[:, None]
    ).astype(jnp.float32)
    leaf_up = (
        jnp.einsum("lpk,lpr->lkr", local_bases, local_weights, preferred_element_type=jnp.float32)
        * leaf_mask[:, :, None]
    ).astype(jnp.bfloat16)
    leaf_coords = select_within(local_points, leaf_skeleton)
    first_leaf = lax.axis_index(("row", "col")) * leaf_count
    offset = first_leaf - REACH
    ext_points = padded(points, ((("row", "col"), 0),), REACH * leaf_size).reshape(
        leaf_count + 2 * REACH, leaf_size, dim_count
    )
    ext_weights = padded(weights, ((("row", "col"), 0),), REACH * leaf_size).reshape(
        leaf_count + 2 * REACH, leaf_size, rhs_count
    )
    ext_wide = ext_points.astype(jnp.float32)
    ext_norms = jnp.sum(ext_wide * ext_wide, axis=-1)[:, None, :]
    own_rows = jnp.concatenate([leaf_coords, leaf_up], axis=-1).reshape(
        leaf_count * rank_count, dim_count + rhs_count
    )
    skeleton_rows = padded(own_rows, ((("row", "col"), 0),), REACH * rank_count)
    skeleton_rows = skeleton_rows.reshape(leaf_count + 2 * REACH, rank_count, dim_count + rhs_count)
    near_local = near_list - offset
    near_total = near_field(local_points, ext_points, ext_weights, ext_norms, near_local)
    node_mask = (jnp.arange(node_width, dtype=jnp.int32) < node_rank[0]).astype(jnp.float32)
    node_up = (
        jnp.einsum(
            "ak,ar->kr",
            node_basis,
            leaf_up.reshape(leaf_count * rank_count, rhs_count),
            preferred_element_type=jnp.float32,
        )
        * node_mask[:, None]
    ).astype(jnp.bfloat16)
    node_coords = select_rows(
        leaf_coords.reshape(leaf_count * rank_count, dim_count), node_skeleton[0]
    )
    column = lax.axis_index("col")
    columns = lax.axis_size("col")
    source_columns = node_far[0] % columns
    all_coords, all_up = (
        lax.all_gather(node_coords[None], "col", axis=0, tiled=True),
        lax.all_gather(node_up[None], "col", axis=0, tiled=True),
    )
    picked_coords = select_rows(all_coords, source_columns)
    picked_up = select_rows(all_up, source_columns)
    kernel = kernel_block(jnp.broadcast_to(node_coords, picked_coords.shape), picked_coords)
    node_side = jnp.einsum("fab,fbr->ar", kernel, picked_up, preferred_element_type=jnp.float32)
    group_mask = (jnp.arange(group_width, dtype=jnp.int32) < group_rank[0]).astype(jnp.float32)
    group_part = (
        jnp.einsum("ag,ar->gr", group_basis, node_up, preferred_element_type=jnp.float32)
        * group_mask[:, None]
    )
    selector = (
        group_skeleton[0][:, None]
        == column * node_width + jnp.arange(node_width, dtype=jnp.int32)[None, :]
    ).astype(jnp.bfloat16)
    coord_part = jnp.dot(selector, node_coords, preferred_element_type=jnp.float32)
    group_sum, coord_sum = lax.psum((group_part, coord_part), "col")
    group_up = group_sum.astype(jnp.bfloat16)
    group_coords = coord_sum.astype(jnp.bfloat16)
    every_group_coords, every_group_up = (
        lax.all_gather(group_coords[None], "row", axis=0, tiled=True),
        lax.all_gather(group_up[None], "row", axis=0, tiled=True),
    )
    picked_group_coords = select_rows(every_group_coords, group_far[0])
    picked_group_up = select_rows(every_group_up, group_far[0])
    group_kernel = kernel_block(
        jnp.broadcast_to(group_coords, picked_group_coords.shape), picked_group_coords
    )
    group_down = (
        jnp.einsum("fab,fbr->ar", group_kernel, picked_group_up, preferred_element_type=jnp.float32)
        * group_mask[:, None]
    ).astype(jnp.bfloat16)
    node_down = (
        (jnp.dot(group_basis, group_down, preferred_element_type=jnp.float32) + node_side)
        * node_mask[:, None]
    ).astype(jnp.bfloat16)
    far_total = jnp.dot(node_basis, node_down, preferred_element_type=jnp.float32).reshape(
        leaf_count, rank_count, rhs_count
    )
    far_local = far_list - offset
    for position in range(far_list.shape[1]):
        sources = select_rows(skeleton_rows, far_local[:, position])
        kernel = kernel_block(leaf_coords, sources[..., :dim_count])
        far_total = far_total + jnp.einsum(
            "lab,lbr->lar", kernel, sources[..., dim_count:], preferred_element_type=jnp.float32
        )
    leaf_down = (far_total * leaf_mask[:, :, None]).astype(jnp.bfloat16)
    result = (
        jnp.einsum("lpk,lkr->lpr", local_bases, leaf_down, preferred_element_type=jnp.float32)
        + near_total
    )
    return result.astype(jnp.bfloat16).reshape(leaf_count * leaf_size, rhs_count)


def solution(mesh):
    in_specs = (
        P(("row", "col"), None),
        P(("row", "col"), None),
        P(("row", "col"), None),
        P(("row", "col")),
        P(("row", "col"), None),
        P(("row", "col"), None),
        P(("row", "col"), None),
        P(("row", "col"), None),
        P(("row", "col")),
        P(("row", "col"), None),
        P(("row", "col"), None),
        P(("row", "col"), None),
        P("row"),
        P("row", None),
        P("row", None),
    )
    out_specs = P(("row", "col"), None)
    return jax.shard_map(body, mesh=mesh, in_specs=in_specs, out_specs=out_specs, check_vma=False)
```

profile of v0, /device:TPU:2, one launch (start us, length us, event | category | flops | bytes accessed | tf_op | source)
XLA Modules:
  0.0 260.4 jit_solution(868141996689551049)
XLA Ops:
  0.9 2.9 %multiply_reduce_fusion.5 = (f32[24,128]{1,0:T(8,128)S(1)}, bf16[24,128,128]{2,1,0:T(8,128)(2,1)S(1)}) fusion(bf16[24,256,128]{2,1,0:T(8,128)(2,1)} %bitcast.135, s32[24,128]{1,0:T(8,128)} %param.19), kind=kOutput, calls=%fused_computation.39 | convolution fusion | flops 203682816 | bytes 2383872 | tf_op jit(solution)/shard_map/bkp,bpc->bkc/dot_general | solution.py:102
  4.8 1.4 fusion.33
  6.2 1.9 collective-permute-start
  8.1 3.6 %collective-permute-start.1 = (bf16[1024,384]{1,0:T(8,128)(2,1)}, bf16[1024,384]{1,0:T(8,128)(2,1)}, u32[]{:S(2)}, u32[]{:S(2)}) collective-permute-start(bf16[1024,384]{1,0:T(8,128)(2,1)} %bitcast.21), channel_id=1, source_target_pairs={{1,0},{2,1},{3,2},{4,3},{5,4},{6,5},{7,6},{8,7},{9,8},{10,9},{11,1... | collective-permute-start | bytes 2359304 | tf_op jit(solution)/shard_map/ppermute | solution.py:23
  12.8 2.0 collective-permute-start.2
  14.9 3.6 %collective-permute-start.3 = (bf16[2048,128]{1,0:T(8,128)(2,1)}, bf16[2048,128]{1,0:T(8,128)(2,1)}, u32[]{:S(2)}, u32[]{:S(2)}) collective-permute-start(bf16[2048,128]{1,0:T(8,128)(2,1)} %get-tuple-element.11), channel_id=1, source_target_pairs={{1,0},{2,1},{3,2},{4,3},{5,4},{6,5},{7,6},{8,7},{9,8},{10,9},{11,1... | collective-permute-start | bytes 1572872 | tf_op jit(solution)/shard_map/ppermute | solution.py:23
  18.6 1.5 fusion.106
  20.1 2.8 %collective-permute-start.4 = (bf16[2048,256]{1,0:T(8,128)(2,1)}, bf16[2048,256]{1,0:T(8,128)(2,1)}, u32[]{:S(2)}, u32[]{:S(2)}) collective-permute-start(bf16[2048,256]{1,0:T(8,128)(2,1)} %get-tuple-element.7), channel_id=1, source_target_pairs={{0,1},{1,2},{2,3},{3,4},{4,5},{5,6},{6,7},{7,8},{8,9},{9,10},{10,1... | collective-permute-start | bytes 3145736 | tf_op jit(solution)/shard_map/ppermute | solution.py:21
  22.9 2.2 multiply_reduce_fusion.8
  26.6 1.7 fusion.29
  28.6 40.5 %all-reduce.2 = (bf16[128,256]{0,1:T(8,128)(2,1)S(1)}, bf16[128,128]{1,0:T(8,128)(2,1)S(1)}) all-reduce(f32[128,256]{0,1:T(8,128)S(1)} %fusion.26, f32[128,128]{1,0:T(8,128)S(1)} %fusion.78), channel_id=1, replica_groups=mesh['row'=4,'col'=8] {'col'}, use_global_device_ids=true, to_apply=%region_3.4 | all-reduce | flops 49152 | bytes 294912 | tf_op jit(solution)/shard_map/psum | solution.py:193
  69.1 13.9 %all-gather = bf16[512,128]{1,0:T(8,128)(2,1)S(1)} all-gather(bf16[128,128]{1,0:T(8,128)(2,1)S(1)} %get-tuple-element.6), channel_id=2, replica_groups=mesh['row'=4,'col'=8] {'row'}, dimensions={0}, use_global_device_ids=true | all-gather | bytes 163840 | tf_op jit(solution)/shard_map/all_gather | solution.py:197
  83.6 11.2 %all-gather.2 = bf16[1024,128]{0,1:T(8,128)(2,1)} all-gather(bf16[128,128]{0,1:T(8,128)(2,1)S(1)} %get-tuple-element.20), channel_id=4, replica_groups=mesh['row'=4,'col'=8] {'col'}, dimensions={0}, use_global_device_ids=true | all-gather | bytes 294912 | tf_op jit(solution)/shard_map/all_gather | solution.py:176
  96.2 1.2 fusion.31
  98.1 12.9 %all-gather.1 = bf16[512,256]{0,1:T(8,128)(2,1)S(1)} all-gather(bf16[128,256]{0,1:T(8,128)(2,1)S(1)} %get-tuple-element.5), channel_id=3, replica_groups=mesh['row'=4,'col'=8] {'row'}, dimensions={0}, use_global_device_ids=true | all-gather | bytes 327680 | tf_op jit(solution)/shard_map/all_gather | solution.py:198
  111.8 1.1 reshape.147
  112.9 1.7 convolution_convert_fusion.5
  114.6 1.8 copy.22
  116.4 1.1 reshape.149
  119.8 10.9 %all-gather.3 = bf16[1024,256]{0,1:T(8,128)(2,1)} all-gather(bf16[128,256]{0,1:T(8,128)(2,1)S(1)} %bitcast.150), channel_id=5, replica_groups=mesh['row'=4,'col'=8] {'col'}, dimensions={0}, use_global_device_ids=true | all-gather | bytes 589824 | tf_op jit(solution)/shard_map/all_gather | solution.py:177
  130.7 2.0 copy.24
  132.8 2.1 reshape.151
  134.9 1.4 convolution_convert_fusion.4
  136.3 2.0 fusion.30
  138.2 1.8 convolution_bitcast_fusion.1
  140.1 3.7 %convolution_bitcast_fusion = f32[3072,256]{0,1:T(8,128)} fusion(bf16[3072,128]{1,0:T(8,128)(2,1)} %param.22, f32[128,256]{0,1:T(8,128)} %convolution_bitcast_fusion.1, bf16[128,256]{1,0:T(8,128)(2,1)} %fusion.30, bf16[128,128]{1,0:T(8,128)(2,1)} %param.26, f32[128]{0:T(128)S(1)} %compare_convert_fusion.1), kind=kOutput, calls=%fused_computation.12 | convolution fusion | flops 209813504 | bytes 4162048 | tf_op jit(solution)/shard_map/dot_general | solution.py:213
  143.7 3.0 %pad_maximum_fusion.2 = bf16[24,128,384]{2,1,0:T(8,128)(2,1)} fusion(bf16[24,128,128]{2,1,0:T(8,128)(2,1)} %copy-done.4, bf16[24,128,256]{2,1,0:T(8,128)(2,1)S(1)} %multiply_convert_fusion.1), kind=kLoop, calls=%fused_computation.16 | loop fusion | flops 4718592 | bytes 4718592 | tf_op jit(solution)/shard_map/concatenate | solution.py:152
  146.7 3.8 %copy.25 = f32[3072,256]{1,0:T(8,128)} copy(f32[3072,256]{0,1:T(8,128)} %convolution_bitcast_fusion) | data formatting | bytes 6291456 | tf_op jit(solution)/shard_map/dot_general | solution.py:213
  151.2 2.7 %collective-permute-start.5 = (bf16[2048,256]{1,0:T(8,128)(2,1)}, bf16[2048,256]{1,0:T(8,128)(2,1)}, u32[]{:S(2)}, u32[]{:S(2)}) collective-permute-start(bf16[2048,256]{1,0:T(8,128)(2,1)} %get-tuple-element.8), channel_id=1, source_target_pairs={{1,0},{2,1},{3,2},{4,3},{5,4},{6,5},{7,6},{8,7},{9,8},{10,9},{11,1... | collective-permute-start | bytes 3145736 | tf_op jit(solution)/shard_map/ppermute | solution.py:23
  153.9 1.1 constant_dynamic-update-slice_fusion.2
  155.2 1.3 constant_dynamic-update-slice_fusion
  156.5 1.5 copy-done.1
  158.0 2.1 multiply_reduce_fusion
  160.1 7.9 %pad_maximum_fusion.1 = bf16[5120,384]{1,0:T(8,128)(2,1)} fusion(bf16[1024,384]{1,0:T(8,128)(2,1)} %collective-permute-done.1, bf16[3072,384]{1,0:T(8,128)(2,1)S(1)} %bitcast.144, bf16[1024,384]{1,0:T(8,128)(2,1)} %collective-permute-done), kind=kLoop, calls=%fused_computation.13 | loop fusion | flops 11796480 | bytes 7864320 | tf_op jit(solution)/shard_map/concatenate | solution.py:19
  168.0 6.5 %reshape_reshape.2 = bf16[40,49152]{1,0:T(8,128)(2,1)} reshape(bf16[5120,384]{1,0:T(8,128)(2,1)} %pad_maximum_fusion.1) | data formatting | bytes 7864320 | tf_op jit(solution)/shard_map/reshape;reshape | solution.py:91
  174.5 3.0 %convolution_convert_fusion = bf16[24,49152]{1,0:T(8,128)(2,1)S(1)} fusion(bf16[40,49152]{1,0:T(8,128)(2,1)} %reshape_reshape.2, s32[24]{0:T(128)S(1)} %get-tuple-element.13), kind=kOutput, calls=%fused_computation | convolution fusion | flops 95552448 | bytes 6291552 | tf_op jit(solution)/shard_map/dot_general | solution.py:91
  178.5 2.0 copy-done.2
  183.8 1.4 copy-done.7
  185.7 4.5 %fusion.9 = f32[24,128,256]{2,1,0:T(8,128)} fusion(bf16[24,128,384]{2,1,0:T(8,128)(2,1)} %bitcast.129, bf16[24,128,128]{2,1,0:T(8,128)(2,1)S(1)} %copy-done.5, f32[24,128]{1,0:T(8,128)S(1)} %multiply_reduce_fusion.4, f32[24,128]{1,0:T(8,128)S(1)} %get-tuple-element.17), kind=kOutput, calls=%fused_computation.29 | convolution fusion | flops 303955968 | bytes 6316032 | tf_op jit(solution)/shard_map/lab,lbr->lar/dot_general | solution.py:220
  190.2 4.4 %fusion.7 = f32[24,128,256]{2,1,0:T(8,128)} fusion(bf16[24,128,384]{2,1,0:T(8,128)(2,1)} %bitcast.131, bf16[24,128,128]{2,1,0:T(8,128)(2,1)S(1)} %copy-done.5, f32[24,128]{1,0:T(8,128)S(1)} %multiply_reduce_fusion.3, f32[24,128]{1,0:T(8,128)S(1)} %get-tuple-element.17), kind=kOutput, calls=%fused_computation.27 | convolution fusion | flops 303955968 | bytes 6316032 | tf_op jit(solution)/shard_map/lab,lbr->lar/dot_general | solution.py:220
  194.6 3.0 %convolution_convert_fusion.1 = bf16[24,49152]{1,0:T(8,128)(2,1)S(1)} fusion(bf16[40,49152]{1,0:T(8,128)(2,1)} %reshape_reshape.2, s32[24]{0:T(128)S(1)} %get-tuple-element.14), kind=kOutput, calls=%fused_computation.1 | convolution fusion | flops 95552448 | bytes 6291552 | tf_op jit(solution)/shard_map/dot_general | solution.py:91
  198.0 1.4 copy-done.8
  199.9 4.4 %fusion.5 = f32[24,128,256]{2,1,0:T(8,128)} fusion(bf16[24,128,384]{2,1,0:T(8,128)(2,1)} %bitcast.133, bf16[24,128,128]{2,1,0:T(8,128)(2,1)S(1)} %copy-done.5, f32[24,128]{1,0:T(8,128)S(1)} %multiply_reduce_fusion.2, f32[24,128]{1,0:T(8,128)S(1)} %get-tuple-element.17), kind=kOutput, calls=%fused_computation.25 | convolution fusion | flops 303955968 | bytes 6316032 | tf_op jit(solution)/shard_map/lab,lbr->lar/dot_general | solution.py:220
  204.4 1.8 exponential_convert_fusion
  206.2 9.7 %fusion.2 = f32[24,256,256]{1,2,0:T(8,128)} fusion(bf16[24,256,128]{2,1,0:T(8,128)(2,1)S(1)} %bitcast.114, f32[24,128,256]{2,1,0:T(8,128)} %fusion.5, f32[24,128,256]{2,1,0:T(8,128)} %fusion.7, f32[24,128,256]{2,1,0:T(8,128)} %bitcast.134, f32[24,128,256]{2,1,0:T(8,128)} %fusion.9, bf16[24,128,128]{2,1,0:T(8,128)(2,1)S(1)} %exponential_convert_fusion, ...), kind=kOutput, calls=%fused_computation.23 | convolution fusion | flops 608698368 | bytes 22818816 | tf_op jit(solution)/shard_map/lpk,lkr->lpr/dot_general | solution.py:225
  215.9 9.8 %pad_maximum_fusion = bf16[10240,256]{1,0:T(8,128)(2,1)} fusion(bf16[2048,256]{1,0:T(8,128)(2,1)} %collective-permute-done.5, bf16[6144,256]{1,0:T(8,128)(2,1)} %param.16, bf16[2048,256]{1,0:T(8,128)(2,1)} %collective-permute-done.4), kind=kLoop, calls=%fused_computation.10 | loop fusion | flops 15728640 | bytes 10485760 | tf_op jit(solution)/shard_map/concatenate | solution.py:19
  225.7 27.4 %shard_map.145 = f32[24,256,256]{2,1,0:T(8,128)} custom-call(s32[120]{0:T(128)} %reshape.159.index_ref, bf16[24,256,128]{2,1,0:T(8,128)(2,1)} %bitcast.136, bf16[40,256,128]{2,1,0:T(8,128)(2,1)} %bitcast.120, bf16[40,256,128]{2,1,0:T(8,128)(2,1)} %bitcast.121, bf16[40,256,128]{2,1,0:T(8,128)(2,1)} %bitcast.122, bf16[40,256,128]{2,1,0:T(8,128)(2,1)} %bitcast.123, ...), custom_call_target="tpu_custom_call" | custom-call | tf_op jit(solution)/shard_map/pallas_call | solution.py:76
  253.1 7.2 %fusion = bf16[24,256,256]{2,1,0:T(8,128)(2,1)} fusion(f32[24,256,256]{2,1,0:T(8,128)} %shard_map.145, f32[24,256,256]{1,2,0:T(8,128)} %fusion.2), kind=kLoop, calls=%fused_computation.9 | loop fusion | flops 3145728 | bytes 15728640 | tf_op jit(solution)/shard_map/convert_element_type | solution.py:228
  (86 shorter events, 15.6 us)
Async XLA Ops:
  0.0 3.8 %copy-start = (bf16[6144,128]{1,0:T(8,128)(2,1)S(1)}, bf16[6144,128]{1,0:T(8,128)(2,1)}, u32[]{:S(2)}) copy-start(bf16[6144,128]{1,0:T(8,128)(2,1)} %param.17) | copy-start | bytes 4718596
  0.0 3.8 %copy-start.3 = (bf16[6144,256]{1,0:T(8,128)(2,1)S(1)}, bf16[6144,256]{1,0:T(8,128)(2,1)}, u32[]{:S(2)}) copy-start(bf16[6144,256]{1,0:T(8,128)(2,1)} %param.16) | copy-start | bytes 9437188
  0.9 3.9 %copy-start.17 = (f32[24,128]{1,0:T(8,128)}, f32[24,128]{1,0:T(8,128)S(1)}, u32[]{:S(2)}) copy-start(f32[24,128]{1,0:T(8,128)S(1)} %fusion.86) | copy-start | bytes 36868
  3.8 1.0 copy-start.4
  4.8 7.0 %copy-start.9 = (bf16[6144,128]{1,0:T(8,128)(2,1)S(1)}, bf16[6144,128]{1,0:T(8,128)(2,1)}, u32[]{:S(2)}) copy-start(bf16[6144,128]{1,0:T(8,128)(2,1)} %param.15) | copy-start | bytes 4718596
  6.2 153.9 %collective-permute-start = (bf16[1024,384]{1,0:T(8,128)(2,1)}, bf16[1024,384]{1,0:T(8,128)(2,1)}, u32[]{:S(2)}, u32[]{:S(2)}) collective-permute-start(bf16[1024,384]{1,0:T(8,128)(2,1)} %bitcast.19), channel_id=1, source_target_pairs={{0,1},{1,2},{2,3},{3,4},{4,5},{5,6},{6,7},{7,8},{8,9},{9,10},{10,1... | collective-permute-start | bytes 2359304 | tf_op jit(solution)/shard_map/ppermute | solution.py:21
  8.1 152.0 %collective-permute-start.1 = (bf16[1024,384]{1,0:T(8,128)(2,1)}, bf16[1024,384]{1,0:T(8,128)(2,1)}, u32[]{:S(2)}, u32[]{:S(2)}) collective-permute-start(bf16[1024,384]{1,0:T(8,128)(2,1)} %bitcast.21), channel_id=1, source_target_pairs={{1,0},{2,1},{3,2},{4,3},{5,4},{6,5},{7,6},{8,7},{9,8},{10,9},{11,1... | collective-permute-start | bytes 2359304 | tf_op jit(solution)/shard_map/ppermute | solution.py:23
  12.8 10.1 %copy-start.25 = (s32[1,128]{1,0:T(1,128)S(1)}, s32[1,128]{1,0:T(1,128)}, u32[]{:S(2)}) copy-start(s32[1,128]{1,0:T(1,128)} %param.24) | copy-start | bytes 1540
  12.8 138.4 %collective-permute-start.2 = (bf16[2048,128]{1,0:T(8,128)(2,1)}, bf16[2048,128]{1,0:T(8,128)(2,1)}, u32[]{:S(2)}, u32[]{:S(2)}) collective-permute-start(bf16[2048,128]{1,0:T(8,128)(2,1)} %get-tuple-element.12), channel_id=1, source_target_pairs={{0,1},{1,2},{2,3},{3,4},{4,5},{5,6},{6,7},{7,8},{8,9},{9,10},{10,1... | collective-permute-start | bytes 1572872 | tf_op jit(solution)/shard_map/ppermute | solution.py:21
  14.9 10.2 %copy-start.23 = (s32[1,128]{1,0:T(1,128)S(1)}, s32[1,128]{1,0:T(1,128)}, u32[]{:S(2)}) copy-start(s32[1,128]{1,0:T(1,128)} %param.28) | copy-start | bytes 1540
  14.9 140.3 %collective-permute-start.3 = (bf16[2048,128]{1,0:T(8,128)(2,1)}, bf16[2048,128]{1,0:T(8,128)(2,1)}, u32[]{:S(2)}, u32[]{:S(2)}) collective-permute-start(bf16[2048,128]{1,0:T(8,128)(2,1)} %get-tuple-element.11), channel_id=1, source_target_pairs={{1,0},{2,1},{3,2},{4,3},{5,4},{6,5},{7,6},{8,7},{9,8},{10,9},{11,1... | collective-permute-start | bytes 1572872 | tf_op jit(solution)/shard_map/ppermute | solution.py:23
  20.1 8.3 %copy-start.15 = (bf16[128,128]{1,0:T(8,128)(2,1)S(1)}, bf16[128,128]{1,0:T(8,128)(2,1)}, u32[]{:S(2)}) copy-start(bf16[128,128]{1,0:T(8,128)(2,1)} %param.26) | copy-start | bytes 98308
  20.1 195.8 %collective-permute-start.4 = (bf16[2048,256]{1,0:T(8,128)(2,1)}, bf16[2048,256]{1,0:T(8,128)(2,1)}, u32[]{:S(2)}, u32[]{:S(2)}) collective-permute-start(bf16[2048,256]{1,0:T(8,128)(2,1)} %get-tuple-element.7), channel_id=1, source_target_pairs={{0,1},{1,2},{2,3},{3,4},{4,5},{5,6},{6,7},{7,8},{8,9},{9,10},{10,1... | collective-permute-start | bytes 3145736 | tf_op jit(solution)/shard_map/ppermute | solution.py:21
  26.6 1.8 copy-start.24
  69.1 29.0 %copy-start.16 = (bf16[128,128]{1,0:T(8,128)(2,1)}, bf16[128,128]{1,0:T(8,128)(2,1)S(1)}, u32[]{:S(2)}) copy-start(bf16[128,128]{1,0:T(8,128)(2,1)S(1)} %get-tuple-element.6) | copy-start | bytes 98308
  97.4 0.7 copy-start.19
  118.1 14.6 %copy-start.22 = (s32[4]{0:T(128)}, s32[4]{0:T(128)S(1)}, u32[]{:S(2)}) copy-start(s32[4]{0:T(128)S(1)} %and_select_fusion) | copy-start | bytes 52
  118.4 0.7 copy-start.13
  119.8 18.4 %copy-start.14 = (bf16[1,4,128,128]{3,1,2,0:T(4,128)(2,1)S(1)}, bf16[1,4,128,128]{3,1,2,0:T(4,128)(2,1)}, u32[]{:S(2)}) copy-start(bf16[1,4,128,128]{3,1,2,0:T(4,128)(2,1)} %copy-done.13) | copy-start | bytes 393220
  140.1 3.7 %copy-start.20 = (s32[24,5]{0,1:T(8,128)S(1)}, s32[24,5]{0,1:T(8,128)}, u32[]{:S(2)}) copy-start(s32[24,5]{0,1:T(8,128)} %param.20) | copy-start | bytes 1444
  146.7 4.4 %copy-start.21 = (s32[24,4]{0,1:T(4,128)S(1)}, s32[24,4]{0,1:T(4,128)}, u32[]{:S(2)}) copy-start(s32[24,4]{0,1:T(4,128)} %param.21) | copy-start | bytes 1156
  146.7 8.3 %copy-start.10 = (bf16[6144,128]{1,0:T(8,128)(2,1)S(1)}, bf16[6144,128]{1,0:T(8,128)(2,1)}, u32[]{:S(2)}) copy-start(bf16[6144,128]{1,0:T(8,128)(2,1)} %param.15) | copy-start | bytes 4718596
  151.2 64.7 %collective-permute-start.5 = (bf16[2048,256]{1,0:T(8,128)(2,1)}, bf16[2048,256]{1,0:T(8,128)(2,1)}, u32[]{:S(2)}, u32[]{:S(2)}) collective-permute-start(bf16[2048,256]{1,0:T(8,128)(2,1)} %get-tuple-element.8), channel_id=1, source_target_pairs={{1,0},{2,1},{3,2},{4,3},{5,4},{6,5},{7,6},{8,7},{9,8},{10,9},{11,1... | collective-permute-start | bytes 3145736 | tf_op jit(solution)/shard_map/ppermute | solution.py:23
  155.2 4.9 %copy-start.12 = (bf16[24,128,384]{2,1,0:T(8,128)(2,1)S(1)}, bf16[24,128,384]{2,1,0:T(8,128)(2,1)}, u32[]{:S(2)}) copy-start(bf16[24,128,384]{2,1,0:T(8,128)(2,1)} %pad_maximum_fusion.2) | copy-start | bytes 7077892
  156.5 1.5 copy-start.1
  177.5 3.0 %copy-start.2 = (bf16[40,49152]{1,0:T(8,128)(2,1)S(1)}, bf16[40,49152]{1,0:T(8,128)(2,1)}, u32[]{:S(2)}) copy-start(bf16[40,49152]{1,0:T(8,128)(2,1)} %reshape_reshape.2) | copy-start | bytes 11796484
  178.0 3.4 %copy-start.11 = (bf16[3,8,128,384]{3,2,1,0:T(8,128)(2,1)}, bf16[3,8,128,384]{3,2,1,0:T(8,128)(2,1)S(1)}, u32[]{:S(2)}) copy-start(bf16[3,8,128,384]{3,2,1,0:T(8,128)(2,1)S(1)} %copy.35) | copy-start | bytes 7077892
  181.9 1.4 copy-start.6
  183.3 2.4 copy-start.5
  183.8 1.4 copy-start.7
  198.0 1.4 copy-start.8
  204.3 1.8 copy-start.18
where the time goes:
time: 263 us; the launch traced here: 260 us
  blocking collectives  89.4 us (34%)
  matrix products  52.9 us (20%)
  other arithmetic  36.9 us (14%)
  local copies, waits for them, and re-layouts  35.2 us (13%)
  Pallas kernels  27.4 us (10%)
  starting transfers between devices  16.7 us (6%)
    psum x1, blocking collectives, body(): group_sum, coord_sum = lax.psum((group_part, coord_part), 'col')  40.5 us
    pallas_call x1, Pallas kernels, near_field(): pl.pallas_call(near_kernel, grid_spec=pltpu.PrefetchScalarGridSpec(num_sc...  27.4 us
    concatenate x2, other arithmetic, padded(): jnp.concatenate([lax.ppermute(tail, axis, [(i, (i + 1) % count) for i in...  17.7 us
    dot_general x9, matrix products, select_rows(): jnp.dot(onehot, table.reshape(count, -1), preferred_element_type=jnp.floa...  14.6 us
    all_gather x1, blocking collectives, body(): lax.all_gather(group_coords[None], 'row', axis=0, tiled=True)  13.9 us
    dot_general x3, matrix products, body(): jnp.einsum('lab,lbr->lar', kernel, sources[..., dim_count:], preferred_el...  13.3 us
    all_gather x1, blocking collectives, body(): lax.all_gather(group_up[None], 'row', axis=0, tiled=True)  12.9 us
    all_gather x1, blocking collectives, body(): lax.all_gather(node_coords[None], 'col', axis=0, tiled=True)  11.2 us
  transfers between devices with their start and end apart: 6, of which 0 were waited for; matrix products, arithmetic and copies ran while one was open for 36% of the time, Pallas kernels for 0%

commit v1 on v0

--- a/solution.py
+++ b/solution.py
@@ -83,6 +83,77 @@
         ),
         out_shape=jax.ShapeDtypeStruct((leaves, size, rhs), jnp.float32),
     )(flat_index, local_points, *([ext_points] * count), *([ext_weights] * count), *([ext_norms] * count))
+
+
+def far_kernel(index_ref, rank_ref, target_ref, basis_ref, down_ref, leaf_base_ref, near_ref, *refs):
+    count = (len(refs) - 1) // 2
+    source_refs = refs[:count]
+    norm_refs = refs[count : 2 * count]
+    out_ref = refs[-1]
+    leaf = pl.program_id(0)
+    target = target_ref[0]
+    dims = target.shape[-1]
+    target_wide = target.astype(jnp.float32)
+    target_square = jnp.sum(target_wide * target_wide, axis=-1, keepdims=True)
+    scale = -2.0 / dims
+    total = jnp.dot(basis_ref[0], down_ref[...], preferred_element_type=jnp.float32)
+    for position in range(count):
+        source = source_refs[position][0]
+        inner = lax.dot_general(
+            target, source[:, :dims], (((1,), (1,)), ((), ())), preferred_element_type=jnp.float32
+        )
+        distance = target_square + norm_refs[position][0] - 2.0 * inner
+        kernel = jnp.exp(distance * scale).astype(jnp.bfloat16)
+        total = total + jnp.dot(kernel, source[:, dims:], preferred_element_type=jnp.float32)
+    rows = lax.broadcasted_iota(jnp.int32, total.shape, 0)
+    leaf_down = jnp.where(rows < rank_ref[leaf], total, 0.0).astype(jnp.bfloat16)
+    result = jnp.dot(leaf_base_ref[0], leaf_down, preferred_element_type=jnp.float32) + near_ref[0]
+    out_ref[0] = result.astype(out_ref.dtype)
+
+
+def far_field(leaf_coords, skeleton_rows, skeleton_norms, far_local, leaf_rank, bases, node_down, leaf_bases, near_total):
+    leaves, rank, dims = leaf_coords.shape
+    width = skeleton_rows.shape[-1]
+    size = leaf_bases.shape[1]
+    rhs = near_total.shape[-1]
+    count = far_local.shape[1]
+    flat_index = far_local.reshape(-1)
+
+    def source_map(position):
+        return lambda l, index, ranks: (index[l * count + position], 0, 0)
+
+    def own(l, index, ranks):
+        return (l, 0, 0)
+
+    in_specs = [
+        pl.BlockSpec((1, rank, dims), own),
+        pl.BlockSpec((1, rank, bases.shape[-1]), own),
+        pl.BlockSpec(node_down.shape, lambda l, index, ranks: (0, 0)),
+        pl.BlockSpec((1, size, rank), own),
+        pl.BlockSpec((1, size, rhs), own),
+    ]
+    in_specs += [pl.BlockSpec((1, rank, width), source_map(p)) for p in range(count)]
+    in_specs += [pl.BlockSpec((1, 1, rank), source_map(p)) for p in range(count)]
+    return pl.pallas_call(
+        far_kernel,
+        grid_spec=pltpu.PrefetchScalarGridSpec(
+            num_scalar_prefetch=2,
+            grid=(leaves,),
+            in_specs=in_specs,
+            out_specs=pl.BlockSpec((1, size, rhs), own),
+        ),
+        out_shape=jax.ShapeDtypeStruct((leaves, size, rhs), jnp.bfloat16),
+    )(
+        flat_index,
+        leaf_rank,
+        leaf_coords,
+        bases,
+        node_down,
+        leaf_bases,
+        near_total,
+        *([skeleton_rows] * count),
+        *([skeleton_norms] * count),
+    )
 
 
 def select_rows(table, index):
@@ -169,36 +240,28 @@
     node_coords = select_rows(
         leaf_coords.reshape(leaf_count * rank_count, dim_count), node_skeleton[0]
     )
-    column = lax.axis_index("col")
     columns = lax.axis_size("col")
     source_columns = node_far[0] % columns
-    all_coords, all_up = (
-        lax.all_gather(node_coords[None], "col", axis=0, tiled=True),
-        lax.all_gather(node_up[None], "col", axis=0, tiled=True),
-    )
+    node_pack = jnp.concatenate([node_coords, node_up, group_basis], axis=1)
+    gathered = lax.all_gather(node_pack[None], "col", axis=0, tiled=True)
+    all_coords = gathered[:, :, :dim_count]
+    all_up = gathered[:, :, dim_count : dim_count + rhs_count]
+    all_parts = gathered[:, :, dim_count + rhs_count :]
     picked_coords = select_rows(all_coords, source_columns)
     picked_up = select_rows(all_up, source_columns)
     kernel = kernel_block(jnp.broadcast_to(node_coords, picked_coords.shape), picked_coords)
     node_side = jnp.einsum("fab,fbr->ar", kernel, picked_up, preferred_element_type=jnp.float32)
     group_mask = (jnp.arange(group_width, dtype=jnp.int32) < group_rank[0]).astype(jnp.float32)
-    group_part = (
-        jnp.einsum("ag,ar->gr", group_basis, node_up, preferred_element_type=jnp.float32)
+    group_up = (
+        jnp.einsum("nag,nar->gr", all_parts, all_up, preferred_element_type=jnp.float32)
         * group_mask[:, None]
-    )
-    selector = (
-        group_skeleton[0][:, None]
-        == column * node_width + jnp.arange(node_width, dtype=jnp.int32)[None, :]
-    ).astype(jnp.bfloat16)
-    coord_part = jnp.dot(selector, node_coords, preferred_element_type=jnp.float32)
-    group_sum, coord_sum = lax.psum((group_part, coord_part), "col")
-    group_up = group_sum.astype(jnp.bfloat16)
-    group_coords = coord_sum.astype(jnp.bfloat16)
-    every_group_coords, every_group_up = (
-        lax.all_gather(group_coords[None], "row", axis=0, tiled=True),
-        lax.all_gather(group_up[None], "row", axis=0, tiled=True),
-    )
-    picked_group_coords = select_rows(every_group_coords, group_far[0])
-    picked_group_up = select_rows(every_group_up, group_far[0])
+    ).astype(jnp.bfloat16)
+    group_coords = select_rows(all_coords.reshape(columns * node_width, dim_count), group_skeleton[0])
+    group_pack = jnp.concatenate([group_coords, group_up], axis=1)
+    every_group = lax.all_gather(group_pack[None], "row", axis=0, tiled=True)
+    picked_group = select_rows(every_group, group_far[0])
+    picked_group_coords = picked_group[:, :, :dim_count]
+    picked_group_up = picked_group[:, :, dim_count:]
     group_kernel = kernel_block(
         jnp.broadcast_to(group_coords, picked_group_coords.shape), picked_group_coords
     )
@@ -210,22 +273,21 @@
         (jnp.dot(group_basis, group_down, preferred_element_type=jnp.float32) + node_side)
         * node_mask[:, None]
     ).astype(jnp.bfloat16)
-    far_total = jnp.dot(node_basis, node_down, preferred_element_type=jnp.float32).reshape(
-        leaf_count, rank_count, rhs_count
-    )
+    skeleton_wide = skeleton_rows[:, :, :dim_count].astype(jnp.float32)
+    skeleton_norms = jnp.sum(skeleton_wide * skeleton_wide, axis=-1)[:, None, :]
     far_local = far_list - offset
-    for position in range(far_list.shape[1]):
-        sources = select_rows(skeleton_rows, far_local[:, position])
-        kernel = kernel_block(leaf_coords, sources[..., :dim_count])
-        far_total = far_total + jnp.einsum(
-            "lab,lbr->lar", kernel, sources[..., dim_count:], preferred_element_type=jnp.float32
-        )
-    leaf_down = (far_total * leaf_mask[:, :, None]).astype(jnp.bfloat16)
-    result = (
-        jnp.einsum("lpk,lkr->lpr", local_bases, leaf_down, preferred_element_type=jnp.float32)
-        + near_total
-    )
-    return result.astype(jnp.bfloat16).reshape(leaf_count * leaf_size, rhs_count)
+    result = far_field(
+        leaf_coords,
+        skeleton_rows,
+        skeleton_norms,
+        far_local,
+        leaf_rank,
+        node_basis.reshape(leaf_count, rank_count, node_width),
+        node_down,
+        local_bases,
+        near_total,
+    )
+    return result.reshape(leaf_count * leaf_size, rhs_count)
 
 
 def solution(mesh):

time: 263 us -> 185 us (0.70)
  blocking collectives: 89.4 us -> 15.2 us
  matrix products: 52.9 us -> 9.19 us
  waiting for transfers between devices: 0.02 us -> 32.2 us
  Pallas kernels: 27.4 us -> 53.6 us
  local copies, waits for them, and re-layouts: 35.2 us -> 12.1 us
  between operations: 1.82 us -> 15.2 us
  other arithmetic: 36.9 us -> 29.8 us
    psum x1 -> x0, blocking collectives: 40.5 us -> none  [body(): group_sum, coord_sum = lax.psum((group_part, coord_part), 'col')]
    all_gather x4 -> x1, blocking collectives: 48.9 us -> 15.2 us  [body(): every_group = lax.all_gather(group_pack[None], 'row', axis=0, tiled=True)]
    dot_general x8 -> x2, matrix products: 29 us -> 1.22 us  [the longest x1 0.97 us: body(): jnp.dot(group_basis, group_down, preferred_element_type=jnp.float32)]
    pallas_call x0 -> x1, Pallas kernels: none -> 26.1 us  [far_field(): pl.pallas_call(far_kernel, grid_spec=pltpu.PrefetchScalarGridSpec(num_sca...]
    ppermute x3, waiting for transfers between devices: 0.01 us -> 17.4 us  [padded(): lax.ppermute(tail, axis, [(i, (i + 1) % count) for i in range(ends)])]
    ppermute x3, waiting for transfers between devices: 0.01 us -> 14.7 us  [padded(): lax.ppermute(head, axis, [((i + 1) % count, i) for i in range(ends)])]
    dot_general x9 -> x5, matrix products: 14.6 us -> 1.97 us  [select_rows(): jnp.dot(onehot, table.reshape(count, -1), preferred_element_type=jnp.floa...]
    convert_element_type x2 -> x0, other arithmetic: 7.24 us -> none  [the longest x1 7.23 us: body(): result.astype(jnp.bfloat16).reshape(leaf_count * leaf_size, rhs_count)]
  transfers between devices with their start and end apart: 6 -> 7, of which waited for: 0 -> 3; matrix products, arithmetic and copies ran while one was open for 36% -> 20% of each run, Pallas kernels for 0% -> 15%
where the time goes in v1:
time: 185 us; the launch traced here: 183 us
  Pallas kernels  53.6 us (29%)
  waiting for transfers between devices  32.2 us (17%)
  other arithmetic  29.8 us (16%)
  starting transfers between devices  15.5 us (8%)
  blocking collectives  15.2 us (8%)
  between operations  15.2 us (8%)
  local copies, waits for them, and re-layouts  12.1 us (7%)
  matrix products  9.19 us (5%)
    pallas_call x1, Pallas kernels, near_field(): pl.pallas_call(near_kernel, grid_spec=pltpu.PrefetchScalarGridSpec(num_sc...  27.5 us
    pallas_call x1, Pallas kernels, far_field(): pl.pallas_call(far_kernel, grid_spec=pltpu.PrefetchScalarGridSpec(num_sca...  26.1 us
    concatenate x2, other arithmetic, padded(): jnp.concatenate([lax.ppermute(tail, axis, [(i, (i + 1) % count) for i in...  20.9 us
    ppermute x3, waiting for transfers between devices, padded(): lax.ppermute(tail, axis, [(i, (i + 1) % count) for i in range(ends)])  17.4 us
    all_gather x1, blocking collectives, body(): every_group = lax.all_gather(group_pack[None], 'row', axis=0, tiled=True)  15.2 us
    ppermute x3, waiting for transfers between devices, padded(): lax.ppermute(head, axis, [((i + 1) % count, i) for i in range(ends)])  14.7 us
    ppermute x3, starting transfers between devices, padded(): lax.ppermute(head, axis, [((i + 1) % count, i) for i in range(ends)])  8.96 us
    ppermute x3, starting transfers between devices, padded(): lax.ppermute(tail, axis, [(i, (i + 1) % count) for i in range(ends)])  6.54 us
  transfers between devices with their start and end apart: 7, of which 3 were waited for; matrix products, arithmetic and copies ran while one was open for 20% of the time, Pallas kernels for 15%

profile of v1, /device:TPU:2, one launch (start us, length us, event | category | flops | bytes accessed | tf_op | source)
XLA Modules:
  0.0 182.8 jit_solution(17159935731148161708)
XLA Ops:
  6.5 0.9 copy.28
  7.4 0.9 fusion.48
  9.7 2.4 %fusion.3.target_ref = bf16[24,128,128]{2,1,0:T(8,128)(2,1)S(1)} fusion(bf16[24,256,128]{2,1,0:T(8,128)(2,1)} %bitcast.105, s32[24,128]{1,0:T(8,128)} %param.19), kind=kOutput, calls=%fused_computation.18 | convolution fusion | flops 202506240 | bytes 2371584 | tf_op jit(solution)/shard_map/bkp,bpc->bkc/dot_general | solution.py:173
  12.1 0.6 multiply_reduce_fusion.4
  12.7 0.3 copy-done.5
  13.0 2.4 %multiply_convert_fusion = bf16[24,128,256]{2,1,0:T(8,128)(2,1)S(1)} fusion(bf16[24,256,128]{2,1,0:T(8,128)(2,1)} %bitcast.109, bf16[24,256,256]{2,1,0:T(8,128)(2,1)S(1)} %bitcast.104, f32[24,128]{1,0:T(8,128)S(1)} %fusion.48), kind=kOutput, calls=%fused_computation.9 | convolution fusion | flops 404226048 | bytes 6303744 | tf_op jit(solution)/shard_map/lpk,lpr->lkr/dot_general | solution.py:209
  15.4 0.6 fusion.21
  16.1 0.7 pad_maximum_fusion.3
  16.8 1.1 fusion.58
  17.9 2.0 %collective-permute-start = (bf16[2048,128]{1,0:T(8,128)(2,1)}, bf16[2048,128]{1,0:T(8,128)(2,1)}, u32[]{:S(2)}, u32[]{:S(2)}) collective-permute-start(bf16[2048,128]{1,0:T(8,128)(2,1)} %get-tuple-element.10), channel_id=1, source_target_pairs={{0,1},{1,2},{2,3},{3,4},{4,5},{5,6},{6,7},{7,8},{8,9},{9,10},{10,1... | collective-permute-start | bytes 1572872 | tf_op jit(solution)/shard_map/ppermute | solution.py:21
  19.9 3.6 %collective-permute-start.1 = (bf16[2048,128]{1,0:T(8,128)(2,1)}, bf16[2048,128]{1,0:T(8,128)(2,1)}, u32[]{:S(2)}, u32[]{:S(2)}) collective-permute-start(bf16[2048,128]{1,0:T(8,128)(2,1)} %get-tuple-element.9), channel_id=1, source_target_pairs={{1,0},{2,1},{3,2},{4,3},{5,4},{6,5},{7,6},{8,7},{9,8},{10,9},{11,1... | collective-permute-start | bytes 1572872 | tf_op jit(solution)/shard_map/ppermute | solution.py:23
  23.6 3.0 %fusion.57 = (bf16[2048,256]{1,0:T(8,128)(2,1)}, bf16[2048,256]{1,0:T(8,128)(2,1)}) fusion(bf16[6144,256]{1,0:T(8,128)(2,1)} %param.16), kind=kLoop, calls=%fused_computation.96 | loop fusion | bytes 4194304 | tf_op jit(solution)/shard_map/slice | solution.py:18
  26.6 2.0 %collective-permute-start.3 = (bf16[2048,256]{1,0:T(8,128)(2,1)}, bf16[2048,256]{1,0:T(8,128)(2,1)}, u32[]{:S(2)}, u32[]{:S(2)}) collective-permute-start(bf16[2048,256]{1,0:T(8,128)(2,1)} %get-tuple-element.6), channel_id=1, source_target_pairs={{1,0},{2,1},{3,2},{4,3},{5,4},{6,5},{7,6},{8,7},{9,8},{10,9},{11,1... | collective-permute-start | bytes 3145736 | tf_op jit(solution)/shard_map/ppermute | solution.py:23
  28.7 2.4 %collective-permute-start.2 = (bf16[2048,256]{1,0:T(8,128)(2,1)}, bf16[2048,256]{1,0:T(8,128)(2,1)}, u32[]{:S(2)}, u32[]{:S(2)}) collective-permute-start(bf16[2048,256]{1,0:T(8,128)(2,1)} %get-tuple-element.5), channel_id=1, source_target_pairs={{0,1},{1,2},{2,3},{3,4},{4,5},{5,6},{6,7},{7,8},{8,9},{9,10},{10,1... | collective-permute-start | bytes 3145736 | tf_op jit(solution)/shard_map/ppermute | solution.py:21
  31.1 1.4 fusion.23
  32.5 3.3 %collective-permute-start.5 = (bf16[1024,384]{1,0:T(8,128)(2,1)}, bf16[1024,384]{1,0:T(8,128)(2,1)}, u32[]{:S(2)}, u32[]{:S(2)}) collective-permute-start(bf16[1024,384]{1,0:T(8,128)(2,1)} %bitcast.23), channel_id=1, source_target_pairs={{1,0},{2,1},{3,2},{4,3},{5,4},{6,5},{7,6},{8,7},{9,8},{10,9},{11,1... | collective-permute-start | bytes 2359304 | tf_op jit(solution)/shard_map/ppermute | solution.py:23
  36.0 0.6 reshape.121.index_ref
  36.7 0.7 reshape.135.index_ref
  37.4 1.6 pad_maximum_fusion.2
  39.0 16.5 %collective-permute-done = bf16[2048,128]{1,0:T(8,128)(2,1)} collective-permute-done((bf16[2048,128]{1,0:T(8,128)(2,1)}, bf16[2048,128]{1,0:T(8,128)(2,1)}, u32[]{:S(2)}, u32[]{:S(2)}) %collective-permute-start) | collective-permute-done | bytes 524320 | tf_op jit(solution)/shard_map/ppermute | solution.py:21
  55.5 2.1 %collective-permute-start.4 = (bf16[1024,384]{1,0:T(8,128)(2,1)S(1)}, bf16[1024,384]{1,0:T(8,128)(2,1)S(1)}, u32[]{:S(2)}, u32[]{:S(2)}) collective-permute-start(bf16[1024,384]{1,0:T(8,128)(2,1)S(1)} %bitcast.127), channel_id=1, source_target_pairs={{0,1},{1,2},{2,3},{3,4},{4,5},{5,6},{6,7},{7,8},{8,9},{9,10},{10,1... | collective-permute-start | bytes 2359304 | tf_op jit(solution)/shard_map/ppermute | solution.py:21
  57.6 1.1 constant_dynamic-update-slice_fusion.2
  58.7 0.2 constant_dynamic-update-slice_fusion.1
  58.9 1.2 constant_dynamic-update-slice_fusion
  60.1 2.1 %multiply_reduce_fusion = f32[10240]{0:T(1024)} fusion(bf16[10240,128]{1,0:T(8,128)(2,1)S(1)} %constant_dynamic-update-slice_fusion), kind=kLoop, calls=%fused_computation.4 | loop fusion | flops 3921920 | bytes 2662400 | tf_op jit(solution)/shard_map/reduce_sum | solution.py:222
  62.2 14.7 %collective-permute-done.5 = bf16[1024,384]{1,0:T(8,128)(2,1)} collective-permute-done((bf16[1024,384]{1,0:T(8,128)(2,1)}, bf16[1024,384]{1,0:T(8,128)(2,1)}, u32[]{:S(2)}, u32[]{:S(2)}) %collective-permute-start.5) | collective-permute-done | bytes 786464 | tf_op jit(solution)/shard_map/ppermute | solution.py:23
  77.0 0.9 collective-permute-done.4
  77.9 6.7 %pad_maximum_fusion.1 = bf16[5120,384]{1,0:T(8,128)(2,1)S(1)} fusion(bf16[1024,384]{1,0:T(8,128)(2,1)} %collective-permute-done.5, bf16[3072,384]{1,0:T(8,128)(2,1)S(1)} %bitcast.107, bf16[1024,384]{1,0:T(8,128)(2,1)S(1)} %collective-permute-done.4), kind=kLoop, calls=%fused_computation.5 | loop fusion | flops 11796480 | bytes 7864320 | tf_op jit(solution)/shard_map/concatenate | solution.py:19
  84.6 1.9 %multiply_reduce_fusion.1 = f32[40,128]{1,0:T(8,128)} fusion(bf16[40,128,384]{2,1,0:T(8,128)(2,1)S(1)} %bitcast.93), kind=kLoop, calls=%fused_computation.12 | loop fusion | flops 1960960 | bytes 1331200 | tf_op jit(solution)/shard_map/reduce_sum | solution.py:277
  86.5 14.2 %pad_maximum_fusion = bf16[10240,256]{1,0:T(8,128)(2,1)} fusion(bf16[2048,256]{1,0:T(8,128)(2,1)} %collective-permute-done.3, bf16[6144,256]{1,0:T(8,128)(2,1)S(1)} %copy-done.3, bf16[2048,256]{1,0:T(8,128)(2,1)} %collective-permute-done.2), kind=kLoop, calls=%fused_computation.3 | loop fusion | flops 15728640 | bytes 10485760 | tf_op jit(solution)/shard_map/concatenate | solution.py:19
  100.7 27.5 %shard_map.145.near_ref = f32[24,256,256]{2,1,0:T(8,128)} custom-call(s32[120]{0:T(128)} %reshape.135.index_ref, bf16[24,256,128]{2,1,0:T(8,128)(2,1)} %bitcast.106, bf16[40,256,128]{2,1,0:T(8,128)(2,1)} %bitcast.98, bf16[40,256,128]{2,1,0:T(8,128)(2,1)} %bitcast.99, bf16[40,256,128]{2,1,0:T(8,128)(2,1)} %bitcast.100, bf16[40,256,128]{2,1,0:T(8,128)(2,1)} %bitcast.101, ...), custom_call_target="tpu_custom_call" | custom-call | tf_op jit(solution)/shard_map/pallas_call | solution.py:76
  128.3 1.5 copy.42
  129.8 0.3 copy.41
  130.2 0.3 copy.46
  130.5 0.2 copy.39
  130.7 0.4 convolution_convert_fusion.1
  131.1 0.3 fusion.8
  131.4 0.1 multiply_reduce_fusion.2
  131.6 0.3 multiply_reduce_fusion.5
  131.9 0.1 copy.32
  132.0 0.2 fusion.17
  132.3 15.2 %all-gather.1 = bf16[512,384]{1,0:T(8,128)(2,1)S(1)} all-gather(bf16[128,384]{1,0:T(8,128)(2,1)S(1)} %pad_maximum_fusion.4), channel_id=3, replica_groups=mesh['row'=4,'col'=8] {'row'}, dimensions={0}, use_global_device_ids=true | all-gather | bytes 491520 | tf_op jit(solution)/shard_map/all_gather | solution.py:261
  147.5 0.1 reshape.129
  147.7 0.4 convolution_convert_fusion
  148.2 0.2 fusion.18
  148.4 0.4 convolution_bitcast_fusion
  148.8 1.0 fusion.16.down_ref
  149.8 26.1 %shard_map.146 = bf16[24,256,256]{2,1,0:T(8,128)(2,1)} custom-call(s32[96]{0:T(128)} %reshape.121.index_ref, s32[24]{0:T(128)} %rank_ref.1, bf16[24,128,128]{2,1,0:T(8,128)(2,1)} %copy-done.5, bf16[24,128,128]{2,1,0:T(8,128)(2,1)} %bitcast.114, bf16[128,256]{1,0:T(8,128)(2,1)} %fusion.16.down_ref, bf16[24,256,128]{2,1,0:T(8,128)(2,1)} %bitcast.110, ...), custom_call_target="tpu_custom_call" | custom-call | tf_op jit(solution)/shard_map/pallas_call | solution.py:137
  (49 shorter events, 0.7 us)
Async XLA Ops:
  6.5 5.6 %copy-start.12 = (s32[1,128]{1,0:T(1,128)S(1)}, s32[1,128]{1,0:T(1,128)}, u32[]{:S(2)}) copy-start(s32[1,128]{1,0:T(1,128)} %param.24) | copy-start | bytes 1540
  6.5 121.7 %all-gather.4.cloned.1.call-start = ((), (), s32[]{:S(2)}) async-start(), calls=%async_computation | async-start | bytes 1179648 | tf_op jit(solution)/shard_map/all_gather | solution.py:246
  7.4 5.5 %copy-start.2 = (bf16[6144,256]{1,0:T(8,128)(2,1)S(1)}, bf16[6144,256]{1,0:T(8,128)(2,1)}, u32[]{:S(2)}) copy-start(bf16[6144,256]{1,0:T(8,128)(2,1)} %param.16) | copy-start | bytes 9437188
  12.1 0.9 copy-start.5
  13.0 2.5 %copy-start.7 = (bf16[3072,128]{1,0:T(8,128)(2,1)S(1)}, bf16[3072,128]{1,0:T(8,128)(2,1)}, u32[]{:S(2)}) copy-start(bf16[3072,128]{1,0:T(8,128)(2,1)} %param.22) | copy-start | bytes 2359300
  15.4 1.4 copy-start.4
  17.9 13.2 %copy-start.6 = (bf16[24,128,128]{2,1,0:T(8,128)(2,1)S(1)}, bf16[24,128,128]{2,1,0:T(8,128)(2,1)}, u32[]{:S(2)}) copy-start(bf16[24,128,128]{2,1,0:T(8,128)(2,1)} %copy-done.5) | copy-start | bytes 2359300
  17.9 37.6 %collective-permute-start = (bf16[2048,128]{1,0:T(8,128)(2,1)}, bf16[2048,128]{1,0:T(8,128)(2,1)}, u32[]{:S(2)}, u32[]{:S(2)}) collective-permute-start(bf16[2048,128]{1,0:T(8,128)(2,1)} %get-tuple-element.10), channel_id=1, source_target_pairs={{0,1},{1,2},{2,3},{3,4},{4,5},{5,6},{6,7},{7,8},{8,9},{9,10},{10,1... | collective-permute-start | bytes 1572872 | tf_op jit(solution)/shard_map/ppermute | solution.py:21
  19.9 39.0 %collective-permute-start.1 = (bf16[2048,128]{1,0:T(8,128)(2,1)}, bf16[2048,128]{1,0:T(8,128)(2,1)}, u32[]{:S(2)}, u32[]{:S(2)}) collective-permute-start(bf16[2048,128]{1,0:T(8,128)(2,1)} %get-tuple-element.9), channel_id=1, source_target_pairs={{1,0},{2,1},{3,2},{4,3},{5,4},{6,5},{7,6},{8,7},{9,8},{10,9},{11,1... | collective-permute-start | bytes 1572872 | tf_op jit(solution)/shard_map/ppermute | solution.py:23
  26.6 9.3 %copy-start.11 = (s32[24,4]{0,1:T(4,128)S(1)}, s32[24,4]{0,1:T(4,128)}, u32[]{:S(2)}) copy-start(s32[24,4]{0,1:T(4,128)} %param.21) | copy-start | bytes 1156
  26.6 10.0 %copy-start.10 = (s32[24,5]{0,1:T(8,128)S(1)}, s32[24,5]{0,1:T(8,128)}, u32[]{:S(2)}) copy-start(s32[24,5]{0,1:T(8,128)} %param.20) | copy-start | bytes 1444
  26.6 59.9 %collective-permute-start.3 = (bf16[2048,256]{1,0:T(8,128)(2,1)}, bf16[2048,256]{1,0:T(8,128)(2,1)}, u32[]{:S(2)}, u32[]{:S(2)}) collective-permute-start(bf16[2048,256]{1,0:T(8,128)(2,1)} %get-tuple-element.6), channel_id=1, source_target_pairs={{1,0},{2,1},{3,2},{4,3},{5,4},{6,5},{7,6},{8,7},{9,8},{10,9},{11,1... | collective-permute-start | bytes 3145736 | tf_op jit(solution)/shard_map/ppermute | solution.py:23
  28.7 57.8 %collective-permute-start.2 = (bf16[2048,256]{1,0:T(8,128)(2,1)}, bf16[2048,256]{1,0:T(8,128)(2,1)}, u32[]{:S(2)}, u32[]{:S(2)}) collective-permute-start(bf16[2048,256]{1,0:T(8,128)(2,1)} %get-tuple-element.5), channel_id=1, source_target_pairs={{0,1},{1,2},{2,3},{3,4},{4,5},{5,6},{6,7},{7,8},{8,9},{9,10},{10,1... | collective-permute-start | bytes 3145736 | tf_op jit(solution)/shard_map/ppermute | solution.py:21
  32.5 6.5 %copy-start.13 = (s32[1,4]{1,0:T(1,128)S(1)}, s32[1,4]{1,0:T(1,128)}, u32[]{:S(2)}) copy-start(s32[1,4]{1,0:T(1,128)} %param.25) | copy-start | bytes 52
  32.5 44.5 %collective-permute-start.5 = (bf16[1024,384]{1,0:T(8,128)(2,1)}, bf16[1024,384]{1,0:T(8,128)(2,1)}, u32[]{:S(2)}, u32[]{:S(2)}) collective-permute-start(bf16[1024,384]{1,0:T(8,128)(2,1)} %bitcast.23), channel_id=1, source_target_pairs={{1,0},{2,1},{3,2},{4,3},{5,4},{6,5},{7,6},{8,7},{9,8},{10,9},{11,1... | collective-permute-start | bytes 2359304 | tf_op jit(solution)/shard_map/ppermute | solution.py:23
  37.4 18.1 %copy-start.8 = (bf16[8,128,384]{2,1,0:T(8,128)(2,1)S(1)}, bf16[8,128,384]{2,1,0:T(8,128)(2,1)}, u32[]{:S(2)}) copy-start(bf16[8,128,384]{2,1,0:T(8,128)(2,1)} %get-tuple-element.7) | copy-start | bytes 2359300
  55.5 22.4 %collective-permute-start.4 = (bf16[1024,384]{1,0:T(8,128)(2,1)S(1)}, bf16[1024,384]{1,0:T(8,128)(2,1)S(1)}, u32[]{:S(2)}, u32[]{:S(2)}) collective-permute-start(bf16[1024,384]{1,0:T(8,128)(2,1)S(1)} %bitcast.127), channel_id=1, source_target_pairs={{0,1},{1,2},{2,3},{3,4},{4,5},{5,6},{6,7},{7,8},{8,9},{9,10},{10,1... | collective-permute-start | bytes 2359304 | tf_op jit(solution)/shard_map/ppermute | solution.py:21
  60.1 24.4 %copy-start.1 = (bf16[10240,128]{1,0:T(8,128)(2,1)}, bf16[10240,128]{1,0:T(8,128)(2,1)S(1)}, u32[]{:S(2)}) copy-start(bf16[10240,128]{1,0:T(8,128)(2,1)S(1)} %constant_dynamic-update-slice_fusion) | copy-start | bytes 7864324
  77.9 8.6 %copy-start.3 = (bf16[6144,256]{1,0:T(8,128)(2,1)S(1)}, bf16[6144,256]{1,0:T(8,128)(2,1)}, u32[]{:S(2)}) copy-start(bf16[6144,256]{1,0:T(8,128)(2,1)} %param.16) | copy-start | bytes 9437188
  84.5 16.2 %copy-start = (bf16[5120,384]{1,0:T(8,128)(2,1)}, bf16[5120,384]{1,0:T(8,128)(2,1)S(1)}, u32[]{:S(2)}) copy-start(bf16[5120,384]{1,0:T(8,128)(2,1)S(1)} %pad_maximum_fusion.1) | copy-start | bytes 11796484
  129.8 1.7 copy-start.14
  130.2 17.5 %copy-start.15 = (s32[1,2]{1,0:T(1,128)S(1)}, s32[1,2]{1,0:T(1,128)}, u32[]{:S(2)}) copy-start(s32[1,2]{1,0:T(1,128)} %param.29) | copy-start | bytes 28
  131.5 17.3 %copy-start.9 = (bf16[128,128]{1,0:T(8,128)(2,1)S(1)}, bf16[128,128]{1,0:T(8,128)(2,1)}, u32[]{:S(2)}) copy-start(bf16[128,128]{1,0:T(8,128)(2,1)} %param.26) | copy-start | bytes 98308
Sparse Core Ops, SparseCore 0:
  16.9 49.8 all-gather.3

commit v2 on v1

v2 whole, which is shorter than its diff:
```python
import jax
import jax.numpy as jnp
from jax import lax
from jax.experimental import pallas as pl
from jax.experimental.pallas import tpu as pltpu
from jax.sharding import PartitionSpec as P

REACH = 8
FLAT = ("row", "col")


def halos(cells, width):
    count = lax.axis_size(FLAT)
    ends = count - 1
    head = cells[:width]
    tail = cells[cells.shape[0] - width :]
    left = lax.ppermute(tail, FLAT, [(i, i + 1) for i in range(ends)])
    right = lax.ppermute(head, FLAT, [(i + 1, i) for i in range(ends)])
    return left, right


def kernel_block(left, right):
    left_square = jnp.sum(jnp.square(left.astype(jnp.float32)), axis=-1)
    right_square = jnp.sum(jnp.square(right.astype(jnp.float32)), axis=-1)
    inner = jnp.einsum("...md,...nd->...mn", left, right, preferred_element_type=jnp.float32)
    distance = left_square[..., :, None] + right_square[..., None, :] - 2.0 * inner
    return jnp.exp(distance * (-2.0 / left.shape[-1])).astype(jnp.bfloat16)


def contract_last(a, b):
    return lax.dot_general(a, b, (((1,), (1,)), ((), ())), preferred_element_type=jnp.float32)


def scaled_kernel(target, target_square, source):
    dims = target.shape[-1]
    scale = -2.0 / dims
    wide = source.astype(jnp.float32)
    square = wide * wide
    high = square.astype(jnp.bfloat16)
    low = (square - high.astype(jnp.float32)).astype(jnp.bfloat16)
    ones = jnp.ones((8, dims), jnp.bfloat16)
    source_square = (contract_last(ones, high) + contract_last(ones, low))[0:1] * scale
    inner = contract_last(target * jnp.asarray(-2.0 * scale, target.dtype), source)
    return jnp.exp((target_square + source_square) + inner).astype(jnp.bfloat16)


def target_square_of(target):
    wide = target.astype(jnp.float32)
    return jnp.sum(wide * wide, axis=-1, keepdims=True) * (-2.0 / target.shape[-1])


def fetch_sources(index_ref, row, count, parts, buffers, sems, slot):
    for position in range(count):
        source = index_ref[row * count + position]
        for which, (left, own, right) in enumerate(parts):
            halo = left.shape[0]
            mine = own.shape[0]
            target = buffers[which].at[slot, position]
            sem = sems.at[which, slot, position]

            @pl.when(source < halo)
            def _():
                pltpu.make_async_copy(left.at[source], target, sem).start()

            @pl.when((source >= halo) & (source < halo + mine))
            def _():
                pltpu.make_async_copy(own.at[source - halo], target, sem).start()

            @pl.when(source >= halo + mine)
            def _():
                pltpu.make_async_copy(right.at[source - halo - mine], target, sem).start()


def wait_sources(count, parts, buffers, sems, slot):
    for position in range(count):
        for which, (left, own, right) in enumerate(parts):
            pltpu.make_async_copy(
                own.at[0], buffers[which].at[slot, position], sems.at[which, slot, position]
            ).wait()


def pipelined_sources(index_ref, count, parts, buffers, sems):
    leaf = pl.program_id(0)
    leaves = pl.num_programs(0)
    slot = leaf % 2

    @pl.when(leaf == 0)
    def _():
        fetch_sources(index_ref, 0, count, parts, buffers, sems, 0)

    @pl.when(leaf + 1 < leaves)
    def _():
        fetch_sources(index_ref, leaf + 1, count, parts, buffers, sems, 1 - slot)

    wait_sources(count, parts, buffers, sems, slot)
    return slot


def near_kernel(index_ref, target_ref, lp, op, rp, lw, ow, rw, out_ref, point_buf, weight_buf, sems):
    count = point_buf.shape[1]
    parts = ((lp, op, rp), (lw, ow, rw))
    slot = pipelined_sources(index_ref, count, parts, (point_buf, weight_buf), sems)
    target = target_ref[0]
    target_square = target_square_of(target)
    total = None
    for position in range(count):
        kernel = scaled_kernel(target, target_square, point_buf[slot, position])
        part = jnp.dot(kernel, weight_buf[slot, position], preferred_element_type=jnp.float32)
        total = part if total is None else total + part
    out_ref[0] = total


def near_field(local_points, left_points, right_points, local_weights, left_weights, right_weights, near_local):
    leaves, size, dims = local_points.shape
    rhs = local_weights.shape[-1]
    count = near_local.shape[1]
    anywhere = pl.BlockSpec(memory_space=pl.ANY)
    return pl.pallas_call(
        near_kernel,
        grid_spec=pltpu.PrefetchScalarGridSpec(
            num_scalar_prefetch=1,
            grid=(leaves,),
            in_specs=[pl.BlockSpec((1, size, dims), lambda l, index: (l, 0, 0))] + [anywhere] * 6,
            out_specs=pl.BlockSpec((1, size, rhs), lambda l, index: (l, 0, 0)),
            scratch_shapes=[
                pltpu.VMEM((2, count, size, dims), local_points.dtype),
                pltpu.VMEM((2, count, size, rhs), local_weights.dtype),
                pltpu.SemaphoreType.DMA((2, 2, count)),
            ],
        ),
        out_shape=jax.ShapeDtypeStruct((leaves, size, rhs), jnp.float32),
        compiler_params=pltpu.CompilerParams(dimension_semantics=("arbitrary",)),
    )(
        near_local.reshape(-1),
        local_points,
        left_points,
        local_points,
        right_points,
        left_weights,
        local_weights,
        right_weights,
    )


def far_kernel(index_ref, rank_ref, target_ref, basis_ref, down_ref, leaf_base_ref, near_ref, ls, os, rs, out_ref, source_buf, sems):
    count = source_buf.shape[1]
    slot = pipelined_sources(index_ref, count, ((ls, os, rs),), (source_buf,), sems)
    leaf = pl.program_id(0)
    target = target_ref[0]
    dims = target.shape[-1]
    target_square = target_square_of(target)
    total = jnp.dot(basis_ref[0], down_ref[...], preferred_element_type=jnp.float32)
    for position in range(count):
        source = source_buf[slot, position]
        kernel = scaled_kernel(target, target_square, source[:, :dims])
        total = total + jnp.dot(kernel, source[:, dims:], preferred_element_type=jnp.float32)
    rows = lax.broadcasted_iota(jnp.int32, total.shape, 0)
    leaf_down = jnp.where(rows < rank_ref[leaf], total, 0.0).astype(jnp.bfloat16)
    result = jnp.dot(leaf_base_ref[0], leaf_down, preferred_element_type=jnp.float32) + near_ref[0]
    out_ref[0] = result.astype(out_ref.dtype)


def far_field(leaf_coords, left_rows, own_rows, right_rows, far_local, leaf_rank, bases, node_down, leaf_bases, near_total):
    leaves, rank, dims = leaf_coords.shape
    width = own_rows.shape[-1]
    size = leaf_bases.shape[1]
    rhs = near_total.shape[-1]
    count = far_local.shape[1]

    def own(l, index, ranks):
        return (l, 0, 0)

    anywhere = pl.BlockSpec(memory_space=pl.ANY)
    in_specs = [
        pl.BlockSpec((1, rank, dims), own),
        pl.BlockSpec((1, rank, bases.shape[-1]), own),
        pl.BlockSpec(node_down.shape, lambda l, index, ranks: (0, 0)),
        pl.BlockSpec((1, size, rank), own),
        pl.BlockSpec((1, size, rhs), own),
        anywhere,
        anywhere,
        anywhere,
    ]
    return pl.pallas_call(
        far_kernel,
        grid_spec=pltpu.PrefetchScalarGridSpec(
            num_scalar_prefetch=2,
            grid=(leaves,),
            in_specs=in_specs,
            out_specs=pl.BlockSpec((1, size, rhs), own),
            scratch_shapes=[
                pltpu.VMEM((2, count, rank, width), own_rows.dtype),
                pltpu.SemaphoreType.DMA((1, 2, count)),
            ],
        ),
        out_shape=jax.ShapeDtypeStruct((leaves, size, rhs), jnp.bfloat16),
        compiler_params=pltpu.CompilerParams(dimension_semantics=("arbitrary",)),
    )(
        far_local.reshape(-1),
        leaf_rank,
        leaf_coords,
        bases,
        node_down,
        leaf_bases,
        near_total,
        left_rows,
        own_rows,
        right_rows,
    )


def select_rows(table, index):
    count = table.shape[0]
    onehot = (index[:, None] == jnp.arange(count, dtype=jnp.int32)[None, :]).astype(table.dtype)
    picked = jnp.dot(onehot, table.reshape(count, -1), preferred_element_type=jnp.float32).astype(
        table.dtype
    )
    return picked.reshape(index.shape + table.shape[1:])


def select_within(table, index):
    count = table.shape[1]
    onehot = (index[:, :, None] == jnp.arange(count, dtype=jnp.int32)[None, None, :]).astype(
        table.dtype
    )
    return jnp.einsum("bkp,bpc->bkc", onehot, table, preferred_element_type=jnp.float32).astype(
        table.dtype
    )


def body(
    points,
    weights,
    leaf_basis,
    leaf_rank,
    leaf_skeleton,
    near_list,
    far_list,
    node_basis,
    node_rank,
    node_skeleton,
    node_far,
    group_basis,
    group_rank,
    group_skeleton,
    group_far,
):
    leaf_count = leaf_rank.shape[0]
    leaf_size = points.shape[0] // leaf_count
    dim_count = points.shape[1]
    rhs_count = weights.shape[1]
    rank_count = leaf_basis.shape[1]
    node_width = node_basis.shape[1]
    group_width = group_basis.shape[1]
    local_points = points.reshape(leaf_count, leaf_size, dim_count)
    local_bases = leaf_basis.reshape(leaf_count, leaf_size, rank_count)
    local_weights = weights.reshape(leaf_count, leaf_size, rhs_count)
    first_leaf = lax.axis_index(FLAT) * leaf_count
    offset = first_leaf - REACH

    left_points, right_points = halos(points, REACH * leaf_size)
    left_weights, right_weights = halos(weights, REACH * leaf_size)

    leaf_mask = (
        lax.broadcasted_iota(jnp.int32, (leaf_count, rank_count), 1) < leaf_rank[:, None]
    ).astype(jnp.float32)
    leaf_up = (
        jnp.einsum("lpk,lpr->lkr", local_bases, local_weights, preferred_element_type=jnp.float32)
        * leaf_mask[:, :, None]
    ).astype(jnp.bfloat16)
    leaf_coords = select_within(local_points, leaf_skeleton)
    own_rows = jnp.concatenate([leaf_coords, leaf_up], axis=-1)
    skeleton_width = dim_count + rhs_count
    left_rows, right_rows = halos(
        own_rows.reshape(leaf_count * rank_count, skeleton_width), REACH * rank_count
    )

    node_mask = (jnp.arange(node_width, dtype=jnp.int32) < node_rank[0]).astype(jnp.float32)
    node_up = (
        jnp.einsum(
            "ak,ar->kr",
            node_basis,
            leaf_up.reshape(leaf_count * rank_count, rhs_count),
            preferred_element_type=jnp.float32,
        )
        * node_mask[:, None]
    ).astype(jnp.bfloat16)
    node_coords = select_rows(
        leaf_coords.reshape(leaf_count * rank_count, dim_count), node_skeleton[0]
    )
    columns = lax.axis_size("col")
    source_columns = node_far[0] % columns
    node_pack = jnp.concatenate([node_coords, node_up, group_basis], axis=1)
    gathered = lax.all_gather(node_pack[None], "col", axis=0, tiled=True)

    near_total = near_field(
        local_points,
        left_points.reshape(REACH, leaf_size, dim_count),
        right_points.reshape(REACH, leaf_size, dim_count),
        local_weights,
        left_weights.reshape(REACH, leaf_size, rhs_count),
        right_weights.reshape(REACH, leaf_size, rhs_count),
        near_list - offset,
    )

    all_coords = gathered[:, :, :dim_count]
    all_up = gathered[:, :, dim_count : dim_count + rhs_count]
    all_parts = gathered[:, :, dim_count + rhs_count :]
    picked_coords = select_rows(all_coords, source_columns)
    picked_up = select_rows(all_up, source_columns)
    kernel = kernel_block(jnp.broadcast_to(node_coords, picked_coords.shape), picked_coords)
    node_side = jnp.einsum("fab,fbr->ar", kernel, picked_up, preferred_element_type=jnp.float32)
    group_mask = (jnp.arange(group_width, dtype=jnp.int32) < group_rank[0]).astype(jnp.float32)
    group_up = (
        jnp.einsum("nag,nar->gr", all_parts, all_up, preferred_element_type=jnp.float32)
        * group_mask[:, None]
    ).astype(jnp.bfloat16)
    group_coords = select_rows(all_coords.reshape(columns * node_width, dim_count), group_skeleton[0])
    group_pack = jnp.concatenate([group_coords, group_up], axis=1)
    every_group = lax.all_gather(group_pack[None], "row", axis=0, tiled=True)
    picked_group = select_rows(every_group, group_far[0])
    picked_group_coords = picked_group[:, :, :dim_count]
    picked_group_up = picked_group[:, :, dim_count:]
    group_kernel = kernel_block(
        jnp.broadcast_to(group_coords, picked_group_coords.shape), picked_group_coords
    )
    group_down = (
        jnp.einsum("fab,fbr->ar", group_kernel, picked_group_up, preferred_element_type=jnp.float32)
        * group_mask[:, None]
    ).astype(jnp.bfloat16)
    node_down = (
        (jnp.dot(group_basis, group_down, preferred_element_type=jnp.float32) + node_side)
        * node_mask[:, None]
    ).astype(jnp.bfloat16)
    result = far_field(
        leaf_coords,
        left_rows.reshape(REACH, rank_count, skeleton_width),
        own_rows,
        right_rows.reshape(REACH, rank_count, skeleton_width),
        far_list - offset,
        leaf_rank,
        node_basis.reshape(leaf_count, rank_count, node_width),
        node_down,
        local_bases,
        near_total,
    )
    return result.reshape(leaf_count * leaf_size, rhs_count)


def solution(mesh):
    in_specs = (
        P(FLAT, None),
        P(FLAT, None),
        P(FLAT, None),
        P(FLAT),
        P(FLAT, None),
        P(FLAT, None),
        P(FLAT, None),
        P(FLAT, None),
        P(FLAT),
        P(FLAT, None),
        P(FLAT, None),
        P(FLAT, None),
        P("row"),
        P("row", None),
        P("row", None),
    )
    out_specs = P(FLAT, None)
    return jax.shard_map(body, mesh=mesh, in_specs=in_specs, out_specs=out_specs, check_vma=False)
```

time: 185 us -> 167 us (0.903)
  other arithmetic: 29.8 us -> 4.97 us
  Pallas kernels: 53.6 us -> 62.3 us
    concatenate x4 -> x2, other arithmetic: 23.9 us -> 3.28 us  [body(): own_rows = jnp.concatenate([leaf_coords, leaf_up], axis=-1)]
    pallas_call x1, Pallas kernels: 26.1 us -> 32 us  [far_field(): pl.pallas_call(far_kernel, grid_spec=pltpu.PrefetchScalarGridSpec(num_sca...]
    reduce_sum x2 -> x0, other arithmetic: 4.07 us -> none  [the longest x1 2.14 us: body(): ext_norms = jnp.sum(ext_wide * ext_wide, axis=-1)[:, None, :]]
    pallas_call x1, Pallas kernels: 27.5 us -> 30.3 us  [near_field(): pl.pallas_call(near_kernel, grid_spec=pltpu.PrefetchScalarGridSpec(num_sc...]
    unnamed x40 -> x34, local copies, waits for them, and re-layouts: 4.94 us -> 4.5 us
  transfers between devices with their start and end apart: 7 -> 7, of which waited for: 3 -> 1; matrix products, arithmetic and copies ran while one was open for 20% -> 9% of each run, Pallas kernels for 15% -> 18%
where the time goes in v2:
time: 167 us; the launch traced here: 165 us
  Pallas kernels  62.3 us (37%)
  waiting for transfers between devices  31.6 us (19%)
  starting transfers between devices  16 us (10%)
  blocking collectives  15.5 us (9%)
  between operations  15.1 us (9%)
  local copies, waits for them, and re-layouts  10.6 us (6%)
  matrix products  9.34 us (6%)
  other arithmetic  4.97 us (3%)
    pallas_call x1, Pallas kernels, far_field(): pl.pallas_call(far_kernel, grid_spec=pltpu.PrefetchScalarGridSpec(num_sca...  32 us
    ppermute x3, waiting for transfers between devices, halos(): left = lax.ppermute(tail, FLAT, [(i, i + 1) for i in range(ends)])  31.6 us
    pallas_call x1, Pallas kernels, near_field(): pl.pallas_call(near_kernel, grid_spec=pltpu.PrefetchScalarGridSpec(num_sc...  30.3 us
    all_gather x1, blocking collectives, body(): every_group = lax.all_gather(group_pack[None], 'row', axis=0, tiled=True)  15.5 us
    ppermute x3, starting transfers between devices, halos(): right = lax.ppermute(head, FLAT, [(i + 1, i) for i in range(ends)])  9.33 us
    ppermute x3, starting transfers between devices, halos(): left = lax.ppermute(tail, FLAT, [(i, i + 1) for i in range(ends)])  6.63 us
    unnamed x34, local copies, waits for them, and re-layouts  4.5 us
    slice x2, local copies, waits for them, and re-layouts, halos(): head = cells[:width]  4.21 us
  transfers between devices with their start and end apart: 7, of which 1 were waited for; matrix products, arithmetic and copies ran while one was open for 9% of the time, Pallas kernels for 18%

profile of v2, /device:TPU:2, one launch (start us, length us, event | category | flops | bytes accessed | tf_op | source)
XLA Modules:
  0.0 165.4 jit_solution(6602683185255376030)
XLA Ops:
  6.5 0.7 fusion.48
  8.6 0.9 copy.28
  9.5 2.5 %fusion.3.target_ref = bf16[24,128,128]{2,1,0:T(8,128)(2,1)S(1)} fusion(bf16[24,256,128]{2,1,0:T(8,128)(2,1)} %bitcast.91, s32[24,128]{1,0:T(8,128)} %param.19), kind=kOutput, calls=%fused_computation.14 | convolution fusion | flops 202506240 | bytes 2371584 | tf_op jit(solution)/shard_map/bkp,bpc->bkc/dot_general | solution.py:226
  12.0 0.6 multiply_reduce_fusion.2
  12.6 0.3 copy-done.2
  12.9 2.4 %multiply_convert_fusion = bf16[24,128,256]{2,1,0:T(8,128)(2,1)S(1)} fusion(bf16[24,256,128]{2,1,0:T(8,128)(2,1)} %bitcast.95, bf16[24,256,256]{2,1,0:T(8,128)(2,1)S(1)} %bitcast.90, f32[24,128]{1,0:T(8,128)S(1)} %fusion.48), kind=kOutput, calls=%fused_computation.6 | convolution fusion | flops 404226048 | bytes 6303744 | tf_op jit(solution)/shard_map/lpk,lpr->lkr/dot_general | solution.py:268
  15.3 0.6 fusion.21
  16.0 0.7 pad_maximum_fusion.1
  16.6 0.0 all-gather.4.cloned.1.call-update
  16.7 0.0 copy-start.1
  16.7 3.1 %fusion.57 = (bf16[2048,256]{1,0:T(8,128)(2,1)}, bf16[2048,256]{1,0:T(8,128)(2,1)}) fusion(bf16[6144,256]{1,0:T(8,128)(2,1)} %param.16), kind=kLoop, calls=%fused_computation.89 | loop fusion | bytes 4194304 | tf_op jit(solution)/shard_map/slice | solution.py:15
  19.8 2.0 %collective-permute-start.2 = (bf16[2048,256]{1,0:T(8,128)(2,1)}, bf16[2048,256]{1,0:T(8,128)(2,1)}, u32[]{:S(2)}, u32[]{:S(2)}) collective-permute-start(bf16[2048,256]{1,0:T(8,128)(2,1)} %get-tuple-element.6), channel_id=1, source_target_pairs={{0,1},{1,2},{2,3},{3,4},{4,5},{5,6},{6,7},{7,8},{8,9},{9,10},{10,1... | collective-permute-start | bytes 3145736 | tf_op jit(solution)/shard_map/ppermute | solution.py:17
  21.8 3.6 %collective-permute-start.3 = (bf16[2048,256]{1,0:T(8,128)(2,1)}, bf16[2048,256]{1,0:T(8,128)(2,1)}, u32[]{:S(2)}, u32[]{:S(2)}) collective-permute-start(bf16[2048,256]{1,0:T(8,128)(2,1)} %get-tuple-element.5), channel_id=1, source_target_pairs={{1,0},{2,1},{3,2},{4,3},{5,4},{6,5},{7,6},{8,7},{9,8},{10,9},{11,1... | collective-permute-start | bytes 3145736 | tf_op jit(solution)/shard_map/ppermute | solution.py:18
  25.5 1.1 fusion.58
  26.6 1.9 %collective-permute-start = (bf16[2048,128]{1,0:T(8,128)(2,1)}, bf16[2048,128]{1,0:T(8,128)(2,1)}, u32[]{:S(2)}, u32[]{:S(2)}) collective-permute-start(bf16[2048,128]{1,0:T(8,128)(2,1)} %get-tuple-element.10), channel_id=1, source_target_pairs={{0,1},{1,2},{2,3},{3,4},{4,5},{5,6},{6,7},{7,8},{8,9},{9,10},{10,1... | collective-permute-start | bytes 1572872 | tf_op jit(solution)/shard_map/ppermute | solution.py:17
  28.5 3.8 %collective-permute-start.1 = (bf16[2048,128]{1,0:T(8,128)(2,1)}, bf16[2048,128]{1,0:T(8,128)(2,1)}, u32[]{:S(2)}, u32[]{:S(2)}) collective-permute-start(bf16[2048,128]{1,0:T(8,128)(2,1)} %get-tuple-element.9), channel_id=1, source_target_pairs={{1,0},{2,1},{3,2},{4,3},{5,4},{6,5},{7,6},{8,7},{9,8},{10,9},{11,1... | collective-permute-start | bytes 1572872 | tf_op jit(solution)/shard_map/ppermute | solution.py:18
  32.3 1.4 fusion.24
  33.8 2.7 %collective-permute-start.4 = (bf16[1024,384]{1,0:T(8,128)(2,1)}, bf16[1024,384]{1,0:T(8,128)(2,1)S(1)}, u32[]{:S(2)}, u32[]{:S(2)}) collective-permute-start(bf16[1024,384]{1,0:T(8,128)(2,1)} %bitcast.22), channel_id=1, source_target_pairs={{0,1},{1,2},{2,3},{3,4},{4,5},{5,6},{6,7},{7,8},{8,9},{9,10},{10,1... | collective-permute-start | bytes 2359304 | tf_op jit(solution)/shard_map/ppermute | solution.py:17
  36.5 0.1 copy.35
  36.6 0.1 copy.36
  36.7 0.6 reshape.140.index_ref
  37.3 0.1 copy.26
  37.4 0.6 reshape.126.index_ref
  38.0 1.8 %pad_maximum_fusion.os = bf16[24,128,384]{2,1,0:T(8,128)(2,1)} fusion(bf16[24,128,128]{2,1,0:T(8,128)(2,1)S(1)} %copy-done.4, bf16[24,128,256]{2,1,0:T(8,128)(2,1)S(1)} %multiply_convert_fusion), kind=kLoop, calls=%fused_computation.5 | loop fusion | flops 4718592 | bytes 4718592 | tf_op jit(solution)/shard_map/concatenate | solution.py:272
  39.9 31.6 %collective-permute-done = bf16[2048,128]{1,0:T(8,128)(2,1)} collective-permute-done((bf16[2048,128]{1,0:T(8,128)(2,1)}, bf16[2048,128]{1,0:T(8,128)(2,1)}, u32[]{:S(2)}, u32[]{:S(2)}) %collective-permute-start) | collective-permute-done | bytes 524320 | tf_op jit(solution)/shard_map/ppermute | solution.py:17
  71.5 1.9 %collective-permute-start.5 = (bf16[1024,384]{1,0:T(8,128)(2,1)}, bf16[1024,384]{1,0:T(8,128)(2,1)}, u32[]{:S(2)}, u32[]{:S(2)}) collective-permute-start(bf16[1024,384]{1,0:T(8,128)(2,1)} %bitcast.24), channel_id=1, source_target_pairs={{1,0},{2,1},{3,2},{4,3},{5,4},{6,5},{7,6},{8,7},{9,8},{10,9},{11,1... | collective-permute-start | bytes 2359304 | tf_op jit(solution)/shard_map/ppermute | solution.py:18
  73.4 30.3 %shard_map.145.near_ref = f32[24,256,256]{2,1,0:T(8,128)} custom-call(s32[120]{0:T(128)} %reshape.140.index_ref, bf16[24,256,128]{2,1,0:T(8,128)(2,1)} %bitcast.92, bf16[8,256,128]{2,1,0:T(8,128)(2,1)} %bitcast.18.lp, bf16[24,256,128]{2,1,0:T(8,128)(2,1)} %bitcast.93, bf16[8,256,128]{2,1,0:T(8,128)(2,1)} %bitcast.19.rp, bf16[8,256,256]{2,1,0:T(8,128)(2,1)} %bitcast.20.lw, ...), custom_call_target="tpu_custom_call" | custom-call | tf_op jit(solution)/shard_map/pallas_call | solution.py:118
  103.7 0.0 all-gather.4.cloned.1.call-done
  103.7 1.5 copy.42
  105.3 0.3 copy.41
  105.7 0.2 copy.39
  105.9 0.0 copy-done.12
  105.9 0.3 multiply_reduce_fusion.3
  106.2 0.1 copy.32
  106.4 0.2 fusion.17
  106.6 15.5 %all-gather.1 = bf16[512,384]{1,0:T(8,128)(2,1)S(1)} all-gather(bf16[128,384]{1,0:T(8,128)(2,1)S(1)} %pad_maximum_fusion.2), channel_id=3, replica_groups=mesh['row'=4,'col'=8] {'row'}, dimensions={0}, use_global_device_ids=true | all-gather | bytes 491520 | tf_op jit(solution)/shard_map/all_gather | solution.py:320
  122.2 0.1 reshape.134
  122.3 0.4 convolution_convert_fusion
  122.8 0.3 copy.46
  123.1 0.3 fusion.8
  123.4 0.4 convolution_convert_fusion.1
  123.8 0.1 multiply_reduce_fusion.1
  123.9 0.1 multiply_reduce_fusion
  124.0 0.4 convolution_bitcast_fusion
  124.4 0.2 fusion.18
  124.6 1.0 fusion.16.down_ref
  125.6 0.9 copy-done.6
  126.5 32.0 %shard_map.146 = bf16[24,256,256]{2,1,0:T(8,128)(2,1)} custom-call(s32[96]{0:T(128)} %reshape.126.index_ref, s32[24]{0:T(128)} %rank_ref.1, bf16[24,128,128]{2,1,0:T(8,128)(2,1)} %copy-done.2, bf16[24,128,128]{2,1,0:T(8,128)(2,1)} %bitcast.100, bf16[128,256]{1,0:T(8,128)(2,1)} %fusion.16.down_ref, bf16[24,256,128]{2,1,0:T(8,128)(2,1)} %bitcast.96, ...), custom_call_target="tpu_custom_call" | custom-call | tf_op jit(solution)/shard_map/pallas_call | solution.py:184
  (38 shorter events, 0.2 us)
Async XLA Ops:
  6.5 5.5 %copy-start.10 = (s32[1,128]{1,0:T(1,128)S(1)}, s32[1,128]{1,0:T(1,128)}, u32[]{:S(2)}) copy-start(s32[1,128]{1,0:T(1,128)} %param.24) | copy-start | bytes 1540
  6.5 97.2 %all-gather.4.cloned.1.call-start = ((), (), s32[]{:S(2)}) async-start(), calls=%async_computation | async-start | bytes 1179648 | tf_op jit(solution)/shard_map/all_gather | solution.py:294
  9.5 3.4 %copy-start = (bf16[6144,256]{1,0:T(8,128)(2,1)S(1)}, bf16[6144,256]{1,0:T(8,128)(2,1)}, u32[]{:S(2)}) copy-start(bf16[6144,256]{1,0:T(8,128)(2,1)} %param.16) | copy-start | bytes 9437188
  12.0 0.9 copy-start.2
  12.9 2.5 %copy-start.5 = (bf16[3072,128]{1,0:T(8,128)(2,1)S(1)}, bf16[3072,128]{1,0:T(8,128)(2,1)}, u32[]{:S(2)}) copy-start(bf16[3072,128]{1,0:T(8,128)(2,1)} %param.22) | copy-start | bytes 2359300
  16.7 8.8 %copy-start.1 = (bf16[6144,128]{1,0:T(8,128)(2,1)S(1)}, bf16[6144,128]{1,0:T(8,128)(2,1)}, u32[]{:S(2)}) copy-start(bf16[6144,128]{1,0:T(8,128)(2,1)} %param.15) | copy-start | bytes 4718596
  19.8 12.5 %copy-start.3 = (bf16[24,128,128]{2,1,0:T(8,128)(2,1)S(1)}, bf16[24,128,128]{2,1,0:T(8,128)(2,1)}, u32[]{:S(2)}) copy-start(bf16[24,128,128]{2,1,0:T(8,128)(2,1)} %copy-done.2) | copy-start | bytes 2359300
  19.8 53.6 %collective-permute-start.2 = (bf16[2048,256]{1,0:T(8,128)(2,1)}, bf16[2048,256]{1,0:T(8,128)(2,1)}, u32[]{:S(2)}, u32[]{:S(2)}) collective-permute-start(bf16[2048,256]{1,0:T(8,128)(2,1)} %get-tuple-element.6), channel_id=1, source_target_pairs={{0,1},{1,2},{2,3},{3,4},{4,5},{5,6},{6,7},{7,8},{8,9},{9,10},{10,1... | collective-permute-start | bytes 3145736 | tf_op jit(solution)/shard_map/ppermute | solution.py:17
  21.8 51.6 %collective-permute-start.3 = (bf16[2048,256]{1,0:T(8,128)(2,1)}, bf16[2048,256]{1,0:T(8,128)(2,1)}, u32[]{:S(2)}, u32[]{:S(2)}) collective-permute-start(bf16[2048,256]{1,0:T(8,128)(2,1)} %get-tuple-element.5), channel_id=1, source_target_pairs={{1,0},{2,1},{3,2},{4,3},{5,4},{6,5},{7,6},{8,7},{9,8},{10,9},{11,1... | collective-permute-start | bytes 3145736 | tf_op jit(solution)/shard_map/ppermute | solution.py:18
  26.6 44.9 %collective-permute-start = (bf16[2048,128]{1,0:T(8,128)(2,1)}, bf16[2048,128]{1,0:T(8,128)(2,1)}, u32[]{:S(2)}, u32[]{:S(2)}) collective-permute-start(bf16[2048,128]{1,0:T(8,128)(2,1)} %get-tuple-element.10), channel_id=1, source_target_pairs={{0,1},{1,2},{2,3},{3,4},{4,5},{5,6},{6,7},{7,8},{8,9},{9,10},{10,1... | collective-permute-start | bytes 1572872 | tf_op jit(solution)/shard_map/ppermute | solution.py:17
  28.5 8.1 %copy-start.8 = (s32[24,5]{0,1:T(8,128)S(1)}, s32[24,5]{0,1:T(8,128)}, u32[]{:S(2)}) copy-start(s32[24,5]{0,1:T(8,128)} %param.20) | copy-start | bytes 1444
  28.5 8.8 %copy-start.9 = (s32[24,4]{0,1:T(4,128)S(1)}, s32[24,4]{0,1:T(4,128)}, u32[]{:S(2)}) copy-start(s32[24,4]{0,1:T(4,128)} %param.21) | copy-start | bytes 1156
  28.5 9.5 %copy-start.4 = (bf16[24,128,128]{2,1,0:T(8,128)(2,1)S(1)}, bf16[24,128,128]{2,1,0:T(8,128)(2,1)}, u32[]{:S(2)}) copy-start(bf16[24,128,128]{2,1,0:T(8,128)(2,1)} %copy-done.2) | copy-start | bytes 2359300
  28.5 44.8 %collective-permute-start.1 = (bf16[2048,128]{1,0:T(8,128)(2,1)}, bf16[2048,128]{1,0:T(8,128)(2,1)}, u32[]{:S(2)}, u32[]{:S(2)}) collective-permute-start(bf16[2048,128]{1,0:T(8,128)(2,1)} %get-tuple-element.9), channel_id=1, source_target_pairs={{1,0},{2,1},{3,2},{4,3},{5,4},{6,5},{7,6},{8,7},{9,8},{10,9},{11,1... | collective-permute-start | bytes 1572872 | tf_op jit(solution)/shard_map/ppermute | solution.py:18
  33.8 91.8 %collective-permute-start.4 = (bf16[1024,384]{1,0:T(8,128)(2,1)}, bf16[1024,384]{1,0:T(8,128)(2,1)S(1)}, u32[]{:S(2)}, u32[]{:S(2)}) collective-permute-start(bf16[1024,384]{1,0:T(8,128)(2,1)} %bitcast.22), channel_id=1, source_target_pairs={{0,1},{1,2},{2,3},{3,4},{4,5},{5,6},{6,7},{7,8},{8,9},{9,10},{10,1... | collective-permute-start | bytes 2359304 | tf_op jit(solution)/shard_map/ppermute | solution.py:17
  38.0 1.9 %copy-start.11 = (s32[1,4]{1,0:T(1,128)S(1)}, s32[1,4]{1,0:T(1,128)}, u32[]{:S(2)}) copy-start(s32[1,4]{1,0:T(1,128)} %param.25) | copy-start | bytes 52
  71.5 54.1 %collective-permute-start.5 = (bf16[1024,384]{1,0:T(8,128)(2,1)}, bf16[1024,384]{1,0:T(8,128)(2,1)}, u32[]{:S(2)}, u32[]{:S(2)}) collective-permute-start(bf16[1024,384]{1,0:T(8,128)(2,1)} %bitcast.24), channel_id=1, source_target_pairs={{1,0},{2,1},{3,2},{4,3},{5,4},{6,5},{7,6},{8,7},{9,8},{10,9},{11,1... | collective-permute-start | bytes 2359304 | tf_op jit(solution)/shard_map/ppermute | solution.py:18
  105.2 0.7 copy-start.12
  105.6 16.7 %copy-start.13 = (s32[1,2]{1,0:T(1,128)S(1)}, s32[1,2]{1,0:T(1,128)}, u32[]{:S(2)}) copy-start(s32[1,2]{1,0:T(1,128)} %param.29) | copy-start | bytes 28
  122.8 1.8 %copy-start.7 = (bf16[128,128]{1,0:T(8,128)(2,1)S(1)}, bf16[128,128]{1,0:T(8,128)(2,1)}, u32[]{:S(2)}) copy-start(bf16[128,128]{1,0:T(8,128)(2,1)} %param.26) | copy-start | bytes 98308
  125.6 0.9 copy-start.6
Sparse Core Ops, SparseCore 0:
  16.8 49.7 all-gather.3

commit v3 on v2

--- a/solution.py
+++ b/solution.py
@@ -31,17 +31,15 @@
     return lax.dot_general(a, b, (((1,), (1,)), ((), ())), preferred_element_type=jnp.float32)
 
 
-def scaled_kernel(target, target_square, source):
+def scaled_kernel(target, target_square, source, source_square):
     dims = target.shape[-1]
-    scale = -2.0 / dims
-    wide = source.astype(jnp.float32)
-    square = wide * wide
-    high = square.astype(jnp.bfloat16)
-    low = (square - high.astype(jnp.float32)).astype(jnp.bfloat16)
-    ones = jnp.ones((8, dims), jnp.bfloat16)
-    source_square = (contract_last(ones, high) + contract_last(ones, low))[0:1] * scale
-    inner = contract_last(target * jnp.asarray(-2.0 * scale, target.dtype), source)
+    inner = contract_last(target * jnp.asarray(4.0 / dims, target.dtype), source)
     return jnp.exp((target_square + source_square) + inner).astype(jnp.bfloat16)
+
+
+def scaled_norms(cells):
+    wide = cells.astype(jnp.float32)
+    return (jnp.sum(wide * wide, axis=-1) * (-2.0 / cells.shape[-1]))[:, None, :]
 
 
 def target_square_of(target):
@@ -55,7 +53,7 @@
         for which, (left, own, right) in enumerate(parts):
             halo = left.shape[0]
             mine = own.shape[0]
-            target = buffers[which].at[slot, position]
+            target = buffers[which](slot, position)
             sem = sems.at[which, slot, position]
 
             @pl.when(source < halo)
@@ -75,7 +73,7 @@
     for position in range(count):
         for which, (left, own, right) in enumerate(parts):
             pltpu.make_async_copy(
-                own.at[0], buffers[which].at[slot, position], sems.at[which, slot, position]
+                own.at[0], buffers[which](slot, position), sems.at[which, slot, position]
             ).wait()
 
 
@@ -96,21 +94,23 @@
     return slot
 
 
-def near_kernel(index_ref, target_ref, lp, op, rp, lw, ow, rw, out_ref, point_buf, weight_buf, sems):
-    count = point_buf.shape[1]
-    parts = ((lp, op, rp), (lw, ow, rw))
-    slot = pipelined_sources(index_ref, count, parts, (point_buf, weight_buf), sems)
+def near_kernel(index_ref, target_ref, lp, op, rp, lw, ow, rw, ln, on, rn, out_ref, point_buf, weight_buf, norm_buf, sems):
+    count, size = point_buf.shape[1], point_buf.shape[2]
+    parts = ((lp, op, rp), (lw, ow, rw), (ln, on, rn))
+    buffers = (
+        lambda slot, position: point_buf.at[slot, position],
+        lambda slot, position: weight_buf.at[slot, position],
+        lambda slot, position: norm_buf.at[slot, :, pl.ds(position * size, size)],
+    )
+    slot = pipelined_sources(index_ref, count, parts, buffers, sems)
     target = target_ref[0]
-    target_square = target_square_of(target)
-    total = None
-    for position in range(count):
-        kernel = scaled_kernel(target, target_square, point_buf[slot, position])
-        part = jnp.dot(kernel, weight_buf[slot, position], preferred_element_type=jnp.float32)
-        total = part if total is None else total + part
-    out_ref[0] = total
-
-
-def near_field(local_points, left_points, right_points, local_weights, left_weights, right_weights, near_local):
+    sources = point_buf[slot].reshape(count * size, point_buf.shape[-1])
+    values = weight_buf[slot].reshape(count * size, weight_buf.shape[-1])
+    kernel = scaled_kernel(target, target_square_of(target), sources, norm_buf[slot])
+    out_ref[0] = jnp.dot(kernel, values, preferred_element_type=jnp.float32)
+
+
+def near_field(local_points, left_points, right_points, local_weights, left_weights, right_weights, local_norms, left_norms, right_norms, near_local):
     leaves, size, dims = local_points.shape
     rhs = local_weights.shape[-1]
     count = near_local.shape[1]
@@ -120,12 +120,13 @@
         grid_spec=pltpu.PrefetchScalarGridSpec(
             num_scalar_prefetch=1,
             grid=(leaves,),
-            in_specs=[pl.BlockSpec((1, size, dims), lambda l, index: (l, 0, 0))] + [anywhere] * 6,
+            in_specs=[pl.BlockSpec((1, size, dims), lambda l, index: (l, 0, 0))] + [anywhere] * 9,
             out_specs=pl.BlockSpec((1, size, rhs), lambda l, index: (l, 0, 0)),
             scratch_shapes=[
                 pltpu.VMEM((2, count, size, dims), local_points.dtype),
                 pltpu.VMEM((2, count, size, rhs), local_weights.dtype),
-                pltpu.SemaphoreType.DMA((2, 2, count)),
+                pltpu.VMEM((2, 1, count * size), jnp.float32),
+                pltpu.SemaphoreType.DMA((3, 2, count)),
             ],
         ),
         out_shape=jax.ShapeDtypeStruct((leaves, size, rhs), jnp.float32),
@@ -139,74 +140,92 @@
         left_weights,
         local_weights,
         right_weights,
-    )
-
-
-def far_kernel(index_ref, rank_ref, target_ref, basis_ref, down_ref, leaf_base_ref, near_ref, ls, os, rs, out_ref, source_buf, sems):
-    count = source_buf.shape[1]
-    slot = pipelined_sources(index_ref, count, ((ls, os, rs),), (source_buf,), sems)
-    leaf = pl.program_id(0)
+        left_norms,
+        local_norms,
+        right_norms,
+    )
+
+
+def far_kernel(index_ref, target_ref, ls, os, rs, ln, on, rn, out_ref, source_buf, norm_buf, sems):
+    count, rank = source_buf.shape[1], source_buf.shape[2]
+    parts = ((ls, os, rs), (ln, on, rn))
+    buffers = (
+        lambda slot, position: source_buf.at[slot, position],
+        lambda slot, position: norm_buf.at[slot, :, pl.ds(position * rank, rank)],
+    )
+    slot = pipelined_sources(index_ref, count, parts, buffers, sems)
     target = target_ref[0]
     dims = target.shape[-1]
-    target_square = target_square_of(target)
-    total = jnp.dot(basis_ref[0], down_ref[...], preferred_element_type=jnp.float32)
-    for position in range(count):
-        source = source_buf[slot, position]
-        kernel = scaled_kernel(target, target_square, source[:, :dims])
-        total = total + jnp.dot(kernel, source[:, dims:], preferred_element_type=jnp.float32)
+    sources = source_buf[slot].reshape(count * rank, source_buf.shape[-1])
+    kernel = scaled_kernel(target, target_square_of(target), sources[:, :dims], norm_buf[slot])
+    out_ref[0] = jnp.dot(kernel, sources[:, dims:], preferred_element_type=jnp.float32)
+
+
+def far_field(leaf_coords, left_rows, own_rows, right_rows, left_norms, own_norms, right_norms, far_local):
+    leaves, rank, dims = leaf_coords.shape
+    width = own_rows.shape[-1]
+    count = far_local.shape[1]
+    anywhere = pl.BlockSpec(memory_space=pl.ANY)
+    return pl.pallas_call(
+        far_kernel,
+        grid_spec=pltpu.PrefetchScalarGridSpec(
+            num_scalar_prefetch=1,
+            grid=(leaves,),
+            in_specs=[pl.BlockSpec((1, rank, dims), lambda l, index: (l, 0, 0))] + [anywhere] * 6,
+            out_specs=pl.BlockSpec((1, rank, width - dims), lambda l, index: (l, 0, 0)),
+            scratch_shapes=[
+                pltpu.VMEM((2, count, rank, width), own_rows.dtype),
+                pltpu.VMEM((2, 1, count * rank), jnp.float32),
+                pltpu.SemaphoreType.DMA((2, 2, count)),
+            ],
+        ),
+        out_shape=jax.ShapeDtypeStruct((leaves, rank, width - dims), jnp.float32),
+        compiler_params=pltpu.CompilerParams(dimension_semantics=("arbitrary",)),
+    )(
+        far_local.reshape(-1),
+        leaf_coords,
+        left_rows,
+        own_rows,
+        right_rows,
+        left_norms,
+        own_norms,
+        right_norms,
+    )
+
+
+def final_kernel(rank_ref, basis_ref, down_ref, far_ref, leaf_base_ref, near_ref, out_ref):
+    leaf = pl.program_id(0)
+    total = jnp.dot(basis_ref[0], down_ref[...], preferred_element_type=jnp.float32) + far_ref[0]
     rows = lax.broadcasted_iota(jnp.int32, total.shape, 0)
     leaf_down = jnp.where(rows < rank_ref[leaf], total, 0.0).astype(jnp.bfloat16)
     result = jnp.dot(leaf_base_ref[0], leaf_down, preferred_element_type=jnp.float32) + near_ref[0]
     out_ref[0] = result.astype(out_ref.dtype)
 
 
-def far_field(leaf_coords, left_rows, own_rows, right_rows, far_local, leaf_rank, bases, node_down, leaf_bases, near_total):
-    leaves, rank, dims = leaf_coords.shape
-    width = own_rows.shape[-1]
+def final_field(leaf_rank, bases, node_down, far_total, leaf_bases, near_total):
+    leaves, rank, width = bases.shape
     size = leaf_bases.shape[1]
     rhs = near_total.shape[-1]
-    count = far_local.shape[1]
-
-    def own(l, index, ranks):
+
+    def own(l, ranks):
         return (l, 0, 0)
 
-    anywhere = pl.BlockSpec(memory_space=pl.ANY)
-    in_specs = [
-        pl.BlockSpec((1, rank, dims), own),
-        pl.BlockSpec((1, rank, bases.shape[-1]), own),
-        pl.BlockSpec(node_down.shape, lambda l, index, ranks: (0, 0)),
-        pl.BlockSpec((1, size, rank), own),
-        pl.BlockSpec((1, size, rhs), own),
-        anywhere,
-        anywhere,
-        anywhere,
-    ]
     return pl.pallas_call(
-        far_kernel,
+        final_kernel,
         grid_spec=pltpu.PrefetchScalarGridSpec(
-            num_scalar_prefetch=2,
+            num_scalar_prefetch=1,
             grid=(leaves,),
-            in_specs=in_specs,
+            in_specs=[
+                pl.BlockSpec((1, rank, width), own),
+                pl.BlockSpec(node_down.shape, lambda l, ranks: (0, 0)),
+                pl.BlockSpec((1, rank, rhs), own),
+                pl.BlockSpec((1, size, rank), own),
+                pl.BlockSpec((1, size, rhs), own),
+            ],
             out_specs=pl.BlockSpec((1, size, rhs), own),
-            scratch_shapes=[
-                pltpu.VMEM((2, count, rank, width), own_rows.dtype),
-                pltpu.SemaphoreType.DMA((1, 2, count)),
-            ],
         ),
         out_shape=jax.ShapeDtypeStruct((leaves, size, rhs), jnp.bfloat16),
-        compiler_params=pltpu.CompilerParams(dimension_semantics=("arbitrary",)),
-    )(
-        far_local.reshape(-1),
-        leaf_rank,
-        leaf_coords,
-        bases,
-        node_down,
-        leaf_bases,
-        near_total,
-        left_rows,
-        own_rows,
-        right_rows,
-    )
+    )(leaf_rank, bases, node_down, far_total, leaf_bases, near_total)
 
 
 def select_rows(table, index):
@@ -293,13 +312,18 @@
     node_pack = jnp.concatenate([node_coords, node_up, group_basis], axis=1)
     gathered = lax.all_gather(node_pack[None], "col", axis=0, tiled=True)
 
+    left_points = left_points.reshape(REACH, leaf_size, dim_count)
+    right_points = right_points.reshape(REACH, leaf_size, dim_count)
     near_total = near_field(
         local_points,
-        left_points.reshape(REACH, leaf_size, dim_count),
-        right_points.reshape(REACH, leaf_size, dim_count),
+        left_points,
+        right_points,
         local_weights,
         left_weights.reshape(REACH, leaf_size, rhs_count),
         right_weights.reshape(REACH, leaf_size, rhs_count),
+        scaled_norms(local_points),
+        scaled_norms(left_points),
+        scaled_norms(right_points),
         near_list - offset,
     )
 
@@ -332,15 +356,23 @@
         (jnp.dot(group_basis, group_down, preferred_element_type=jnp.float32) + node_side)
         * node_mask[:, None]
     ).astype(jnp.bfloat16)
-    result = far_field(
+    left_rows = left_rows.reshape(REACH, rank_count, skeleton_width)
+    right_rows = right_rows.reshape(REACH, rank_count, skeleton_width)
+    far_total = far_field(
         leaf_coords,
-        left_rows.reshape(REACH, rank_count, skeleton_width),
+        left_rows,
         own_rows,
-        right_rows.reshape(REACH, rank_count, skeleton_width),
+        right_rows,
+        scaled_norms(left_rows[:, :, :dim_count]),
+        scaled_norms(leaf_coords),
+        scaled_norms(right_rows[:, :, :dim_count]),
         far_list - offset,
+    )
+    result = final_field(
         leaf_rank,
         node_basis.reshape(leaf_count, rank_count, node_width),
         node_down,
+        far_total,
         local_bases,
         near_total,
     )

time: 167 us -> 162 us (0.970)
  waiting for transfers between devices: 31.6 us -> 14.9 us
  other arithmetic: 4.97 us -> 16.1 us
  Pallas kernels: 62.3 us -> 67.5 us
  matrix products: 9.34 us -> 6.43 us
    pallas_call x0 -> x1, Pallas kernels: none -> 19.8 us  [final_field(): pl.pallas_call(final_kernel, grid_spec=pltpu.PrefetchScalarGridSpec(num_s...]
    ppermute x3, waiting for transfers between devices: 31.6 us -> 14.9 us  [halos(): left = lax.ppermute(tail, FLAT, [(i, i + 1) for i in range(ends)])]
    pallas_call x1, Pallas kernels: 32 us -> 20.6 us  [far_field(): pl.pallas_call(far_kernel, grid_spec=pltpu.PrefetchScalarGridSpec(num_sca...]
    reduce_sum x0 -> x5, other arithmetic: none -> 5.97 us  [scaled_norms(): jnp.sum(wide * wide, axis=-1) * (-2.0 / cells.shape[-1])]
    mul x0 -> x6, other arithmetic: none -> 3.58 us  [scaled_norms(): jnp.sum(wide * wide, axis=-1) * (-2.0 / cells.shape[-1])]
    pallas_call x1, Pallas kernels: 30.3 us -> 27.1 us  [near_field(): pl.pallas_call(near_kernel, grid_spec=pltpu.PrefetchScalarGridSpec(num_sc...]
    ppermute x3, starting transfers between devices: 9.33 us -> 6.51 us  [halos(): right = lax.ppermute(head, FLAT, [(i + 1, i) for i in range(ends)])]
    concatenate x2, other arithmetic: 3.28 us -> 5.52 us  [body(): own_rows = jnp.concatenate([leaf_coords, leaf_up], axis=-1)]
  transfers between devices with their start and end apart: 7 -> 7, of which waited for: 1 -> 1; matrix products, arithmetic and copies ran while one was open for 9% -> 14% of each run, Pallas kernels for 18% -> 30%
where the time goes in v3:
time: 162 us; the launch traced here: 160 us
  Pallas kernels  67.5 us (42%)
  other arithmetic  16.1 us (10%)
  between operations  15.1 us (9%)
  waiting for transfers between devices  14.9 us (9%)
  starting transfers between devices  14.7 us (9%)
  blocking collectives  14.5 us (9%)
  local copies, waits for them, and re-layouts  10.5 us (6%)
  matrix products  6.43 us (4%)
    pallas_call x1, Pallas kernels, near_field(): pl.pallas_call(near_kernel, grid_spec=pltpu.PrefetchScalarGridSpec(num_sc...  27.1 us
    pallas_call x1, Pallas kernels, far_field(): pl.pallas_call(far_kernel, grid_spec=pltpu.PrefetchScalarGridSpec(num_sca...  20.6 us
    pallas_call x1, Pallas kernels, final_field(): pl.pallas_call(final_kernel, grid_spec=pltpu.PrefetchScalarGridSpec(num_s...  19.8 us
    ppermute x3, waiting for transfers between devices, halos(): left = lax.ppermute(tail, FLAT, [(i, i + 1) for i in range(ends)])  14.9 us
    all_gather x1, blocking collectives, body(): every_group = lax.all_gather(group_pack[None], 'row', axis=0, tiled=True)  14.5 us
    ppermute x3, starting transfers between devices, halos(): left = lax.ppermute(tail, FLAT, [(i, i + 1) for i in range(ends)])  8.18 us
    ppermute x3, starting transfers between devices, halos(): right = lax.ppermute(head, FLAT, [(i + 1, i) for i in range(ends)])  6.51 us
    reduce_sum x5, other arithmetic, scaled_norms(): jnp.sum(wide * wide, axis=-1) * (-2.0 / cells.shape[-1])  5.97 us
  transfers between devices with their start and end apart: 7, of which 1 were waited for; matrix products, arithmetic and copies ran while one was open for 14% of the time, Pallas kernels for 30%

profile of v3, /device:TPU:2, one launch (start us, length us, event | category | flops | bytes accessed | tf_op | source)
XLA Modules:
  0.0 159.7 jit_solution(12587322412302173908)
XLA Ops:
  6.6 2.4 %fusion.58 = (bf16[2048,128]{1,0:T(8,128)(2,1)}, bf16[2048,128]{1,0:T(8,128)(2,1)}) fusion(bf16[6144,128]{1,0:T(8,128)(2,1)} %param.15), kind=kLoop, calls=%fused_computation.102 | loop fusion | bytes 2097152 | tf_op jit(solution)/shard_map/slice | solution.py:15
  9.0 1.9 %collective-permute-start.3 = (bf16[2048,128]{1,0:T(8,128)(2,1)}, bf16[2048,128]{1,0:T(8,128)(2,1)}, u32[]{:S(2)}, u32[]{:S(2)}) collective-permute-start(bf16[2048,128]{1,0:T(8,128)(2,1)} %get-tuple-element.9), channel_id=1, source_target_pairs={{1,0},{2,1},{3,2},{4,3},{5,4},{6,5},{7,6},{8,7},{9,8},{10,9},{11,1... | collective-permute-start | bytes 1572872 | tf_op jit(solution)/shard_map/ppermute | solution.py:18
  10.9 2.4 %collective-permute-start.2 = (bf16[2048,128]{1,0:T(8,128)(2,1)}, bf16[2048,128]{1,0:T(8,128)(2,1)}, u32[]{:S(2)}, u32[]{:S(2)}) collective-permute-start(bf16[2048,128]{1,0:T(8,128)(2,1)} %get-tuple-element.10), channel_id=1, source_target_pairs={{0,1},{1,2},{2,3},{3,4},{4,5},{5,6},{6,7},{7,8},{8,9},{9,10},{10,1... | collective-permute-start | bytes 1572872 | tf_op jit(solution)/shard_map/ppermute | solution.py:17
  14.9 1.1 multiply_reduce_fusion.1
  16.0 0.6 multiply_reduce_fusion.8
  16.6 0.3 copy-done.3
  16.9 0.6 copy-done.4
  17.5 1.0 multiply_convert_fusion
  18.6 0.6 fusion.21
  19.2 0.7 pad_maximum_fusion.1
  19.9 2.6 %fusion.24 = (bf16[8,128,384]{2,1,0:T(8,128)(2,1)}, bf16[8,128,384]{2,1,0:T(8,128)(2,1)}) fusion(bf16[24,128,256]{2,1,0:T(8,128)(2,1)S(1)} %multiply_convert_fusion, bf16[24,128,128]{2,1,0:T(8,128)(2,1)} %copy-done.3), kind=kLoop, calls=%fused_computation.47 | loop fusion | flops 3145728 | bytes 3932160 | tf_op jit(solution)/shard_map/concatenate | solution.py:291
  22.5 3.9 %collective-permute-start = (bf16[1024,384]{1,0:T(8,128)(2,1)}, bf16[1024,384]{1,0:T(8,128)(2,1)}, u32[]{:S(2)}, u32[]{:S(2)}) collective-permute-start(bf16[1024,384]{1,0:T(8,128)(2,1)} %bitcast.18), channel_id=1, source_target_pairs={{0,1},{1,2},{2,3},{3,4},{4,5},{5,6},{6,7},{7,8},{8,9},{9,10},{10,1... | collective-permute-start | bytes 2359304 | tf_op jit(solution)/shard_map/ppermute | solution.py:17
  26.4 1.9 %collective-permute-start.1 = (bf16[1024,384]{1,0:T(8,128)(2,1)}, bf16[1024,384]{1,0:T(8,128)(2,1)}, u32[]{:S(2)}, u32[]{:S(2)}) collective-permute-start(bf16[1024,384]{1,0:T(8,128)(2,1)} %bitcast.20), channel_id=1, source_target_pairs={{1,0},{2,1},{3,2},{4,3},{5,4},{6,5},{7,6},{8,7},{9,8},{10,9},{11,1... | collective-permute-start | bytes 2359304 | tf_op jit(solution)/shard_map/ppermute | solution.py:18
  28.4 1.5 fusion.57
  29.9 2.7 %collective-permute-start.5 = (bf16[2048,256]{1,0:T(8,128)(2,1)}, bf16[2048,256]{1,0:T(8,128)(2,1)}, u32[]{:S(2)}, u32[]{:S(2)}) collective-permute-start(bf16[2048,256]{1,0:T(8,128)(2,1)} %get-tuple-element.5), channel_id=1, source_target_pairs={{1,0},{2,1},{3,2},{4,3},{5,4},{6,5},{7,6},{8,7},{9,8},{10,9},{11,1... | collective-permute-start | bytes 3145736 | tf_op jit(solution)/shard_map/ppermute | solution.py:18
  32.5 0.9 multiply_reduce_fusion
  33.4 0.6 broadcast_multiply_fusion
  34.0 0.6 broadcast_multiply_fusion.1
  34.7 2.9 %pad_maximum_fusion.os = bf16[24,128,384]{2,1,0:T(8,128)(2,1)} fusion(bf16[24,128,128]{2,1,0:T(8,128)(2,1)} %copy-done.3, bf16[24,128,256]{2,1,0:T(8,128)(2,1)S(1)} %multiply_convert_fusion), kind=kLoop, calls=%fused_computation.5 | loop fusion | flops 4718592 | bytes 4718592 | tf_op jit(solution)/shard_map/concatenate | solution.py:291
  37.8 0.7 reshape.211.index_ref
  38.6 0.7 reshape.208.index_ref
  39.2 1.9 %collective-permute-start.4 = (bf16[2048,256]{1,0:T(8,128)(2,1)}, bf16[2048,256]{1,0:T(8,128)(2,1)S(1)}, u32[]{:S(2)}, u32[]{:S(2)}) collective-permute-start(bf16[2048,256]{1,0:T(8,128)(2,1)} %get-tuple-element.6), channel_id=1, source_target_pairs={{0,1},{1,2},{2,3},{3,4},{4,5},{5,6},{6,7},{7,8},{8,9},{9,10},{10,1... | collective-permute-start | bytes 3145736 | tf_op jit(solution)/shard_map/ppermute | solution.py:17
  41.2 1.4 multiply_reduce_fusion.2
  42.6 0.6 broadcast_multiply_fusion.2
  43.2 1.4 multiply_reduce_fusion.3
  44.6 0.6 broadcast_multiply_fusion.3
  45.2 14.9 %collective-permute-done = bf16[1024,384]{1,0:T(8,128)(2,1)} collective-permute-done((bf16[1024,384]{1,0:T(8,128)(2,1)}, bf16[1024,384]{1,0:T(8,128)(2,1)}, u32[]{:S(2)}, u32[]{:S(2)}) %collective-permute-start) | collective-permute-done | bytes 786464 | tf_op jit(solution)/shard_map/ppermute | solution.py:17
  60.0 1.2 multiply_reduce_fusion.5
  61.2 1.2 multiply_reduce_fusion.4
  62.4 0.6 broadcast_multiply_fusion.5
  63.0 0.6 broadcast_multiply_fusion.4
  63.6 20.6 %shard_map.145.far_ref = f32[24,128,256]{2,1,0:T(8,128)} custom-call(s32[96]{0:T(128)} %reshape.208.index_ref, bf16[24,128,128]{2,1,0:T(8,128)(2,1)} %copy-done.3, bf16[8,128,384]{2,1,0:T(8,128)(2,1)} %bitcast.19.ls, bf16[24,128,384]{2,1,0:T(8,128)(2,1)} %pad_maximum_fusion.os, bf16[8,128,384]{2,1,0:T(8,128)(2,1)} %bitcast.21.rs, f32[8,1,128]{2,1,0:T(1,128)} %bitcast.123, ...), custom_call_target="tpu_custom_call" | custom-call | tf_op jit(solution)/shard_map/pallas_call | solution.py:169
  84.2 1.0 copy-done.6
  85.2 27.1 %shard_map.146.near_ref = f32[24,256,256]{2,1,0:T(8,128)} custom-call(s32[120]{0:T(128)} %reshape.211.index_ref, bf16[24,256,128]{2,1,0:T(8,128)(2,1)} %bitcast.99, bf16[8,256,128]{2,1,0:T(8,128)(2,1)} %bitcast.26.lp, bf16[24,256,128]{2,1,0:T(8,128)(2,1)} %bitcast.100, bf16[8,256,128]{2,1,0:T(8,128)(2,1)} %bitcast.27.rp, bf16[8,256,256]{2,1,0:T(8,128)(2,1)} %bitcast.110, ...), custom_call_target="tpu_custom_call" | custom-call | tf_op jit(solution)/shard_map/pallas_call | solution.py:118
  112.3 1.5 copy.44
  113.9 0.3 copy.43
  114.2 0.2 copy.41
  114.5 0.3 multiply_reduce_fusion.9
  114.9 0.3 fusion.8
  115.4 0.2 fusion.17
  115.7 14.5 %all-gather.1 = bf16[512,384]{1,0:T(8,128)(2,1)S(1)} all-gather(bf16[128,384]{1,0:T(8,128)(2,1)S(1)} %pad_maximum_fusion.2), channel_id=3, replica_groups=mesh['row'=4,'col'=8] {'row'}, dimensions={0}, use_global_device_ids=true | all-gather | bytes 491520 | tf_op jit(solution)/shard_map/all_gather | solution.py:344
  130.3 0.4 convolution_convert_fusion
  130.8 0.3 copy.48
  131.1 0.4 convolution_convert_fusion.1
  131.5 0.2 fusion.18
  131.7 0.4 convolution_bitcast_fusion
  132.1 1.0 fusion.16.down_ref
  133.0 19.8 %shard_map.147 = bf16[24,256,256]{2,1,0:T(8,128)(2,1)} custom-call(s32[24]{0:T(128)} %rank_ref.1, bf16[24,128,128]{2,1,0:T(8,128)(2,1)} %bitcast.108, bf16[128,256]{1,0:T(8,128)(2,1)} %fusion.16.down_ref, f32[24,128,256]{2,1,0:T(8,128)} %shard_map.145.far_ref, bf16[24,256,128]{2,1,0:T(8,128)(2,1)} %bitcast.103, f32[24,256,256]{2,1,0:T(8,128)} %shard_map.146.near_ref), custom_call_target="tpu_custom_call" | custom-call | tf_op jit(solution)/shard_map/pallas_call | solution.py:213
  (54 shorter events, 1.4 us)
Async XLA Ops:
  6.5 8.3 %copy-start.2 = (bf16[6144,128]{1,0:T(8,128)(2,1)S(1)}, bf16[6144,128]{1,0:T(8,128)(2,1)}, u32[]{:S(2)}) copy-start(bf16[6144,128]{1,0:T(8,128)(2,1)} %param.15) | copy-start | bytes 4718596
  6.5 8.1 %copy-start.9 = (s32[24]{0:T(128)S(1)}, s32[24]{0:T(128)}, u32[]{:S(2)}) copy-start(s32[24]{0:T(128)} %rank_ref.1) | copy-start | bytes 292
  6.5 8.1 %copy-start.7 = (bf16[128,128]{1,0:T(8,128)(2,1)S(1)}, bf16[128,128]{1,0:T(8,128)(2,1)}, u32[]{:S(2)}) copy-start(bf16[128,128]{1,0:T(8,128)(2,1)} %param.26) | copy-start | bytes 98308
  6.5 8.3 %copy-start.11 = (s32[24,128]{1,0:T(8,128)S(1)}, s32[24,128]{1,0:T(8,128)}, u32[]{:S(2)}) copy-start(s32[24,128]{1,0:T(8,128)} %param.19) | copy-start | bytes 36868
  6.5 105.7 %all-gather.4.cloned.1.call-start = ((), (), s32[]{:S(2)}) async-start(), calls=%async_computation | async-start | bytes 1179648 | tf_op jit(solution)/shard_map/all_gather | solution.py:313
  9.0 30.3 %collective-permute-start.3 = (bf16[2048,128]{1,0:T(8,128)(2,1)}, bf16[2048,128]{1,0:T(8,128)(2,1)}, u32[]{:S(2)}, u32[]{:S(2)}) collective-permute-start(bf16[2048,128]{1,0:T(8,128)(2,1)} %get-tuple-element.9), channel_id=1, source_target_pairs={{1,0},{2,1},{3,2},{4,3},{5,4},{6,5},{7,6},{8,7},{9,8},{10,9},{11,1... | collective-permute-start | bytes 1572872 | tf_op jit(solution)/shard_map/ppermute | solution.py:18
  10.9 32.3 %collective-permute-start.2 = (bf16[2048,128]{1,0:T(8,128)(2,1)}, bf16[2048,128]{1,0:T(8,128)(2,1)}, u32[]{:S(2)}, u32[]{:S(2)}) collective-permute-start(bf16[2048,128]{1,0:T(8,128)(2,1)} %get-tuple-element.10), channel_id=1, source_target_pairs={{0,1},{1,2},{2,3},{3,4},{4,5},{5,6},{6,7},{7,8},{8,9},{9,10},{10,1... | collective-permute-start | bytes 1572872 | tf_op jit(solution)/shard_map/ppermute | solution.py:17
  14.7 1.3 copy-start.12
  14.8 2.0 %copy-start = (bf16[6144,256]{1,0:T(8,128)(2,1)S(1)}, bf16[6144,256]{1,0:T(8,128)(2,1)}, u32[]{:S(2)}) copy-start(bf16[6144,256]{1,0:T(8,128)(2,1)} %param.16) | copy-start | bytes 9437188
  14.8 2.6 %copy-start.4 = (bf16[6144,128]{1,0:T(8,128)(2,1)S(1)}, bf16[6144,128]{1,0:T(8,128)(2,1)}, u32[]{:S(2)}) copy-start(bf16[6144,128]{1,0:T(8,128)(2,1)} %param.17) | copy-start | bytes 4718596
  16.0 0.9 copy-start.3
  17.5 1.1 copy-start.5
  19.9 8.4 %copy-start.1 = (bf16[6144,256]{1,0:T(8,128)(2,1)S(1)}, bf16[6144,256]{1,0:T(8,128)(2,1)}, u32[]{:S(2)}) copy-start(bf16[6144,256]{1,0:T(8,128)(2,1)} %param.16) | copy-start | bytes 9437188
  22.5 37.5 %collective-permute-start = (bf16[1024,384]{1,0:T(8,128)(2,1)}, bf16[1024,384]{1,0:T(8,128)(2,1)}, u32[]{:S(2)}, u32[]{:S(2)}) collective-permute-start(bf16[1024,384]{1,0:T(8,128)(2,1)} %bitcast.18), channel_id=1, source_target_pairs={{0,1},{1,2},{2,3},{3,4},{4,5},{5,6},{6,7},{7,8},{8,9},{9,10},{10,1... | collective-permute-start | bytes 2359304 | tf_op jit(solution)/shard_map/ppermute | solution.py:17
  26.4 34.8 %collective-permute-start.1 = (bf16[1024,384]{1,0:T(8,128)(2,1)}, bf16[1024,384]{1,0:T(8,128)(2,1)}, u32[]{:S(2)}, u32[]{:S(2)}) collective-permute-start(bf16[1024,384]{1,0:T(8,128)(2,1)} %bitcast.20), channel_id=1, source_target_pairs={{1,0},{2,1},{3,2},{4,3},{5,4},{6,5},{7,6},{8,7},{9,8},{10,9},{11,1... | collective-permute-start | bytes 2359304 | tf_op jit(solution)/shard_map/ppermute | solution.py:18
  29.8 4.8 %copy-start.8 = (s32[24,5]{0,1:T(8,128)S(1)}, s32[24,5]{0,1:T(8,128)}, u32[]{:S(2)}) copy-start(s32[24,5]{0,1:T(8,128)} %param.20) | copy-start | bytes 1444
  29.9 4.8 %copy-start.10 = (s32[24,4]{0,1:T(4,128)S(1)}, s32[24,4]{0,1:T(4,128)}, u32[]{:S(2)}) copy-start(s32[24,4]{0,1:T(4,128)} %param.21) | copy-start | bytes 1156
  29.9 4.8 %copy-start.13 = (s32[1,4]{1,0:T(1,128)S(1)}, s32[1,4]{1,0:T(1,128)}, u32[]{:S(2)}) copy-start(s32[1,4]{1,0:T(1,128)} %param.25) | copy-start | bytes 52
  29.9 54.3 %collective-permute-start.5 = (bf16[2048,256]{1,0:T(8,128)(2,1)}, bf16[2048,256]{1,0:T(8,128)(2,1)}, u32[]{:S(2)}, u32[]{:S(2)}) collective-permute-start(bf16[2048,256]{1,0:T(8,128)(2,1)} %get-tuple-element.5), channel_id=1, source_target_pairs={{1,0},{2,1},{3,2},{4,3},{5,4},{6,5},{7,6},{8,7},{9,8},{10,9},{11,1... | collective-permute-start | bytes 3145736 | tf_op jit(solution)/shard_map/ppermute | solution.py:18
  39.2 45.0 %collective-permute-start.4 = (bf16[2048,256]{1,0:T(8,128)(2,1)}, bf16[2048,256]{1,0:T(8,128)(2,1)S(1)}, u32[]{:S(2)}, u32[]{:S(2)}) collective-permute-start(bf16[2048,256]{1,0:T(8,128)(2,1)} %get-tuple-element.6), channel_id=1, source_target_pairs={{0,1},{1,2},{2,3},{3,4},{4,5},{5,6},{6,7},{7,8},{8,9},{9,10},{10,1... | collective-permute-start | bytes 3145736 | tf_op jit(solution)/shard_map/ppermute | solution.py:17
  84.2 1.0 copy-start.6
  113.8 0.7 copy-start.14
  114.5 15.8 %copy-start.15 = (s32[1,2]{1,0:T(1,128)S(1)}, s32[1,2]{1,0:T(1,128)}, u32[]{:S(2)}) copy-start(s32[1,2]{1,0:T(1,128)} %param.29) | copy-start | bytes 28
Sparse Core Ops, SparseCore 0:
  20.0 39.8 all-gather.3

commit v4 on v3

--- a/solution.py
+++ b/solution.py
@@ -146,7 +146,7 @@
     )
 
 
-def far_kernel(index_ref, target_ref, ls, os, rs, ln, on, rn, out_ref, source_buf, norm_buf, sems):
+def far_kernel(index_ref, target_ref, ls, os, rs, ln, on, rn, after_ref, out_ref, source_buf, norm_buf, sems):
     count, rank = source_buf.shape[1], source_buf.shape[2]
     parts = ((ls, os, rs), (ln, on, rn))
     buffers = (
@@ -161,7 +161,7 @@
     out_ref[0] = jnp.dot(kernel, sources[:, dims:], preferred_element_type=jnp.float32)
 
 
-def far_field(leaf_coords, left_rows, own_rows, right_rows, left_norms, own_norms, right_norms, far_local):
+def far_field(leaf_coords, left_rows, own_rows, right_rows, left_norms, own_norms, right_norms, far_local, after):
     leaves, rank, dims = leaf_coords.shape
     width = own_rows.shape[-1]
     count = far_local.shape[1]
@@ -171,7 +171,7 @@
         grid_spec=pltpu.PrefetchScalarGridSpec(
             num_scalar_prefetch=1,
             grid=(leaves,),
-            in_specs=[pl.BlockSpec((1, rank, dims), lambda l, index: (l, 0, 0))] + [anywhere] * 6,
+            in_specs=[pl.BlockSpec((1, rank, dims), lambda l, index: (l, 0, 0))] + [anywhere] * 7,
             out_specs=pl.BlockSpec((1, rank, width - dims), lambda l, index: (l, 0, 0)),
             scratch_shapes=[
                 pltpu.VMEM((2, count, rank, width), own_rows.dtype),
@@ -190,22 +190,30 @@
         left_norms,
         own_norms,
         right_norms,
+        after,
     )
 
 
 def final_kernel(rank_ref, basis_ref, down_ref, far_ref, leaf_base_ref, near_ref, out_ref):
-    leaf = pl.program_id(0)
-    total = jnp.dot(basis_ref[0], down_ref[...], preferred_element_type=jnp.float32) + far_ref[0]
-    rows = lax.broadcasted_iota(jnp.int32, total.shape, 0)
-    leaf_down = jnp.where(rows < rank_ref[leaf], total, 0.0).astype(jnp.bfloat16)
-    result = jnp.dot(leaf_base_ref[0], leaf_down, preferred_element_type=jnp.float32) + near_ref[0]
-    out_ref[0] = result.astype(out_ref.dtype)
+    block = basis_ref.shape[0]
+    step = pl.program_id(0)
+    down = down_ref[...]
+    for inside in range(block):
+        total = jnp.dot(basis_ref[inside], down, preferred_element_type=jnp.float32) + far_ref[inside]
+        rows = lax.broadcasted_iota(jnp.int32, total.shape, 0)
+        leaf_down = jnp.where(rows < rank_ref[step * block + inside], total, 0.0).astype(jnp.bfloat16)
+        result = (
+            jnp.dot(leaf_base_ref[inside], leaf_down, preferred_element_type=jnp.float32)
+            + near_ref[inside]
+        )
+        out_ref[inside] = result.astype(out_ref.dtype)
 
 
 def final_field(leaf_rank, bases, node_down, far_total, leaf_bases, near_total):
     leaves, rank, width = bases.shape
     size = leaf_bases.shape[1]
     rhs = near_total.shape[-1]
+    block = max(b for b in (1, 2, 3, 4) if leaves % b == 0)
 
     def own(l, ranks):
         return (l, 0, 0)
@@ -214,15 +222,15 @@
         final_kernel,
         grid_spec=pltpu.PrefetchScalarGridSpec(
             num_scalar_prefetch=1,
-            grid=(leaves,),
+            grid=(leaves // block,),
             in_specs=[
-                pl.BlockSpec((1, rank, width), own),
+                pl.BlockSpec((block, rank, width), own),
                 pl.BlockSpec(node_down.shape, lambda l, ranks: (0, 0)),
-                pl.BlockSpec((1, rank, rhs), own),
-                pl.BlockSpec((1, size, rank), own),
-                pl.BlockSpec((1, size, rhs), own),
+                pl.BlockSpec((block, rank, rhs), own),
+                pl.BlockSpec((block, size, rank), own),
+                pl.BlockSpec((block, size, rhs), own),
             ],
-            out_specs=pl.BlockSpec((1, size, rhs), own),
+            out_specs=pl.BlockSpec((block, size, rhs), own),
         ),
         out_shape=jax.ShapeDtypeStruct((leaves, size, rhs), jnp.bfloat16),
     )(leaf_rank, bases, node_down, far_total, leaf_bases, near_total)
@@ -341,21 +349,6 @@
     ).astype(jnp.bfloat16)
     group_coords = select_rows(all_coords.reshape(columns * node_width, dim_count), group_skeleton[0])
     group_pack = jnp.concatenate([group_coords, group_up], axis=1)
-    every_group = lax.all_gather(group_pack[None], "row", axis=0, tiled=True)
-    picked_group = select_rows(every_group, group_far[0])
-    picked_group_coords = picked_group[:, :, :dim_count]
-    picked_group_up = picked_group[:, :, dim_count:]
-    group_kernel = kernel_block(
-        jnp.broadcast_to(group_coords, picked_group_coords.shape), picked_group_coords
-    )
-    group_down = (
-        jnp.einsum("fab,fbr->ar", group_kernel, picked_group_up, preferred_element_type=jnp.float32)
-        * group_mask[:, None]
-    ).astype(jnp.bfloat16)
-    node_down = (
-        (jnp.dot(group_basis, group_down, preferred_element_type=jnp.float32) + node_side)
-        * node_mask[:, None]
-    ).astype(jnp.bfloat16)
     left_rows = left_rows.reshape(REACH, rank_count, skeleton_width)
     right_rows = right_rows.reshape(REACH, rank_count, skeleton_width)
     far_total = far_field(
@@ -367,7 +360,28 @@
         scaled_norms(leaf_coords),
         scaled_norms(right_rows[:, :, :dim_count]),
         far_list - offset,
-    )
+        group_pack,
+    )
+    rows = lax.axis_size("row")
+    received = [group_pack] + [
+        lax.ppermute(group_pack, "row", [(r, (r + shift) % rows) for r in range(rows)])
+        for shift in range(1, rows)
+    ]
+    shifts = (lax.axis_index("row") - group_far[0]) % rows
+    picked_group = select_rows(jnp.stack(received), shifts)
+    picked_group_coords = picked_group[:, :, :dim_count]
+    picked_group_up = picked_group[:, :, dim_count:]
+    group_kernel = kernel_block(
+        jnp.broadcast_to(group_coords, picked_group_coords.shape), picked_group_coords
+    )
+    group_down = (
+        jnp.einsum("fab,fbr->ar", group_kernel, picked_group_up, preferred_element_type=jnp.float32)
+        * group_mask[:, None]
+    ).astype(jnp.bfloat16)
+    node_down = (
+        (jnp.dot(group_basis, group_down, preferred_element_type=jnp.float32) + node_side)
+        * node_mask[:, None]
+    ).astype(jnp.bfloat16)
     result = final_field(
         leaf_rank,
         node_basis.reshape(leaf_count, rank_count, node_width),

time: 162 us -> 153 us (0.944)
  the two profiles are of different devices: /device:TPU:2 before, /device:TPU:13 now
where the time goes in v4:
time: 153 us; the launch traced here: 150 us
  Pallas kernels  57.1 us (37%)
  waiting for transfers between devices  22.8 us (15%)
  starting transfers between devices  21.5 us (14%)
  other arithmetic  16.1 us (11%)
  between operations  15.2 us (10%)
  local copies, waits for them, and re-layouts  10.8 us (7%)
  matrix products  7.07 us (5%)
    pallas_call x1, Pallas kernels, near_field(): pl.pallas_call(near_kernel, grid_spec=pltpu.PrefetchScalarGridSpec(num_sc...  27.1 us
    ppermute x3, waiting for transfers between devices, halos(): right = lax.ppermute(head, FLAT, [(i + 1, i) for i in range(ends)])  22.7 us
    pallas_call x1, Pallas kernels, far_field(): pl.pallas_call(far_kernel, grid_spec=pltpu.PrefetchScalarGridSpec(num_sca...  20.6 us
    pallas_call x1, Pallas kernels, final_field(): pl.pallas_call(final_kernel, grid_spec=pltpu.PrefetchScalarGridSpec(num_s...  9.36 us
    ppermute x3, starting transfers between devices, halos(): right = lax.ppermute(head, FLAT, [(i + 1, i) for i in range(ends)])  8.46 us
    ppermute x3, starting transfers between devices, halos(): left = lax.ppermute(tail, FLAT, [(i, i + 1) for i in range(ends)])  8.28 us
    reduce_sum x5, other arithmetic, scaled_norms(): jnp.sum(wide * wide, axis=-1) * (-2.0 / cells.shape[-1])  5.97 us
    concatenate x2, other arithmetic, body(): own_rows = jnp.concatenate([leaf_coords, leaf_up], axis=-1)  5.5 us
  transfers between devices with their start and end apart: 10, of which 2 were waited for; matrix products, arithmetic and copies ran while one was open for 16% of the time, Pallas kernels for 32%

profile of v4, /device:TPU:13, one launch (start us, length us, event | category | flops | bytes accessed | tf_op | source)
XLA Modules:
  0.0 150.4 jit_solution(14507380525669866663)
XLA Ops:
  6.6 2.4 %fusion.66 = (bf16[2048,128]{1,0:T(8,128)(2,1)}, bf16[2048,128]{1,0:T(8,128)(2,1)}) fusion(bf16[6144,128]{1,0:T(8,128)(2,1)} %param.15), kind=kLoop, calls=%fused_computation.114 | loop fusion | bytes 2097152 | tf_op jit(solution)/shard_map/slice | solution.py:15
  8.9 2.6 %collective-permute-start.6 = (bf16[2048,128]{1,0:T(8,128)(2,1)}, bf16[2048,128]{1,0:T(8,128)(2,1)}, u32[]{:S(2)}, u32[]{:S(2)}) collective-permute-start(bf16[2048,128]{1,0:T(8,128)(2,1)} %get-tuple-element.9), channel_id=1, source_target_pairs={{1,0},{2,1},{3,2},{4,3},{5,4},{6,5},{7,6},{8,7},{9,8},{10,9},{11,1... | collective-permute-start | bytes 1572872 | tf_op jit(solution)/shard_map/ppermute | solution.py:18
  11.5 3.0 %collective-permute-start.5 = (bf16[2048,128]{1,0:T(8,128)(2,1)}, bf16[2048,128]{1,0:T(8,128)(2,1)}, u32[]{:S(2)}, u32[]{:S(2)}) collective-permute-start(bf16[2048,128]{1,0:T(8,128)(2,1)} %get-tuple-element.10), channel_id=1, source_target_pairs={{0,1},{1,2},{2,3},{3,4},{4,5},{5,6},{6,7},{7,8},{8,9},{9,10},{10,1... | collective-permute-start | bytes 1572872 | tf_op jit(solution)/shard_map/ppermute | solution.py:17
  16.1 1.1 multiply_reduce_fusion.1
  17.2 0.6 multiply_reduce_fusion.8
  17.8 0.3 copy-done.3
  18.1 0.6 copy-done.4
  18.7 1.0 multiply_convert_fusion
  19.9 0.6 fusion.21
  20.5 0.7 pad_maximum_fusion.3
  21.2 2.6 %fusion.24 = (bf16[8,128,384]{2,1,0:T(8,128)(2,1)}, bf16[8,128,384]{2,1,0:T(8,128)(2,1)}) fusion(bf16[24,128,256]{2,1,0:T(8,128)(2,1)S(1)} %multiply_convert_fusion, bf16[24,128,128]{2,1,0:T(8,128)(2,1)} %copy-done.3), kind=kLoop, calls=%fused_computation.47 | loop fusion | flops 3145728 | bytes 3932160 | tf_op jit(solution)/shard_map/concatenate | solution.py:299
  23.8 2.4 %collective-permute-start.3 = (bf16[1024,384]{1,0:T(8,128)(2,1)}, bf16[1024,384]{1,0:T(8,128)(2,1)}, u32[]{:S(2)}, u32[]{:S(2)}) collective-permute-start(bf16[1024,384]{1,0:T(8,128)(2,1)} %bitcast.18), channel_id=1, source_target_pairs={{0,1},{1,2},{2,3},{3,4},{4,5},{5,6},{6,7},{7,8},{8,9},{9,10},{10,1... | collective-permute-start | bytes 2359304 | tf_op jit(solution)/shard_map/ppermute | solution.py:17
  26.2 1.9 %collective-permute-start.4 = (bf16[1024,384]{1,0:T(8,128)(2,1)}, bf16[1024,384]{1,0:T(8,128)(2,1)}, u32[]{:S(2)}, u32[]{:S(2)}) collective-permute-start(bf16[1024,384]{1,0:T(8,128)(2,1)} %bitcast.20), channel_id=1, source_target_pairs={{1,0},{2,1},{3,2},{4,3},{5,4},{6,5},{7,6},{8,7},{9,8},{10,9},{11,1... | collective-permute-start | bytes 2359304 | tf_op jit(solution)/shard_map/ppermute | solution.py:18
  28.1 1.5 fusion.65
  29.6 4.0 %collective-permute-start.8 = (bf16[2048,256]{1,0:T(8,128)(2,1)}, bf16[2048,256]{1,0:T(8,128)(2,1)}, u32[]{:S(2)}, u32[]{:S(2)}) collective-permute-start(bf16[2048,256]{1,0:T(8,128)(2,1)} %get-tuple-element.5), channel_id=1, source_target_pairs={{1,0},{2,1},{3,2},{4,3},{5,4},{6,5},{7,6},{8,7},{9,8},{10,9},{11,1... | collective-permute-start | bytes 3145736 | tf_op jit(solution)/shard_map/ppermute | solution.py:18
  33.6 0.9 multiply_reduce_fusion
  34.5 0.6 broadcast_multiply_fusion
  35.2 0.6 broadcast_multiply_fusion.1
  35.8 2.9 %pad_maximum_fusion.os = bf16[24,128,384]{2,1,0:T(8,128)(2,1)} fusion(bf16[24,128,128]{2,1,0:T(8,128)(2,1)} %copy-done.3, bf16[24,128,256]{2,1,0:T(8,128)(2,1)S(1)} %multiply_convert_fusion), kind=kLoop, calls=%fused_computation.5 | loop fusion | flops 4718592 | bytes 4718592 | tf_op jit(solution)/shard_map/concatenate | solution.py:299
  38.9 0.6 reshape.233.index_ref
  39.6 0.6 reshape.230.index_ref
  40.2 2.9 %collective-permute-start.7 = (bf16[2048,256]{1,0:T(8,128)(2,1)}, bf16[2048,256]{1,0:T(8,128)(2,1)S(1)}, u32[]{:S(2)}, u32[]{:S(2)}) collective-permute-start(bf16[2048,256]{1,0:T(8,128)(2,1)} %get-tuple-element.6), channel_id=1, source_target_pairs={{0,1},{1,2},{2,3},{3,4},{4,5},{5,6},{6,7},{7,8},{8,9},{9,10},{10,1... | collective-permute-start | bytes 3145736 | tf_op jit(solution)/shard_map/ppermute | solution.py:17
  43.1 1.4 multiply_reduce_fusion.2
  44.5 0.6 broadcast_multiply_fusion.2
  45.1 1.4 multiply_reduce_fusion.3
  46.5 0.6 broadcast_multiply_fusion.3
  47.1 1.2 multiply_reduce_fusion.5
  48.3 11.5 %collective-permute-done.4 = bf16[1024,384]{1,0:T(8,128)(2,1)} collective-permute-done((bf16[1024,384]{1,0:T(8,128)(2,1)}, bf16[1024,384]{1,0:T(8,128)(2,1)}, u32[]{:S(2)}, u32[]{:S(2)}) %collective-permute-start.4) | collective-permute-done | bytes 786464 | tf_op jit(solution)/shard_map/ppermute | solution.py:18
  59.8 1.2 multiply_reduce_fusion.4
  60.9 0.6 broadcast_multiply_fusion.5
  61.5 0.6 broadcast_multiply_fusion.4
  62.1 11.2 %collective-permute-done.8 = bf16[2048,256]{1,0:T(8,128)(2,1)} collective-permute-done((bf16[2048,256]{1,0:T(8,128)(2,1)}, bf16[2048,256]{1,0:T(8,128)(2,1)}, u32[]{:S(2)}, u32[]{:S(2)}) %collective-permute-start.8) | collective-permute-done | bytes 1048608 | tf_op jit(solution)/shard_map/ppermute | solution.py:18
  73.3 1.1 copy-done.6
  74.4 27.1 %shard_map.146.near_ref = f32[24,256,256]{2,1,0:T(8,128)} custom-call(s32[120]{0:T(128)} %reshape.233.index_ref, bf16[24,256,128]{2,1,0:T(8,128)(2,1)} %bitcast.112, bf16[8,256,128]{2,1,0:T(8,128)(2,1)} %bitcast.26.lp, bf16[24,256,128]{2,1,0:T(8,128)(2,1)} %bitcast.113, bf16[8,256,128]{2,1,0:T(8,128)(2,1)} %bitcast.27.rp, bf16[8,256,256]{2,1,0:T(8,128)(2,1)} %bitcast.123, ...), custom_call_target="tpu_custom_call" | custom-call | tf_op jit(solution)/shard_map/pallas_call | solution.py:118
  101.5 1.5 copy.43
  103.1 0.3 copy.42
  103.7 0.4 multiply_reduce_fusion.9
  104.0 0.2 fusion.17
  104.4 2.5 %collective-permute-start.1 = (bf16[128,384]{1,0:T(8,128)(2,1)S(1)}, bf16[128,384]{1,0:T(8,128)(2,1)S(1)}, u32[]{:S(2)}, u32[]{:S(2)}) collective-permute-start(bf16[128,384]{1,0:T(8,128)(2,1)S(1)} %get-tuple-element.14.after_ref), channel_id=1, source_target_pairs={{0,16},{8,24},{16,0},{24,8},{1,17},{9,25},{17,1},{25,9},{2,18},{10... | collective-permute-start | bytes 294920 | tf_op jit(solution)/shard_map/ppermute | solution.py:367
  106.9 2.2 %collective-permute-start = (bf16[128,384]{1,0:T(8,128)(2,1)S(1)}, bf16[128,384]{1,0:T(8,128)(2,1)S(1)}, u32[]{:S(2)}, u32[]{:S(2)}) collective-permute-start(bf16[128,384]{1,0:T(8,128)(2,1)S(1)} %get-tuple-element.14.after_ref), channel_id=1, source_target_pairs={{0,8},{8,16},{16,24},{24,0},{1,9},{9,17},{17,25},{25,1},{2,10},{10... | collective-permute-start | bytes 294920 | tf_op jit(solution)/shard_map/ppermute | solution.py:367
  109.1 0.3 fusion.8
  109.7 0.3 copy.51
  110.0 0.4 convolution_convert_fusion.1
  110.3 20.6 %shard_map.145.far_ref = f32[24,128,256]{2,1,0:T(8,128)} custom-call(s32[96]{0:T(128)} %reshape.230.index_ref, bf16[24,128,128]{2,1,0:T(8,128)(2,1)} %copy-done.3, bf16[8,128,384]{2,1,0:T(8,128)(2,1)} %bitcast.19.ls, bf16[24,128,384]{2,1,0:T(8,128)(2,1)} %pad_maximum_fusion.os, bf16[8,128,384]{2,1,0:T(8,128)(2,1)} %bitcast.21.rs, f32[8,1,128]{2,1,0:T(1,128)} %bitcast.143, ...), custom_call_target="tpu_custom_call" | custom-call | tf_op jit(solution)/shard_map/pallas_call | solution.py:169
  131.0 0.4 convolution_bitcast_fusion
  131.9 1.0 convolution_convert_fusion
  133.3 1.0 fusion.16.down_ref
  134.2 9.4 %shard_map.147 = bf16[24,256,256]{2,1,0:T(8,128)(2,1)} custom-call(s32[24]{0:T(128)} %rank_ref.1, bf16[24,128,128]{2,1,0:T(8,128)(2,1)} %bitcast.121, bf16[128,256]{1,0:T(8,128)(2,1)} %fusion.16.down_ref, f32[24,128,256]{2,1,0:T(8,128)} %shard_map.145.far_ref, bf16[24,256,128]{2,1,0:T(8,128)(2,1)} %bitcast.116, f32[24,256,256]{2,1,0:T(8,128)} %shard_map.146.near_ref), custom_call_target="tpu_custom_call" | custom-call | tf_op jit(solution)/shard_map/pallas_call | solution.py:221
  (64 shorter events, 2.3 us)
Async XLA Ops:
  6.5 9.5 %copy-start.2 = (bf16[6144,128]{1,0:T(8,128)(2,1)S(1)}, bf16[6144,128]{1,0:T(8,128)(2,1)}, u32[]{:S(2)}) copy-start(bf16[6144,128]{1,0:T(8,128)(2,1)} %param.15) | copy-start | bytes 4718596
  6.5 9.3 %copy-start.10 = (s32[24]{0:T(128)S(1)}, s32[24]{0:T(128)}, u32[]{:S(2)}) copy-start(s32[24]{0:T(128)} %rank_ref.1) | copy-start | bytes 292
  6.5 9.4 %copy-start.8 = (bf16[128,128]{1,0:T(8,128)(2,1)S(1)}, bf16[128,128]{1,0:T(8,128)(2,1)}, u32[]{:S(2)}) copy-start(bf16[128,128]{1,0:T(8,128)(2,1)} %param.26) | copy-start | bytes 98308
  6.5 9.5 %copy-start.12 = (s32[24,128]{1,0:T(8,128)S(1)}, s32[24,128]{1,0:T(8,128)}, u32[]{:S(2)}) copy-start(s32[24,128]{1,0:T(8,128)} %param.19) | copy-start | bytes 36868
  6.5 94.9 %all-gather.3.cloned.1.call-start = ((), (), s32[]{:S(2)}) async-start(), calls=%async_computation | async-start | bytes 1179648 | tf_op jit(solution)/shard_map/all_gather | solution.py:321
  8.9 31.3 %collective-permute-start.6 = (bf16[2048,128]{1,0:T(8,128)(2,1)}, bf16[2048,128]{1,0:T(8,128)(2,1)}, u32[]{:S(2)}, u32[]{:S(2)}) collective-permute-start(bf16[2048,128]{1,0:T(8,128)(2,1)} %get-tuple-element.9), channel_id=1, source_target_pairs={{1,0},{2,1},{3,2},{4,3},{5,4},{6,5},{7,6},{8,7},{9,8},{10,9},{11,1... | collective-permute-start | bytes 1572872 | tf_op jit(solution)/shard_map/ppermute | solution.py:18
  11.5 33.6 %collective-permute-start.5 = (bf16[2048,128]{1,0:T(8,128)(2,1)}, bf16[2048,128]{1,0:T(8,128)(2,1)}, u32[]{:S(2)}, u32[]{:S(2)}) collective-permute-start(bf16[2048,128]{1,0:T(8,128)(2,1)} %get-tuple-element.10), channel_id=1, source_target_pairs={{0,1},{1,2},{2,3},{3,4},{4,5},{5,6},{6,7},{7,8},{8,9},{9,10},{10,1... | collective-permute-start | bytes 1572872 | tf_op jit(solution)/shard_map/ppermute | solution.py:17
  15.9 1.3 copy-start.13
  16.1 2.0 %copy-start = (bf16[6144,256]{1,0:T(8,128)(2,1)S(1)}, bf16[6144,256]{1,0:T(8,128)(2,1)}, u32[]{:S(2)}) copy-start(bf16[6144,256]{1,0:T(8,128)(2,1)} %param.16) | copy-start | bytes 9437188
  16.1 2.6 %copy-start.4 = (bf16[6144,128]{1,0:T(8,128)(2,1)S(1)}, bf16[6144,128]{1,0:T(8,128)(2,1)}, u32[]{:S(2)}) copy-start(bf16[6144,128]{1,0:T(8,128)(2,1)} %param.17) | copy-start | bytes 4718596
  17.2 0.9 copy-start.3
  18.7 1.1 copy-start.5
  21.2 6.9 %copy-start.1 = (bf16[6144,256]{1,0:T(8,128)(2,1)S(1)}, bf16[6144,256]{1,0:T(8,128)(2,1)}, u32[]{:S(2)}) copy-start(bf16[6144,256]{1,0:T(8,128)(2,1)} %param.16) | copy-start | bytes 9437188
  23.8 23.3 %collective-permute-start.3 = (bf16[1024,384]{1,0:T(8,128)(2,1)}, bf16[1024,384]{1,0:T(8,128)(2,1)}, u32[]{:S(2)}, u32[]{:S(2)}) collective-permute-start(bf16[1024,384]{1,0:T(8,128)(2,1)} %bitcast.18), channel_id=1, source_target_pairs={{0,1},{1,2},{2,3},{3,4},{4,5},{5,6},{6,7},{7,8},{8,9},{9,10},{10,1... | collective-permute-start | bytes 2359304 | tf_op jit(solution)/shard_map/ppermute | solution.py:17
  26.2 33.6 %collective-permute-start.4 = (bf16[1024,384]{1,0:T(8,128)(2,1)}, bf16[1024,384]{1,0:T(8,128)(2,1)}, u32[]{:S(2)}, u32[]{:S(2)}) collective-permute-start(bf16[1024,384]{1,0:T(8,128)(2,1)} %bitcast.20), channel_id=1, source_target_pairs={{1,0},{2,1},{3,2},{4,3},{5,4},{6,5},{7,6},{8,7},{9,8},{10,9},{11,1... | collective-permute-start | bytes 2359304 | tf_op jit(solution)/shard_map/ppermute | solution.py:18
  29.6 4.9 %copy-start.11 = (s32[24,4]{0,1:T(4,128)S(1)}, s32[24,4]{0,1:T(4,128)}, u32[]{:S(2)}) copy-start(s32[24,4]{0,1:T(4,128)} %param.21) | copy-start | bytes 1156
  29.6 4.9 %copy-start.9 = (s32[24,5]{0,1:T(8,128)S(1)}, s32[24,5]{0,1:T(8,128)}, u32[]{:S(2)}) copy-start(s32[24,5]{0,1:T(8,128)} %param.20) | copy-start | bytes 1444
  29.6 6.1 %copy-start.14 = (s32[1,2]{1,0:T(1,128)S(1)}, s32[1,2]{1,0:T(1,128)}, u32[]{:S(2)}) copy-start(s32[1,2]{1,0:T(1,128)} %param.29) | copy-start | bytes 28
  29.6 6.1 %copy-start.15 = (s32[1,4]{1,0:T(1,128)S(1)}, s32[1,4]{1,0:T(1,128)}, u32[]{:S(2)}) copy-start(s32[1,4]{1,0:T(1,128)} %param.25) | copy-start | bytes 52
  29.6 43.7 %collective-permute-start.8 = (bf16[2048,256]{1,0:T(8,128)(2,1)}, bf16[2048,256]{1,0:T(8,128)(2,1)}, u32[]{:S(2)}, u32[]{:S(2)}) collective-permute-start(bf16[2048,256]{1,0:T(8,128)(2,1)} %get-tuple-element.5), channel_id=1, source_target_pairs={{1,0},{2,1},{3,2},{4,3},{5,4},{6,5},{7,6},{8,7},{9,8},{10,9},{11,1... | collective-permute-start | bytes 3145736 | tf_op jit(solution)/shard_map/ppermute | solution.py:18
  40.2 33.1 %collective-permute-start.7 = (bf16[2048,256]{1,0:T(8,128)(2,1)}, bf16[2048,256]{1,0:T(8,128)(2,1)S(1)}, u32[]{:S(2)}, u32[]{:S(2)}) collective-permute-start(bf16[2048,256]{1,0:T(8,128)(2,1)} %get-tuple-element.6), channel_id=1, source_target_pairs={{0,1},{1,2},{2,3},{3,4},{4,5},{5,6},{6,7},{7,8},{8,9},{9,10},{10,1... | collective-permute-start | bytes 3145736 | tf_op jit(solution)/shard_map/ppermute | solution.py:17
  73.3 1.1 copy-start.6
  103.0 0.7 copy-start.16
  104.3 6.0 %copy-start.7 = (bf16[128,384]{1,0:T(8,128)(2,1)}, bf16[128,384]{1,0:T(8,128)(2,1)S(1)}, u32[]{:S(2)}) copy-start(bf16[128,384]{1,0:T(8,128)(2,1)S(1)} %get-tuple-element.14.after_ref) | copy-start | bytes 294916
  104.3 27.0 %collective-permute-start.2 = (bf16[128,384]{1,0:T(8,128)(2,1)S(1)}, bf16[128,384]{1,0:T(8,128)(2,1)S(1)}, u32[]{:S(2)}, u32[]{:S(2)}) collective-permute-start(bf16[128,384]{1,0:T(8,128)(2,1)S(1)} %get-tuple-element.14.after_ref), channel_id=1, source_target_pairs={{0,24},{8,0},{16,8},{24,16},{1,25},{9,1},{17,9},{25,17},{2,26},{10... | collective-permute-start | bytes 294920 | tf_op jit(solution)/shard_map/ppermute | solution.py:367
  104.4 27.2 %collective-permute-start.1 = (bf16[128,384]{1,0:T(8,128)(2,1)S(1)}, bf16[128,384]{1,0:T(8,128)(2,1)S(1)}, u32[]{:S(2)}, u32[]{:S(2)}) collective-permute-start(bf16[128,384]{1,0:T(8,128)(2,1)S(1)} %get-tuple-element.14.after_ref), channel_id=1, source_target_pairs={{0,16},{8,24},{16,0},{24,8},{1,17},{9,25},{17,1},{25,9},{2,18},{10... | collective-permute-start | bytes 294920 | tf_op jit(solution)/shard_map/ppermute | solution.py:367
  106.9 24.9 %collective-permute-start = (bf16[128,384]{1,0:T(8,128)(2,1)S(1)}, bf16[128,384]{1,0:T(8,128)(2,1)S(1)}, u32[]{:S(2)}, u32[]{:S(2)}) collective-permute-start(bf16[128,384]{1,0:T(8,128)(2,1)S(1)} %get-tuple-element.14.after_ref), channel_id=1, source_target_pairs={{0,8},{8,16},{16,24},{24,0},{1,9},{9,17},{17,25},{25,1},{2,10},{10... | collective-permute-start | bytes 294920 | tf_op jit(solution)/shard_map/ppermute | solution.py:367
Sparse Core Ops, SparseCore 0:
  21.3 43.9 all-gather.2

commit v5 on v4

--- a/solution.py
+++ b/solution.py
@@ -12,8 +12,8 @@
 def halos(cells, width):
     count = lax.axis_size(FLAT)
     ends = count - 1
-    head = cells[:width]
-    tail = cells[cells.shape[0] - width :]
+    head = jnp.concatenate([cell[:width] for cell in cells], axis=1)
+    tail = jnp.concatenate([cell[cell.shape[0] - width :] for cell in cells], axis=1)
     left = lax.ppermute(tail, FLAT, [(i, i + 1) for i in range(ends)])
     right = lax.ppermute(head, FLAT, [(i + 1, i) for i in range(ends)])
     return left, right
@@ -50,31 +50,44 @@
 def fetch_sources(index_ref, row, count, parts, buffers, sems, slot):
     for position in range(count):
         source = index_ref[row * count + position]
-        for which, (left, own, right) in enumerate(parts):
-            halo = left.shape[0]
-            mine = own.shape[0]
+        for which, (halo, mine, left, own, right) in enumerate(parts):
             target = buffers[which](slot, position)
             sem = sems.at[which, slot, position]
 
             @pl.when(source < halo)
             def _():
-                pltpu.make_async_copy(left.at[source], target, sem).start()
+                pltpu.make_async_copy(left(source), target, sem).start()
 
             @pl.when((source >= halo) & (source < halo + mine))
             def _():
-                pltpu.make_async_copy(own.at[source - halo], target, sem).start()
+                pltpu.make_async_copy(own(source - halo), target, sem).start()
 
             @pl.when(source >= halo + mine)
             def _():
-                pltpu.make_async_copy(right.at[source - halo - mine], target, sem).start()
+                pltpu.make_async_copy(right(source - halo - mine), target, sem).start()
 
 
 def wait_sources(count, parts, buffers, sems, slot):
     for position in range(count):
-        for which, (left, own, right) in enumerate(parts):
+        for which, (halo, mine, left, own, right) in enumerate(parts):
             pltpu.make_async_copy(
-                own.at[0], buffers[which](slot, position), sems.at[which, slot, position]
+                own(0), buffers[which](slot, position), sems.at[which, slot, position]
             ).wait()
+
+
+def rows_of(ref):
+    return lambda index: ref.at[index]
+
+
+def whole_rows(left, own, right):
+    return (left.shape[0], own.shape[0], rows_of(left), rows_of(own), rows_of(right))
+
+
+def lane_rows(left, own, right, start, width):
+    def halo_at(ref):
+        return lambda index: ref.at[index, :, pl.ds(start, width)]
+
+    return (left.shape[0], own.shape[0], halo_at(left), rows_of(own), halo_at(right))
 
 
 def pipelined_sources(index_ref, count, parts, buffers, sems):
@@ -94,9 +107,13 @@
     return slot
 
 
-def near_kernel(index_ref, target_ref, lp, op, rp, lw, ow, rw, ln, on, rn, out_ref, point_buf, weight_buf, norm_buf, sems):
-    count, size = point_buf.shape[1], point_buf.shape[2]
-    parts = ((lp, op, rp), (lw, ow, rw), (ln, on, rn))
+def near_kernel(index_ref, target_ref, lpw, op, rpw, ow, ln, on, rn, out_ref, point_buf, weight_buf, norm_buf, sems):
+    count, size, dims = point_buf.shape[1], point_buf.shape[2], point_buf.shape[3]
+    parts = (
+        lane_rows(lpw, op, rpw, 0, dims),
+        lane_rows(lpw, ow, rpw, dims, weight_buf.shape[-1]),
+        whole_rows(ln, on, rn),
+    )
     buffers = (
         lambda slot, position: point_buf.at[slot, position],
         lambda slot, position: weight_buf.at[slot, position],
@@ -110,7 +127,7 @@
     out_ref[0] = jnp.dot(kernel, values, preferred_element_type=jnp.float32)
 
 
-def near_field(local_points, left_points, right_points, local_weights, left_weights, right_weights, local_norms, left_norms, right_norms, near_local):
+def near_field(local_points, local_weights, left_pairs, right_pairs, local_norms, left_norms, right_norms, near_local):
     leaves, size, dims = local_points.shape
     rhs = local_weights.shape[-1]
     count = near_local.shape[1]
@@ -120,7 +137,7 @@
         grid_spec=pltpu.PrefetchScalarGridSpec(
             num_scalar_prefetch=1,
             grid=(leaves,),
-            in_specs=[pl.BlockSpec((1, size, dims), lambda l, index: (l, 0, 0))] + [anywhere] * 9,
+            in_specs=[pl.BlockSpec((1, size, dims), lambda l, index: (l, 0, 0))] + [anywhere] * 7,
             out_specs=pl.BlockSpec((1, size, rhs), lambda l, index: (l, 0, 0)),
             scratch_shapes=[
                 pltpu.VMEM((2, count, size, dims), local_points.dtype),
@@ -134,12 +151,10 @@
     )(
         near_local.reshape(-1),
         local_points,
-        left_points,
+        left_pairs,
         local_points,
-        right_points,
-        left_weights,
+        right_pairs,
         local_weights,
-        right_weights,
         left_norms,
         local_norms,
         right_norms,
@@ -148,7 +163,7 @@
 
 def far_kernel(index_ref, target_ref, ls, os, rs, ln, on, rn, after_ref, out_ref, source_buf, norm_buf, sems):
     count, rank = source_buf.shape[1], source_buf.shape[2]
-    parts = ((ls, os, rs), (ln, on, rn))
+    parts = (whole_rows(ls, os, rs), whole_rows(ln, on, rn))
     buffers = (
         lambda slot, position: source_buf.at[slot, position],
         lambda slot, position: norm_buf.at[slot, :, pl.ds(position * rank, rank)],
@@ -285,8 +300,9 @@
     first_leaf = lax.axis_index(FLAT) * leaf_count
     offset = first_leaf - REACH
 
-    left_points, right_points = halos(points, REACH * leaf_size)
-    left_weights, right_weights = halos(weights, REACH * leaf_size)
+    left_pairs, right_pairs = halos((points, weights), REACH * leaf_size)
+    left_pairs = left_pairs.reshape(REACH, leaf_size, dim_count + rhs_count)
+    right_pairs = right_pairs.reshape(REACH, leaf_size, dim_count + rhs_count)
 
     leaf_mask = (
         lax.broadcasted_iota(jnp.int32, (leaf_count, rank_count), 1) < leaf_rank[:, None]
@@ -299,7 +315,7 @@
     own_rows = jnp.concatenate([leaf_coords, leaf_up], axis=-1)
     skeleton_width = dim_count + rhs_count
     left_rows, right_rows = halos(
-        own_rows.reshape(leaf_count * rank_count, skeleton_width), REACH * rank_count
+        (own_rows.reshape(leaf_count * rank_count, skeleton_width),), REACH * rank_count
     )
 
     node_mask = (jnp.arange(node_width, dtype=jnp.int32) < node_rank[0]).astype(jnp.float32)
@@ -320,20 +336,17 @@
     node_pack = jnp.concatenate([node_coords, node_up, group_basis], axis=1)
     gathered = lax.all_gather(node_pack[None], "col", axis=0, tiled=True)
 
-    left_points = left_points.reshape(REACH, leaf_size, dim_count)
-    right_points = right_points.reshape(REACH, leaf_size, dim_count)
     near_total = near_field(
         local_points,
-        left_points,
-        right_points,
         local_weights,
-        left_weights.reshape(REACH, leaf_size, rhs_count),
-        right_weights.reshape(REACH, leaf_size, rhs_count),
+        left_pairs,
+        right_pairs,
         scaled_norms(local_points),
-        scaled_norms(left_points),
-        scaled_norms(right_points),
+        scaled_norms(left_pairs[:, :, :dim_count]),
+        scaled_norms(right_pairs[:, :, :dim_count]),
         near_list - offset,
     )
+    near_total, left_rows, right_rows = lax.optimization_barrier((near_total, left_rows, right_rows))
 
     all_coords = gathered[:, :, :dim_count]
     all_up = gathered[:, :, dim_count : dim_count + rhs_count]

time: 153 us -> 156 us (1.020)
  the two profiles are of different devices: /device:TPU:13 before, /device:TPU:2 now
where the time goes in v5:
time: 156 us; the launch traced here: 154 us
  Pallas kernels  57.1 us (37%)
  waiting for transfers between devices  31.7 us (20%)
  other arithmetic  16.1 us (10%)
  starting transfers between devices  16 us (10%)
  between operations  15.2 us (10%)
  local copies, waits for them, and re-layouts  9.36 us (6%)
  matrix products  8.57 us (5%)
    ppermute x2, waiting for transfers between devices, halos(): left = lax.ppermute(tail, FLAT, [(i, i + 1) for i in range(ends)])  31.7 us
    pallas_call x1, Pallas kernels, near_field(): pl.pallas_call(near_kernel, grid_spec=pltpu.PrefetchScalarGridSpec(num_sc...  27.1 us
    pallas_call x1, Pallas kernels, far_field(): pl.pallas_call(far_kernel, grid_spec=pltpu.PrefetchScalarGridSpec(num_sca...  20.6 us
    pallas_call x1, Pallas kernels, final_field(): pl.pallas_call(final_kernel, grid_spec=pltpu.PrefetchScalarGridSpec(num_s...  9.36 us
    ppermute x2, starting transfers between devices, halos(): right = lax.ppermute(head, FLAT, [(i + 1, i) for i in range(ends)])  7.41 us
    reduce_sum x5, other arithmetic, scaled_norms(): jnp.sum(wide * wide, axis=-1) * (-2.0 / cells.shape[-1])  5.97 us
    ppermute x3, starting transfers between devices, body(): lax.ppermute(group_pack, 'row', [(r, (r + shift) % rows) for r in range(r...  4.67 us
    unnamed x40, local copies, waits for them, and re-layouts  4.62 us
  transfers between devices with their start and end apart: 8, of which 1 were waited for; matrix products, arithmetic and copies ran while one was open for 14% of the time, Pallas kernels for 31%

profile of v5, /device:TPU:2, one launch (start us, length us, event | category | flops | bytes accessed | tf_op | source)
XLA Modules:
  0.0 154.0 jit_solution(12760860592065325290)
XLA Ops:
  6.5 0.9 copy.28
  7.4 0.7 fusion.53
  9.5 2.6 %multiply_reduce_fusion.1 = (f32[24,128]{1,0:T(8,128)S(1)}, bf16[24,128,128]{2,1,0:T(8,128)(2,1)S(1)}) fusion(bf16[24,256,128]{2,1,0:T(8,128)(2,1)} %bitcast.110, s32[24,128]{1,0:T(8,128)} %param.19), kind=kOutput, calls=%fused_computation.14 | convolution fusion | flops 203682816 | bytes 2383872 | tf_op jit(solution)/shard_map/bkp,bpc->bkc/dot_general | solution.py:268
  12.1 0.6 multiply_reduce_fusion.8
  12.7 0.3 copy-done.2
  13.0 1.0 multiply_convert_fusion
  14.1 0.6 fusion.21
  14.7 0.7 pad_maximum_fusion.5
  15.5 1.8 %fusion.65 = (bf16[2048,256]{1,0:T(8,128)(2,1)S(1)}, bf16[2048,256]{1,0:T(8,128)(2,1)S(1)}) fusion(bf16[6144,256]{1,0:T(8,128)(2,1)} %param.16), kind=kLoop, calls=%fused_computation.115 | loop fusion | bytes 4194304 | tf_op jit(solution)/shard_map/slice | solution.py:15
  17.3 0.2 copy-done.1
  17.6 1.4 pad_maximum_fusion.1
  18.9 1.9 %collective-permute-start.3 = (bf16[2048,384]{1,0:T(8,128)(2,1)}, bf16[2048,384]{1,0:T(8,128)(2,1)}, u32[]{:S(2)}, u32[]{:S(2)}) collective-permute-start(bf16[2048,384]{1,0:T(8,128)(2,1)} %pad_maximum_fusion.1), channel_id=1, source_target_pairs={{0,1},{1,2},{2,3},{3,4},{4,5},{5,6},{6,7},{7,8},{8,9},{9,10},{10,1... | collective-permute-start | bytes 4718600 | tf_op jit(solution)/shard_map/ppermute | solution.py:17
  20.9 1.4 pad_maximum_fusion.2
  22.2 3.8 %collective-permute-start.4 = (bf16[2048,384]{1,0:T(8,128)(2,1)}, bf16[2048,384]{1,0:T(8,128)(2,1)}, u32[]{:S(2)}, u32[]{:S(2)}) collective-permute-start(bf16[2048,384]{1,0:T(8,128)(2,1)} %pad_maximum_fusion.2), channel_id=1, source_target_pairs={{1,0},{2,1},{3,2},{4,3},{5,4},{6,5},{7,6},{8,7},{9,8},{10,9},{11,1... | collective-permute-start | bytes 4718600 | tf_op jit(solution)/shard_map/ppermute | solution.py:18
  26.0 1.4 fusion.24
  27.4 2.0 %collective-permute-start.5 = (bf16[1024,384]{1,0:T(8,128)(2,1)}, bf16[1024,384]{1,0:T(8,128)(2,1)}, u32[]{:S(2)}, u32[]{:S(2)}) collective-permute-start(bf16[1024,384]{1,0:T(8,128)(2,1)} %bitcast.22), channel_id=1, source_target_pairs={{0,1},{1,2},{2,3},{3,4},{4,5},{5,6},{6,7},{7,8},{8,9},{9,10},{10,1... | collective-permute-start | bytes 2359304 | tf_op jit(solution)/shard_map/ppermute | solution.py:17
  29.5 3.6 %collective-permute-start.6 = (bf16[1024,384]{1,0:T(8,128)(2,1)}, bf16[1024,384]{1,0:T(8,128)(2,1)}, u32[]{:S(2)}, u32[]{:S(2)}) collective-permute-start(bf16[1024,384]{1,0:T(8,128)(2,1)} %bitcast.23), channel_id=1, source_target_pairs={{1,0},{2,1},{3,2},{4,3},{5,4},{6,5},{7,6},{8,7},{9,8},{10,9},{11,1... | collective-permute-start | bytes 2359304 | tf_op jit(solution)/shard_map/ppermute | solution.py:18
  33.2 0.9 multiply_reduce_fusion
  34.1 0.6 broadcast_multiply_fusion.1
  34.7 0.6 broadcast_multiply_fusion
  35.3 1.8 %pad_maximum_fusion.os = bf16[24,128,384]{2,1,0:T(8,128)(2,1)} fusion(bf16[24,128,128]{2,1,0:T(8,128)(2,1)S(1)} %copy-done.4, bf16[24,128,256]{2,1,0:T(8,128)(2,1)S(1)} %multiply_convert_fusion), kind=kLoop, calls=%fused_computation.5 | loop fusion | flops 4718592 | bytes 4718592 | tf_op jit(solution)/shard_map/concatenate | solution.py:315
  37.3 0.6 reshape.214.index_ref
  38.1 0.7 reshape.215.index_ref
  38.8 31.7 %collective-permute-done.3 = bf16[2048,384]{1,0:T(8,128)(2,1)} collective-permute-done((bf16[2048,384]{1,0:T(8,128)(2,1)}, bf16[2048,384]{1,0:T(8,128)(2,1)}, u32[]{:S(2)}, u32[]{:S(2)}) %collective-permute-start.3) | collective-permute-done | bytes 1572896 | tf_op jit(solution)/shard_map/ppermute | solution.py:17
  70.5 1.4 multiply_reduce_fusion.3
  71.9 0.6 copy.37.ln
  72.5 1.4 multiply_reduce_fusion.2
  73.9 0.6 mul.200.rn
  74.5 27.1 %shard_map.145.near_ref = f32[24,256,256]{2,1,0:T(8,128)} custom-call(s32[120]{0:T(128)} %reshape.215.index_ref, bf16[24,256,128]{2,1,0:T(8,128)(2,1)} %bitcast.111, bf16[8,256,384]{2,1,0:T(8,128)(2,1)} %bitcast.18.lpw, bf16[24,256,128]{2,1,0:T(8,128)(2,1)} %bitcast.112, bf16[8,256,384]{2,1,0:T(8,128)(2,1)} %bitcast.19.rpw, bf16[24,256,256]{2,1,0:T(8,128)(2,1)} %bitcast.108, ...), custom_call_target="tpu_custom_call" | custom-call | tf_op jit(solution)/shard_map/pallas_call | solution.py:135
  101.6 1.2 multiply_reduce_fusion.5
  102.7 1.2 multiply_reduce_fusion.4
  103.9 0.6 broadcast_multiply_fusion.4
  104.5 0.6 broadcast_multiply_fusion.3
  105.1 1.5 copy.45
  106.7 0.3 copy.44
  107.0 0.2 copy.42
  107.3 0.4 multiply_reduce_fusion.9
  107.6 0.2 fusion.17
  108.0 3.0 %collective-permute-start.1 = (bf16[128,384]{1,0:T(8,128)(2,1)S(1)}, bf16[128,384]{1,0:T(8,128)(2,1)S(1)}, u32[]{:S(2)}, u32[]{:S(2)}) collective-permute-start(bf16[128,384]{1,0:T(8,128)(2,1)S(1)} %get-tuple-element.20.after_ref), channel_id=1, source_target_pairs={{0,16},{8,24},{16,0},{24,8},{1,17},{9,25},{17,1},{25,9},{2,18},{10... | collective-permute-start | bytes 294920 | tf_op jit(solution)/shard_map/ppermute | solution.py:380
  111.0 1.6 %collective-permute-start = (bf16[128,384]{1,0:T(8,128)(2,1)S(1)}, bf16[128,384]{1,0:T(8,128)(2,1)S(1)}, u32[]{:S(2)}, u32[]{:S(2)}) collective-permute-start(bf16[128,384]{1,0:T(8,128)(2,1)S(1)} %get-tuple-element.20.after_ref), channel_id=1, source_target_pairs={{0,8},{8,16},{16,24},{24,0},{1,9},{9,17},{17,25},{25,1},{2,10},{10... | collective-permute-start | bytes 294920 | tf_op jit(solution)/shard_map/ppermute | solution.py:380
  112.6 0.3 copy.53
  112.9 0.4 convolution_convert_fusion.1
  113.3 0.3 fusion.8
  113.9 20.6 %shard_map.146.far_ref = f32[24,128,256]{2,1,0:T(8,128)} custom-call(s32[96]{0:T(128)} %reshape.214.index_ref, bf16[24,128,128]{2,1,0:T(8,128)(2,1)} %copy-done.2, bf16[8,128,384]{2,1,0:T(8,128)(2,1)} %bitcast.24.ls, bf16[24,128,384]{2,1,0:T(8,128)(2,1)} %pad_maximum_fusion.os, bf16[8,128,384]{2,1,0:T(8,128)(2,1)} %bitcast.25.rs, f32[8,1,128]{2,1,0:T(1,128)} %bitcast.138, ...), custom_call_target="tpu_custom_call" | custom-call | tf_op jit(solution)/shard_map/pallas_call | solution.py:184
  134.5 0.4 convolution_bitcast_fusion
  135.5 1.0 convolution_convert_fusion
  136.8 1.0 fusion.16.down_ref
  137.8 9.4 %shard_map.147 = bf16[24,256,256]{2,1,0:T(8,128)(2,1)} custom-call(s32[24]{0:T(128)} %rank_ref.1, bf16[24,128,128]{2,1,0:T(8,128)(2,1)} %bitcast.119, bf16[128,256]{1,0:T(8,128)(2,1)} %fusion.16.down_ref, f32[24,128,256]{2,1,0:T(8,128)} %shard_map.146.far_ref, bf16[24,256,128]{2,1,0:T(8,128)(2,1)} %bitcast.114, f32[24,256,256]{2,1,0:T(8,128)} %shard_map.145.near_ref), custom_call_target="tpu_custom_call" | custom-call | tf_op jit(solution)/shard_map/pallas_call | solution.py:236
  (60 shorter events, 1.9 us)
Async XLA Ops:
  6.5 98.6 %all-gather.3.cloned.1.call-start = ((), (), s32[]{:S(2)}) async-start(), calls=%async_computation | async-start | bytes 1179648 | tf_op jit(solution)/shard_map/all_gather | solution.py:337
  6.5 5.6 %copy-start.11 = (s32[1,128]{1,0:T(1,128)S(1)}, s32[1,128]{1,0:T(1,128)}, u32[]{:S(2)}) copy-start(s32[1,128]{1,0:T(1,128)} %param.24) | copy-start | bytes 1540
  9.5 3.5 %copy-start = (bf16[6144,256]{1,0:T(8,128)(2,1)S(1)}, bf16[6144,256]{1,0:T(8,128)(2,1)}, u32[]{:S(2)}) copy-start(bf16[6144,256]{1,0:T(8,128)(2,1)} %param.16) | copy-start | bytes 9437188
  9.5 3.5 %copy-start.5 = (bf16[6144,128]{1,0:T(8,128)(2,1)S(1)}, bf16[6144,128]{1,0:T(8,128)(2,1)}, u32[]{:S(2)}) copy-start(bf16[6144,128]{1,0:T(8,128)(2,1)} %param.17) | copy-start | bytes 4718596
  12.1 0.9 copy-start.2
  13.0 1.1 copy-start.6
  15.4 2.0 %copy-start.1 = (bf16[6144,128]{1,0:T(8,128)(2,1)S(1)}, bf16[6144,128]{1,0:T(8,128)(2,1)}, u32[]{:S(2)}) copy-start(bf16[6144,128]{1,0:T(8,128)(2,1)} %param.15) | copy-start | bytes 4718596
  18.9 51.5 %collective-permute-start.3 = (bf16[2048,384]{1,0:T(8,128)(2,1)}, bf16[2048,384]{1,0:T(8,128)(2,1)}, u32[]{:S(2)}, u32[]{:S(2)}) collective-permute-start(bf16[2048,384]{1,0:T(8,128)(2,1)} %pad_maximum_fusion.1), channel_id=1, source_target_pairs={{0,1},{1,2},{2,3},{3,4},{4,5},{5,6},{6,7},{7,8},{8,9},{9,10},{10,1... | collective-permute-start | bytes 4718600 | tf_op jit(solution)/shard_map/ppermute | solution.py:17
  20.8 5.1 %copy-start.3 = (bf16[24,128,128]{2,1,0:T(8,128)(2,1)S(1)}, bf16[24,128,128]{2,1,0:T(8,128)(2,1)}, u32[]{:S(2)}) copy-start(bf16[24,128,128]{2,1,0:T(8,128)(2,1)} %copy-done.2) | copy-start | bytes 2359300
  22.2 10.9 %copy-start.12 = (s32[1,4]{1,0:T(1,128)S(1)}, s32[1,4]{1,0:T(1,128)}, u32[]{:S(2)}) copy-start(s32[1,4]{1,0:T(1,128)} %param.25) | copy-start | bytes 52
  22.2 11.0 %copy-start.10 = (s32[24,4]{0,1:T(4,128)S(1)}, s32[24,4]{0,1:T(4,128)}, u32[]{:S(2)}) copy-start(s32[24,4]{0,1:T(4,128)} %param.21) | copy-start | bytes 1156
  22.2 50.2 %collective-permute-start.4 = (bf16[2048,384]{1,0:T(8,128)(2,1)}, bf16[2048,384]{1,0:T(8,128)(2,1)}, u32[]{:S(2)}, u32[]{:S(2)}) collective-permute-start(bf16[2048,384]{1,0:T(8,128)(2,1)} %pad_maximum_fusion.2), channel_id=1, source_target_pairs={{1,0},{2,1},{3,2},{4,3},{5,4},{6,5},{7,6},{8,7},{9,8},{10,9},{11,1... | collective-permute-start | bytes 4718600 | tf_op jit(solution)/shard_map/ppermute | solution.py:18
  27.4 6.7 %copy-start.9 = (s32[24,5]{0,1:T(8,128)S(1)}, s32[24,5]{0,1:T(8,128)}, u32[]{:S(2)}) copy-start(s32[24,5]{0,1:T(8,128)} %param.20) | copy-start | bytes 1444
  27.4 7.9 %copy-start.13 = (s32[1,2]{1,0:T(1,128)S(1)}, s32[1,2]{1,0:T(1,128)}, u32[]{:S(2)}) copy-start(s32[1,2]{1,0:T(1,128)} %param.29) | copy-start | bytes 28
  27.4 74.1 %collective-permute-start.5 = (bf16[1024,384]{1,0:T(8,128)(2,1)}, bf16[1024,384]{1,0:T(8,128)(2,1)}, u32[]{:S(2)}, u32[]{:S(2)}) collective-permute-start(bf16[1024,384]{1,0:T(8,128)(2,1)} %bitcast.22), channel_id=1, source_target_pairs={{0,1},{1,2},{2,3},{3,4},{4,5},{5,6},{6,7},{7,8},{8,9},{9,10},{10,1... | collective-permute-start | bytes 2359304 | tf_op jit(solution)/shard_map/ppermute | solution.py:17
  29.5 72.1 %collective-permute-start.6 = (bf16[1024,384]{1,0:T(8,128)(2,1)}, bf16[1024,384]{1,0:T(8,128)(2,1)}, u32[]{:S(2)}, u32[]{:S(2)}) collective-permute-start(bf16[1024,384]{1,0:T(8,128)(2,1)} %bitcast.23), channel_id=1, source_target_pairs={{1,0},{2,1},{3,2},{4,3},{5,4},{6,5},{7,6},{8,7},{9,8},{10,9},{11,1... | collective-permute-start | bytes 2359304 | tf_op jit(solution)/shard_map/ppermute | solution.py:18
  33.2 2.2 %copy-start.4 = (bf16[24,128,128]{2,1,0:T(8,128)(2,1)S(1)}, bf16[24,128,128]{2,1,0:T(8,128)(2,1)}, u32[]{:S(2)}) copy-start(bf16[24,128,128]{2,1,0:T(8,128)(2,1)} %copy-done.2) | copy-start | bytes 2359300
  106.6 0.7 copy-start.14
  107.9 5.9 %copy-start.7 = (bf16[128,384]{1,0:T(8,128)(2,1)}, bf16[128,384]{1,0:T(8,128)(2,1)S(1)}, u32[]{:S(2)}) copy-start(bf16[128,384]{1,0:T(8,128)(2,1)S(1)} %get-tuple-element.20.after_ref) | copy-start | bytes 294916
  107.9 27.0 %collective-permute-start.2 = (bf16[128,384]{1,0:T(8,128)(2,1)S(1)}, bf16[128,384]{1,0:T(8,128)(2,1)S(1)}, u32[]{:S(2)}, u32[]{:S(2)}) collective-permute-start(bf16[128,384]{1,0:T(8,128)(2,1)S(1)} %get-tuple-element.20.after_ref), channel_id=1, source_target_pairs={{0,24},{8,0},{16,8},{24,16},{1,25},{9,1},{17,9},{25,17},{2,26},{10... | collective-permute-start | bytes 294920 | tf_op jit(solution)/shard_map/ppermute | solution.py:380
  108.0 27.1 %collective-permute-start.1 = (bf16[128,384]{1,0:T(8,128)(2,1)S(1)}, bf16[128,384]{1,0:T(8,128)(2,1)S(1)}, u32[]{:S(2)}, u32[]{:S(2)}) collective-permute-start(bf16[128,384]{1,0:T(8,128)(2,1)S(1)} %get-tuple-element.20.after_ref), channel_id=1, source_target_pairs={{0,16},{8,24},{16,0},{24,8},{1,17},{9,25},{17,1},{25,9},{2,18},{10... | collective-permute-start | bytes 294920 | tf_op jit(solution)/shard_map/ppermute | solution.py:380
  111.0 24.2 %collective-permute-start = (bf16[128,384]{1,0:T(8,128)(2,1)S(1)}, bf16[128,384]{1,0:T(8,128)(2,1)S(1)}, u32[]{:S(2)}, u32[]{:S(2)}) collective-permute-start(bf16[128,384]{1,0:T(8,128)(2,1)S(1)} %get-tuple-element.20.after_ref), channel_id=1, source_target_pairs={{0,8},{8,16},{16,24},{24,0},{1,9},{9,17},{17,25},{25,1},{2,10},{10... | collective-permute-start | bytes 294920 | tf_op jit(solution)/shard_map/ppermute | solution.py:380
  135.4 1.4 copy-start.8
Sparse Core Ops, SparseCore 0:
  15.6 49.8 all-gather.2

commit v6 on v5

--- a/solution.py
+++ b/solution.py
@@ -53,6 +53,9 @@
         for which, (halo, mine, left, own, right) in enumerate(parts):
             target = buffers[which](slot, position)
             sem = sems.at[which, slot, position]
+            if left is None:
+                pltpu.make_async_copy(own(source - halo), target, sem).start()
+                continue
 
             @pl.when(source < halo)
             def _():
@@ -83,6 +86,10 @@
     return (left.shape[0], own.shape[0], rows_of(left), rows_of(own), rows_of(right))
 
 
+def own_rows_only(own):
+    return (REACH, own.shape[0], None, rows_of(own), None)
+
+
 def lane_rows(left, own, right, start, width):
     def halo_at(ref):
         return lambda index: ref.at[index, :, pl.ds(start, width)]
@@ -90,55 +97,81 @@
     return (left.shape[0], own.shape[0], halo_at(left), rows_of(own), halo_at(right))
 
 
-def pipelined_sources(index_ref, count, parts, buffers, sems):
-    leaf = pl.program_id(0)
-    leaves = pl.num_programs(0)
-    slot = leaf % 2
-
-    @pl.when(leaf == 0)
+def pipelined_sources(index_ref, count, parts, buffers, sems, leaf_of):
+    step = pl.program_id(0)
+    steps = pl.num_programs(0)
+    slot = step % 2
+
+    @pl.when(step == 0)
     def _():
-        fetch_sources(index_ref, 0, count, parts, buffers, sems, 0)
-
-    @pl.when(leaf + 1 < leaves)
+        fetch_sources(index_ref, leaf_of(0), count, parts, buffers, sems, 0)
+
+    @pl.when(step + 1 < steps)
     def _():
-        fetch_sources(index_ref, leaf + 1, count, parts, buffers, sems, 1 - slot)
+        fetch_sources(index_ref, leaf_of(step + 1), count, parts, buffers, sems, 1 - slot)
 
     wait_sources(count, parts, buffers, sems, slot)
     return slot
 
 
-def near_kernel(index_ref, target_ref, lpw, op, rpw, ow, ln, on, rn, out_ref, point_buf, weight_buf, norm_buf, sems):
+def leaf_order(leaves, edges):
+    low, high = REACH, leaves - REACH
+    if high <= low:
+        return (lambda step: step), leaves, None
+    if not edges:
+        return (lambda step: step + low), high - low, None
+    gap = high - low
+    return (lambda step: step + gap * jnp.asarray(step >= low, jnp.int32)), leaves - gap, gap
+
+
+def near_kernel(leaf_of, halo, index_ref, target_ref, *refs):
+    inputs = 8 if halo else 3
+    out_ref = refs[inputs]
+    point_buf, weight_buf, norm_buf, sems = refs[inputs + 1 :]
     count, size, dims = point_buf.shape[1], point_buf.shape[2], point_buf.shape[3]
-    parts = (
-        lane_rows(lpw, op, rpw, 0, dims),
-        lane_rows(lpw, ow, rpw, dims, weight_buf.shape[-1]),
-        whole_rows(ln, on, rn),
-    )
+    if halo:
+        lpw, op, rpw, ow, ln, on, rn = refs[:7]
+        parts = (
+            lane_rows(lpw, op, rpw, 0, dims),
+            lane_rows(lpw, ow, rpw, dims, weight_buf.shape[-1]),
+            whole_rows(ln, on, rn),
+        )
+    else:
+        parts = tuple(own_rows_only(ref) for ref in refs[:3])
     buffers = (
         lambda slot, position: point_buf.at[slot, position],
         lambda slot, position: weight_buf.at[slot, position],
         lambda slot, position: norm_buf.at[slot, :, pl.ds(position * size, size)],
     )
-    slot = pipelined_sources(index_ref, count, parts, buffers, sems)
+    slot = pipelined_sources(index_ref, count, parts, buffers, sems, leaf_of)
     target = target_ref[0]
-    sources = point_buf[slot].reshape(count * size, point_buf.shape[-1])
+    sources = point_buf[slot].reshape(count * size, dims)
     values = weight_buf[slot].reshape(count * size, weight_buf.shape[-1])
     kernel = scaled_kernel(target, target_square_of(target), sources, norm_buf[slot])
     out_ref[0] = jnp.dot(kernel, values, preferred_element_type=jnp.float32)
 
 
-def near_field(local_points, local_weights, left_pairs, right_pairs, local_norms, left_norms, right_norms, near_local):
+def near_field(local_points, local_weights, local_norms, near_local, halo_inputs=None, previous=None):
     leaves, size, dims = local_points.shape
     rhs = local_weights.shape[-1]
     count = near_local.shape[1]
+    halo = halo_inputs is not None
+    leaf_of, steps, gap = leaf_order(leaves, halo)
     anywhere = pl.BlockSpec(memory_space=pl.ANY)
+    if halo:
+        left_pairs, right_pairs, left_norms, right_norms = halo_inputs
+        inputs = (left_pairs, local_points, right_pairs, local_weights, left_norms, local_norms, right_norms, previous)
+    else:
+        inputs = (local_points, local_weights, local_norms)
+    aliases = {len(inputs) + 1: 0} if previous is not None else {}
+    by_leaf = lambda step, index: (leaf_of(step), 0, 0)
     return pl.pallas_call(
-        near_kernel,
+        lambda *refs: near_kernel(leaf_of, halo, *refs),
         grid_spec=pltpu.PrefetchScalarGridSpec(
             num_scalar_prefetch=1,
-            grid=(leaves,),
-            in_specs=[pl.BlockSpec((1, size, dims), lambda l, index: (l, 0, 0))] + [anywhere] * 7,
-            out_specs=pl.BlockSpec((1, size, rhs), lambda l, index: (l, 0, 0)),
+            grid=(steps,),
+            in_specs=[pl.BlockSpec((1, size, dims), by_leaf)] + [anywhere] * len(inputs),
+            out_specs=pl.BlockSpec((1, size, rhs), by_leaf),
             scratch_shapes=[
                 pltpu.VMEM((2, count, size, dims), local_points.dtype),
                 pltpu.VMEM((2, count, size, rhs), local_weights.dtype),
@@ -147,28 +180,26 @@
             ],
         ),
         out_shape=jax.ShapeDtypeStruct((leaves, size, rhs), jnp.float32),
+        input_output_aliases=aliases,
         compiler_params=pltpu.CompilerParams(dimension_semantics=("arbitrary",)),
-    )(
-        near_local.reshape(-1),
-        local_points,
-        left_pairs,
-        local_points,
-        right_pairs,
-        local_weights,
-        left_norms,
-        local_norms,
-        right_norms,
-    )
-
-
-def far_kernel(index_ref, target_ref, ls, os, rs, ln, on, rn, after_ref, out_ref, source_buf, norm_buf, sems):
+    )(near_local.reshape(-1), local_points, *inputs)
+
+
+def far_kernel(leaf_of, halo, index_ref, target_ref, *refs):
+    inputs = 8 if halo else 2
+    out_ref = refs[inputs]
+    source_buf, norm_buf, sems = refs[inputs + 1 :]
     count, rank = source_buf.shape[1], source_buf.shape[2]
-    parts = (whole_rows(ls, os, rs), whole_rows(ln, on, rn))
+    if halo:
+        ls, os, rs, ln, on, rn = refs[:6]
+        parts = (whole_rows(ls, os, rs), whole_rows(ln, on, rn))
+    else:
+        parts = tuple(own_rows_only(ref) for ref in refs[:2])
     buffers = (
         lambda slot, position: source_buf.at[slot, position],
         lambda slot, position: norm_buf.at[slot, :, pl.ds(position * rank, rank)],
     )
-    slot = pipelined_sources(index_ref, count, parts, buffers, sems)
+    slot = pipelined_sources(index_ref, count, parts, buffers, sems, leaf_of)
     target = target_ref[0]
     dims = target.shape[-1]
     sources = source_buf[slot].reshape(count * rank, source_buf.shape[-1])
@@ -176,18 +207,27 @@
     out_ref[0] = jnp.dot(kernel, sources[:, dims:], preferred_element_type=jnp.float32)
 
 
-def far_field(leaf_coords, left_rows, own_rows, right_rows, left_norms, own_norms, right_norms, far_local, after):
+def far_field(leaf_coords, own_rows, own_norms, far_local, halo_inputs=None, previous=None, after=None):
     leaves, rank, dims = leaf_coords.shape
     width = own_rows.shape[-1]
     count = far_local.shape[1]
+    halo = halo_inputs is not None
+    leaf_of, steps, gap = leaf_order(leaves, halo)
     anywhere = pl.BlockSpec(memory_space=pl.ANY)
+    if halo:
+        left_rows, right_rows, left_norms, right_norms = halo_inputs
+        inputs = (left_rows, own_rows, right_rows, left_norms, own_norms, right_norms, after, previous)
+    else:
+        inputs = (own_rows, own_norms)
+    aliases = {len(inputs) + 1: 0} if previous is not None else {}
+    by_leaf = lambda step, index: (leaf_of(step), 0, 0)
     return pl.pallas_call(
-        far_kernel,
+        lambda *refs: far_kernel(leaf_of, halo, *refs),
         grid_spec=pltpu.PrefetchScalarGridSpec(
             num_scalar_prefetch=1,
-            grid=(leaves,),
-            in_specs=[pl.BlockSpec((1, rank, dims), lambda l, index: (l, 0, 0))] + [anywhere] * 7,
-            out_specs=pl.BlockSpec((1, rank, width - dims), lambda l, index: (l, 0, 0)),
+            grid=(steps,),
+            in_specs=[pl.BlockSpec((1, rank, dims), by_leaf)] + [anywhere] * len(inputs),
+            out_specs=pl.BlockSpec((1, rank, width - dims), by_leaf),
             scratch_shapes=[
                 pltpu.VMEM((2, count, rank, width), own_rows.dtype),
                 pltpu.VMEM((2, 1, count * rank), jnp.float32),
@@ -195,18 +235,9 @@
             ],
         ),
         out_shape=jax.ShapeDtypeStruct((leaves, rank, width - dims), jnp.float32),
+        input_output_aliases=aliases,
         compiler_params=pltpu.CompilerParams(dimension_semantics=("arbitrary",)),
-    )(
-        far_local.reshape(-1),
-        leaf_coords,
-        left_rows,
-        own_rows,
-        right_rows,
-        left_norms,
-        own_norms,
-        right_norms,
-        after,
-    )
+    )(far_local.reshape(-1), leaf_coords, *inputs)
 
 
 def final_kernel(rank_ref, basis_ref, down_ref, far_ref, leaf_base_ref, near_ref, out_ref):
@@ -336,15 +367,21 @@
     node_pack = jnp.concatenate([node_coords, node_up, group_basis], axis=1)
     gathered = lax.all_gather(node_pack[None], "col", axis=0, tiled=True)
 
+    near_local = near_list - offset
+    local_norms = scaled_norms(local_points)
+    near_inner = near_field(local_points, local_weights, local_norms, near_local)
     near_total = near_field(
         local_points,
         local_weights,
-        left_pairs,
-        right_pairs,
-        scaled_norms(local_points),
-        scaled_norms(left_pairs[:, :, :dim_count]),
-        scaled_norms(right_pairs[:, :, :dim_count]),
-        near_list - offset,
+        local_norms,
+        near_local,
+        (
+            left_pairs,
+            right_pairs,
+            scaled_norms(left_pairs[:, :, :dim_count]),
+            scaled_norms(right_pairs[:, :, :dim_count]),
+        ),
+        near_inner,
     )
     near_total, left_rows, right_rows = lax.optimization_barrier((near_total, left_rows, right_rows))
 
@@ -364,15 +401,21 @@
     group_pack = jnp.concatenate([group_coords, group_up], axis=1)
     left_rows = left_rows.reshape(REACH, rank_count, skeleton_width)
     right_rows = right_rows.reshape(REACH, rank_count, skeleton_width)
+    far_local = far_list - offset
+    coord_norms = scaled_norms(leaf_coords)
+    far_inner = far_field(leaf_coords, own_rows, coord_norms, far_local)
     far_total = far_field(
         leaf_coords,
-        left_rows,
         own_rows,
-        right_rows,
-        scaled_norms(left_rows[:, :, :dim_count]),
-        scaled_norms(leaf_coords),
-        scaled_norms(right_rows[:, :, :dim_count]),
-        far_list - offset,
+        coord_norms,
+        far_local,
+        (
+            left_rows,
+            right_rows,
+            scaled_norms(left_rows[:, :, :dim_count]),
+            scaled_norms(right_rows[:, :, :dim_count]),
+        ),
+        far_inner,
         group_pack,
     )
     rows = lax.axis_size("row")

time: 156 us -> 143 us (0.917)
  waiting for transfers between devices: 31.7 us -> 11.8 us
  Pallas kernels: 57.1 us -> 63.4 us
    ppermute x2, waiting for transfers between devices: 31.7 us -> 11.8 us  [halos(): left = lax.ppermute(tail, FLAT, [(i, i + 1) for i in range(ends)])]
    pallas_call x2 -> x4, Pallas kernels: 47.7 us -> 54.1 us  [the longest x2 30.4 us: near_field(): pl.pallas_call(lambda *refs: near_kernel(leaf_of, halo, *refs), grid_spec...]
  transfers between devices with their start and end apart: 8 -> 8, of which waited for: 1 -> 1; matrix products, arithmetic and copies ran while one was open for 14% -> 15% of each run, Pallas kernels for 31% -> 38%
where the time goes in v6:
time: 143 us; the launch traced here: 140 us
  Pallas kernels  63.4 us (44%)
  other arithmetic  16.1 us (11%)
  starting transfers between devices  16 us (11%)
  between operations  15.2 us (11%)
  waiting for transfers between devices  11.8 us (8%)
  local copies, waits for them, and re-layouts  9.33 us (7%)
  matrix products  8.56 us (6%)
    pallas_call x2, Pallas kernels, near_field(): pl.pallas_call(lambda *refs: near_kernel(leaf_of, halo, *refs), grid_spec...  30.4 us
    pallas_call x2, Pallas kernels, far_field(): pl.pallas_call(lambda *refs: far_kernel(leaf_of, halo, *refs), grid_spec=...  23.7 us
    ppermute x2, waiting for transfers between devices, halos(): left = lax.ppermute(tail, FLAT, [(i, i + 1) for i in range(ends)])  11.8 us
    pallas_call x1, Pallas kernels, final_field(): pl.pallas_call(final_kernel, grid_spec=pltpu.PrefetchScalarGridSpec(num_s...  9.36 us
    ppermute x2, starting transfers between devices, halos(): right = lax.ppermute(head, FLAT, [(i + 1, i) for i in range(ends)])  7.41 us
    reduce_sum x5, other arithmetic, scaled_norms(): jnp.sum(wide * wide, axis=-1) * (-2.0 / cells.shape[-1])  5.97 us
    ppermute x3, starting transfers between devices, body(): lax.ppermute(group_pack, 'row', [(r, (r + shift) % rows) for r in range(r...  4.66 us
    unnamed x40, local copies, waits for them, and re-layouts  4.63 us
  transfers between devices with their start and end apart: 8, of which 1 were waited for; matrix products, arithmetic and copies ran while one was open for 15% of the time, Pallas kernels for 38%

profile of v6, /device:TPU:2, one launch (start us, length us, event | category | flops | bytes accessed | tf_op | source)
XLA Modules:
  0.0 140.4 jit_solution(3908963520266569029)
XLA Ops:
  6.5 0.9 copy.30
  7.4 0.7 fusion.53
  9.5 2.6 %multiply_reduce_fusion.1 = (f32[24,128]{1,0:T(8,128)S(1)}, bf16[24,128,128]{2,1,0:T(8,128)(2,1)S(1)}) fusion(bf16[24,256,128]{2,1,0:T(8,128)(2,1)} %bitcast.107, s32[24,128]{1,0:T(8,128)} %param.19), kind=kOutput, calls=%fused_computation.14 | convolution fusion | flops 203682816 | bytes 2383872 | tf_op jit(solution)/shard_map/bkp,bpc->bkc/dot_general | solution.py:299
  12.1 0.6 multiply_reduce_fusion.8
  12.7 0.3 copy-done.2
  13.0 1.0 multiply_convert_fusion
  14.1 0.6 fusion.21
  14.8 0.7 pad_maximum_fusion.5
  15.5 1.8 %fusion.65 = (bf16[2048,256]{1,0:T(8,128)(2,1)S(1)}, bf16[2048,256]{1,0:T(8,128)(2,1)S(1)}) fusion(bf16[6144,256]{1,0:T(8,128)(2,1)} %param.16), kind=kLoop, calls=%fused_computation.115 | loop fusion | bytes 4194304 | tf_op jit(solution)/shard_map/slice | solution.py:15
  17.6 1.4 pad_maximum_fusion.1
  19.0 1.9 %collective-permute-start.3 = (bf16[2048,384]{1,0:T(8,128)(2,1)}, bf16[2048,384]{1,0:T(8,128)(2,1)}, u32[]{:S(2)}, u32[]{:S(2)}) collective-permute-start(bf16[2048,384]{1,0:T(8,128)(2,1)} %pad_maximum_fusion.1), channel_id=1, source_target_pairs={{0,1},{1,2},{2,3},{3,4},{4,5},{5,6},{6,7},{7,8},{8,9},{9,10},{10,1... | collective-permute-start | bytes 4718600 | tf_op jit(solution)/shard_map/ppermute | solution.py:17
  20.9 1.4 pad_maximum_fusion.2
  22.3 3.8 %collective-permute-start.4 = (bf16[2048,384]{1,0:T(8,128)(2,1)}, bf16[2048,384]{1,0:T(8,128)(2,1)}, u32[]{:S(2)}, u32[]{:S(2)}) collective-permute-start(bf16[2048,384]{1,0:T(8,128)(2,1)} %pad_maximum_fusion.2), channel_id=1, source_target_pairs={{1,0},{2,1},{3,2},{4,3},{5,4},{6,5},{7,6},{8,7},{9,8},{10,9},{11,1... | collective-permute-start | bytes 4718600 | tf_op jit(solution)/shard_map/ppermute | solution.py:18
  26.0 1.4 fusion.24
  27.4 2.0 %collective-permute-start.5 = (bf16[1024,384]{1,0:T(8,128)(2,1)}, bf16[1024,384]{1,0:T(8,128)(2,1)}, u32[]{:S(2)}, u32[]{:S(2)}) collective-permute-start(bf16[1024,384]{1,0:T(8,128)(2,1)} %bitcast.22), channel_id=1, source_target_pairs={{0,1},{1,2},{2,3},{3,4},{4,5},{5,6},{6,7},{7,8},{8,9},{9,10},{10,1... | collective-permute-start | bytes 2359304 | tf_op jit(solution)/shard_map/ppermute | solution.py:17
  29.5 3.6 %collective-permute-start.6 = (bf16[1024,384]{1,0:T(8,128)(2,1)}, bf16[1024,384]{1,0:T(8,128)(2,1)}, u32[]{:S(2)}, u32[]{:S(2)}) collective-permute-start(bf16[1024,384]{1,0:T(8,128)(2,1)} %bitcast.23), channel_id=1, source_target_pairs={{1,0},{2,1},{3,2},{4,3},{5,4},{6,5},{7,6},{8,7},{9,8},{10,9},{11,1... | collective-permute-start | bytes 2359304 | tf_op jit(solution)/shard_map/ppermute | solution.py:18
  33.2 0.9 multiply_reduce_fusion
  34.1 0.6 broadcast_multiply_fusion.1
  34.7 0.6 broadcast_multiply_fusion
  35.3 1.8 %pad_maximum_fusion.refs_2_.refs_3_ = bf16[24,128,384]{2,1,0:T(8,128)(2,1)} fusion(bf16[24,128,128]{2,1,0:T(8,128)(2,1)S(1)} %copy-done.4, bf16[24,128,256]{2,1,0:T(8,128)(2,1)S(1)} %multiply_convert_fusion), kind=kLoop, calls=%fused_computation.5 | loop fusion | flops 4718592 | bytes 4718592 | tf_op jit(solution)/shard_map/concatenate | solution.py:346
  37.3 0.7 reshape.216.refs_0_
  38.1 0.6 reshape.217.refs_0_
  38.7 11.2 %shard_map.145.refs_9_ = f32[24,256,256]{2,1,0:T(8,128)} custom-call(s32[120]{0:T(128)} %reshape.217.refs_0_, bf16[24,256,128]{2,1,0:T(8,128)(2,1)} %bitcast.108, bf16[24,256,128]{2,1,0:T(8,128)(2,1)} %bitcast.109, bf16[24,256,256]{2,1,0:T(8,128)(2,1)} %bitcast.112, f32[24,1,256]{2,1,0:T(1,128)} %bitcast.131), custom_call_target="tpu_custom_call" | custom-call | tf_op jit(solution)/shard_map/pallas_call | solution.py:168
  49.9 8.8 %shard_map.147.refs_9_ = f32[24,128,256]{2,1,0:T(8,128)} custom-call(s32[96]{0:T(128)} %reshape.216.refs_0_, bf16[24,128,128]{2,1,0:T(8,128)(2,1)} %copy-done.2, bf16[24,128,384]{2,1,0:T(8,128)(2,1)} %pad_maximum_fusion.refs_2_.refs_3_, f32[24,1,128]{2,1,0:T(1,128)} %bitcast.138), custom_call_target="tpu_custom_call" | custom-call | tf_op jit(solution)/shard_map/pallas_call | solution.py:224
  58.7 11.8 %collective-permute-done.3 = bf16[2048,384]{1,0:T(8,128)(2,1)} collective-permute-done((bf16[2048,384]{1,0:T(8,128)(2,1)}, bf16[2048,384]{1,0:T(8,128)(2,1)}, u32[]{:S(2)}, u32[]{:S(2)}) %collective-permute-start.3) | collective-permute-done | bytes 1572896 | tf_op jit(solution)/shard_map/ppermute | solution.py:17
  70.5 1.4 multiply_reduce_fusion.3
  71.9 0.6 copy.39.refs_6_
  72.5 1.4 multiply_reduce_fusion.2
  73.9 0.6 mul.200.refs_8_
  74.5 19.2 %shard_map.146.near_ref = f32[24,256,256]{2,1,0:T(8,128)} custom-call(s32[120]{0:T(128)} %reshape.217.refs_0_, bf16[24,256,128]{2,1,0:T(8,128)(2,1)} %bitcast.110, bf16[8,256,384]{2,1,0:T(8,128)(2,1)} %bitcast.18.refs_2_, bf16[24,256,128]{2,1,0:T(8,128)(2,1)} %bitcast.111, bf16[8,256,384]{2,1,0:T(8,128)(2,1)} %bitcast.19.refs_4_, ...), custom_call_target="tpu_custom_call", output_to_operand_aliasing={{}: (9, {})} | custom-call | tf_op jit(solution)/shard_map/pallas_call | solution.py:168
  93.7 1.2 multiply_reduce_fusion.5
  94.9 1.2 multiply_reduce_fusion.4
  96.1 0.6 broadcast_multiply_fusion.4
  96.7 0.6 broadcast_multiply_fusion.3
  97.3 1.5 %copy.47 = bf16[64,8,8,128]{3,2,1,0:T(8,128)(2,1)S(1)} copy(bf16[64,8,8,128]{3,1,2,0:T(8,128)(2,1)} %bitcast.124) | data formatting | bytes 2097152
  98.9 0.3 copy.46
  99.5 0.4 multiply_reduce_fusion.9
  99.8 0.2 fusion.17
  100.2 3.0 %collective-permute-start.1 = (bf16[128,384]{1,0:T(8,128)(2,1)S(1)}, bf16[128,384]{1,0:T(8,128)(2,1)S(1)}, u32[]{:S(2)}, u32[]{:S(2)}) collective-permute-start(bf16[128,384]{1,0:T(8,128)(2,1)S(1)} %get-tuple-element.20.refs_8_), channel_id=1, source_target_pairs={{0,16},{8,24},{16,0},{24,8},{1,17},{9,25},{17,1},{25,9},{2,18},{10... | collective-permute-start | bytes 294920 | tf_op jit(solution)/shard_map/ppermute | solution.py:423
  103.2 1.6 %collective-permute-start = (bf16[128,384]{1,0:T(8,128)(2,1)S(1)}, bf16[128,384]{1,0:T(8,128)(2,1)S(1)}, u32[]{:S(2)}, u32[]{:S(2)}) collective-permute-start(bf16[128,384]{1,0:T(8,128)(2,1)S(1)} %get-tuple-element.20.refs_8_), channel_id=1, source_target_pairs={{0,8},{8,16},{16,24},{24,0},{1,9},{9,17},{17,25},{25,1},{2,10},{10... | collective-permute-start | bytes 294920 | tf_op jit(solution)/shard_map/ppermute | solution.py:423
  104.8 0.3 copy.55
  105.1 0.4 convolution_convert_fusion.1
  105.4 0.3 fusion.8
  106.1 14.8 %shard_map.148.far_ref = f32[24,128,256]{2,1,0:T(8,128)} custom-call(s32[96]{0:T(128)} %reshape.216.refs_0_, bf16[24,128,128]{2,1,0:T(8,128)(2,1)} %copy-done.2, bf16[8,128,384]{2,1,0:T(8,128)(2,1)} %bitcast.24.refs_2_, bf16[24,128,384]{2,1,0:T(8,128)(2,1)} %pad_maximum_fusion.refs_2_.refs_3_, ...), custom_call_target="tpu_custom_call", output_to_operand_aliasing={{}: (9, {})} | custom-call | tf_op jit(solution)/shard_map/pallas_call | solution.py:224
  120.9 0.4 convolution_bitcast_fusion
  121.8 1.0 convolution_convert_fusion
  123.2 1.0 fusion.16.down_ref
  124.2 9.4 %shard_map.149 = bf16[24,256,256]{2,1,0:T(8,128)(2,1)} custom-call(s32[24]{0:T(128)} %rank_ref.1, bf16[24,128,128]{2,1,0:T(8,128)(2,1)} %bitcast.122, bf16[128,256]{1,0:T(8,128)(2,1)} %fusion.16.down_ref, f32[24,128,256]{2,1,0:T(8,128)} %shard_map.148.far_ref, bf16[24,256,128]{2,1,0:T(8,128)(2,1)} %bitcast.117, f32[24,256,256]{2,1,0:T(8,128)} %shard_map.146.near_ref), custom_call_target="tpu_custom_call" | custom-call | tf_op jit(solution)/shard_map/pallas_call | solution.py:267
  (62 shorter events, 2.4 us)
Async XLA Ops:
  6.5 90.7 %all-gather.3.cloned.1.call-start = ((), (), s32[]{:S(2)}) async-start(), calls=%async_computation | async-start | bytes 1179648 | tf_op jit(solution)/shard_map/all_gather | solution.py:368
  6.5 5.6 %copy-start.11 = (s32[1,128]{1,0:T(1,128)S(1)}, s32[1,128]{1,0:T(1,128)}, u32[]{:S(2)}) copy-start(s32[1,128]{1,0:T(1,128)} %param.24) | copy-start | bytes 1540
  9.5 3.5 %copy-start.1 = (bf16[6144,256]{1,0:T(8,128)(2,1)S(1)}, bf16[6144,256]{1,0:T(8,128)(2,1)}, u32[]{:S(2)}) copy-start(bf16[6144,256]{1,0:T(8,128)(2,1)} %param.16) | copy-start | bytes 9437188
  9.5 3.5 %copy-start.5 = (bf16[6144,128]{1,0:T(8,128)(2,1)S(1)}, bf16[6144,128]{1,0:T(8,128)(2,1)}, u32[]{:S(2)}) copy-start(bf16[6144,128]{1,0:T(8,128)(2,1)} %param.17) | copy-start | bytes 4718596
  12.1 0.9 copy-start.2
  13.0 1.1 copy-start.6
  15.5 2.0 %copy-start = (bf16[6144,128]{1,0:T(8,128)(2,1)S(1)}, bf16[6144,128]{1,0:T(8,128)(2,1)}, u32[]{:S(2)}) copy-start(bf16[6144,128]{1,0:T(8,128)(2,1)} %param.15) | copy-start | bytes 4718596
  19.0 51.5 %collective-permute-start.3 = (bf16[2048,384]{1,0:T(8,128)(2,1)}, bf16[2048,384]{1,0:T(8,128)(2,1)}, u32[]{:S(2)}, u32[]{:S(2)}) collective-permute-start(bf16[2048,384]{1,0:T(8,128)(2,1)} %pad_maximum_fusion.1), channel_id=1, source_target_pairs={{0,1},{1,2},{2,3},{3,4},{4,5},{5,6},{6,7},{7,8},{8,9},{9,10},{10,1... | collective-permute-start | bytes 4718600 | tf_op jit(solution)/shard_map/ppermute | solution.py:17
  20.9 5.1 %copy-start.3 = (bf16[24,128,128]{2,1,0:T(8,128)(2,1)S(1)}, bf16[24,128,128]{2,1,0:T(8,128)(2,1)}, u32[]{:S(2)}) copy-start(bf16[24,128,128]{2,1,0:T(8,128)(2,1)} %copy-done.2) | copy-start | bytes 2359300
  22.2 10.9 %copy-start.12 = (s32[1,4]{1,0:T(1,128)S(1)}, s32[1,4]{1,0:T(1,128)}, u32[]{:S(2)}) copy-start(s32[1,4]{1,0:T(1,128)} %param.25) | copy-start | bytes 52
  22.2 10.9 %copy-start.10 = (s32[24,4]{0,1:T(4,128)S(1)}, s32[24,4]{0,1:T(4,128)}, u32[]{:S(2)}) copy-start(s32[24,4]{0,1:T(4,128)} %param.21) | copy-start | bytes 1156
  22.3 50.3 %collective-permute-start.4 = (bf16[2048,384]{1,0:T(8,128)(2,1)}, bf16[2048,384]{1,0:T(8,128)(2,1)}, u32[]{:S(2)}, u32[]{:S(2)}) collective-permute-start(bf16[2048,384]{1,0:T(8,128)(2,1)} %pad_maximum_fusion.2), channel_id=1, source_target_pairs={{1,0},{2,1},{3,2},{4,3},{5,4},{6,5},{7,6},{8,7},{9,8},{10,9},{11,1... | collective-permute-start | bytes 4718600 | tf_op jit(solution)/shard_map/ppermute | solution.py:18
  27.4 6.7 %copy-start.9 = (s32[24,5]{0,1:T(8,128)S(1)}, s32[24,5]{0,1:T(8,128)}, u32[]{:S(2)}) copy-start(s32[24,5]{0,1:T(8,128)} %param.20) | copy-start | bytes 1444
  27.4 7.9 %copy-start.13 = (s32[1,2]{1,0:T(1,128)S(1)}, s32[1,2]{1,0:T(1,128)}, u32[]{:S(2)}) copy-start(s32[1,2]{1,0:T(1,128)} %param.29) | copy-start | bytes 28
  27.4 66.3 %collective-permute-start.5 = (bf16[1024,384]{1,0:T(8,128)(2,1)}, bf16[1024,384]{1,0:T(8,128)(2,1)}, u32[]{:S(2)}, u32[]{:S(2)}) collective-permute-start(bf16[1024,384]{1,0:T(8,128)(2,1)} %bitcast.22), channel_id=1, source_target_pairs={{0,1},{1,2},{2,3},{3,4},{4,5},{5,6},{6,7},{7,8},{8,9},{9,10},{10,1... | collective-permute-start | bytes 2359304 | tf_op jit(solution)/shard_map/ppermute | solution.py:17
  29.5 64.3 %collective-permute-start.6 = (bf16[1024,384]{1,0:T(8,128)(2,1)}, bf16[1024,384]{1,0:T(8,128)(2,1)}, u32[]{:S(2)}, u32[]{:S(2)}) collective-permute-start(bf16[1024,384]{1,0:T(8,128)(2,1)} %bitcast.23), channel_id=1, source_target_pairs={{1,0},{2,1},{3,2},{4,3},{5,4},{6,5},{7,6},{8,7},{9,8},{10,9},{11,1... | collective-permute-start | bytes 2359304 | tf_op jit(solution)/shard_map/ppermute | solution.py:18
  33.2 2.2 %copy-start.4 = (bf16[24,128,128]{2,1,0:T(8,128)(2,1)S(1)}, bf16[24,128,128]{2,1,0:T(8,128)(2,1)}, u32[]{:S(2)}) copy-start(bf16[24,128,128]{2,1,0:T(8,128)(2,1)} %copy-done.2) | copy-start | bytes 2359300
  98.8 0.7 copy-start.14
  100.1 5.9 %copy-start.7 = (bf16[128,384]{1,0:T(8,128)(2,1)}, bf16[128,384]{1,0:T(8,128)(2,1)S(1)}, u32[]{:S(2)}) copy-start(bf16[128,384]{1,0:T(8,128)(2,1)S(1)} %get-tuple-element.20.refs_8_) | copy-start | bytes 294916
  100.1 21.2 %collective-permute-start.2 = (bf16[128,384]{1,0:T(8,128)(2,1)S(1)}, bf16[128,384]{1,0:T(8,128)(2,1)S(1)}, u32[]{:S(2)}, u32[]{:S(2)}) collective-permute-start(bf16[128,384]{1,0:T(8,128)(2,1)S(1)} %get-tuple-element.20.refs_8_), channel_id=1, source_target_pairs={{0,24},{8,0},{16,8},{24,16},{1,25},{9,1},{17,9},{25,17},{2,26},{10... | collective-permute-start | bytes 294920 | tf_op jit(solution)/shard_map/ppermute | solution.py:423
  100.2 21.3 %collective-permute-start.1 = (bf16[128,384]{1,0:T(8,128)(2,1)S(1)}, bf16[128,384]{1,0:T(8,128)(2,1)S(1)}, u32[]{:S(2)}, u32[]{:S(2)}) collective-permute-start(bf16[128,384]{1,0:T(8,128)(2,1)S(1)} %get-tuple-element.20.refs_8_), channel_id=1, source_target_pairs={{0,16},{8,24},{16,0},{24,8},{1,17},{9,25},{17,1},{25,9},{2,18},{10... | collective-permute-start | bytes 294920 | tf_op jit(solution)/shard_map/ppermute | solution.py:423
  103.2 18.4 %collective-permute-start = (bf16[128,384]{1,0:T(8,128)(2,1)S(1)}, bf16[128,384]{1,0:T(8,128)(2,1)S(1)}, u32[]{:S(2)}, u32[]{:S(2)}) collective-permute-start(bf16[128,384]{1,0:T(8,128)(2,1)S(1)} %get-tuple-element.20.refs_8_), channel_id=1, source_target_pairs={{0,8},{8,16},{16,24},{24,0},{1,9},{9,17},{17,25},{25,1},{2,10},{10... | collective-permute-start | bytes 294920 | tf_op jit(solution)/shard_map/ppermute | solution.py:423
  121.8 1.4 copy-start.8
Sparse Core Ops, SparseCore 0:
  15.6 49.8 all-gather.2

commit v7 on v6

--- a/solution.py
+++ b/solution.py
@@ -4,6 +4,7 @@
 from jax.experimental import pallas as pl
 from jax.experimental.pallas import tpu as pltpu
 from jax.sharding import PartitionSpec as P
+
 
 REACH = 8
 FLAT = ("row", "col")
@@ -156,7 +157,7 @@
     rhs = local_weights.shape[-1]
     count = near_local.shape[1]
     halo = halo_inputs is not None
-    leaf_of, steps, gap = leaf_order(leaves, halo)
+    leaf_of, steps, _ = leaf_order(leaves, halo)
     anywhere = pl.BlockSpec(memory_space=pl.ANY)
     if halo:
         left_pairs, right_pairs, left_norms, right_norms = halo_inputs
@@ -212,7 +213,7 @@
     width = own_rows.shape[-1]
     count = far_local.shape[1]
     halo = halo_inputs is not None
-    leaf_of, steps, gap = leaf_order(leaves, halo)
+    leaf_of, steps, _ = leaf_order(leaves, halo)
     anywhere = pl.BlockSpec(memory_space=pl.ANY)
     if halo:
         left_rows, right_rows, left_norms, right_norms = halo_inputs
@@ -335,9 +336,7 @@
     left_pairs = left_pairs.reshape(REACH, leaf_size, dim_count + rhs_count)
     right_pairs = right_pairs.reshape(REACH, leaf_size, dim_count + rhs_count)
 
-    leaf_mask = (
-        lax.broadcasted_iota(jnp.int32, (leaf_count, rank_count), 1) < leaf_rank[:, None]
-    ).astype(jnp.float32)
+    leaf_mask = (lax.broadcasted_iota(jnp.int32, (leaf_count, rank_count), 1) < leaf_rank[:, None]).astype(jnp.float32)
     leaf_up = (
         jnp.einsum("lpk,lpr->lkr", local_bases, local_weights, preferred_element_type=jnp.float32)
         * leaf_mask[:, :, None]
@@ -468,4 +467,5 @@
         P("row", None),
     )
     out_specs = P(FLAT, None)
+
     return jax.shard_map(body, mesh=mesh, in_specs=in_specs, out_specs=out_specs, check_vma=False)

time: 143 us -> 143 us (level)
  no operation moved by 1% of the time
where the time goes in v7:
time: 143 us; the launch traced here: 140 us
  Pallas kernels  63.4 us (44%)
  other arithmetic  16.1 us (11%)
  starting transfers between devices  16 us (11%)
  between operations  15.2 us (11%)
  waiting for transfers between devices  11.8 us (8%)
  local copies, waits for them, and re-layouts  9.33 us (7%)
  matrix products  8.56 us (6%)
    pallas_call x2, Pallas kernels, near_field(): pl.pallas_call(lambda *refs: near_kernel(leaf_of, halo, *refs), grid_spec...  30.4 us
    pallas_call x2, Pallas kernels, far_field(): pl.pallas_call(lambda *refs: far_kernel(leaf_of, halo, *refs), grid_spec=...  23.7 us
    ppermute x2, waiting for transfers between devices, halos(): left = lax.ppermute(tail, FLAT, [(i, i + 1) for i in range(ends)])  11.8 us
    pallas_call x1, Pallas kernels, final_field(): pl.pallas_call(final_kernel, grid_spec=pltpu.PrefetchScalarGridSpec(num_s...  9.36 us
    ppermute x2, starting transfers between devices, halos(): right = lax.ppermute(head, FLAT, [(i + 1, i) for i in range(ends)])  7.41 us
    reduce_sum x5, other arithmetic, scaled_norms(): jnp.sum(wide * wide, axis=-1) * (-2.0 / cells.shape[-1])  5.97 us
    ppermute x3, starting transfers between devices, body(): lax.ppermute(group_pack, 'row', [(r, (r + shift) % rows) for r in range(r...  4.66 us
    unnamed x40, local copies, waits for them, and re-layouts  4.63 us
  transfers between devices with their start and end apart: 8, of which 1 were waited for; matrix products, arithmetic and copies ran while one was open for 15% of the time, Pallas kernels for 38%

profile of v7, /device:TPU:2, one launch (start us, length us, event | category | flops | bytes accessed | tf_op | source)
XLA Modules:
  0.0 140.4 jit_solution(3908963520266569029)
XLA Ops:
  6.5 0.9 copy.30
  7.4 0.7 fusion.53
  9.5 2.6 %multiply_reduce_fusion.1 = (f32[24,128]{1,0:T(8,128)S(1)}, bf16[24,128,128]{2,1,0:T(8,128)(2,1)S(1)}) fusion(bf16[24,256,128]{2,1,0:T(8,128)(2,1)} %bitcast.107, s32[24,128]{1,0:T(8,128)} %param.19), kind=kOutput, calls=%fused_computation.14 | convolution fusion | flops 203682816 | bytes 2383872 | tf_op jit(solution)/shard_map/bkp,bpc->bkc/dot_general | solution.py:300
  12.1 0.6 multiply_reduce_fusion.8
  12.7 0.3 copy-done.2
  13.0 1.0 multiply_convert_fusion
  14.1 0.6 fusion.21
  14.8 0.7 pad_maximum_fusion.5
  15.5 1.8 %fusion.65 = (bf16[2048,256]{1,0:T(8,128)(2,1)S(1)}, bf16[2048,256]{1,0:T(8,128)(2,1)S(1)}) fusion(bf16[6144,256]{1,0:T(8,128)(2,1)} %param.16), kind=kLoop, calls=%fused_computation.115 | loop fusion | bytes 4194304 | tf_op jit(solution)/shard_map/slice | solution.py:16
  17.6 1.4 pad_maximum_fusion.1
  19.0 1.9 %collective-permute-start.3 = (bf16[2048,384]{1,0:T(8,128)(2,1)}, bf16[2048,384]{1,0:T(8,128)(2,1)}, u32[]{:S(2)}, u32[]{:S(2)}) collective-permute-start(bf16[2048,384]{1,0:T(8,128)(2,1)} %pad_maximum_fusion.1), channel_id=1, source_target_pairs={{0,1},{1,2},{2,3},{3,4},{4,5},{5,6},{6,7},{7,8},{8,9},{9,10},{10,1... | collective-permute-start | bytes 4718600 | tf_op jit(solution)/shard_map/ppermute | solution.py:18
  20.9 1.4 pad_maximum_fusion.2
  22.3 3.8 %collective-permute-start.4 = (bf16[2048,384]{1,0:T(8,128)(2,1)}, bf16[2048,384]{1,0:T(8,128)(2,1)}, u32[]{:S(2)}, u32[]{:S(2)}) collective-permute-start(bf16[2048,384]{1,0:T(8,128)(2,1)} %pad_maximum_fusion.2), channel_id=1, source_target_pairs={{1,0},{2,1},{3,2},{4,3},{5,4},{6,5},{7,6},{8,7},{9,8},{10,9},{11,1... | collective-permute-start | bytes 4718600 | tf_op jit(solution)/shard_map/ppermute | solution.py:19
  26.0 1.4 fusion.24
  27.4 2.0 %collective-permute-start.5 = (bf16[1024,384]{1,0:T(8,128)(2,1)}, bf16[1024,384]{1,0:T(8,128)(2,1)}, u32[]{:S(2)}, u32[]{:S(2)}) collective-permute-start(bf16[1024,384]{1,0:T(8,128)(2,1)} %bitcast.22), channel_id=1, source_target_pairs={{0,1},{1,2},{2,3},{3,4},{4,5},{5,6},{6,7},{7,8},{8,9},{9,10},{10,1... | collective-permute-start | bytes 2359304 | tf_op jit(solution)/shard_map/ppermute | solution.py:18
  29.5 3.6 %collective-permute-start.6 = (bf16[1024,384]{1,0:T(8,128)(2,1)}, bf16[1024,384]{1,0:T(8,128)(2,1)}, u32[]{:S(2)}, u32[]{:S(2)}) collective-permute-start(bf16[1024,384]{1,0:T(8,128)(2,1)} %bitcast.23), channel_id=1, source_target_pairs={{1,0},{2,1},{3,2},{4,3},{5,4},{6,5},{7,6},{8,7},{9,8},{10,9},{11,1... | collective-permute-start | bytes 2359304 | tf_op jit(solution)/shard_map/ppermute | solution.py:19
  33.2 0.9 multiply_reduce_fusion
  34.1 0.6 broadcast_multiply_fusion.1
  34.7 0.6 broadcast_multiply_fusion
  35.3 1.8 %pad_maximum_fusion.refs_2_.refs_3_ = bf16[24,128,384]{2,1,0:T(8,128)(2,1)} fusion(bf16[24,128,128]{2,1,0:T(8,128)(2,1)S(1)} %copy-done.4, bf16[24,128,256]{2,1,0:T(8,128)(2,1)S(1)} %multiply_convert_fusion), kind=kLoop, calls=%fused_computation.5 | loop fusion | flops 4718592 | bytes 4718592 | tf_op jit(solution)/shard_map/concatenate | solution.py:345
  37.3 0.7 reshape.216.refs_0_
  38.1 0.6 reshape.217.refs_0_
  38.7 11.2 %shard_map.145.refs_9_ = f32[24,256,256]{2,1,0:T(8,128)} custom-call(s32[120]{0:T(128)} %reshape.217.refs_0_, bf16[24,256,128]{2,1,0:T(8,128)(2,1)} %bitcast.108, bf16[24,256,128]{2,1,0:T(8,128)(2,1)} %bitcast.109, bf16[24,256,256]{2,1,0:T(8,128)(2,1)} %bitcast.112, f32[24,1,256]{2,1,0:T(1,128)} %bitcast.131), custom_call_target="tpu_custom_call" | custom-call | tf_op jit(solution)/shard_map/pallas_call | solution.py:169
  49.9 8.8 %shard_map.147.refs_9_ = f32[24,128,256]{2,1,0:T(8,128)} custom-call(s32[96]{0:T(128)} %reshape.216.refs_0_, bf16[24,128,128]{2,1,0:T(8,128)(2,1)} %copy-done.2, bf16[24,128,384]{2,1,0:T(8,128)(2,1)} %pad_maximum_fusion.refs_2_.refs_3_, f32[24,1,128]{2,1,0:T(1,128)} %bitcast.138), custom_call_target="tpu_custom_call" | custom-call | tf_op jit(solution)/shard_map/pallas_call | solution.py:225
  58.7 11.8 %collective-permute-done.3 = bf16[2048,384]{1,0:T(8,128)(2,1)} collective-permute-done((bf16[2048,384]{1,0:T(8,128)(2,1)}, bf16[2048,384]{1,0:T(8,128)(2,1)}, u32[]{:S(2)}, u32[]{:S(2)}) %collective-permute-start.3) | collective-permute-done | bytes 1572896 | tf_op jit(solution)/shard_map/ppermute | solution.py:18
  70.5 1.4 multiply_reduce_fusion.3
  71.9 0.6 copy.39.refs_6_
  72.5 1.4 multiply_reduce_fusion.2
  73.9 0.6 mul.200.refs_8_
  74.5 19.2 %shard_map.146.near_ref = f32[24,256,256]{2,1,0:T(8,128)} custom-call(s32[120]{0:T(128)} %reshape.217.refs_0_, bf16[24,256,128]{2,1,0:T(8,128)(2,1)} %bitcast.110, bf16[8,256,384]{2,1,0:T(8,128)(2,1)} %bitcast.18.refs_2_, bf16[24,256,128]{2,1,0:T(8,128)(2,1)} %bitcast.111, bf16[8,256,384]{2,1,0:T(8,128)(2,1)} %bitcast.19.refs_4_, ...), custom_call_target="tpu_custom_call", output_to_operand_aliasing={{}: (9, {})} | custom-call | tf_op jit(solution)/shard_map/pallas_call | solution.py:169
  93.8 1.2 multiply_reduce_fusion.5
  94.9 1.2 multiply_reduce_fusion.4
  96.1 0.6 broadcast_multiply_fusion.4
  96.7 0.6 broadcast_multiply_fusion.3
  97.3 1.5 %copy.47 = bf16[64,8,8,128]{3,2,1,0:T(8,128)(2,1)S(1)} copy(bf16[64,8,8,128]{3,1,2,0:T(8,128)(2,1)} %bitcast.124) | data formatting | bytes 2097152
  98.9 0.3 copy.46
  99.5 0.4 multiply_reduce_fusion.9
  99.8 0.2 fusion.17
  100.2 3.0 %collective-permute-start.1 = (bf16[128,384]{1,0:T(8,128)(2,1)S(1)}, bf16[128,384]{1,0:T(8,128)(2,1)S(1)}, u32[]{:S(2)}, u32[]{:S(2)}) collective-permute-start(bf16[128,384]{1,0:T(8,128)(2,1)S(1)} %get-tuple-element.20.refs_8_), channel_id=1, source_target_pairs={{0,16},{8,24},{16,0},{24,8},{1,17},{9,25},{17,1},{25,9},{2,18},{10... | collective-permute-start | bytes 294920 | tf_op jit(solution)/shard_map/ppermute | solution.py:422
  103.2 1.6 %collective-permute-start = (bf16[128,384]{1,0:T(8,128)(2,1)S(1)}, bf16[128,384]{1,0:T(8,128)(2,1)S(1)}, u32[]{:S(2)}, u32[]{:S(2)}) collective-permute-start(bf16[128,384]{1,0:T(8,128)(2,1)S(1)} %get-tuple-element.20.refs_8_), channel_id=1, source_target_pairs={{0,8},{8,16},{16,24},{24,0},{1,9},{9,17},{17,25},{25,1},{2,10},{10... | collective-permute-start | bytes 294920 | tf_op jit(solution)/shard_map/ppermute | solution.py:422
  104.8 0.3 copy.55
  105.1 0.3 convolution_convert_fusion.1
  105.4 0.3 fusion.8
  106.1 14.8 %shard_map.148.far_ref = f32[24,128,256]{2,1,0:T(8,128)} custom-call(s32[96]{0:T(128)} %reshape.216.refs_0_, bf16[24,128,128]{2,1,0:T(8,128)(2,1)} %copy-done.2, bf16[8,128,384]{2,1,0:T(8,128)(2,1)} %bitcast.24.refs_2_, bf16[24,128,384]{2,1,0:T(8,128)(2,1)} %pad_maximum_fusion.refs_2_.refs_3_, ...), custom_call_target="tpu_custom_call", output_to_operand_aliasing={{}: (9, {})} | custom-call | tf_op jit(solution)/shard_map/pallas_call | solution.py:225
  120.9 0.4 convolution_bitcast_fusion
  121.8 1.0 convolution_convert_fusion
  123.2 1.0 fusion.16.down_ref
  124.2 9.4 %shard_map.149 = bf16[24,256,256]{2,1,0:T(8,128)(2,1)} custom-call(s32[24]{0:T(128)} %rank_ref.1, bf16[24,128,128]{2,1,0:T(8,128)(2,1)} %bitcast.122, bf16[128,256]{1,0:T(8,128)(2,1)} %fusion.16.down_ref, f32[24,128,256]{2,1,0:T(8,128)} %shard_map.148.far_ref, bf16[24,256,128]{2,1,0:T(8,128)(2,1)} %bitcast.117, f32[24,256,256]{2,1,0:T(8,128)} %shard_map.146.near_ref), custom_call_target="tpu_custom_call" | custom-call | tf_op jit(solution)/shard_map/pallas_call | solution.py:268
  (62 shorter events, 2.4 us)
Async XLA Ops:
  6.5 90.7 %all-gather.3.cloned.1.call-start = ((), (), s32[]{:S(2)}) async-start(), calls=%async_computation | async-start | bytes 1179648 | tf_op jit(solution)/shard_map/all_gather | solution.py:367
  6.5 5.6 %copy-start.11 = (s32[1,128]{1,0:T(1,128)S(1)}, s32[1,128]{1,0:T(1,128)}, u32[]{:S(2)}) copy-start(s32[1,128]{1,0:T(1,128)} %param.24) | copy-start | bytes 1540
  9.5 3.5 %copy-start.1 = (bf16[6144,256]{1,0:T(8,128)(2,1)S(1)}, bf16[6144,256]{1,0:T(8,128)(2,1)}, u32[]{:S(2)}) copy-start(bf16[6144,256]{1,0:T(8,128)(2,1)} %param.16) | copy-start | bytes 9437188
  9.5 3.5 %copy-start.5 = (bf16[6144,128]{1,0:T(8,128)(2,1)S(1)}, bf16[6144,128]{1,0:T(8,128)(2,1)}, u32[]{:S(2)}) copy-start(bf16[6144,128]{1,0:T(8,128)(2,1)} %param.17) | copy-start | bytes 4718596
  12.1 0.9 copy-start.2
  13.0 1.1 copy-start.6
  15.5 2.0 %copy-start = (bf16[6144,128]{1,0:T(8,128)(2,1)S(1)}, bf16[6144,128]{1,0:T(8,128)(2,1)}, u32[]{:S(2)}) copy-start(bf16[6144,128]{1,0:T(8,128)(2,1)} %param.15) | copy-start | bytes 4718596
  19.0 51.5 %collective-permute-start.3 = (bf16[2048,384]{1,0:T(8,128)(2,1)}, bf16[2048,384]{1,0:T(8,128)(2,1)}, u32[]{:S(2)}, u32[]{:S(2)}) collective-permute-start(bf16[2048,384]{1,0:T(8,128)(2,1)} %pad_maximum_fusion.1), channel_id=1, source_target_pairs={{0,1},{1,2},{2,3},{3,4},{4,5},{5,6},{6,7},{7,8},{8,9},{9,10},{10,1... | collective-permute-start | bytes 4718600 | tf_op jit(solution)/shard_map/ppermute | solution.py:18
  20.9 5.1 %copy-start.3 = (bf16[24,128,128]{2,1,0:T(8,128)(2,1)S(1)}, bf16[24,128,128]{2,1,0:T(8,128)(2,1)}, u32[]{:S(2)}) copy-start(bf16[24,128,128]{2,1,0:T(8,128)(2,1)} %copy-done.2) | copy-start | bytes 2359300
  22.2 10.9 %copy-start.12 = (s32[1,4]{1,0:T(1,128)S(1)}, s32[1,4]{1,0:T(1,128)}, u32[]{:S(2)}) copy-start(s32[1,4]{1,0:T(1,128)} %param.25) | copy-start | bytes 52
  22.2 10.9 %copy-start.10 = (s32[24,4]{0,1:T(4,128)S(1)}, s32[24,4]{0,1:T(4,128)}, u32[]{:S(2)}) copy-start(s32[24,4]{0,1:T(4,128)} %param.21) | copy-start | bytes 1156
  22.3 50.3 %collective-permute-start.4 = (bf16[2048,384]{1,0:T(8,128)(2,1)}, bf16[2048,384]{1,0:T(8,128)(2,1)}, u32[]{:S(2)}, u32[]{:S(2)}) collective-permute-start(bf16[2048,384]{1,0:T(8,128)(2,1)} %pad_maximum_fusion.2), channel_id=1, source_target_pairs={{1,0},{2,1},{3,2},{4,3},{5,4},{6,5},{7,6},{8,7},{9,8},{10,9},{11,1... | collective-permute-start | bytes 4718600 | tf_op jit(solution)/shard_map/ppermute | solution.py:19
  27.4 6.7 %copy-start.9 = (s32[24,5]{0,1:T(8,128)S(1)}, s32[24,5]{0,1:T(8,128)}, u32[]{:S(2)}) copy-start(s32[24,5]{0,1:T(8,128)} %param.20) | copy-start | bytes 1444
  27.4 7.9 %copy-start.13 = (s32[1,2]{1,0:T(1,128)S(1)}, s32[1,2]{1,0:T(1,128)}, u32[]{:S(2)}) copy-start(s32[1,2]{1,0:T(1,128)} %param.29) | copy-start | bytes 28
  27.4 66.3 %collective-permute-start.5 = (bf16[1024,384]{1,0:T(8,128)(2,1)}, bf16[1024,384]{1,0:T(8,128)(2,1)}, u32[]{:S(2)}, u32[]{:S(2)}) collective-permute-start(bf16[1024,384]{1,0:T(8,128)(2,1)} %bitcast.22), channel_id=1, source_target_pairs={{0,1},{1,2},{2,3},{3,4},{4,5},{5,6},{6,7},{7,8},{8,9},{9,10},{10,1... | collective-permute-start | bytes 2359304 | tf_op jit(solution)/shard_map/ppermute | solution.py:18
  29.5 64.3 %collective-permute-start.6 = (bf16[1024,384]{1,0:T(8,128)(2,1)}, bf16[1024,384]{1,0:T(8,128)(2,1)}, u32[]{:S(2)}, u32[]{:S(2)}) collective-permute-start(bf16[1024,384]{1,0:T(8,128)(2,1)} %bitcast.23), channel_id=1, source_target_pairs={{1,0},{2,1},{3,2},{4,3},{5,4},{6,5},{7,6},{8,7},{9,8},{10,9},{11,1... | collective-permute-start | bytes 2359304 | tf_op jit(solution)/shard_map/ppermute | solution.py:19
  33.2 2.2 %copy-start.4 = (bf16[24,128,128]{2,1,0:T(8,128)(2,1)S(1)}, bf16[24,128,128]{2,1,0:T(8,128)(2,1)}, u32[]{:S(2)}) copy-start(bf16[24,128,128]{2,1,0:T(8,128)(2,1)} %copy-done.2) | copy-start | bytes 2359300
  98.8 0.7 copy-start.14
  100.1 5.9 %copy-start.7 = (bf16[128,384]{1,0:T(8,128)(2,1)}, bf16[128,384]{1,0:T(8,128)(2,1)S(1)}, u32[]{:S(2)}) copy-start(bf16[128,384]{1,0:T(8,128)(2,1)S(1)} %get-tuple-element.20.refs_8_) | copy-start | bytes 294916
  100.1 21.2 %collective-permute-start.2 = (bf16[128,384]{1,0:T(8,128)(2,1)S(1)}, bf16[128,384]{1,0:T(8,128)(2,1)S(1)}, u32[]{:S(2)}, u32[]{:S(2)}) collective-permute-start(bf16[128,384]{1,0:T(8,128)(2,1)S(1)} %get-tuple-element.20.refs_8_), channel_id=1, source_target_pairs={{0,24},{8,0},{16,8},{24,16},{1,25},{9,1},{17,9},{25,17},{2,26},{10... | collective-permute-start | bytes 294920 | tf_op jit(solution)/shard_map/ppermute | solution.py:422
  100.2 21.3 %collective-permute-start.1 = (bf16[128,384]{1,0:T(8,128)(2,1)S(1)}, bf16[128,384]{1,0:T(8,128)(2,1)S(1)}, u32[]{:S(2)}, u32[]{:S(2)}) collective-permute-start(bf16[128,384]{1,0:T(8,128)(2,1)S(1)} %get-tuple-element.20.refs_8_), channel_id=1, source_target_pairs={{0,16},{8,24},{16,0},{24,8},{1,17},{9,25},{17,1},{25,9},{2,18},{10... | collective-permute-start | bytes 294920 | tf_op jit(solution)/shard_map/ppermute | solution.py:422
  103.2 18.4 %collective-permute-start = (bf16[128,384]{1,0:T(8,128)(2,1)S(1)}, bf16[128,384]{1,0:T(8,128)(2,1)S(1)}, u32[]{:S(2)}, u32[]{:S(2)}) collective-permute-start(bf16[128,384]{1,0:T(8,128)(2,1)S(1)} %get-tuple-element.20.refs_8_), channel_id=1, source_target_pairs={{0,8},{8,16},{16,24},{24,0},{1,9},{9,17},{17,25},{25,1},{2,10},{10... | collective-permute-start | bytes 294920 | tf_op jit(solution)/shard_map/ppermute | solution.py:422
  121.8 1.4 copy-start.8
Sparse Core Ops, SparseCore 0:
  15.6 49.8 all-gather.2

commit v8 on v7

--- a/solution.py
+++ b/solution.py
@@ -126,7 +126,7 @@
 
 
 def near_kernel(leaf_of, halo, index_ref, target_ref, *refs):
-    inputs = 8 if halo else 3
+    inputs = 9 if halo else 3
     out_ref = refs[inputs]
     point_buf, weight_buf, norm_buf, sems = refs[inputs + 1 :]
     count, size, dims = point_buf.shape[1], point_buf.shape[2], point_buf.shape[3]
@@ -152,7 +152,7 @@
     out_ref[0] = jnp.dot(kernel, values, preferred_element_type=jnp.float32)
 
 
-def near_field(local_points, local_weights, local_norms, near_local, halo_inputs=None, previous=None):
+def near_field(local_points, local_weights, local_norms, near_local, halo_inputs=None, previous=None, after=None):
     leaves, size, dims = local_points.shape
     rhs = local_weights.shape[-1]
     count = near_local.shape[1]
@@ -161,7 +161,7 @@
     anywhere = pl.BlockSpec(memory_space=pl.ANY)
     if halo:
         left_pairs, right_pairs, left_norms, right_norms = halo_inputs
-        inputs = (left_pairs, local_points, right_pairs, local_weights, left_norms, local_norms, right_norms, previous)
+        inputs = (left_pairs, local_points, right_pairs, local_weights, left_norms, local_norms, right_norms, after, previous)
     else:
         inputs = (local_points, local_weights, local_norms)
     aliases = {len(inputs) + 1: 0} if previous is not None else {}
@@ -187,7 +187,7 @@
 
 
 def far_kernel(leaf_of, halo, index_ref, target_ref, *refs):
-    inputs = 8 if halo else 2
+    inputs = 7 if halo else 2
     out_ref = refs[inputs]
     source_buf, norm_buf, sems = refs[inputs + 1 :]
     count, rank = source_buf.shape[1], source_buf.shape[2]
@@ -208,7 +208,7 @@
     out_ref[0] = jnp.dot(kernel, sources[:, dims:], preferred_element_type=jnp.float32)
 
 
-def far_field(leaf_coords, own_rows, own_norms, far_local, halo_inputs=None, previous=None, after=None):
+def far_field(leaf_coords, own_rows, own_norms, far_local, halo_inputs=None, previous=None):
     leaves, rank, dims = leaf_coords.shape
     width = own_rows.shape[-1]
     count = far_local.shape[1]
@@ -217,7 +217,7 @@
     anywhere = pl.BlockSpec(memory_space=pl.ANY)
     if halo:
         left_rows, right_rows, left_norms, right_norms = halo_inputs
-        inputs = (left_rows, own_rows, right_rows, left_norms, own_norms, right_norms, after, previous)
+        inputs = (left_rows, own_rows, right_rows, left_norms, own_norms, right_norms, previous)
     else:
         inputs = (own_rows, own_norms)
     aliases = {len(inputs) + 1: 0} if previous is not None else {}
@@ -336,7 +336,9 @@
     left_pairs = left_pairs.reshape(REACH, leaf_size, dim_count + rhs_count)
     right_pairs = right_pairs.reshape(REACH, leaf_size, dim_count + rhs_count)
 
-    leaf_mask = (lax.broadcasted_iota(jnp.int32, (leaf_count, rank_count), 1) < leaf_rank[:, None]).astype(jnp.float32)
+    leaf_mask = (
+        lax.broadcasted_iota(jnp.int32, (leaf_count, rank_count), 1) < leaf_rank[:, None]
+    ).astype(jnp.float32)
     leaf_up = (
         jnp.einsum("lpk,lpr->lkr", local_bases, local_weights, preferred_element_type=jnp.float32)
         * leaf_mask[:, :, None]
@@ -369,21 +371,6 @@
     near_local = near_list - offset
     local_norms = scaled_norms(local_points)
     near_inner = near_field(local_points, local_weights, local_norms, near_local)
-    near_total = near_field(
-        local_points,
-        local_weights,
-        local_norms,
-        near_local,
-        (
-            left_pairs,
-            right_pairs,
-            scaled_norms(left_pairs[:, :, :dim_count]),
-            scaled_norms(right_pairs[:, :, :dim_count]),
-        ),
-        near_inner,
-    )
-    near_total, left_rows, right_rows = lax.optimization_barrier((near_total, left_rows, right_rows))
-
     all_coords = gathered[:, :, :dim_count]
     all_up = gathered[:, :, dim_count : dim_count + rhs_count]
     all_parts = gathered[:, :, dim_count + rhs_count :]
@@ -398,6 +385,22 @@
     ).astype(jnp.bfloat16)
     group_coords = select_rows(all_coords.reshape(columns * node_width, dim_count), group_skeleton[0])
     group_pack = jnp.concatenate([group_coords, group_up], axis=1)
+    near_total = near_field(
+        local_points,
+        local_weights,
+        local_norms,
+        near_local,
+        (
+            left_pairs,
+            right_pairs,
+            scaled_norms(left_pairs[:, :, :dim_count]),
+            scaled_norms(right_pairs[:, :, :dim_count]),
+        ),
+        near_inner,
+        group_pack,
+    )
+    near_total, left_rows, right_rows = lax.optimization_barrier((near_total, left_rows, right_rows))
+
     left_rows = left_rows.reshape(REACH, rank_count, skeleton_width)
     right_rows = right_rows.reshape(REACH, rank_count, skeleton_width)
     far_local = far_list - offset
@@ -415,7 +418,6 @@
             scaled_norms(right_rows[:, :, :dim_count]),
         ),
         far_inner,
-        group_pack,
     )
     rows = lax.axis_size("row")
     received = [group_pack] + [

time: 143 us -> 143 us (level)
  transfers between devices with their start and end apart: 8 -> 8, of which waited for: 1 -> 1; matrix products, arithmetic and copies ran while one was open for 15% -> 17% of each run, Pallas kernels for 38% -> 39%
where the time goes in v8:
time: 143 us; the launch traced here: 140 us
  Pallas kernels  63.7 us (45%)
  other arithmetic  16 us (11%)
  starting transfers between devices  15.9 us (11%)
  between operations  15.2 us (11%)
  waiting for transfers between devices  11.7 us (8%)
  local copies, waits for them, and re-layouts  9.29 us (6%)
  matrix products  8.57 us (6%)
    pallas_call x2, Pallas kernels, near_field(): pl.pallas_call(lambda *refs: near_kernel(leaf_of, halo, *refs), grid_spec...  30.5 us
    pallas_call x2, Pallas kernels, far_field(): pl.pallas_call(lambda *refs: far_kernel(leaf_of, halo, *refs), grid_spec=...  23.8 us
    ppermute x2, waiting for transfers between devices, halos(): left = lax.ppermute(tail, FLAT, [(i, i + 1) for i in range(ends)])  11.6 us
    pallas_call x1, Pallas kernels, final_field(): pl.pallas_call(final_kernel, grid_spec=pltpu.PrefetchScalarGridSpec(num_s...  9.36 us
    ppermute x2, starting transfers between devices, halos(): right = lax.ppermute(head, FLAT, [(i + 1, i) for i in range(ends)])  7.41 us
    reduce_sum x5, other arithmetic, scaled_norms(): jnp.sum(wide * wide, axis=-1) * (-2.0 / cells.shape[-1])  5.97 us
    ppermute x3, starting transfers between devices, body(): lax.ppermute(group_pack, 'row', [(r, (r + shift) % rows) for r in range(r...  4.66 us
    unnamed x40, local copies, waits for them, and re-layouts  4.59 us
  transfers between devices with their start and end apart: 8, of which 1 were waited for; matrix products, arithmetic and copies ran while one was open for 17% of the time, Pallas kernels for 39%

profile of v8, /device:TPU:2, one launch (start us, length us, event | category | flops | bytes accessed | tf_op | source)
XLA Modules:
  0.0 140.3 jit_solution(6951556199516529574)
XLA Ops:
  6.5 0.9 copy.30
  7.4 0.7 fusion.53
  9.5 2.6 %multiply_reduce_fusion.1 = (f32[24,128]{1,0:T(8,128)S(1)}, bf16[24,128,128]{2,1,0:T(8,128)(2,1)S(1)}) fusion(bf16[24,256,128]{2,1,0:T(8,128)(2,1)} %bitcast.107, s32[24,128]{1,0:T(8,128)} %param.19), kind=kOutput, calls=%fused_computation.14 | convolution fusion | flops 203682816 | bytes 2383872 | tf_op jit(solution)/shard_map/bkp,bpc->bkc/dot_general | solution.py:300
  12.1 0.6 multiply_reduce_fusion.8
  12.7 0.3 copy-done.2
  13.0 1.0 multiply_convert_fusion
  14.1 0.6 fusion.21
  14.8 0.7 pad_maximum_fusion.5
  15.5 1.8 %fusion.65 = (bf16[2048,256]{1,0:T(8,128)(2,1)S(1)}, bf16[2048,256]{1,0:T(8,128)(2,1)S(1)}) fusion(bf16[6144,256]{1,0:T(8,128)(2,1)} %param.16), kind=kLoop, calls=%fused_computation.115 | loop fusion | bytes 4194304 | tf_op jit(solution)/shard_map/slice | solution.py:16
  17.6 1.4 pad_maximum_fusion.1
  19.0 1.9 %collective-permute-start.3 = (bf16[2048,384]{1,0:T(8,128)(2,1)}, bf16[2048,384]{1,0:T(8,128)(2,1)}, u32[]{:S(2)}, u32[]{:S(2)}) collective-permute-start(bf16[2048,384]{1,0:T(8,128)(2,1)} %pad_maximum_fusion.1), channel_id=1, source_target_pairs={{0,1},{1,2},{2,3},{3,4},{4,5},{5,6},{6,7},{7,8},{8,9},{9,10},{10,1... | collective-permute-start | bytes 4718600 | tf_op jit(solution)/shard_map/ppermute | solution.py:18
  20.9 1.4 pad_maximum_fusion.2
  22.3 3.8 %collective-permute-start.4 = (bf16[2048,384]{1,0:T(8,128)(2,1)}, bf16[2048,384]{1,0:T(8,128)(2,1)}, u32[]{:S(2)}, u32[]{:S(2)}) collective-permute-start(bf16[2048,384]{1,0:T(8,128)(2,1)} %pad_maximum_fusion.2), channel_id=1, source_target_pairs={{1,0},{2,1},{3,2},{4,3},{5,4},{6,5},{7,6},{8,7},{9,8},{10,9},{11,1... | collective-permute-start | bytes 4718600 | tf_op jit(solution)/shard_map/ppermute | solution.py:19
  26.0 1.4 fusion.24
  27.4 1.9 %collective-permute-start.5 = (bf16[1024,384]{1,0:T(8,128)(2,1)}, bf16[1024,384]{1,0:T(8,128)(2,1)}, u32[]{:S(2)}, u32[]{:S(2)}) collective-permute-start(bf16[1024,384]{1,0:T(8,128)(2,1)} %bitcast.22), channel_id=1, source_target_pairs={{0,1},{1,2},{2,3},{3,4},{4,5},{5,6},{6,7},{7,8},{8,9},{9,10},{10,1... | collective-permute-start | bytes 2359304 | tf_op jit(solution)/shard_map/ppermute | solution.py:18
  29.4 3.6 %collective-permute-start.6 = (bf16[1024,384]{1,0:T(8,128)(2,1)}, bf16[1024,384]{1,0:T(8,128)(2,1)}, u32[]{:S(2)}, u32[]{:S(2)}) collective-permute-start(bf16[1024,384]{1,0:T(8,128)(2,1)} %bitcast.23), channel_id=1, source_target_pairs={{1,0},{2,1},{3,2},{4,3},{5,4},{6,5},{7,6},{8,7},{9,8},{10,9},{11,1... | collective-permute-start | bytes 2359304 | tf_op jit(solution)/shard_map/ppermute | solution.py:19
  33.1 0.9 multiply_reduce_fusion
  34.1 0.7 reshape.216.refs_0_
  34.9 0.6 reshape.217.refs_0_
  35.5 0.6 broadcast_multiply_fusion
  36.1 11.3 %shard_map.145.refs_10_ = f32[24,256,256]{2,1,0:T(8,128)} custom-call(s32[120]{0:T(128)} %reshape.217.refs_0_, bf16[24,256,128]{2,1,0:T(8,128)(2,1)} %bitcast.108, bf16[24,256,128]{2,1,0:T(8,128)(2,1)} %bitcast.109, bf16[24,256,256]{2,1,0:T(8,128)(2,1)} %bitcast.112, f32[24,1,256]{2,1,0:T(1,128)} %bitcast.131), custom_call_target="tpu_custom_call" | custom-call | tf_op jit(solution)/shard_map/pallas_call | solution.py:169
  47.5 1.8 %pad_maximum_fusion.refs_2_.refs_3_ = bf16[24,128,384]{2,1,0:T(8,128)(2,1)} fusion(bf16[24,128,128]{2,1,0:T(8,128)(2,1)S(1)} %copy-done.4, bf16[24,128,256]{2,1,0:T(8,128)(2,1)S(1)} %multiply_convert_fusion), kind=kLoop, calls=%fused_computation.5 | loop fusion | flops 4718592 | bytes 4718592 | tf_op jit(solution)/shard_map/concatenate | solution.py:347
  49.2 0.6 broadcast_multiply_fusion.1
  49.8 9.0 %shard_map.147.refs_8_ = f32[24,128,256]{2,1,0:T(8,128)} custom-call(s32[96]{0:T(128)} %reshape.216.refs_0_, bf16[24,128,128]{2,1,0:T(8,128)(2,1)} %copy-done.2, bf16[24,128,384]{2,1,0:T(8,128)(2,1)} %pad_maximum_fusion.refs_2_.refs_3_, f32[24,1,128]{2,1,0:T(1,128)} %bitcast.138), custom_call_target="tpu_custom_call" | custom-call | tf_op jit(solution)/shard_map/pallas_call | solution.py:225
  58.9 11.6 %collective-permute-done.3 = bf16[2048,384]{1,0:T(8,128)(2,1)} collective-permute-done((bf16[2048,384]{1,0:T(8,128)(2,1)}, bf16[2048,384]{1,0:T(8,128)(2,1)}, u32[]{:S(2)}, u32[]{:S(2)}) %collective-permute-start.3) | collective-permute-done | bytes 1572896 | tf_op jit(solution)/shard_map/ppermute | solution.py:18
  70.5 1.4 multiply_reduce_fusion.3
  71.9 0.6 copy.39.refs_6_
  72.5 1.4 multiply_reduce_fusion.2
  73.9 0.6 mul.200.refs_8_
  74.5 1.5 %copy.47 = bf16[64,8,8,128]{3,2,1,0:T(8,128)(2,1)S(1)} copy(bf16[64,8,8,128]{3,1,2,0:T(8,128)(2,1)} %bitcast.124) | data formatting | bytes 2097152
  76.1 0.3 copy.46
  76.7 0.2 fusion.17
  76.9 0.4 multiply_reduce_fusion.9
  77.4 3.0 %collective-permute-start.1 = (bf16[128,384]{1,0:T(8,128)(2,1)S(1)}, bf16[128,384]{1,0:T(8,128)(2,1)S(1)}, u32[]{:S(2)}, u32[]{:S(2)}) collective-permute-start(bf16[128,384]{1,0:T(8,128)(2,1)S(1)} %get-tuple-element.20.refs_9_), channel_id=1, source_target_pairs={{0,16},{8,24},{16,0},{24,8},{1,17},{9,25},{17,1},{25,9},{2,18},{10... | collective-permute-start | bytes 294920 | tf_op jit(solution)/shard_map/ppermute | solution.py:424
  80.4 1.6 %collective-permute-start = (bf16[128,384]{1,0:T(8,128)(2,1)S(1)}, bf16[128,384]{1,0:T(8,128)(2,1)S(1)}, u32[]{:S(2)}, u32[]{:S(2)}) collective-permute-start(bf16[128,384]{1,0:T(8,128)(2,1)S(1)} %get-tuple-element.20.refs_9_), channel_id=1, source_target_pairs={{0,8},{8,16},{16,24},{24,0},{1,9},{9,17},{17,25},{25,1},{2,10},{10... | collective-permute-start | bytes 294920 | tf_op jit(solution)/shard_map/ppermute | solution.py:424
  82.0 0.3 copy.55
  82.5 19.2 %shard_map.146.near_ref = f32[24,256,256]{2,1,0:T(8,128)} custom-call(s32[120]{0:T(128)} %reshape.217.refs_0_, bf16[24,256,128]{2,1,0:T(8,128)(2,1)} %bitcast.110, bf16[8,256,384]{2,1,0:T(8,128)(2,1)} %bitcast.18.refs_2_, bf16[24,256,128]{2,1,0:T(8,128)(2,1)} %bitcast.111, bf16[8,256,384]{2,1,0:T(8,128)(2,1)} %bitcast.19.refs_4_, ...), custom_call_target="tpu_custom_call", output_to_operand_aliasing={{}: (10, {})} | custom-call | tf_op jit(solution)/shard_map/pallas_call | solution.py:169
  101.7 0.3 fusion.8
  102.1 0.4 convolution_convert_fusion.1
  102.5 1.2 multiply_reduce_fusion.5
  103.7 0.6 broadcast_multiply_fusion.4
  104.3 1.2 multiply_reduce_fusion.4
  105.4 0.6 broadcast_multiply_fusion.3
  106.0 14.8 %shard_map.148.far_ref = f32[24,128,256]{2,1,0:T(8,128)} custom-call(s32[96]{0:T(128)} %reshape.216.refs_0_, bf16[24,128,128]{2,1,0:T(8,128)(2,1)} %copy-done.2, bf16[8,128,384]{2,1,0:T(8,128)(2,1)} %bitcast.24.refs_2_, bf16[24,128,384]{2,1,0:T(8,128)(2,1)} %pad_maximum_fusion.refs_2_.refs_3_, ...), custom_call_target="tpu_custom_call", output_to_operand_aliasing={{}: (8, {})} | custom-call | tf_op jit(solution)/shard_map/pallas_call | solution.py:225
  120.9 0.4 convolution_bitcast_fusion
  121.8 1.0 convolution_convert_fusion
  123.2 1.0 fusion.16.down_ref
  124.1 9.4 %shard_map.149 = bf16[24,256,256]{2,1,0:T(8,128)(2,1)} custom-call(s32[24]{0:T(128)} %rank_ref.1, bf16[24,128,128]{2,1,0:T(8,128)(2,1)} %bitcast.122, bf16[128,256]{1,0:T(8,128)(2,1)} %fusion.16.down_ref, f32[24,128,256]{2,1,0:T(8,128)} %shard_map.148.far_ref, bf16[24,256,128]{2,1,0:T(8,128)(2,1)} %bitcast.117, f32[24,256,256]{2,1,0:T(8,128)} %shard_map.146.near_ref), custom_call_target="tpu_custom_call" | custom-call | tf_op jit(solution)/shard_map/pallas_call | solution.py:268
  (62 shorter events, 2.3 us)
Async XLA Ops:
  6.5 68.0 %all-gather.3.cloned.1.call-start = ((), (), s32[]{:S(2)}) async-start(), calls=%async_computation | async-start | bytes 1179648 | tf_op jit(solution)/shard_map/all_gather | solution.py:369
  6.5 5.6 %copy-start.11 = (s32[1,128]{1,0:T(1,128)S(1)}, s32[1,128]{1,0:T(1,128)}, u32[]{:S(2)}) copy-start(s32[1,128]{1,0:T(1,128)} %param.24) | copy-start | bytes 1540
  9.5 3.5 %copy-start.1 = (bf16[6144,256]{1,0:T(8,128)(2,1)S(1)}, bf16[6144,256]{1,0:T(8,128)(2,1)}, u32[]{:S(2)}) copy-start(bf16[6144,256]{1,0:T(8,128)(2,1)} %param.16) | copy-start | bytes 9437188
  9.5 3.5 %copy-start.5 = (bf16[6144,128]{1,0:T(8,128)(2,1)S(1)}, bf16[6144,128]{1,0:T(8,128)(2,1)}, u32[]{:S(2)}) copy-start(bf16[6144,128]{1,0:T(8,128)(2,1)} %param.17) | copy-start | bytes 4718596
  12.1 0.9 copy-start.2
  13.0 1.1 copy-start.6
  15.5 2.0 %copy-start = (bf16[6144,128]{1,0:T(8,128)(2,1)S(1)}, bf16[6144,128]{1,0:T(8,128)(2,1)}, u32[]{:S(2)}) copy-start(bf16[6144,128]{1,0:T(8,128)(2,1)} %param.15) | copy-start | bytes 4718596
  19.0 51.5 %collective-permute-start.3 = (bf16[2048,384]{1,0:T(8,128)(2,1)}, bf16[2048,384]{1,0:T(8,128)(2,1)}, u32[]{:S(2)}, u32[]{:S(2)}) collective-permute-start(bf16[2048,384]{1,0:T(8,128)(2,1)} %pad_maximum_fusion.1), channel_id=1, source_target_pairs={{0,1},{1,2},{2,3},{3,4},{4,5},{5,6},{6,7},{7,8},{8,9},{9,10},{10,1... | collective-permute-start | bytes 4718600 | tf_op jit(solution)/shard_map/ppermute | solution.py:18
  20.9 5.1 %copy-start.3 = (bf16[24,128,128]{2,1,0:T(8,128)(2,1)S(1)}, bf16[24,128,128]{2,1,0:T(8,128)(2,1)}, u32[]{:S(2)}) copy-start(bf16[24,128,128]{2,1,0:T(8,128)(2,1)} %copy-done.2) | copy-start | bytes 2359300
  22.2 10.8 %copy-start.10 = (s32[24,4]{0,1:T(4,128)S(1)}, s32[24,4]{0,1:T(4,128)}, u32[]{:S(2)}) copy-start(s32[24,4]{0,1:T(4,128)} %param.21) | copy-start | bytes 1156
  22.2 10.8 %copy-start.9 = (s32[24,5]{0,1:T(8,128)S(1)}, s32[24,5]{0,1:T(8,128)}, u32[]{:S(2)}) copy-start(s32[24,5]{0,1:T(8,128)} %param.20) | copy-start | bytes 1444
  22.3 50.3 %collective-permute-start.4 = (bf16[2048,384]{1,0:T(8,128)(2,1)}, bf16[2048,384]{1,0:T(8,128)(2,1)}, u32[]{:S(2)}, u32[]{:S(2)}) collective-permute-start(bf16[2048,384]{1,0:T(8,128)(2,1)} %pad_maximum_fusion.2), channel_id=1, source_target_pairs={{1,0},{2,1},{3,2},{4,3},{5,4},{6,5},{7,6},{8,7},{9,8},{10,9},{11,1... | collective-permute-start | bytes 4718600 | tf_op jit(solution)/shard_map/ppermute | solution.py:19
  27.4 75.1 %collective-permute-start.5 = (bf16[1024,384]{1,0:T(8,128)(2,1)}, bf16[1024,384]{1,0:T(8,128)(2,1)}, u32[]{:S(2)}, u32[]{:S(2)}) collective-permute-start(bf16[1024,384]{1,0:T(8,128)(2,1)} %bitcast.22), channel_id=1, source_target_pairs={{0,1},{1,2},{2,3},{3,4},{4,5},{5,6},{6,7},{7,8},{8,9},{9,10},{10,1... | collective-permute-start | bytes 2359304 | tf_op jit(solution)/shard_map/ppermute | solution.py:18
  29.4 73.2 %collective-permute-start.6 = (bf16[1024,384]{1,0:T(8,128)(2,1)}, bf16[1024,384]{1,0:T(8,128)(2,1)}, u32[]{:S(2)}, u32[]{:S(2)}) collective-permute-start(bf16[1024,384]{1,0:T(8,128)(2,1)} %bitcast.23), channel_id=1, source_target_pairs={{1,0},{2,1},{3,2},{4,3},{5,4},{6,5},{7,6},{8,7},{9,8},{10,9},{11,1... | collective-permute-start | bytes 2359304 | tf_op jit(solution)/shard_map/ppermute | solution.py:19
  36.1 11.3 %copy-start.4 = (bf16[24,128,128]{2,1,0:T(8,128)(2,1)S(1)}, bf16[24,128,128]{2,1,0:T(8,128)(2,1)}, u32[]{:S(2)}) copy-start(bf16[24,128,128]{2,1,0:T(8,128)(2,1)} %copy-done.2) | copy-start | bytes 2359300
  49.8 9.0 %copy-start.12 = (s32[1,4]{1,0:T(1,128)S(1)}, s32[1,4]{1,0:T(1,128)}, u32[]{:S(2)}) copy-start(s32[1,4]{1,0:T(1,128)} %param.25) | copy-start | bytes 52
  49.8 9.0 %copy-start.13 = (s32[1,2]{1,0:T(1,128)S(1)}, s32[1,2]{1,0:T(1,128)}, u32[]{:S(2)}) copy-start(s32[1,2]{1,0:T(1,128)} %param.29) | copy-start | bytes 28
  76.1 0.9 copy-start.14
  77.3 5.1 %copy-start.7 = (bf16[128,384]{1,0:T(8,128)(2,1)}, bf16[128,384]{1,0:T(8,128)(2,1)S(1)}, u32[]{:S(2)}) copy-start(bf16[128,384]{1,0:T(8,128)(2,1)S(1)} %get-tuple-element.20.refs_9_) | copy-start | bytes 294916
  77.3 43.9 %collective-permute-start.2 = (bf16[128,384]{1,0:T(8,128)(2,1)S(1)}, bf16[128,384]{1,0:T(8,128)(2,1)S(1)}, u32[]{:S(2)}, u32[]{:S(2)}) collective-permute-start(bf16[128,384]{1,0:T(8,128)(2,1)S(1)} %get-tuple-element.20.refs_9_), channel_id=1, source_target_pairs={{0,24},{8,0},{16,8},{24,16},{1,25},{9,1},{17,9},{25,17},{2,26},{10... | collective-permute-start | bytes 294920 | tf_op jit(solution)/shard_map/ppermute | solution.py:424
  77.4 44.0 %collective-permute-start.1 = (bf16[128,384]{1,0:T(8,128)(2,1)S(1)}, bf16[128,384]{1,0:T(8,128)(2,1)S(1)}, u32[]{:S(2)}, u32[]{:S(2)}) collective-permute-start(bf16[128,384]{1,0:T(8,128)(2,1)S(1)} %get-tuple-element.20.refs_9_), channel_id=1, source_target_pairs={{0,16},{8,24},{16,0},{24,8},{1,17},{9,25},{17,1},{25,9},{2,18},{10... | collective-permute-start | bytes 294920 | tf_op jit(solution)/shard_map/ppermute | solution.py:424
  80.4 41.2 %collective-permute-start = (bf16[128,384]{1,0:T(8,128)(2,1)S(1)}, bf16[128,384]{1,0:T(8,128)(2,1)S(1)}, u32[]{:S(2)}, u32[]{:S(2)}) collective-permute-start(bf16[128,384]{1,0:T(8,128)(2,1)S(1)} %get-tuple-element.20.refs_9_), channel_id=1, source_target_pairs={{0,8},{8,16},{16,24},{24,0},{1,9},{9,17},{17,25},{25,1},{2,10},{10... | collective-permute-start | bytes 294920 | tf_op jit(solution)/shard_map/ppermute | solution.py:424
  121.8 1.4 copy-start.8
Sparse Core Ops, SparseCore 0:
  15.6 49.8 all-gather.2

commit v9 on v8

--- a/solution.py
+++ b/solution.py
@@ -187,7 +187,7 @@
 
 
 def far_kernel(leaf_of, halo, index_ref, target_ref, *refs):
-    inputs = 7 if halo else 2
+    inputs = 7 if halo else 3
     out_ref = refs[inputs]
     source_buf, norm_buf, sems = refs[inputs + 1 :]
     count, rank = source_buf.shape[1], source_buf.shape[2]
@@ -208,7 +208,7 @@
     out_ref[0] = jnp.dot(kernel, sources[:, dims:], preferred_element_type=jnp.float32)
 
 
-def far_field(leaf_coords, own_rows, own_norms, far_local, halo_inputs=None, previous=None):
+def far_field(leaf_coords, own_rows, own_norms, far_local, halo_inputs=None, previous=None, after=None):
     leaves, rank, dims = leaf_coords.shape
     width = own_rows.shape[-1]
     count = far_local.shape[1]
@@ -219,7 +219,7 @@
         left_rows, right_rows, left_norms, right_norms = halo_inputs
         inputs = (left_rows, own_rows, right_rows, left_norms, own_norms, right_norms, previous)
     else:
-        inputs = (own_rows, own_norms)
+        inputs = (own_rows, own_norms, after)
     aliases = {len(inputs) + 1: 0} if previous is not None else {}
     by_leaf = lambda step, index: (leaf_of(step), 0, 0)
     return pl.pallas_call(
@@ -385,6 +385,9 @@
     ).astype(jnp.bfloat16)
     group_coords = select_rows(all_coords.reshape(columns * node_width, dim_count), group_skeleton[0])
     group_pack = jnp.concatenate([group_coords, group_up], axis=1)
+    far_local = far_list - offset
+    coord_norms = scaled_norms(leaf_coords)
+    far_inner = far_field(leaf_coords, own_rows, coord_norms, far_local, after=group_pack)
     near_total = near_field(
         local_points,
         local_weights,
@@ -403,9 +406,6 @@
 
     left_rows = left_rows.reshape(REACH, rank_count, skeleton_width)
     right_rows = right_rows.reshape(REACH, rank_count, skeleton_width)
-    far_local = far_list - offset
-    coord_norms = scaled_norms(leaf_coords)
-    far_inner = far_field(leaf_coords, own_rows, coord_norms, far_local)
     far_total = far_field(
         leaf_coords,
         own_rows,

time: 143 us -> 151 us (1.056)
  waiting for transfers between devices: 11.7 us -> 20.6 us
    ppermute x2, waiting for transfers between devices: 11.6 us -> 20.6 us  [halos(): left = lax.ppermute(tail, FLAT, [(i, i + 1) for i in range(ends)])]
  transfers between devices with their start and end apart: 8 -> 8, of which waited for: 1 -> 1; matrix products, arithmetic and copies ran while one was open for 17% -> 16% of each run, Pallas kernels for 39% -> 36%
where the time goes in v9:
time: 151 us; the launch traced here: 149 us
  Pallas kernels  63.6 us (42%)
  waiting for transfers between devices  20.6 us (14%)
  other arithmetic  16 us (11%)
  starting transfers between devices  15.9 us (11%)
  between operations  15.2 us (10%)
  local copies, waits for them, and re-layouts  9.33 us (6%)
  matrix products  8.57 us (6%)
    pallas_call x2, Pallas kernels, near_field(): pl.pallas_call(lambda *refs: near_kernel(leaf_of, halo, *refs), grid_spec...  30.5 us
    pallas_call x2, Pallas kernels, far_field(): pl.pallas_call(lambda *refs: far_kernel(leaf_of, halo, *refs), grid_spec=...  23.7 us
    ppermute x2, waiting for transfers between devices, halos(): left = lax.ppermute(tail, FLAT, [(i, i + 1) for i in range(ends)])  20.6 us
    pallas_call x1, Pallas kernels, final_field(): pl.pallas_call(final_kernel, grid_spec=pltpu.PrefetchScalarGridSpec(num_s...  9.38 us
    ppermute x2, starting transfers between devices, halos(): right = lax.ppermute(head, FLAT, [(i + 1, i) for i in range(ends)])  7.41 us
    reduce_sum x5, other arithmetic, scaled_norms(): jnp.sum(wide * wide, axis=-1) * (-2.0 / cells.shape[-1])  5.97 us
    ppermute x3, starting transfers between devices, body(): lax.ppermute(group_pack, 'row', [(r, (r + shift) % rows) for r in range(r...  4.66 us
    unnamed x40, local copies, waits for them, and re-layouts  4.6 us
  transfers between devices with their start and end apart: 8, of which 1 were waited for; matrix products, arithmetic and copies ran while one was open for 16% of the time, Pallas kernels for 36%

profile of v9, /device:TPU:2, one launch (start us, length us, event | category | flops | bytes accessed | tf_op | source)
XLA Modules:
  0.0 149.2 jit_solution(2257764143366741201)
XLA Ops:
  6.5 0.9 copy.30
  7.4 0.7 fusion.53
  9.5 2.6 %multiply_reduce_fusion.1 = (f32[24,128]{1,0:T(8,128)S(1)}, bf16[24,128,128]{2,1,0:T(8,128)(2,1)S(1)}) fusion(bf16[24,256,128]{2,1,0:T(8,128)(2,1)} %bitcast.107, s32[24,128]{1,0:T(8,128)} %param.19), kind=kOutput, calls=%fused_computation.14 | convolution fusion | flops 203682816 | bytes 2383872 | tf_op jit(solution)/shard_map/bkp,bpc->bkc/dot_general | solution.py:300
  12.1 0.6 multiply_reduce_fusion.8
  12.7 0.3 copy-done.2
  13.0 1.0 multiply_convert_fusion
  14.1 0.6 fusion.21
  14.8 0.7 pad_maximum_fusion.5
  15.5 1.8 %fusion.65 = (bf16[2048,256]{1,0:T(8,128)(2,1)S(1)}, bf16[2048,256]{1,0:T(8,128)(2,1)S(1)}) fusion(bf16[6144,256]{1,0:T(8,128)(2,1)} %param.16), kind=kLoop, calls=%fused_computation.115 | loop fusion | bytes 4194304 | tf_op jit(solution)/shard_map/slice | solution.py:16
  17.6 1.4 pad_maximum_fusion.1
  18.9 1.9 %collective-permute-start.3 = (bf16[2048,384]{1,0:T(8,128)(2,1)}, bf16[2048,384]{1,0:T(8,128)(2,1)}, u32[]{:S(2)}, u32[]{:S(2)}) collective-permute-start(bf16[2048,384]{1,0:T(8,128)(2,1)} %pad_maximum_fusion.1), channel_id=1, source_target_pairs={{0,1},{1,2},{2,3},{3,4},{4,5},{5,6},{6,7},{7,8},{8,9},{9,10},{10,1... | collective-permute-start | bytes 4718600 | tf_op jit(solution)/shard_map/ppermute | solution.py:18
  20.9 1.3 pad_maximum_fusion.2
  22.2 3.8 %collective-permute-start.4 = (bf16[2048,384]{1,0:T(8,128)(2,1)}, bf16[2048,384]{1,0:T(8,128)(2,1)}, u32[]{:S(2)}, u32[]{:S(2)}) collective-permute-start(bf16[2048,384]{1,0:T(8,128)(2,1)} %pad_maximum_fusion.2), channel_id=1, source_target_pairs={{1,0},{2,1},{3,2},{4,3},{5,4},{6,5},{7,6},{8,7},{9,8},{10,9},{11,1... | collective-permute-start | bytes 4718600 | tf_op jit(solution)/shard_map/ppermute | solution.py:19
  26.0 1.4 fusion.24
  27.4 1.9 %collective-permute-start.5 = (bf16[1024,384]{1,0:T(8,128)(2,1)}, bf16[1024,384]{1,0:T(8,128)(2,1)}, u32[]{:S(2)}, u32[]{:S(2)}) collective-permute-start(bf16[1024,384]{1,0:T(8,128)(2,1)} %bitcast.22), channel_id=1, source_target_pairs={{0,1},{1,2},{2,3},{3,4},{4,5},{5,6},{6,7},{7,8},{8,9},{9,10},{10,1... | collective-permute-start | bytes 2359304 | tf_op jit(solution)/shard_map/ppermute | solution.py:18
  29.3 3.6 %collective-permute-start.6 = (bf16[1024,384]{1,0:T(8,128)(2,1)}, bf16[1024,384]{1,0:T(8,128)(2,1)}, u32[]{:S(2)}, u32[]{:S(2)}) collective-permute-start(bf16[1024,384]{1,0:T(8,128)(2,1)} %bitcast.23), channel_id=1, source_target_pairs={{1,0},{2,1},{3,2},{4,3},{5,4},{6,5},{7,6},{8,7},{9,8},{10,9},{11,1... | collective-permute-start | bytes 2359304 | tf_op jit(solution)/shard_map/ppermute | solution.py:19
  33.0 0.9 multiply_reduce_fusion
  34.1 0.6 reshape.216.refs_0_
  34.8 0.7 reshape.217.refs_0_
  35.5 0.6 broadcast_multiply_fusion
  36.1 11.3 %shard_map.145.refs_10_ = f32[24,256,256]{2,1,0:T(8,128)} custom-call(s32[120]{0:T(128)} %reshape.217.refs_0_, bf16[24,256,128]{2,1,0:T(8,128)(2,1)} %bitcast.108, bf16[24,256,128]{2,1,0:T(8,128)(2,1)} %bitcast.109, bf16[24,256,256]{2,1,0:T(8,128)(2,1)} %bitcast.112, f32[24,1,256]{2,1,0:T(1,128)} %bitcast.131), custom_call_target="tpu_custom_call" | custom-call | tf_op jit(solution)/shard_map/pallas_call | solution.py:169
  47.5 1.8 %pad_maximum_fusion.refs_2_.refs_3_ = bf16[24,128,384]{2,1,0:T(8,128)(2,1)} fusion(bf16[24,128,128]{2,1,0:T(8,128)(2,1)S(1)} %copy-done.4, bf16[24,128,256]{2,1,0:T(8,128)(2,1)S(1)} %multiply_convert_fusion), kind=kLoop, calls=%fused_computation.5 | loop fusion | flops 4718592 | bytes 4718592 | tf_op jit(solution)/shard_map/concatenate | solution.py:347
  49.3 0.6 broadcast_multiply_fusion.1
  49.9 20.6 %collective-permute-done.3 = bf16[2048,384]{1,0:T(8,128)(2,1)} collective-permute-done((bf16[2048,384]{1,0:T(8,128)(2,1)}, bf16[2048,384]{1,0:T(8,128)(2,1)}, u32[]{:S(2)}, u32[]{:S(2)}) %collective-permute-start.3) | collective-permute-done | bytes 1572896 | tf_op jit(solution)/shard_map/ppermute | solution.py:18
  70.5 1.4 multiply_reduce_fusion.3
  71.9 0.6 copy.39.refs_6_
  72.5 1.4 multiply_reduce_fusion.2
  73.9 0.6 mul.200.refs_8_
  74.5 1.5 copy.47
  76.1 0.3 copy.46
  76.6 0.2 fusion.17
  76.9 0.4 multiply_reduce_fusion.9
  77.4 3.0 %collective-permute-start.1 = (bf16[128,384]{1,0:T(8,128)(2,1)S(1)}, bf16[128,384]{1,0:T(8,128)(2,1)S(1)}, u32[]{:S(2)}, u32[]{:S(2)}) collective-permute-start(bf16[128,384]{1,0:T(8,128)(2,1)S(1)} %get-tuple-element.20.refs_9_.refs_4_), channel_id=1, source_target_pairs={{0,16},{8,24},{16,0},{24,8},{1,17},{9,25},{17,1},{25,9},{2,18},{10... | collective-permute-start | bytes 294920 | tf_op jit(solution)/shard_map/ppermute | solution.py:424
  80.4 1.6 %collective-permute-start = (bf16[128,384]{1,0:T(8,128)(2,1)S(1)}, bf16[128,384]{1,0:T(8,128)(2,1)S(1)}, u32[]{:S(2)}, u32[]{:S(2)}) collective-permute-start(bf16[128,384]{1,0:T(8,128)(2,1)S(1)} %get-tuple-element.20.refs_9_.refs_4_), channel_id=1, source_target_pairs={{0,8},{8,16},{16,24},{24,0},{1,9},{9,17},{17,25},{25,1},{2,10},{10... | collective-permute-start | bytes 294920 | tf_op jit(solution)/shard_map/ppermute | solution.py:424
  82.0 0.3 copy.55
  82.4 19.2 %shard_map.146.near_ref = f32[24,256,256]{2,1,0:T(8,128)} custom-call(s32[120]{0:T(128)} %reshape.217.refs_0_, bf16[24,256,128]{2,1,0:T(8,128)(2,1)} %bitcast.110, bf16[8,256,384]{2,1,0:T(8,128)(2,1)} %bitcast.18.refs_2_, bf16[24,256,128]{2,1,0:T(8,128)(2,1)} %bitcast.111, bf16[8,256,384]{2,1,0:T(8,128)(2,1)} %bitcast.19.refs_4_, ...), custom_call_target="tpu_custom_call", output_to_operand_aliasing={{}: (10, {})} | custom-call | tf_op jit(solution)/shard_map/pallas_call | solution.py:169
  101.6 0.3 fusion.8
  102.1 0.4 convolution_convert_fusion.1
  102.5 1.2 multiply_reduce_fusion.5
  103.6 0.6 broadcast_multiply_fusion.4
  104.2 1.2 multiply_reduce_fusion.4
  105.4 0.6 broadcast_multiply_fusion.3
  106.0 8.8 %shard_map.147.refs_8_ = f32[24,128,256]{2,1,0:T(8,128)} custom-call(s32[96]{0:T(128)} %reshape.216.refs_0_, bf16[24,128,128]{2,1,0:T(8,128)(2,1)} %copy-done.2, bf16[24,128,384]{2,1,0:T(8,128)(2,1)} %pad_maximum_fusion.refs_2_.refs_3_, f32[24,1,128]{2,1,0:T(1,128)} %bitcast.138, bf16[128,384]{1,0:T(8,128)(2,1)} %copy-done.7), custom_call_target="tpu_custom_call" | custom-call | tf_op jit(solution)/shard_map/pallas_call | solution.py:225
  114.8 14.8 %shard_map.148.far_ref = f32[24,128,256]{2,1,0:T(8,128)} custom-call(s32[96]{0:T(128)} %reshape.216.refs_0_, bf16[24,128,128]{2,1,0:T(8,128)(2,1)} %copy-done.2, bf16[8,128,384]{2,1,0:T(8,128)(2,1)} %bitcast.24.refs_2_, bf16[24,128,384]{2,1,0:T(8,128)(2,1)} %pad_maximum_fusion.refs_2_.refs_3_, ...), custom_call_target="tpu_custom_call", output_to_operand_aliasing={{}: (8, {})} | custom-call | tf_op jit(solution)/shard_map/pallas_call | solution.py:225
  129.7 0.4 convolution_bitcast_fusion
  130.6 1.0 convolution_convert_fusion
  132.0 1.0 fusion.16.down_ref
  132.9 9.4 %shard_map.149 = bf16[24,256,256]{2,1,0:T(8,128)(2,1)} custom-call(s32[24]{0:T(128)} %rank_ref.1, bf16[24,128,128]{2,1,0:T(8,128)(2,1)} %bitcast.122, bf16[128,256]{1,0:T(8,128)(2,1)} %fusion.16.down_ref, f32[24,128,256]{2,1,0:T(8,128)} %shard_map.148.far_ref, bf16[24,256,128]{2,1,0:T(8,128)(2,1)} %bitcast.117, f32[24,256,256]{2,1,0:T(8,128)} %shard_map.146.near_ref), custom_call_target="tpu_custom_call" | custom-call | tf_op jit(solution)/shard_map/pallas_call | solution.py:268
  (62 shorter events, 2.4 us)
Async XLA Ops:
  6.5 67.9 %all-gather.3.cloned.1.call-start = ((), (), s32[]{:S(2)}) async-start(), calls=%async_computation | async-start | bytes 1179648 | tf_op jit(solution)/shard_map/all_gather | solution.py:369
  6.5 5.6 %copy-start.11 = (s32[1,128]{1,0:T(1,128)S(1)}, s32[1,128]{1,0:T(1,128)}, u32[]{:S(2)}) copy-start(s32[1,128]{1,0:T(1,128)} %param.24) | copy-start | bytes 1540
  9.5 3.5 %copy-start.1 = (bf16[6144,256]{1,0:T(8,128)(2,1)S(1)}, bf16[6144,256]{1,0:T(8,128)(2,1)}, u32[]{:S(2)}) copy-start(bf16[6144,256]{1,0:T(8,128)(2,1)} %param.16) | copy-start | bytes 9437188
  9.5 3.5 %copy-start.5 = (bf16[6144,128]{1,0:T(8,128)(2,1)S(1)}, bf16[6144,128]{1,0:T(8,128)(2,1)}, u32[]{:S(2)}) copy-start(bf16[6144,128]{1,0:T(8,128)(2,1)} %param.17) | copy-start | bytes 4718596
  12.1 0.9 copy-start.2
  13.0 1.1 copy-start.6
  15.4 2.0 %copy-start = (bf16[6144,128]{1,0:T(8,128)(2,1)S(1)}, bf16[6144,128]{1,0:T(8,128)(2,1)}, u32[]{:S(2)}) copy-start(bf16[6144,128]{1,0:T(8,128)(2,1)} %param.15) | copy-start | bytes 4718596
  18.9 51.5 %collective-permute-start.3 = (bf16[2048,384]{1,0:T(8,128)(2,1)}, bf16[2048,384]{1,0:T(8,128)(2,1)}, u32[]{:S(2)}, u32[]{:S(2)}) collective-permute-start(bf16[2048,384]{1,0:T(8,128)(2,1)} %pad_maximum_fusion.1), channel_id=1, source_target_pairs={{0,1},{1,2},{2,3},{3,4},{4,5},{5,6},{6,7},{7,8},{8,9},{9,10},{10,1... | collective-permute-start | bytes 4718600 | tf_op jit(solution)/shard_map/ppermute | solution.py:18
  20.8 5.1 %copy-start.3 = (bf16[24,128,128]{2,1,0:T(8,128)(2,1)S(1)}, bf16[24,128,128]{2,1,0:T(8,128)(2,1)}, u32[]{:S(2)}) copy-start(bf16[24,128,128]{2,1,0:T(8,128)(2,1)} %copy-done.2) | copy-start | bytes 2359300
  22.2 10.8 %copy-start.10 = (s32[24,4]{0,1:T(4,128)S(1)}, s32[24,4]{0,1:T(4,128)}, u32[]{:S(2)}) copy-start(s32[24,4]{0,1:T(4,128)} %param.21) | copy-start | bytes 1156
  22.2 10.8 %copy-start.9 = (s32[24,5]{0,1:T(8,128)S(1)}, s32[24,5]{0,1:T(8,128)}, u32[]{:S(2)}) copy-start(s32[24,5]{0,1:T(8,128)} %param.20) | copy-start | bytes 1444
  22.2 50.3 %collective-permute-start.4 = (bf16[2048,384]{1,0:T(8,128)(2,1)}, bf16[2048,384]{1,0:T(8,128)(2,1)}, u32[]{:S(2)}, u32[]{:S(2)}) collective-permute-start(bf16[2048,384]{1,0:T(8,128)(2,1)} %pad_maximum_fusion.2), channel_id=1, source_target_pairs={{1,0},{2,1},{3,2},{4,3},{5,4},{6,5},{7,6},{8,7},{9,8},{10,9},{11,1... | collective-permute-start | bytes 4718600 | tf_op jit(solution)/shard_map/ppermute | solution.py:19
  27.4 75.1 %collective-permute-start.5 = (bf16[1024,384]{1,0:T(8,128)(2,1)}, bf16[1024,384]{1,0:T(8,128)(2,1)}, u32[]{:S(2)}, u32[]{:S(2)}) collective-permute-start(bf16[1024,384]{1,0:T(8,128)(2,1)} %bitcast.22), channel_id=1, source_target_pairs={{0,1},{1,2},{2,3},{3,4},{4,5},{5,6},{6,7},{7,8},{8,9},{9,10},{10,1... | collective-permute-start | bytes 2359304 | tf_op jit(solution)/shard_map/ppermute | solution.py:18
  29.3 73.2 %collective-permute-start.6 = (bf16[1024,384]{1,0:T(8,128)(2,1)}, bf16[1024,384]{1,0:T(8,128)(2,1)}, u32[]{:S(2)}, u32[]{:S(2)}) collective-permute-start(bf16[1024,384]{1,0:T(8,128)(2,1)} %bitcast.23), channel_id=1, source_target_pairs={{1,0},{2,1},{3,2},{4,3},{5,4},{6,5},{7,6},{8,7},{9,8},{10,9},{11,1... | collective-permute-start | bytes 2359304 | tf_op jit(solution)/shard_map/ppermute | solution.py:19
  36.1 11.3 %copy-start.4 = (bf16[24,128,128]{2,1,0:T(8,128)(2,1)S(1)}, bf16[24,128,128]{2,1,0:T(8,128)(2,1)}, u32[]{:S(2)}) copy-start(bf16[24,128,128]{2,1,0:T(8,128)(2,1)} %copy-done.2) | copy-start | bytes 2359300
  47.5 1.8 %copy-start.12 = (s32[1,4]{1,0:T(1,128)S(1)}, s32[1,4]{1,0:T(1,128)}, u32[]{:S(2)}) copy-start(s32[1,4]{1,0:T(1,128)} %param.25) | copy-start | bytes 52
  47.5 1.8 %copy-start.13 = (s32[1,2]{1,0:T(1,128)S(1)}, s32[1,2]{1,0:T(1,128)}, u32[]{:S(2)}) copy-start(s32[1,2]{1,0:T(1,128)} %param.29) | copy-start | bytes 28
  76.0 0.9 copy-start.14
  77.3 5.1 %copy-start.7 = (bf16[128,384]{1,0:T(8,128)(2,1)}, bf16[128,384]{1,0:T(8,128)(2,1)S(1)}, u32[]{:S(2)}) copy-start(bf16[128,384]{1,0:T(8,128)(2,1)S(1)} %get-tuple-element.20.refs_9_.refs_4_) | copy-start | bytes 294916
  77.3 52.8 %collective-permute-start.2 = (bf16[128,384]{1,0:T(8,128)(2,1)S(1)}, bf16[128,384]{1,0:T(8,128)(2,1)S(1)}, u32[]{:S(2)}, u32[]{:S(2)}) collective-permute-start(bf16[128,384]{1,0:T(8,128)(2,1)S(1)} %get-tuple-element.20.refs_9_.refs_4_), channel_id=1, source_target_pairs={{0,24},{8,0},{16,8},{24,16},{1,25},{9,1},{17,9},{25,17},{2,26},{10... | collective-permute-start | bytes 294920 | tf_op jit(solution)/shard_map/ppermute | solution.py:424
  77.4 52.9 %collective-permute-start.1 = (bf16[128,384]{1,0:T(8,128)(2,1)S(1)}, bf16[128,384]{1,0:T(8,128)(2,1)S(1)}, u32[]{:S(2)}, u32[]{:S(2)}) collective-permute-start(bf16[128,384]{1,0:T(8,128)(2,1)S(1)} %get-tuple-element.20.refs_9_.refs_4_), channel_id=1, source_target_pairs={{0,16},{8,24},{16,0},{24,8},{1,17},{9,25},{17,1},{25,9},{2,18},{10... | collective-permute-start | bytes 294920 | tf_op jit(solution)/shard_map/ppermute | solution.py:424
  80.4 50.0 %collective-permute-start = (bf16[128,384]{1,0:T(8,128)(2,1)S(1)}, bf16[128,384]{1,0:T(8,128)(2,1)S(1)}, u32[]{:S(2)}, u32[]{:S(2)}) collective-permute-start(bf16[128,384]{1,0:T(8,128)(2,1)S(1)} %get-tuple-element.20.refs_9_.refs_4_), channel_id=1, source_target_pairs={{0,8},{8,16},{16,24},{24,0},{1,9},{9,17},{17,25},{25,1},{2,10},{10... | collective-permute-start | bytes 294920 | tf_op jit(solution)/shard_map/ppermute | solution.py:424
  130.6 1.4 copy-start.8
Sparse Core Ops, SparseCore 0:
  15.6 49.8 all-gather.2

commit v10 on v8

--- a/solution.py
+++ b/solution.py
@@ -39,8 +39,10 @@
 
 
 def scaled_norms(cells):
-    wide = cells.astype(jnp.float32)
-    return (jnp.sum(wide * wide, axis=-1) * (-2.0 / cells.shape[-1]))[:, None, :]
+    factor = (2.0 / cells.shape[-1]) ** 0.5
+    assert factor * factor == 2.0 / cells.shape[-1]
+    wide = cells.astype(jnp.float32) * factor
+    return jnp.sum(wide * -wide, axis=-1)
 
 
 def target_square_of(target):
@@ -81,6 +83,18 @@
 
 def rows_of(ref):
     return lambda index: ref.at[index]
+
+
+def row_of(ref):
+    return lambda index: ref.at[pl.ds(index, 1)]
+
+
+def norm_rows(left, own, right):
+    return (left.shape[0], own.shape[0], row_of(left), row_of(own), row_of(right))
+
+
+def own_norms_only(own):
+    return (REACH, own.shape[0], None, row_of(own), None)
 
 
 def whole_rows(left, own, right):
@@ -135,10 +149,10 @@
         parts = (
             lane_rows(lpw, op, rpw, 0, dims),
             lane_rows(lpw, ow, rpw, dims, weight_buf.shape[-1]),
-            whole_rows(ln, on, rn),
+            norm_rows(ln, on, rn),
         )
     else:
-        parts = tuple(own_rows_only(ref) for ref in refs[:3])
+        parts = (own_rows_only(refs[0]), own_rows_only(refs[1]), own_norms_only(refs[2]))
     buffers = (
         lambda slot, position: point_buf.at[slot, position],
         lambda slot, position: weight_buf.at[slot, position],
@@ -193,9 +207,9 @@
     count, rank = source_buf.shape[1], source_buf.shape[2]
     if halo:
         ls, os, rs, ln, on, rn = refs[:6]
-        parts = (whole_rows(ls, os, rs), whole_rows(ln, on, rn))
+        parts = (whole_rows(ls, os, rs), norm_rows(ln, on, rn))
     else:
-        parts = tuple(own_rows_only(ref) for ref in refs[:2])
+        parts = (own_rows_only(refs[0]), own_norms_only(refs[1]))
     buffers = (
         lambda slot, position: source_buf.at[slot, position],
         lambda slot, position: norm_buf.at[slot, :, pl.ds(position * rank, rank)],

time: 143 us -> 143 us (level)
    mul x6 -> x0, other arithmetic: 2.39 us -> none  [scaled_norms(): jnp.sum(wide * wide, axis=-1) * (-2.0 / cells.shape[-1])]
    reduce_sum x5, other arithmetic: 5.97 us -> 8.35 us  [scaled_norms(): return jnp.sum(wide * -wide, axis=-1)]
  transfers between devices with their start and end apart: 8 -> 8, of which waited for: 1 -> 1; matrix products, arithmetic and copies ran while one was open for 17% -> 16% of each run, Pallas kernels for 39% -> 39%
where the time goes in v10:
time: 143 us; the launch traced here: 141 us
  Pallas kernels  63.7 us (45%)
  other arithmetic  16 us (11%)
  starting transfers between devices  15.9 us (11%)
  between operations  15.1 us (11%)
  waiting for transfers between devices  12.3 us (9%)
  matrix products  9.2 us (6%)
  local copies, waits for them, and re-layouts  8.7 us (6%)
    pallas_call x2, Pallas kernels, near_field(): pl.pallas_call(lambda *refs: near_kernel(leaf_of, halo, *refs), grid_spec...  30.5 us
    pallas_call x2, Pallas kernels, far_field(): pl.pallas_call(lambda *refs: far_kernel(leaf_of, halo, *refs), grid_spec=...  23.8 us
    ppermute x2, waiting for transfers between devices, halos(): left = lax.ppermute(tail, FLAT, [(i, i + 1) for i in range(ends)])  12.3 us
    pallas_call x1, Pallas kernels, final_field(): pl.pallas_call(final_kernel, grid_spec=pltpu.PrefetchScalarGridSpec(num_s...  9.36 us
    reduce_sum x5, other arithmetic, scaled_norms(): return jnp.sum(wide * -wide, axis=-1)  8.35 us
    ppermute x2, starting transfers between devices, halos(): right = lax.ppermute(head, FLAT, [(i + 1, i) for i in range(ends)])  7.41 us
    ppermute x3, starting transfers between devices, body(): lax.ppermute(group_pack, 'row', [(r, (r + shift) % rows) for r in range(r...  4.66 us
    unnamed x40, local copies, waits for them, and re-layouts  4.61 us
  transfers between devices with their start and end apart: 8, of which 1 were waited for; matrix products, arithmetic and copies ran while one was open for 16% of the time, Pallas kernels for 39%

profile of v10, /device:TPU:2, one launch (start us, length us, event | category | flops | bytes accessed | tf_op | source)
XLA Modules:
  0.0 140.9 jit_solution(2458665603899820773)
XLA Ops:
  6.5 0.9 copy.28
  7.4 0.7 fusion.59
  9.5 3.2 %fusion.2 = (f32[24,128]{1,0:T(8,128)}, bf16[24,128,128]{2,1,0:T(8,128)(2,1)S(1)}) fusion(bf16[24,256,128]{2,1,0:T(8,128)(2,1)} %bitcast.99, s32[24,128]{1,0:T(8,128)} %param.19), kind=kOutput, calls=%fused_computation.14 | convolution fusion | flops 204469248 | bytes 2383872 | tf_op jit(solution)/shard_map/bkp,bpc->bkc/dot_general | solution.py:314
  12.7 0.6 multiply_reduce_fusion.2
  13.3 0.3 copy-done.2
  13.6 1.0 multiply_convert_fusion
  14.6 0.2 copy-done.6
  14.8 0.6 fusion.23
  15.4 0.7 pad_maximum_fusion.5
  16.1 1.8 %fusion.71 = (bf16[2048,256]{1,0:T(8,128)(2,1)S(1)}, bf16[2048,256]{1,0:T(8,128)(2,1)S(1)}) fusion(bf16[6144,256]{1,0:T(8,128)(2,1)} %param.16), kind=kLoop, calls=%fused_computation.115 | loop fusion | bytes 4194304 | tf_op jit(solution)/shard_map/slice | solution.py:16
  17.9 0.2 copy-done
  18.2 1.4 pad_maximum_fusion.1
  19.6 1.9 %collective-permute-start.3 = (bf16[2048,384]{1,0:T(8,128)(2,1)}, bf16[2048,384]{1,0:T(8,128)(2,1)}, u32[]{:S(2)}, u32[]{:S(2)}) collective-permute-start(bf16[2048,384]{1,0:T(8,128)(2,1)} %pad_maximum_fusion.1), channel_id=1, source_target_pairs={{0,1},{1,2},{2,3},{3,4},{4,5},{5,6},{6,7},{7,8},{8,9},{9,10},{10,1... | collective-permute-start | bytes 4718600 | tf_op jit(solution)/shard_map/ppermute | solution.py:18
  21.5 1.4 pad_maximum_fusion.2
  22.9 3.8 %collective-permute-start.4 = (bf16[2048,384]{1,0:T(8,128)(2,1)}, bf16[2048,384]{1,0:T(8,128)(2,1)}, u32[]{:S(2)}, u32[]{:S(2)}) collective-permute-start(bf16[2048,384]{1,0:T(8,128)(2,1)} %pad_maximum_fusion.2), channel_id=1, source_target_pairs={{1,0},{2,1},{3,2},{4,3},{5,4},{6,5},{7,6},{8,7},{9,8},{10,9},{11,1... | collective-permute-start | bytes 4718600 | tf_op jit(solution)/shard_map/ppermute | solution.py:19
  26.7 1.4 fusion.28
  28.1 1.9 %collective-permute-start.5 = (bf16[1024,384]{1,0:T(8,128)(2,1)}, bf16[1024,384]{1,0:T(8,128)(2,1)}, u32[]{:S(2)}, u32[]{:S(2)}) collective-permute-start(bf16[1024,384]{1,0:T(8,128)(2,1)} %bitcast.20), channel_id=1, source_target_pairs={{0,1},{1,2},{2,3},{3,4},{4,5},{5,6},{6,7},{7,8},{8,9},{9,10},{10,1... | collective-permute-start | bytes 2359304 | tf_op jit(solution)/shard_map/ppermute | solution.py:18
  30.0 3.6 %collective-permute-start.6 = (bf16[1024,384]{1,0:T(8,128)(2,1)}, bf16[1024,384]{1,0:T(8,128)(2,1)}, u32[]{:S(2)}, u32[]{:S(2)}) collective-permute-start(bf16[1024,384]{1,0:T(8,128)(2,1)} %bitcast.21), channel_id=1, source_target_pairs={{1,0},{2,1},{3,2},{4,3},{5,4},{6,5},{7,6},{8,7},{9,8},{10,9},{11,1... | collective-permute-start | bytes 2359304 | tf_op jit(solution)/shard_map/ppermute | solution.py:19
  33.9 0.6 reshape.158.refs_0_
  34.6 0.6 reshape.159.refs_0_
  35.2 0.9 fusion
  36.1 0.6 reduce_sum.98.refs_4_.refs_7_
  36.7 11.3 %shard_map.145.refs_10_ = f32[24,256,256]{2,1,0:T(8,128)} custom-call(s32[120]{0:T(128)} %reshape.159.refs_0_, bf16[24,256,128]{2,1,0:T(8,128)(2,1)} %bitcast.100, bf16[24,256,128]{2,1,0:T(8,128)(2,1)} %bitcast.101, bf16[24,256,256]{2,1,0:T(8,128)(2,1)} %bitcast.104, f32[24,256]{1,0:T(8,128)} %reduce_sum.98.refs_4_.refs_7_), custom_call_target="tpu_custom_call" | custom-call | tf_op jit(solution)/shard_map/pallas_call | solution.py:183
  48.1 1.8 %pad_maximum_fusion.refs_2_.refs_3_ = bf16[24,128,384]{2,1,0:T(8,128)(2,1)} fusion(bf16[24,128,128]{2,1,0:T(8,128)(2,1)S(1)} %copy-done.4, bf16[24,128,256]{2,1,0:T(8,128)(2,1)S(1)} %multiply_convert_fusion), kind=kLoop, calls=%fused_computation.6 | loop fusion | flops 4718592 | bytes 4718592 | tf_op jit(solution)/shard_map/concatenate | solution.py:361
  49.8 9.0 %shard_map.147.refs_8_ = f32[24,128,256]{2,1,0:T(8,128)} custom-call(s32[96]{0:T(128)} %reshape.158.refs_0_, bf16[24,128,128]{2,1,0:T(8,128)(2,1)} %copy-done.2, bf16[24,128,384]{2,1,0:T(8,128)(2,1)} %pad_maximum_fusion.refs_2_.refs_3_, f32[24,128]{1,0:T(8,128)} %get-tuple-element.25.refs_3_.refs_6_), custom_call_target="tpu_custom_call" | custom-call | tf_op jit(solution)/shard_map/pallas_call | solution.py:239
  58.9 12.3 %collective-permute-done.3 = bf16[2048,384]{1,0:T(8,128)(2,1)} collective-permute-done((bf16[2048,384]{1,0:T(8,128)(2,1)}, bf16[2048,384]{1,0:T(8,128)(2,1)}, u32[]{:S(2)}, u32[]{:S(2)}) %collective-permute-start.3) | collective-permute-done | bytes 1572896 | tf_op jit(solution)/shard_map/ppermute | solution.py:18
  71.1 2.0 %fusion.25.refs_6_ = f32[8,256]{1,0:T(8,128)} fusion(bf16[8,256,384]{2,1,0:T(8,128)(2,1)} %bitcast.18.refs_2_), kind=kLoop, calls=%fused_computation.50 | loop fusion | flops 1308672 | bytes 532480 | tf_op jit(solution)/shard_map/reduce_sum | solution.py:45
  73.1 2.0 %fusion.26.refs_8_ = f32[8,256]{1,0:T(8,128)} fusion(bf16[8,256,384]{2,1,0:T(8,128)(2,1)} %bitcast.19.refs_4_), kind=kLoop, calls=%fused_computation.51 | loop fusion | flops 1308672 | bytes 532480 | tf_op jit(solution)/shard_map/reduce_sum | solution.py:45
  75.1 1.5 %copy.43 = bf16[64,8,8,128]{3,2,1,0:T(8,128)(2,1)S(1)} copy(bf16[64,8,8,128]{3,1,2,0:T(8,128)(2,1)} %bitcast.116) | data formatting | bytes 2097152
  76.7 0.3 copy.42
  77.0 0.2 copy.40
  77.3 0.2 fusion.19
  77.5 0.4 multiply_reduce_fusion.3
  78.0 3.0 %collective-permute-start.1 = (bf16[128,384]{1,0:T(8,128)(2,1)S(1)}, bf16[128,384]{1,0:T(8,128)(2,1)S(1)}, u32[]{:S(2)}, u32[]{:S(2)}) collective-permute-start(bf16[128,384]{1,0:T(8,128)(2,1)S(1)} %get-tuple-element.20.refs_9_), channel_id=1, source_target_pairs={{0,16},{8,24},{16,0},{24,8},{1,17},{9,25},{17,1},{25,9},{2,18},{10... | collective-permute-start | bytes 294920 | tf_op jit(solution)/shard_map/ppermute | solution.py:438
  81.0 1.6 %collective-permute-start = (bf16[128,384]{1,0:T(8,128)(2,1)S(1)}, bf16[128,384]{1,0:T(8,128)(2,1)S(1)}, u32[]{:S(2)}, u32[]{:S(2)}) collective-permute-start(bf16[128,384]{1,0:T(8,128)(2,1)S(1)} %get-tuple-element.20.refs_9_), channel_id=1, source_target_pairs={{0,8},{8,16},{16,24},{24,0},{1,9},{9,17},{17,25},{25,1},{2,10},{10... | collective-permute-start | bytes 294920 | tf_op jit(solution)/shard_map/ppermute | solution.py:438
  82.6 0.3 copy.51
  82.9 0.2 copy.44
  83.1 19.2 %shard_map.146.near_ref = f32[24,256,256]{2,1,0:T(8,128)} custom-call(s32[120]{0:T(128)} %reshape.159.refs_0_, bf16[24,256,128]{2,1,0:T(8,128)(2,1)} %bitcast.102, bf16[8,256,384]{2,1,0:T(8,128)(2,1)} %bitcast.18.refs_2_, bf16[24,256,128]{2,1,0:T(8,128)(2,1)} %bitcast.103, bf16[8,256,384]{2,1,0:T(8,128)(2,1)} %bitcast.19.refs_4_, ...), custom_call_target="tpu_custom_call", output_to_operand_aliasing={{}: (10, {})} | custom-call | tf_op jit(solution)/shard_map/pallas_call | solution.py:183
  102.2 0.3 fusion.10
  102.7 0.4 convolution_convert_fusion.1
  103.1 1.8 %fusion.30.refs_5_ = f32[8,128]{1,0:T(8,128)} fusion(bf16[8,128,384]{2,1,0:T(8,128)(2,1)} %bitcast.22.refs_2_), kind=kLoop, calls=%fused_computation.57 | loop fusion | flops 654336 | bytes 266240 | tf_op jit(solution)/shard_map/reduce_sum | solution.py:45
  104.8 1.7 %fusion.31.refs_7_ = f32[8,128]{1,0:T(8,128)} fusion(bf16[8,128,384]{2,1,0:T(8,128)(2,1)} %bitcast.23.refs_4_), kind=kLoop, calls=%fused_computation.58 | loop fusion | flops 654336 | bytes 266240 | tf_op jit(solution)/shard_map/reduce_sum | solution.py:45
  106.6 14.8 %shard_map.148.far_ref = f32[24,128,256]{2,1,0:T(8,128)} custom-call(s32[96]{0:T(128)} %reshape.158.refs_0_, bf16[24,128,128]{2,1,0:T(8,128)(2,1)} %copy-done.2, bf16[8,128,384]{2,1,0:T(8,128)(2,1)} %bitcast.22.refs_2_, bf16[24,128,384]{2,1,0:T(8,128)(2,1)} %pad_maximum_fusion.refs_2_.refs_3_, ...), custom_call_target="tpu_custom_call", output_to_operand_aliasing={{}: (8, {})} | custom-call | tf_op jit(solution)/shard_map/pallas_call | solution.py:239
  121.4 0.4 convolution_bitcast_fusion
  122.3 1.0 convolution_convert_fusion
  123.5 0.2 fusion.20
  123.7 1.0 fusion.18.down_ref
  124.7 9.4 %shard_map.149 = bf16[24,256,256]{2,1,0:T(8,128)(2,1)} custom-call(s32[24]{0:T(128)} %rank_ref.1, bf16[24,128,128]{2,1,0:T(8,128)(2,1)} %bitcast.114, bf16[128,256]{1,0:T(8,128)(2,1)} %fusion.18.down_ref, f32[24,128,256]{2,1,0:T(8,128)} %shard_map.148.far_ref, bf16[24,256,128]{2,1,0:T(8,128)(2,1)} %bitcast.109, f32[24,256,256]{2,1,0:T(8,128)} %shard_map.146.near_ref), custom_call_target="tpu_custom_call" | custom-call | tf_op jit(solution)/shard_map/pallas_call | solution.py:282
  (55 shorter events, 1.4 us)
Async XLA Ops:
  6.5 68.6 %all-gather.3.cloned.1.call-start = ((), (), s32[]{:S(2)}) async-start(), calls=%async_computation | async-start | bytes 1179648 | tf_op jit(solution)/shard_map/all_gather | solution.py:383
  6.5 6.2 %copy-start.11 = (s32[1,128]{1,0:T(1,128)S(1)}, s32[1,128]{1,0:T(1,128)}, u32[]{:S(2)}) copy-start(s32[1,128]{1,0:T(1,128)} %param.24) | copy-start | bytes 1540
  9.5 4.2 %copy-start.1 = (bf16[6144,256]{1,0:T(8,128)(2,1)S(1)}, bf16[6144,256]{1,0:T(8,128)(2,1)}, u32[]{:S(2)}) copy-start(bf16[6144,256]{1,0:T(8,128)(2,1)} %param.16) | copy-start | bytes 9437188
  9.5 4.1 %copy-start.5 = (bf16[6144,128]{1,0:T(8,128)(2,1)S(1)}, bf16[6144,128]{1,0:T(8,128)(2,1)}, u32[]{:S(2)}) copy-start(bf16[6144,128]{1,0:T(8,128)(2,1)} %param.17) | copy-start | bytes 4718596
  12.7 0.9 copy-start.2
  13.6 1.1 copy-start.6
  16.1 2.0 %copy-start = (bf16[6144,128]{1,0:T(8,128)(2,1)S(1)}, bf16[6144,128]{1,0:T(8,128)(2,1)}, u32[]{:S(2)}) copy-start(bf16[6144,128]{1,0:T(8,128)(2,1)} %param.15) | copy-start | bytes 4718596
  19.6 51.5 %collective-permute-start.3 = (bf16[2048,384]{1,0:T(8,128)(2,1)}, bf16[2048,384]{1,0:T(8,128)(2,1)}, u32[]{:S(2)}, u32[]{:S(2)}) collective-permute-start(bf16[2048,384]{1,0:T(8,128)(2,1)} %pad_maximum_fusion.1), channel_id=1, source_target_pairs={{0,1},{1,2},{2,3},{3,4},{4,5},{5,6},{6,7},{7,8},{8,9},{9,10},{10,1... | collective-permute-start | bytes 4718600 | tf_op jit(solution)/shard_map/ppermute | solution.py:18
  21.5 5.1 %copy-start.3 = (bf16[24,128,128]{2,1,0:T(8,128)(2,1)S(1)}, bf16[24,128,128]{2,1,0:T(8,128)(2,1)}, u32[]{:S(2)}) copy-start(bf16[24,128,128]{2,1,0:T(8,128)(2,1)} %copy-done.2) | copy-start | bytes 2359300
  22.9 10.9 %copy-start.10 = (s32[24,4]{0,1:T(4,128)S(1)}, s32[24,4]{0,1:T(4,128)}, u32[]{:S(2)}) copy-start(s32[24,4]{0,1:T(4,128)} %param.21) | copy-start | bytes 1156
  22.9 11.6 %copy-start.9 = (s32[24,5]{0,1:T(8,128)S(1)}, s32[24,5]{0,1:T(8,128)}, u32[]{:S(2)}) copy-start(s32[24,5]{0,1:T(8,128)} %param.20) | copy-start | bytes 1444
  22.9 50.2 %collective-permute-start.4 = (bf16[2048,384]{1,0:T(8,128)(2,1)}, bf16[2048,384]{1,0:T(8,128)(2,1)}, u32[]{:S(2)}, u32[]{:S(2)}) collective-permute-start(bf16[2048,384]{1,0:T(8,128)(2,1)} %pad_maximum_fusion.2), channel_id=1, source_target_pairs={{1,0},{2,1},{3,2},{4,3},{5,4},{6,5},{7,6},{8,7},{9,8},{10,9},{11,1... | collective-permute-start | bytes 4718600 | tf_op jit(solution)/shard_map/ppermute | solution.py:19
  28.1 75.0 %collective-permute-start.5 = (bf16[1024,384]{1,0:T(8,128)(2,1)}, bf16[1024,384]{1,0:T(8,128)(2,1)}, u32[]{:S(2)}, u32[]{:S(2)}) collective-permute-start(bf16[1024,384]{1,0:T(8,128)(2,1)} %bitcast.20), channel_id=1, source_target_pairs={{0,1},{1,2},{2,3},{3,4},{4,5},{5,6},{6,7},{7,8},{8,9},{9,10},{10,1... | collective-permute-start | bytes 2359304 | tf_op jit(solution)/shard_map/ppermute | solution.py:18
  30.0 73.1 %collective-permute-start.6 = (bf16[1024,384]{1,0:T(8,128)(2,1)}, bf16[1024,384]{1,0:T(8,128)(2,1)}, u32[]{:S(2)}, u32[]{:S(2)}) collective-permute-start(bf16[1024,384]{1,0:T(8,128)(2,1)} %bitcast.21), channel_id=1, source_target_pairs={{1,0},{2,1},{3,2},{4,3},{5,4},{6,5},{7,6},{8,7},{9,8},{10,9},{11,1... | collective-permute-start | bytes 2359304 | tf_op jit(solution)/shard_map/ppermute | solution.py:19
  36.7 11.3 %copy-start.4 = (bf16[24,128,128]{2,1,0:T(8,128)(2,1)S(1)}, bf16[24,128,128]{2,1,0:T(8,128)(2,1)}, u32[]{:S(2)}) copy-start(bf16[24,128,128]{2,1,0:T(8,128)(2,1)} %copy-done.2) | copy-start | bytes 2359300
  49.8 9.0 %copy-start.12 = (s32[1,4]{1,0:T(1,128)S(1)}, s32[1,4]{1,0:T(1,128)}, u32[]{:S(2)}) copy-start(s32[1,4]{1,0:T(1,128)} %param.25) | copy-start | bytes 52
  49.8 9.0 %copy-start.13 = (s32[1,2]{1,0:T(1,128)S(1)}, s32[1,2]{1,0:T(1,128)}, u32[]{:S(2)}) copy-start(s32[1,2]{1,0:T(1,128)} %param.29) | copy-start | bytes 28
  76.6 0.9 copy-start.14
  77.9 5.1 %copy-start.7 = (bf16[128,384]{1,0:T(8,128)(2,1)}, bf16[128,384]{1,0:T(8,128)(2,1)S(1)}, u32[]{:S(2)}) copy-start(bf16[128,384]{1,0:T(8,128)(2,1)S(1)} %get-tuple-element.20.refs_9_) | copy-start | bytes 294916
  77.9 43.9 %collective-permute-start.2 = (bf16[128,384]{1,0:T(8,128)(2,1)S(1)}, bf16[128,384]{1,0:T(8,128)(2,1)S(1)}, u32[]{:S(2)}, u32[]{:S(2)}) collective-permute-start(bf16[128,384]{1,0:T(8,128)(2,1)S(1)} %get-tuple-element.20.refs_9_), channel_id=1, source_target_pairs={{0,24},{8,0},{16,8},{24,16},{1,25},{9,1},{17,9},{25,17},{2,26},{10... | collective-permute-start | bytes 294920 | tf_op jit(solution)/shard_map/ppermute | solution.py:438
  78.0 44.0 %collective-permute-start.1 = (bf16[128,384]{1,0:T(8,128)(2,1)S(1)}, bf16[128,384]{1,0:T(8,128)(2,1)S(1)}, u32[]{:S(2)}, u32[]{:S(2)}) collective-permute-start(bf16[128,384]{1,0:T(8,128)(2,1)S(1)} %get-tuple-element.20.refs_9_), channel_id=1, source_target_pairs={{0,16},{8,24},{16,0},{24,8},{1,17},{9,25},{17,1},{25,9},{2,18},{10... | collective-permute-start | bytes 294920 | tf_op jit(solution)/shard_map/ppermute | solution.py:438
  81.0 41.1 %collective-permute-start = (bf16[128,384]{1,0:T(8,128)(2,1)S(1)}, bf16[128,384]{1,0:T(8,128)(2,1)S(1)}, u32[]{:S(2)}, u32[]{:S(2)}) collective-permute-start(bf16[128,384]{1,0:T(8,128)(2,1)S(1)} %get-tuple-element.20.refs_9_), channel_id=1, source_target_pairs={{0,8},{8,16},{16,24},{24,0},{1,9},{9,17},{17,25},{25,1},{2,10},{10... | collective-permute-start | bytes 294920 | tf_op jit(solution)/shard_map/ppermute | solution.py:438
  122.3 1.4 copy-start.8
Sparse Core Ops, SparseCore 0:
  16.2 49.8 all-gather.2

commit v11 on v10

--- a/solution.py
+++ b/solution.py
@@ -18,6 +18,21 @@
     left = lax.ppermute(tail, FLAT, [(i, i + 1) for i in range(ends)])
     right = lax.ppermute(head, FLAT, [(i + 1, i) for i in range(ends)])
     return left, right
+
+
+def doubling_gather(block, axis):
+    count = lax.axis_size(axis)
+    assert count & (count - 1) == 0
+    me = lax.axis_index(axis)
+    distance = 1
+    while distance < count:
+        other = lax.ppermute(block, axis, [(i, i ^ distance) for i in range(count)])
+        upper = (me & distance) != 0
+        block = jnp.where(
+            upper, jnp.concatenate([other, block], axis=0), jnp.concatenate([block, other], axis=0)
+        )
+        distance *= 2
+    return block
 
 
 def kernel_block(left, right):
@@ -380,7 +395,7 @@
     columns = lax.axis_size("col")
     source_columns = node_far[0] % columns
     node_pack = jnp.concatenate([node_coords, node_up, group_basis], axis=1)
-    gathered = lax.all_gather(node_pack[None], "col", axis=0, tiled=True)
+    gathered = doubling_gather(node_pack[None], "col")
 
     near_local = near_list - offset
     local_norms = scaled_norms(local_points)

time: 143 us -> 143 us (level)
  the two profiles are of different devices: /device:TPU:2 before, /device:TPU:9 now
where the time goes in v11:
time: 143 us; the launch traced here: 141 us
  Pallas kernels  63.6 us (44%)
  starting transfers between devices  22.9 us (16%)
  waiting for transfers between devices  19.2 us (13%)
  other arithmetic  13.2 us (9%)
  matrix products  12.4 us (9%)
  local copies, waits for them, and re-layouts  8.06 us (6%)
  between operations  1.88 us (1%)
    pallas_call x2, Pallas kernels, near_field(): pl.pallas_call(lambda *refs: near_kernel(leaf_of, halo, *refs), grid_spec...  30.5 us
    pallas_call x2, Pallas kernels, far_field(): pl.pallas_call(lambda *refs: far_kernel(leaf_of, halo, *refs), grid_spec=...  23.8 us
    ppermute x3, waiting for transfers between devices, doubling_gather(): other = lax.ppermute(block, axis, [(i, i ^ distance) for i in range(count)])  19.2 us
    ppermute x2, starting transfers between devices, halos(): left = lax.ppermute(tail, FLAT, [(i, i + 1) for i in range(ends)])  14.2 us
    pallas_call x1, Pallas kernels, final_field(): pl.pallas_call(final_kernel, grid_spec=pltpu.PrefetchScalarGridSpec(num_s...  9.36 us
    reduce_sum x4, other arithmetic, scaled_norms(): return jnp.sum(wide * -wide, axis=-1)  5.93 us
    unnamed x57, local copies, waits for them, and re-layouts  5.2 us
    ppermute x2, starting transfers between devices, halos(): right = lax.ppermute(head, FLAT, [(i + 1, i) for i in range(ends)])  4.01 us
  transfers between devices with their start and end apart: 10, of which 2 were waited for; matrix products, arithmetic and copies ran while one was open for 17% of the time, Pallas kernels for 28%

profile of v11, /device:TPU:9, one launch (start us, length us, event | category | flops | bytes accessed | tf_op | source)
XLA Modules:
  0.0 141.2 jit_solution(5425959909319046075)
XLA Ops:
  0.0 0.9 copy.27
  0.9 0.7 fusion.59
  2.3 3.2 %fusion.2 = (f32[24,128]{1,0:T(8,128)}, bf16[24,128,128]{2,1,0:T(8,128)(2,1)S(1)}) fusion(bf16[24,256,128]{2,1,0:T(8,128)(2,1)} %bitcast.96, s32[24,128]{1,0:T(8,128)} %param.19), kind=kOutput, calls=%fused_computation.14 | convolution fusion | flops 204469248 | bytes 2383872 | tf_op jit(solution)/shard_map/bkp,bpc->bkc/dot_general | solution.py:329
  5.5 1.1 multiply_reduce_fusion.2
  6.6 1.0 multiply_convert_fusion
  7.7 0.6 fusion.23
  8.4 0.7 collective-permute-start
  9.3 0.5 copy-done
  9.9 1.4 pad_maximum_fusion.1
  11.2 3.7 %collective-permute-start.6 = (bf16[2048,384]{1,0:T(8,128)(2,1)}, bf16[2048,384]{1,0:T(8,128)(2,1)}, u32[]{:S(2)}, u32[]{:S(2)}) collective-permute-start(bf16[2048,384]{1,0:T(8,128)(2,1)} %pad_maximum_fusion.1), channel_id=1, source_target_pairs={{0,1},{1,2},{2,3},{3,4},{4,5},{5,6},{6,7},{7,8},{8,9},{9,10},{10,1... | collective-permute-start | bytes 4718600 | tf_op jit(solution)/shard_map/ppermute | solution.py:18
  14.9 1.3 pad_maximum_fusion.2
  16.3 1.9 %collective-permute-start.7 = (bf16[2048,384]{1,0:T(8,128)(2,1)}, bf16[2048,384]{1,0:T(8,128)(2,1)}, u32[]{:S(2)}, u32[]{:S(2)}) collective-permute-start(bf16[2048,384]{1,0:T(8,128)(2,1)} %pad_maximum_fusion.2), channel_id=1, source_target_pairs={{1,0},{2,1},{3,2},{4,3},{5,4},{6,5},{7,6},{8,7},{9,8},{10,9},{11,1... | collective-permute-start | bytes 4718600 | tf_op jit(solution)/shard_map/ppermute | solution.py:19
  19.1 0.6 reshape.158.refs_0_
  19.8 0.7 reshape.159.refs_0_
  20.5 0.9 fusion
  21.4 0.6 reduce_sum.98.refs_4_.refs_7_
  22.0 11.3 %shard_map.145.refs_10_ = f32[24,256,256]{2,1,0:T(8,128)} custom-call(s32[120]{0:T(128)} %reshape.159.refs_0_, bf16[24,256,128]{2,1,0:T(8,128)(2,1)} %bitcast.97, bf16[24,256,128]{2,1,0:T(8,128)(2,1)} %bitcast.98, bf16[24,256,256]{2,1,0:T(8,128)(2,1)} %bitcast.101, f32[24,256]{1,0:T(8,128)} %reduce_sum.98.refs_4_.refs_7_), custom_call_target="tpu_custom_call" | custom-call | tf_op jit(solution)/shard_map/pallas_call | solution.py:198
  33.4 1.3 collective-permute-start.1
  34.6 1.8 %pad_maximum_fusion.refs_2_.refs_3_ = bf16[24,128,384]{2,1,0:T(8,128)(2,1)} fusion(bf16[24,128,128]{2,1,0:T(8,128)(2,1)S(1)} %copy-done.3, bf16[24,128,256]{2,1,0:T(8,128)(2,1)S(1)} %multiply_convert_fusion), kind=kLoop, calls=%fused_computation.6 | loop fusion | flops 4718592 | bytes 4718592 | tf_op jit(solution)/shard_map/concatenate | solution.py:376
  36.4 8.9 %shard_map.147.refs_8_ = f32[24,128,256]{2,1,0:T(8,128)} custom-call(s32[96]{0:T(128)} %reshape.158.refs_0_, bf16[24,128,128]{2,1,0:T(8,128)(2,1)} %copy-done.2, bf16[24,128,384]{2,1,0:T(8,128)(2,1)} %pad_maximum_fusion.refs_2_.refs_3_, f32[24,128]{1,0:T(8,128)} %get-tuple-element.23.refs_3_.refs_6_), custom_call_target="tpu_custom_call" | custom-call | tf_op jit(solution)/shard_map/pallas_call | solution.py:254
  45.4 1.4 %fusion.28 = (bf16[8,128,384]{2,1,0:T(8,128)(2,1)}, bf16[8,128,384]{2,1,0:T(8,128)(2,1)}) fusion(bf16[24,128,256]{2,1,0:T(8,128)(2,1)S(1)} %multiply_convert_fusion, bf16[24,128,128]{2,1,0:T(8,128)(2,1)S(1)} %copy-done.4), kind=kLoop, calls=%fused_computation.54 | loop fusion | flops 3145728 | bytes 3932160 | tf_op jit(solution)/shard_map/concatenate | solution.py:376
  46.8 8.1 %collective-permute-done.1 = bf16[2,128,512]{1,2,0:T(8,128)(2,1)S(1)} collective-permute-done((bf16[2,128,512]{1,2,0:T(8,128)(2,1)S(1)}, bf16[2,128,512]{1,2,0:T(8,128)(2,1)S(1)}, u32[]{:S(2)}, u32[]{:S(2)}) %collective-permute-start.1) | collective-permute-done | bytes 262176 | tf_op jit(solution)/shard_map/ppermute | solution.py:29
  55.2 11.1 %collective-permute-done.2 = bf16[4,128,512]{1,2,0:T(8,128)(2,1)S(1)} collective-permute-done((bf16[4,128,512]{1,2,0:T(8,128)(2,1)S(1)}, bf16[4,128,512]{1,2,0:T(8,128)(2,1)S(1)}, u32[]{:S(2)}, u32[]{:S(2)}) %collective-permute-start.2) | collective-permute-done | bytes 524320 | tf_op jit(solution)/shard_map/ppermute | solution.py:29
  66.2 0.2 maximum_select_fusion
  66.4 0.2 copy.28
  66.6 0.3 fusion.19
  67.0 0.9 multiply_reduce_fusion.3
  68.0 0.2 collective-permute-start.5
  68.3 2.3 %collective-permute-start.4 = (bf16[128,384]{1,0:T(8,128)(2,1)S(1)}, bf16[128,384]{1,0:T(8,128)(2,1)}, u32[]{:S(2)}, u32[]{:S(2)}) collective-permute-start(bf16[128,384]{1,0:T(8,128)(2,1)S(1)} %get-tuple-element.18.refs_9_), channel_id=1, source_target_pairs={{0,16},{8,24},{16,0},{24,8},{1,17},{9,25},{17,1},{25,9},{2,18},{10... | collective-permute-start | bytes 294920 | tf_op jit(solution)/shard_map/ppermute | solution.py:453
  70.6 0.2 copy.34
  70.8 0.3 copy.48
  71.1 0.8 copy.41
  72.0 0.3 fusion.10
  72.4 0.4 convolution_convert_fusion.1
  72.8 1.0 convolution_bitcast_fusion
  73.8 10.6 %collective-permute-start.8 = (bf16[1024,384]{1,0:T(8,128)(2,1)S(1)}, bf16[1024,384]{1,0:T(8,128)(2,1)S(1)}, u32[]{:S(2)}, u32[]{:S(2)}) collective-permute-start(bf16[1024,384]{1,0:T(8,128)(2,1)S(1)} %bitcast.121), channel_id=1, source_target_pairs={{0,1},{1,2},{2,3},{3,4},{4,5},{5,6},{6,7},{7,8},{8,9},{9,10},{10,1... | collective-permute-start | bytes 2359304 | tf_op jit(solution)/shard_map/ppermute | solution.py:18
  84.6 2.1 %collective-permute-start.9 = (bf16[1024,384]{1,0:T(8,128)(2,1)S(1)}, bf16[1024,384]{1,0:T(8,128)(2,1)S(1)}, u32[]{:S(2)}, u32[]{:S(2)}) collective-permute-start(bf16[1024,384]{1,0:T(8,128)(2,1)S(1)} %bitcast.120), channel_id=1, source_target_pairs={{1,0},{2,1},{3,2},{4,3},{5,4},{6,5},{7,6},{8,7},{9,8},{10,9},{11,1... | collective-permute-start | bytes 2359304 | tf_op jit(solution)/shard_map/ppermute | solution.py:19
  86.7 1.0 copy.43
  87.8 1.0 copy.42
  88.9 1.0 convolution_convert_fusion
  90.1 0.8 fusion.20
  90.9 1.8 %fusion.18.down_ref = bf16[128,256]{1,0:T(8,128)(2,1)} fusion(f32[128,256]{1,0:T(8,128)S(1)} %copy-done.13, bf16[128,128]{1,0:T(8,128)(2,1)S(1)} %copy-done.14, bf16[2,128,128]{2,1,0:T(8,128)(2,1)} %fusion.20, bf16[2,128,384]{2,1,0:T(8,128)(2,1)S(1)} %bitcast.119, f32[128]{0:T(128)S(1)} %compare_convert_fusion.1, f32[128]{0:T(128)S(1)} %compare_convert_fusion), kind=kOutput, calls=%fused_computation.42 | convolution fusion | flops 25329664 | bytes 427008 | tf_op jit(solution)/shard_map/dot_general | solution.py:468
  92.7 2.0 %fusion.25.refs_6_ = f32[8,256]{1,0:T(8,128)} fusion(bf16[8,256,384]{2,1,0:T(8,128)(2,1)} %bitcast.19.refs_2_), kind=kLoop, calls=%fused_computation.50 | loop fusion | flops 1308672 | bytes 532480 | tf_op jit(solution)/shard_map/reduce_sum | solution.py:60
  94.7 2.0 %fusion.26.refs_8_ = f32[8,256]{1,0:T(8,128)} fusion(bf16[8,256,384]{2,1,0:T(8,128)(2,1)} %bitcast.20.refs_4_), kind=kLoop, calls=%fused_computation.51 | loop fusion | flops 1308672 | bytes 532480 | tf_op jit(solution)/shard_map/reduce_sum | solution.py:60
  96.6 19.2 %shard_map.146.near_ref = f32[24,256,256]{2,1,0:T(8,128)} custom-call(s32[120]{0:T(128)} %reshape.159.refs_0_, bf16[24,256,128]{2,1,0:T(8,128)(2,1)} %bitcast.99, bf16[8,256,384]{2,1,0:T(8,128)(2,1)} %bitcast.19.refs_2_, bf16[24,256,128]{2,1,0:T(8,128)(2,1)} %bitcast.100, bf16[8,256,384]{2,1,0:T(8,128)(2,1)} %bitcast.20.refs_4_, ...), custom_call_target="tpu_custom_call", output_to_operand_aliasing={{}: (10, {})} | custom-call | tf_op jit(solution)/shard_map/pallas_call | solution.py:198
  115.9 1.1 fusion.30
  117.0 14.8 %shard_map.148.far_ref = f32[24,128,256]{2,1,0:T(8,128)} custom-call(s32[96]{0:T(128)} %reshape.158.refs_0_, bf16[24,128,128]{2,1,0:T(8,128)(2,1)} %copy-done.2, bf16[8,128,384]{2,1,0:T(8,128)(2,1)} %bitcast.112, bf16[24,128,384]{2,1,0:T(8,128)(2,1)} %pad_maximum_fusion.refs_2_.refs_3_, ...), custom_call_target="tpu_custom_call", output_to_operand_aliasing={{}: (8, {})} | custom-call | tf_op jit(solution)/shard_map/pallas_call | solution.py:254
  131.8 9.4 %shard_map.149 = bf16[24,256,256]{2,1,0:T(8,128)(2,1)} custom-call(s32[24]{0:T(128)} %rank_ref.1, bf16[24,128,128]{2,1,0:T(8,128)(2,1)} %bitcast.108, bf16[128,256]{1,0:T(8,128)(2,1)} %fusion.18.down_ref, f32[24,128,256]{2,1,0:T(8,128)} %shard_map.148.far_ref, bf16[24,256,128]{2,1,0:T(8,128)(2,1)} %bitcast.106, f32[24,256,256]{2,1,0:T(8,128)} %shard_map.146.near_ref), custom_call_target="tpu_custom_call" | custom-call | tf_op jit(solution)/shard_map/pallas_call | solution.py:297
  (80 shorter events, 1.7 us)
Async XLA Ops:
  0.0 5.5 %copy-start.19 = (s32[1,128]{1,0:T(1,128)S(1)}, s32[1,128]{1,0:T(1,128)}, u32[]{:S(2)}) copy-start(s32[1,128]{1,0:T(1,128)} %param.24) | copy-start | bytes 1540
  2.3 4.3 %copy-start.1 = (bf16[6144,256]{1,0:T(8,128)(2,1)S(1)}, bf16[6144,256]{1,0:T(8,128)(2,1)}, u32[]{:S(2)}) copy-start(bf16[6144,256]{1,0:T(8,128)(2,1)} %param.16) | copy-start | bytes 9437188
  2.3 4.3 %copy-start.5 = (bf16[6144,128]{1,0:T(8,128)(2,1)S(1)}, bf16[6144,128]{1,0:T(8,128)(2,1)}, u32[]{:S(2)}) copy-start(bf16[6144,128]{1,0:T(8,128)(2,1)} %param.17) | copy-start | bytes 4718596
  5.5 1.1 copy-start.2
  6.6 1.1 copy-start.6
  8.4 1.4 copy-start
  8.4 24.9 %collective-permute-start = (bf16[1,128,512]{1,2,0:T(8,128)(2,1)S(1)}, bf16[1,128,512]{1,2,0:T(8,128)(2,1)S(1)}, u32[]{:S(2)}, u32[]{:S(2)}) collective-permute-start(bf16[1,128,512]{1,2,0:T(8,128)(2,1)S(1)} %maximum_bitcast_fusion), channel_id=1, source_target_pairs={{0,1},{1,0},{2,3},{3,2},{4,5},{5,4},{6,7},{7,6},{8,9},{9,8},{10,11... | collective-permute-start | bytes 393224 | tf_op jit(solution)/shard_map/ppermute | solution.py:29
  11.2 81.4 %collective-permute-start.6 = (bf16[2048,384]{1,0:T(8,128)(2,1)}, bf16[2048,384]{1,0:T(8,128)(2,1)}, u32[]{:S(2)}, u32[]{:S(2)}) collective-permute-start(bf16[2048,384]{1,0:T(8,128)(2,1)} %pad_maximum_fusion.1), channel_id=1, source_target_pairs={{0,1},{1,2},{2,3},{3,4},{4,5},{5,6},{6,7},{7,8},{8,9},{9,10},{10,1... | collective-permute-start | bytes 4718600 | tf_op jit(solution)/shard_map/ppermute | solution.py:18
  14.9 4.1 %copy-start.18 = (s32[24,4]{0,1:T(4,128)S(1)}, s32[24,4]{0,1:T(4,128)}, u32[]{:S(2)}) copy-start(s32[24,4]{0,1:T(4,128)} %param.21) | copy-start | bytes 1156
  14.9 4.8 %copy-start.17 = (s32[24,5]{0,1:T(8,128)S(1)}, s32[24,5]{0,1:T(8,128)}, u32[]{:S(2)}) copy-start(s32[24,5]{0,1:T(8,128)} %param.20) | copy-start | bytes 1444
  16.3 78.4 %collective-permute-start.7 = (bf16[2048,384]{1,0:T(8,128)(2,1)}, bf16[2048,384]{1,0:T(8,128)(2,1)}, u32[]{:S(2)}, u32[]{:S(2)}) collective-permute-start(bf16[2048,384]{1,0:T(8,128)(2,1)} %pad_maximum_fusion.2), channel_id=1, source_target_pairs={{1,0},{2,1},{3,2},{4,3},{5,4},{6,5},{7,6},{8,7},{9,8},{10,9},{11,1... | collective-permute-start | bytes 4718600 | tf_op jit(solution)/shard_map/ppermute | solution.py:19
  22.0 12.6 %copy-start.3 = (bf16[24,128,128]{2,1,0:T(8,128)(2,1)S(1)}, bf16[24,128,128]{2,1,0:T(8,128)(2,1)}, u32[]{:S(2)}) copy-start(bf16[24,128,128]{2,1,0:T(8,128)(2,1)} %copy-done.2) | copy-start | bytes 2359300
  33.4 21.6 %collective-permute-start.1 = (bf16[2,128,512]{1,2,0:T(8,128)(2,1)S(1)}, bf16[2,128,512]{1,2,0:T(8,128)(2,1)S(1)}, u32[]{:S(2)}, u32[]{:S(2)}) collective-permute-start(bf16[2,128,512]{1,2,0:T(8,128)(2,1)S(1)} %maximum_select_fusion.2), channel_id=1, source_target_pairs={{0,2},{1,3},{2,0},{3,1},{4,6},{5,7},{6,4},{7,5},{8,10},{9,11},{10,... | collective-permute-start | bytes 786440 | tf_op jit(solution)/shard_map/ppermute | solution.py:29
  36.4 8.9 %copy-start.4 = (bf16[24,128,128]{2,1,0:T(8,128)(2,1)S(1)}, bf16[24,128,128]{2,1,0:T(8,128)(2,1)}, u32[]{:S(2)}) copy-start(bf16[24,128,128]{2,1,0:T(8,128)(2,1)} %copy-done.2) | copy-start | bytes 2359300
  45.4 9.7 %copy-start.20 = (s32[1,4]{1,0:T(1,128)S(1)}, s32[1,4]{1,0:T(1,128)}, u32[]{:S(2)}) copy-start(s32[1,4]{1,0:T(1,128)} %param.25) | copy-start | bytes 52
  45.4 9.8 %copy-start.21 = (s32[1,2]{1,0:T(1,128)S(1)}, s32[1,2]{1,0:T(1,128)}, u32[]{:S(2)}) copy-start(s32[1,2]{1,0:T(1,128)} %param.29) | copy-start | bytes 28
  55.0 11.2 %collective-permute-start.2 = (bf16[4,128,512]{1,2,0:T(8,128)(2,1)S(1)}, bf16[4,128,512]{1,2,0:T(8,128)(2,1)S(1)}, u32[]{:S(2)}, u32[]{:S(2)}) collective-permute-start(bf16[4,128,512]{1,2,0:T(8,128)(2,1)S(1)} %maximum_select_fusion.1), channel_id=1, source_target_pairs={{0,4},{1,5},{2,6},{3,7},{4,0},{5,1},{6,2},{7,3},{8,12},{9,13},{10,... | collective-permute-start | bytes 1572872 | tf_op jit(solution)/shard_map/ppermute | solution.py:29
  66.4 0.7 copy-start.22
  68.0 2.8 %copy-start.15 = (bf16[128,128]{1,0:T(8,128)(2,1)}, bf16[128,128]{1,0:T(8,128)(2,1)S(1)}, u32[]{:S(2)}) copy-start(bf16[128,128]{1,0:T(8,128)(2,1)S(1)} %get-tuple-element.22) | copy-start | bytes 98308
  68.0 4.7 %copy-start.11 = (bf16[128,384]{1,0:T(8,128)(2,1)}, bf16[128,384]{1,0:T(8,128)(2,1)S(1)}, u32[]{:S(2)}) copy-start(bf16[128,384]{1,0:T(8,128)(2,1)S(1)} %get-tuple-element.18.refs_9_) | copy-start | bytes 294916
  68.0 5.8 %collective-permute-start.5 = (bf16[128,384]{1,0:T(8,128)(2,1)S(1)}, bf16[128,384]{1,0:T(8,128)(2,1)S(1)}, u32[]{:S(2)}, u32[]{:S(2)}) collective-permute-start(bf16[128,384]{1,0:T(8,128)(2,1)S(1)} %get-tuple-element.18.refs_9_), channel_id=1, source_target_pairs={{0,24},{8,0},{16,8},{24,16},{1,25},{9,1},{17,9},{25,17},{2,26},{10... | collective-permute-start | bytes 294920 | tf_op jit(solution)/shard_map/ppermute | solution.py:453
  68.3 16.3 %collective-permute-start.4 = (bf16[128,384]{1,0:T(8,128)(2,1)S(1)}, bf16[128,384]{1,0:T(8,128)(2,1)}, u32[]{:S(2)}, u32[]{:S(2)}) collective-permute-start(bf16[128,384]{1,0:T(8,128)(2,1)S(1)} %get-tuple-element.18.refs_9_), channel_id=1, source_target_pairs={{0,16},{8,24},{16,0},{24,8},{1,17},{9,25},{17,1},{25,9},{2,18},{10... | collective-permute-start | bytes 294920 | tf_op jit(solution)/shard_map/ppermute | solution.py:453
  70.6 17.2 %collective-permute-start.3 = (bf16[128,384]{1,0:T(8,128)(2,1)S(1)}, bf16[128,384]{1,0:T(8,128)(2,1)}, u32[]{:S(2)}, u32[]{:S(2)}) collective-permute-start(bf16[128,384]{1,0:T(8,128)(2,1)S(1)} %get-tuple-element.18.refs_9_), channel_id=1, source_target_pairs={{0,8},{8,16},{16,24},{24,0},{1,9},{9,17},{17,25},{25,1},{2,10},{10... | collective-permute-start | bytes 294920 | tf_op jit(solution)/shard_map/ppermute | solution.py:453
  70.8 2.0 %copy-start.24 = (f32[128]{0:T(128)S(1)}, f32[128]{0:T(128)}, u32[]{:S(2)}) copy-start(f32[128]{0:T(128)} %get-tuple-element.19) | copy-start | bytes 1540
  70.8 3.0 %copy-start.10 = (bf16[8,128,384]{2,1,0:T(8,128)(2,1)S(1)}, bf16[8,128,384]{2,1,0:T(8,128)(2,1)}, u32[]{:S(2)}) copy-start(bf16[8,128,384]{2,1,0:T(8,128)(2,1)} %get-tuple-element.14) | copy-start | bytes 2359300
  71.1 13.5 %copy-start.9 = (bf16[8,128,384]{2,1,0:T(8,128)(2,1)S(1)}, bf16[8,128,384]{2,1,0:T(8,128)(2,1)}, u32[]{:S(2)}) copy-start(bf16[8,128,384]{2,1,0:T(8,128)(2,1)} %get-tuple-element.13) | copy-start | bytes 2359300
  72.2 16.6 %copy-start.12 = (bf16[1,1,128,384]{3,1,2,0:T(2,128)(2,1)S(1)}, bf16[1,1,128,384]{3,1,2,0:T(2,128)(2,1)}, u32[]{:S(2)}) copy-start(bf16[1,1,128,384]{3,1,2,0:T(2,128)(2,1)} %copy.41) | copy-start | bytes 294916
  73.8 42.0 %collective-permute-start.8 = (bf16[1024,384]{1,0:T(8,128)(2,1)S(1)}, bf16[1024,384]{1,0:T(8,128)(2,1)S(1)}, u32[]{:S(2)}, u32[]{:S(2)}) collective-permute-start(bf16[1024,384]{1,0:T(8,128)(2,1)S(1)} %bitcast.121), channel_id=1, source_target_pairs={{0,1},{1,2},{2,3},{3,4},{4,5},{5,6},{6,7},{7,8},{8,9},{9,10},{10,1... | collective-permute-start | bytes 2359304 | tf_op jit(solution)/shard_map/ppermute | solution.py:18
  84.6 31.3 %collective-permute-start.9 = (bf16[1024,384]{1,0:T(8,128)(2,1)S(1)}, bf16[1024,384]{1,0:T(8,128)(2,1)S(1)}, u32[]{:S(2)}, u32[]{:S(2)}) collective-permute-start(bf16[1024,384]{1,0:T(8,128)(2,1)S(1)} %bitcast.120), channel_id=1, source_target_pairs={{1,0},{2,1},{3,2},{4,3},{5,4},{6,5},{7,6},{8,7},{9,8},{10,9},{11,1... | collective-permute-start | bytes 2359304 | tf_op jit(solution)/shard_map/ppermute | solution.py:19
  88.8 1.2 copy-start.16
  88.8 1.2 copy-start.23
  88.8 2.0 %copy-start.13 = (f32[128,256]{1,0:T(8,128)S(1)}, f32[128,256]{1,0:T(8,128)}, u32[]{:S(2)}) copy-start(f32[128,256]{1,0:T(8,128)} %convolution_bitcast_fusion) | copy-start | bytes 393220
  88.9 2.0 %copy-start.14 = (bf16[128,128]{1,0:T(8,128)(2,1)S(1)}, bf16[128,128]{1,0:T(8,128)(2,1)}, u32[]{:S(2)}) copy-start(bf16[128,128]{1,0:T(8,128)(2,1)} %param.26) | copy-start | bytes 98308
  115.8 1.1 copy-start.7
  115.9 1.1 copy-start.8

commit v12 on v10

--- a/solution.py
+++ b/solution.py
@@ -32,8 +32,16 @@
     return lax.dot_general(a, b, (((1,), (1,)), ((), ())), preferred_element_type=jnp.float32)
 
 
-def scaled_kernel(target, target_square, source, source_square):
+def scaled_kernel(target, target_square, source, source_square=None):
     dims = target.shape[-1]
+    if source_square is None:
+        wide = source.astype(jnp.float32)
+        square = wide * wide
+        high = square.astype(jnp.bfloat16)
+        low = (square - high.astype(jnp.float32)).astype(jnp.bfloat16)
+        ones = jnp.ones((8, dims), jnp.bfloat16)
+        summed = contract_last(ones, high) + contract_last(ones, low)
+        source_square = summed[0:1] * (-2.0 / dims)
     inner = contract_last(target * jnp.asarray(4.0 / dims, target.dtype), source)
     return jnp.exp((target_square + source_square) + inner).astype(jnp.bfloat16)
 
@@ -89,10 +97,6 @@
     return lambda index: ref.at[pl.ds(index, 1)]
 
 
-def norm_rows(left, own, right):
-    return (left.shape[0], own.shape[0], row_of(left), row_of(own), row_of(right))
-
-
 def own_norms_only(own):
     return (REACH, own.shape[0], None, row_of(own), None)
 
@@ -140,29 +144,28 @@
 
 
 def near_kernel(leaf_of, halo, index_ref, target_ref, *refs):
-    inputs = 9 if halo else 3
+    inputs = 6 if halo else 3
     out_ref = refs[inputs]
     point_buf, weight_buf, norm_buf, sems = refs[inputs + 1 :]
     count, size, dims = point_buf.shape[1], point_buf.shape[2], point_buf.shape[3]
+    buffers = [
+        lambda slot, position: point_buf.at[slot, position],
+        lambda slot, position: weight_buf.at[slot, position],
+    ]
     if halo:
-        lpw, op, rpw, ow, ln, on, rn = refs[:7]
+        lpw, op, rpw, ow = refs[:4]
         parts = (
             lane_rows(lpw, op, rpw, 0, dims),
             lane_rows(lpw, ow, rpw, dims, weight_buf.shape[-1]),
-            norm_rows(ln, on, rn),
         )
     else:
         parts = (own_rows_only(refs[0]), own_rows_only(refs[1]), own_norms_only(refs[2]))
-    buffers = (
-        lambda slot, position: point_buf.at[slot, position],
-        lambda slot, position: weight_buf.at[slot, position],
-        lambda slot, position: norm_buf.at[slot, :, pl.ds(position * size, size)],
-    )
+        buffers.append(lambda slot, position: norm_buf.at[slot, :, pl.ds(position * size, size)])
     slot = pipelined_sources(index_ref, count, parts, buffers, sems, leaf_of)
     target = target_ref[0]
     sources = point_buf[slot].reshape(count * size, dims)
     values = weight_buf[slot].reshape(count * size, weight_buf.shape[-1])
-    kernel = scaled_kernel(target, target_square_of(target), sources, norm_buf[slot])
+    kernel = scaled_kernel(target, target_square_of(target), sources, None if halo else norm_buf[slot])
     out_ref[0] = jnp.dot(kernel, values, preferred_element_type=jnp.float32)
 
 
@@ -174,8 +177,8 @@
     leaf_of, steps, _ = leaf_order(leaves, halo)
     anywhere = pl.BlockSpec(memory_space=pl.ANY)
     if halo:
-        left_pairs, right_pairs, left_norms, right_norms = halo_inputs
-        inputs = (left_pairs, local_points, right_pairs, local_weights, left_norms, local_norms, right_norms, after, previous)
+        left_pairs, right_pairs = halo_inputs
+        inputs = (left_pairs, local_points, right_pairs, local_weights, after, previous)
     else:
         inputs = (local_points, local_weights, local_norms)
     aliases = {len(inputs) + 1: 0} if previous is not None else {}
@@ -201,24 +204,24 @@
 
 
 def far_kernel(leaf_of, halo, index_ref, target_ref, *refs):
-    inputs = 7 if halo else 2
+    inputs = 4 if halo else 2
     out_ref = refs[inputs]
     source_buf, norm_buf, sems = refs[inputs + 1 :]
     count, rank = source_buf.shape[1], source_buf.shape[2]
+    buffers = [lambda slot, position: source_buf.at[slot, position]]
     if halo:
-        ls, os, rs, ln, on, rn = refs[:6]
-        parts = (whole_rows(ls, os, rs), norm_rows(ln, on, rn))
+        ls, os, rs = refs[:3]
+        parts = (whole_rows(ls, os, rs),)
     else:
         parts = (own_rows_only(refs[0]), own_norms_only(refs[1]))
-    buffers = (
-        lambda slot, position: source_buf.at[slot, position],
-        lambda slot, position: norm_buf.at[slot, :, pl.ds(position * rank, rank)],
-    )
+        buffers.append(lambda slot, position: norm_buf.at[slot, :, pl.ds(position * rank, rank)])
     slot = pipelined_sources(index_ref, count, parts, buffers, sems, leaf_of)
     target = target_ref[0]
     dims = target.shape[-1]
     sources = source_buf[slot].reshape(count * rank, source_buf.shape[-1])
-    kernel = scaled_kernel(target, target_square_of(target), sources[:, :dims], norm_buf[slot])
+    kernel = scaled_kernel(
+        target, target_square_of(target), sources[:, :dims], None if halo else norm_buf[slot]
+    )
     out_ref[0] = jnp.dot(kernel, sources[:, dims:], preferred_element_type=jnp.float32)
 
 
@@ -230,8 +233,8 @@
     leaf_of, steps, _ = leaf_order(leaves, halo)
     anywhere = pl.BlockSpec(memory_space=pl.ANY)
     if halo:
-        left_rows, right_rows, left_norms, right_norms = halo_inputs
-        inputs = (left_rows, own_rows, right_rows, left_norms, own_norms, right_norms, previous)
+        left_rows, right_rows = halo_inputs
+        inputs = (left_rows, own_rows, right_rows, previous)
     else:
         inputs = (own_rows, own_norms)
     aliases = {len(inputs) + 1: 0} if previous is not None else {}
@@ -404,12 +407,7 @@
         local_weights,
         local_norms,
         near_local,
-        (
-            left_pairs,
-            right_pairs,
-            scaled_norms(left_pairs[:, :, :dim_count]),
-            scaled_norms(right_pairs[:, :, :dim_count]),
-        ),
+        (left_pairs, right_pairs),
         near_inner,
         group_pack,
     )
@@ -425,12 +423,7 @@
         own_rows,
         coord_norms,
         far_local,
-        (
-            left_rows,
-            right_rows,
-            scaled_norms(left_rows[:, :, :dim_count]),
-            scaled_norms(right_rows[:, :, :dim_count]),
-        ),
+        (left_rows, right_rows),
         far_inner,
     )
     rows = lax.axis_size("row")

time: 143 us -> 136 us (0.951)
  the two profiles are of different devices: /device:TPU:2 before, /device:TPU:0 now
where the time goes in v12:
time: 136 us; the launch traced here: 134 us
  Pallas kernels  65.8 us (48%)
  starting transfers between devices  15.8 us (12%)
  between operations  15.1 us (11%)
  waiting for transfers between devices  10.5 us (8%)
  matrix products  9.21 us (7%)
  local copies, waits for them, and re-layouts  8.71 us (6%)
  other arithmetic  8.54 us (6%)
    pallas_call x2, Pallas kernels, near_field(): pl.pallas_call(lambda *refs: near_kernel(leaf_of, halo, *refs), grid_spec...  32.2 us
    pallas_call x2, Pallas kernels, far_field(): pl.pallas_call(lambda *refs: far_kernel(leaf_of, halo, *refs), grid_spec=...  24.2 us
    all_gather x1, waiting for transfers between devices, body(): gathered = lax.all_gather(node_pack[None], 'col', axis=0, tiled=True)  10.4 us
    pallas_call x1, Pallas kernels, final_field(): pl.pallas_call(final_kernel, grid_spec=pltpu.PrefetchScalarGridSpec(num_s...  9.37 us
    ppermute x2, starting transfers between devices, halos(): left = lax.ppermute(tail, FLAT, [(i, i + 1) for i in range(ends)])  8.56 us
    unnamed x40, local copies, waits for them, and re-layouts  4.61 us
    ppermute x3, starting transfers between devices, body(): lax.ppermute(group_pack, 'row', [(r, (r + shift) % rows) for r in range(r...  4.55 us
    dot_general x1, matrix products, select_within(): jnp.einsum('bkp,bpc->bkc', onehot, table, preferred_element_type=jnp.floa...  3.23 us
  transfers between devices with their start and end apart: 8, of which 1 were waited for; matrix products, arithmetic and copies ran while one was open for 12% of the time, Pallas kernels for 42%

profile of v12, /device:TPU:0, one launch (start us, length us, event | category | flops | bytes accessed | tf_op | source)
XLA Modules:
  0.0 133.6 jit_solution(2725177219553252808)
XLA Ops:
  6.5 0.9 copy.28
  7.4 0.7 fusion.55
  9.5 3.2 %fusion.2 = (f32[24,128]{1,0:T(8,128)}, bf16[24,128,128]{2,1,0:T(8,128)(2,1)S(1)}) fusion(bf16[24,256,128]{2,1,0:T(8,128)(2,1)} %bitcast.99, s32[24,128]{1,0:T(8,128)} %param.19), kind=kOutput, calls=%fused_computation.14 | convolution fusion | flops 204469248 | bytes 2383872 | tf_op jit(solution)/shard_map/bkp,bpc->bkc/dot_general | solution.py:317
  12.7 0.6 multiply_reduce_fusion.2
  13.3 0.3 copy-done.2
  13.6 1.0 multiply_convert_fusion
  14.6 0.2 copy-done.6
  14.8 0.6 fusion.23
  15.4 0.7 pad_maximum_fusion.5
  16.1 1.8 %fusion.67 = (bf16[2048,256]{1,0:T(8,128)(2,1)S(1)}, bf16[2048,256]{1,0:T(8,128)(2,1)S(1)}) fusion(bf16[6144,256]{1,0:T(8,128)(2,1)} %param.16), kind=kLoop, calls=%fused_computation.107 | loop fusion | bytes 4194304 | tf_op jit(solution)/shard_map/slice | solution.py:16
  17.9 0.2 copy-done
  18.2 1.4 %pad_maximum_fusion.1 = bf16[2048,384]{1,0:T(8,128)(2,1)} fusion(bf16[2048,256]{1,0:T(8,128)(2,1)S(1)} %get-tuple-element.12, bf16[2048,128]{1,0:T(8,128)(2,1)S(1)} %get-tuple-element.16), kind=kLoop, calls=%fused_computation.15 | loop fusion | flops 3145728 | bytes 3145728 | tf_op jit(solution)/shard_map/concatenate | solution.py:17
  19.6 3.5 %collective-permute-start.3 = (bf16[2048,384]{1,0:T(8,128)(2,1)}, bf16[2048,384]{1,0:T(8,128)(2,1)}, u32[]{:S(2)}, u32[]{:S(2)}) collective-permute-start(bf16[2048,384]{1,0:T(8,128)(2,1)} %pad_maximum_fusion.1), channel_id=1, source_target_pairs={{0,1},{1,2},{2,3},{3,4},{4,5},{5,6},{6,7},{7,8},{8,9},{9,10},{10,1... | collective-permute-start | bytes 4718600 | tf_op jit(solution)/shard_map/ppermute | solution.py:18
  23.1 1.4 %pad_maximum_fusion.2 = bf16[2048,384]{1,0:T(8,128)(2,1)} fusion(bf16[2048,256]{1,0:T(8,128)(2,1)S(1)} %get-tuple-element.11, bf16[2048,128]{1,0:T(8,128)(2,1)S(1)} %get-tuple-element.15), kind=kLoop, calls=%fused_computation.16 | loop fusion | flops 3145728 | bytes 3145728 | tf_op jit(solution)/shard_map/concatenate | solution.py:16
  24.4 1.4 %collective-permute-start.4 = (bf16[2048,384]{1,0:T(8,128)(2,1)}, bf16[2048,384]{1,0:T(8,128)(2,1)}, u32[]{:S(2)}, u32[]{:S(2)}) collective-permute-start(bf16[2048,384]{1,0:T(8,128)(2,1)} %pad_maximum_fusion.2), channel_id=1, source_target_pairs={{1,0},{2,1},{3,2},{4,3},{5,4},{6,5},{7,6},{8,7},{9,8},{10,9},{11,1... | collective-permute-start | bytes 4718600 | tf_op jit(solution)/shard_map/ppermute | solution.py:19
  25.9 1.4 %fusion.26 = (bf16[8,128,384]{2,1,0:T(8,128)(2,1)}, bf16[8,128,384]{2,1,0:T(8,128)(2,1)}) fusion(bf16[24,128,256]{2,1,0:T(8,128)(2,1)S(1)} %multiply_convert_fusion, bf16[24,128,128]{2,1,0:T(8,128)(2,1)S(1)} %copy-done.3), kind=kLoop, calls=%fused_computation.49 | loop fusion | flops 3145728 | bytes 3932160 | tf_op jit(solution)/shard_map/concatenate | solution.py:364
  27.3 5.0 %collective-permute-start.5 = (bf16[1024,384]{1,0:T(8,128)(2,1)}, bf16[1024,384]{1,0:T(8,128)(2,1)}, u32[]{:S(2)}, u32[]{:S(2)}) collective-permute-start(bf16[1024,384]{1,0:T(8,128)(2,1)} %bitcast.20), channel_id=1, source_target_pairs={{0,1},{1,2},{2,3},{3,4},{4,5},{5,6},{6,7},{7,8},{8,9},{9,10},{10,1... | collective-permute-start | bytes 2359304 | tf_op jit(solution)/shard_map/ppermute | solution.py:18
  32.3 1.3 collective-permute-start.6
  33.9 0.7 reshape.158.refs_0_
  34.5 0.9 fusion
  35.5 0.6 reshape.159.refs_0_
  36.1 0.6 reduce_sum.61.refs_4_
  36.7 11.4 %shard_map.145.refs_7_ = f32[24,256,256]{2,1,0:T(8,128)} custom-call(s32[120]{0:T(128)} %reshape.159.refs_0_, bf16[24,256,128]{2,1,0:T(8,128)(2,1)} %bitcast.100, bf16[24,256,128]{2,1,0:T(8,128)(2,1)} %bitcast.101, bf16[24,256,256]{2,1,0:T(8,128)(2,1)} %bitcast.104, f32[24,256]{1,0:T(8,128)} %reduce_sum.61.refs_4_), custom_call_target="tpu_custom_call" | custom-call | tf_op jit(solution)/shard_map/pallas_call | solution.py:186
  48.2 1.8 %pad_maximum_fusion.refs_2_.refs_3_ = bf16[24,128,384]{2,1,0:T(8,128)(2,1)} fusion(bf16[24,128,128]{2,1,0:T(8,128)(2,1)S(1)} %copy-done.4, bf16[24,128,256]{2,1,0:T(8,128)(2,1)S(1)} %multiply_convert_fusion), kind=kLoop, calls=%fused_computation.6 | loop fusion | flops 4718592 | bytes 4718592 | tf_op jit(solution)/shard_map/concatenate | solution.py:364
  49.9 8.9 %shard_map.147.refs_5_ = f32[24,128,256]{2,1,0:T(8,128)} custom-call(s32[96]{0:T(128)} %reshape.158.refs_0_, bf16[24,128,128]{2,1,0:T(8,128)(2,1)} %copy-done.2, bf16[24,128,384]{2,1,0:T(8,128)(2,1)} %pad_maximum_fusion.refs_2_.refs_3_, f32[24,128]{1,0:T(8,128)} %get-tuple-element.25.refs_3_), custom_call_target="tpu_custom_call" | custom-call | tf_op jit(solution)/shard_map/pallas_call | solution.py:242
  59.0 10.4 %all-gather.3.cloned.1.call-done = bf16[1024,512]{0,1:T(8,128)(2,1)} async-done(((bf16[128,512]{0,1:T(8,128)(2,1)}), bf16[1024,512]{0,1:T(8,128)(2,1)}) %all-gather.3.cloned.1.call-update) | async-done | bytes 1048592 | tf_op jit(solution)/shard_map/all_gather | solution.py:386
  69.4 1.5 %copy.43 = bf16[64,8,8,128]{3,2,1,0:T(8,128)(2,1)S(1)} copy(bf16[64,8,8,128]{3,1,2,0:T(8,128)(2,1)} %bitcast.116) | data formatting | bytes 2097152
  70.9 0.3 copy.42
  71.3 0.3 copy.51
  71.6 0.2 copy.40
  71.8 0.2 fusion.19
  72.1 0.4 multiply_reduce_fusion.3
  72.5 3.4 %collective-permute-start.2 = (bf16[128,384]{1,0:T(8,128)(2,1)S(1)}, bf16[128,384]{1,0:T(8,128)(2,1)S(1)}, u32[]{:S(2)}, u32[]{:S(2)}) collective-permute-start(bf16[128,384]{1,0:T(8,128)(2,1)S(1)} %get-tuple-element.20.refs_6_), channel_id=1, source_target_pairs={{0,24},{8,0},{16,8},{24,16},{1,25},{9,1},{17,9},{25,17},{2,26},{10... | collective-permute-start | bytes 294920 | tf_op jit(solution)/shard_map/ppermute | solution.py:431
  75.9 0.2 copy.44
  76.1 1.1 collective-permute-start
  77.2 20.8 %shard_map.146.near_ref = f32[24,256,256]{2,1,0:T(8,128)} custom-call(s32[120]{0:T(128)} %reshape.159.refs_0_, bf16[24,256,128]{2,1,0:T(8,128)(2,1)} %bitcast.102, bf16[8,256,384]{2,1,0:T(8,128)(2,1)} %bitcast.18.refs_2_, bf16[24,256,128]{2,1,0:T(8,128)(2,1)} %bitcast.103, bf16[8,256,384]{2,1,0:T(8,128)(2,1)} %bitcast.19.refs_4_, ...), custom_call_target="tpu_custom_call", output_to_operand_aliasing={{}: (7, {})} | custom-call | tf_op jit(solution)/shard_map/pallas_call | solution.py:186
  98.0 0.3 fusion.10
  98.3 0.1 multiply_reduce_fusion
  98.5 0.4 convolution_convert_fusion.1
  98.9 15.2 %shard_map.148.far_ref = f32[24,128,256]{2,1,0:T(8,128)} custom-call(s32[96]{0:T(128)} %reshape.158.refs_0_, bf16[24,128,128]{2,1,0:T(8,128)(2,1)} %copy-done.2, bf16[8,128,384]{2,1,0:T(8,128)(2,1)} %bitcast.22.refs_2_, bf16[24,128,384]{2,1,0:T(8,128)(2,1)} %pad_maximum_fusion.refs_2_.refs_3_, ...), custom_call_target="tpu_custom_call", output_to_operand_aliasing={{}: (5, {})} | custom-call | tf_op jit(solution)/shard_map/pallas_call | solution.py:242
  114.1 0.4 convolution_bitcast_fusion
  114.5 0.2 copy.47
  114.7 0.2 copy.46
  114.9 0.2 copy.45
  115.0 1.0 convolution_convert_fusion
  116.2 0.2 fusion.20
  116.4 1.0 fusion.18.down_ref
  117.4 9.4 %shard_map.149 = bf16[24,256,256]{2,1,0:T(8,128)(2,1)} custom-call(s32[24]{0:T(128)} %rank_ref.1, bf16[24,128,128]{2,1,0:T(8,128)(2,1)} %bitcast.114, bf16[128,256]{1,0:T(8,128)(2,1)} %fusion.18.down_ref, f32[24,128,256]{2,1,0:T(8,128)} %shard_map.148.far_ref, bf16[24,256,128]{2,1,0:T(8,128)(2,1)} %bitcast.109, f32[24,256,256]{2,1,0:T(8,128)} %shard_map.146.near_ref), custom_call_target="tpu_custom_call" | custom-call | tf_op jit(solution)/shard_map/pallas_call | solution.py:285
  (51 shorter events, 0.8 us)
Async XLA Ops:
  6.5 62.9 %all-gather.3.cloned.1.call-start = ((), (), s32[]{:S(2)}) async-start(), calls=%async_computation | async-start | bytes 1179648 | tf_op jit(solution)/shard_map/all_gather | solution.py:386
  6.5 6.2 %copy-start.11 = (s32[1,128]{1,0:T(1,128)S(1)}, s32[1,128]{1,0:T(1,128)}, u32[]{:S(2)}) copy-start(s32[1,128]{1,0:T(1,128)} %param.24) | copy-start | bytes 1540
  9.5 4.2 %copy-start.1 = (bf16[6144,256]{1,0:T(8,128)(2,1)S(1)}, bf16[6144,256]{1,0:T(8,128)(2,1)}, u32[]{:S(2)}) copy-start(bf16[6144,256]{1,0:T(8,128)(2,1)} %param.16) | copy-start | bytes 9437188
  9.5 4.1 %copy-start.5 = (bf16[6144,128]{1,0:T(8,128)(2,1)S(1)}, bf16[6144,128]{1,0:T(8,128)(2,1)}, u32[]{:S(2)}) copy-start(bf16[6144,128]{1,0:T(8,128)(2,1)} %param.17) | copy-start | bytes 4718596
  12.7 0.9 copy-start.2
  13.6 1.1 copy-start.6
  16.1 2.0 %copy-start = (bf16[6144,128]{1,0:T(8,128)(2,1)S(1)}, bf16[6144,128]{1,0:T(8,128)(2,1)}, u32[]{:S(2)}) copy-start(bf16[6144,128]{1,0:T(8,128)(2,1)} %param.15) | copy-start | bytes 4718596
  19.6 56.5 %collective-permute-start.3 = (bf16[2048,384]{1,0:T(8,128)(2,1)}, bf16[2048,384]{1,0:T(8,128)(2,1)}, u32[]{:S(2)}, u32[]{:S(2)}) collective-permute-start(bf16[2048,384]{1,0:T(8,128)(2,1)} %pad_maximum_fusion.1), channel_id=1, source_target_pairs={{0,1},{1,2},{2,3},{3,4},{4,5},{5,6},{6,7},{7,8},{8,9},{9,10},{10,1... | collective-permute-start | bytes 4718600 | tf_op jit(solution)/shard_map/ppermute | solution.py:18
  23.1 2.8 %copy-start.3 = (bf16[24,128,128]{2,1,0:T(8,128)(2,1)S(1)}, bf16[24,128,128]{2,1,0:T(8,128)(2,1)}, u32[]{:S(2)}) copy-start(bf16[24,128,128]{2,1,0:T(8,128)(2,1)} %copy-done.2) | copy-start | bytes 2359300
  24.4 9.3 %copy-start.10 = (s32[24,4]{0,1:T(4,128)S(1)}, s32[24,4]{0,1:T(4,128)}, u32[]{:S(2)}) copy-start(s32[24,4]{0,1:T(4,128)} %param.21) | copy-start | bytes 1156
  24.4 51.7 %collective-permute-start.4 = (bf16[2048,384]{1,0:T(8,128)(2,1)}, bf16[2048,384]{1,0:T(8,128)(2,1)}, u32[]{:S(2)}, u32[]{:S(2)}) collective-permute-start(bf16[2048,384]{1,0:T(8,128)(2,1)} %pad_maximum_fusion.2), channel_id=1, source_target_pairs={{1,0},{2,1},{3,2},{4,3},{5,4},{6,5},{7,6},{8,7},{9,8},{10,9},{11,1... | collective-permute-start | bytes 4718600 | tf_op jit(solution)/shard_map/ppermute | solution.py:19
  27.3 8.1 %copy-start.9 = (s32[24,5]{0,1:T(8,128)S(1)}, s32[24,5]{0,1:T(8,128)}, u32[]{:S(2)}) copy-start(s32[24,5]{0,1:T(8,128)} %param.20) | copy-start | bytes 1444
  27.3 71.6 %collective-permute-start.5 = (bf16[1024,384]{1,0:T(8,128)(2,1)}, bf16[1024,384]{1,0:T(8,128)(2,1)}, u32[]{:S(2)}, u32[]{:S(2)}) collective-permute-start(bf16[1024,384]{1,0:T(8,128)(2,1)} %bitcast.20), channel_id=1, source_target_pairs={{0,1},{1,2},{2,3},{3,4},{4,5},{5,6},{6,7},{7,8},{8,9},{9,10},{10,1... | collective-permute-start | bytes 2359304 | tf_op jit(solution)/shard_map/ppermute | solution.py:18
  32.3 66.5 %collective-permute-start.6 = (bf16[1024,384]{1,0:T(8,128)(2,1)}, bf16[1024,384]{1,0:T(8,128)(2,1)}, u32[]{:S(2)}, u32[]{:S(2)}) collective-permute-start(bf16[1024,384]{1,0:T(8,128)(2,1)} %bitcast.21), channel_id=1, source_target_pairs={{1,0},{2,1},{3,2},{4,3},{5,4},{6,5},{7,6},{8,7},{9,8},{10,9},{11,1... | collective-permute-start | bytes 2359304 | tf_op jit(solution)/shard_map/ppermute | solution.py:19
  36.7 11.4 %copy-start.4 = (bf16[24,128,128]{2,1,0:T(8,128)(2,1)S(1)}, bf16[24,128,128]{2,1,0:T(8,128)(2,1)}, u32[]{:S(2)}) copy-start(bf16[24,128,128]{2,1,0:T(8,128)(2,1)} %copy-done.2) | copy-start | bytes 2359300
  49.9 9.0 %copy-start.12 = (s32[1,4]{1,0:T(1,128)S(1)}, s32[1,4]{1,0:T(1,128)}, u32[]{:S(2)}) copy-start(s32[1,4]{1,0:T(1,128)} %param.25) | copy-start | bytes 52
  49.9 9.0 %copy-start.13 = (s32[1,2]{1,0:T(1,128)S(1)}, s32[1,2]{1,0:T(1,128)}, u32[]{:S(2)}) copy-start(s32[1,2]{1,0:T(1,128)} %param.29) | copy-start | bytes 28
  71.3 0.8 copy-start.14
  72.5 4.8 %copy-start.7 = (bf16[128,384]{1,0:T(8,128)(2,1)}, bf16[128,384]{1,0:T(8,128)(2,1)S(1)}, u32[]{:S(2)}) copy-start(bf16[128,384]{1,0:T(8,128)(2,1)S(1)} %get-tuple-element.20.refs_6_) | copy-start | bytes 294916
  72.5 42.0 %collective-permute-start.2 = (bf16[128,384]{1,0:T(8,128)(2,1)S(1)}, bf16[128,384]{1,0:T(8,128)(2,1)S(1)}, u32[]{:S(2)}, u32[]{:S(2)}) collective-permute-start(bf16[128,384]{1,0:T(8,128)(2,1)S(1)} %get-tuple-element.20.refs_6_), channel_id=1, source_target_pairs={{0,24},{8,0},{16,8},{24,16},{1,25},{9,1},{17,9},{25,17},{2,26},{10... | collective-permute-start | bytes 294920 | tf_op jit(solution)/shard_map/ppermute | solution.py:431
  76.0 38.6 %collective-permute-start.1 = (bf16[128,384]{1,0:T(8,128)(2,1)S(1)}, bf16[128,384]{1,0:T(8,128)(2,1)S(1)}, u32[]{:S(2)}, u32[]{:S(2)}) collective-permute-start(bf16[128,384]{1,0:T(8,128)(2,1)S(1)} %get-tuple-element.20.refs_6_), channel_id=1, source_target_pairs={{0,16},{8,24},{16,0},{24,8},{1,17},{9,25},{17,1},{25,9},{2,18},{10... | collective-permute-start | bytes 294920 | tf_op jit(solution)/shard_map/ppermute | solution.py:431
  76.1 38.7 %collective-permute-start = (bf16[128,384]{1,0:T(8,128)(2,1)S(1)}, bf16[128,384]{1,0:T(8,128)(2,1)S(1)}, u32[]{:S(2)}, u32[]{:S(2)}) collective-permute-start(bf16[128,384]{1,0:T(8,128)(2,1)S(1)} %get-tuple-element.20.refs_6_), channel_id=1, source_target_pairs={{0,8},{8,16},{16,24},{24,0},{1,9},{9,17},{17,25},{25,1},{2,10},{10... | collective-permute-start | bytes 294920 | tf_op jit(solution)/shard_map/ppermute | solution.py:431
  115.0 1.4 %copy-start.8 = (bf16[128,128]{1,0:T(8,128)(2,1)S(1)}, bf16[128,128]{1,0:T(8,128)(2,1)}, u32[]{:S(2)}) copy-start(bf16[128,128]{1,0:T(8,128)(2,1)} %param.26) | copy-start | bytes 98308
Sparse Core Ops, SparseCore 0:
  16.2 53.1 all-gather.2

commit v13 on v12

--- a/solution.py
+++ b/solution.py
@@ -144,7 +144,7 @@
 
 
 def near_kernel(leaf_of, halo, index_ref, target_ref, *refs):
-    inputs = 6 if halo else 3
+    inputs = 5 if halo else 3
     out_ref = refs[inputs]
     point_buf, weight_buf, norm_buf, sems = refs[inputs + 1 :]
     count, size, dims = point_buf.shape[1], point_buf.shape[2], point_buf.shape[3]
@@ -169,7 +169,7 @@
     out_ref[0] = jnp.dot(kernel, values, preferred_element_type=jnp.float32)
 
 
-def near_field(local_points, local_weights, local_norms, near_local, halo_inputs=None, previous=None, after=None):
+def near_field(local_points, local_weights, local_norms, near_local, halo_inputs=None, previous=None):
     leaves, size, dims = local_points.shape
     rhs = local_weights.shape[-1]
     count = near_local.shape[1]
@@ -178,7 +178,7 @@
     anywhere = pl.BlockSpec(memory_space=pl.ANY)
     if halo:
         left_pairs, right_pairs = halo_inputs
-        inputs = (left_pairs, local_points, right_pairs, local_weights, after, previous)
+        inputs = (left_pairs, local_points, right_pairs, local_weights, previous)
     else:
         inputs = (local_points, local_weights, local_norms)
     aliases = {len(inputs) + 1: 0} if previous is not None else {}
@@ -204,7 +204,7 @@
 
 
 def far_kernel(leaf_of, halo, index_ref, target_ref, *refs):
-    inputs = 4 if halo else 2
+    inputs = 5 if halo else 2
     out_ref = refs[inputs]
     source_buf, norm_buf, sems = refs[inputs + 1 :]
     count, rank = source_buf.shape[1], source_buf.shape[2]
@@ -225,7 +225,7 @@
     out_ref[0] = jnp.dot(kernel, sources[:, dims:], preferred_element_type=jnp.float32)
 
 
-def far_field(leaf_coords, own_rows, own_norms, far_local, halo_inputs=None, previous=None):
+def far_field(leaf_coords, own_rows, own_norms, far_local, halo_inputs=None, previous=None, after=None):
     leaves, rank, dims = leaf_coords.shape
     width = own_rows.shape[-1]
     count = far_local.shape[1]
@@ -234,7 +234,7 @@
     anywhere = pl.BlockSpec(memory_space=pl.ANY)
     if halo:
         left_rows, right_rows = halo_inputs
-        inputs = (left_rows, own_rows, right_rows, previous)
+        inputs = (left_rows, own_rows, right_rows, after, previous)
     else:
         inputs = (own_rows, own_norms)
     aliases = {len(inputs) + 1: 0} if previous is not None else {}
@@ -353,9 +353,7 @@
     left_pairs = left_pairs.reshape(REACH, leaf_size, dim_count + rhs_count)
     right_pairs = right_pairs.reshape(REACH, leaf_size, dim_count + rhs_count)
 
-    leaf_mask = (
-        lax.broadcasted_iota(jnp.int32, (leaf_count, rank_count), 1) < leaf_rank[:, None]
-    ).astype(jnp.float32)
+    leaf_mask = (lax.broadcasted_iota(jnp.int32, (leaf_count, rank_count), 1) < leaf_rank[:, None]).astype(jnp.float32)
     leaf_up = (
         jnp.einsum("lpk,lpr->lkr", local_bases, local_weights, preferred_element_type=jnp.float32)
         * leaf_mask[:, :, None]
@@ -409,7 +407,6 @@
         near_local,
         (left_pairs, right_pairs),
         near_inner,
-        group_pack,
     )
     near_total, left_rows, right_rows = lax.optimization_barrier((near_total, left_rows, right_rows))
 
@@ -425,14 +422,15 @@
         far_local,
         (left_rows, right_rows),
         far_inner,
+        group_pack,
     )
     rows = lax.axis_size("row")
-    received = [group_pack] + [
-        lax.ppermute(group_pack, "row", [(r, (r + shift) % rows) for r in range(rows)])
-        for shift in range(1, rows)
-    ]
-    shifts = (lax.axis_index("row") - group_far[0]) % rows
-    picked_group = select_rows(jnp.stack(received), shifts)
+    mine = lax.axis_index("row")
+    slots = jnp.where(
+        (jnp.arange(rows, dtype=jnp.int32) == mine)[:, None, None], group_pack[None], jnp.zeros_like(group_pack)[None]
+    )
+    every_group = lax.psum(slots, "row")
+    picked_group = select_rows(every_group, group_far[0])
     picked_group_coords = picked_group[:, :, :dim_count]
     picked_group_up = picked_group[:, :, dim_count:]
     group_kernel = kernel_block(

time: 136 us -> 157 us (1.15)
  waiting for transfers between devices: 10.5 us -> 35 us
  starting transfers between devices: 15.8 us -> 11.3 us
    psum x0 -> x1, waiting for transfers between devices: none -> 34.9 us  [body(): every_group = lax.psum(slots, 'row')]
    all_gather x1, waiting for transfers between devices: 10.4 us -> 0.02 us  [body(): gathered = lax.all_gather(node_pack[None], 'col', axis=0, tiled=True)]
    ppermute x3 -> x0, starting transfers between devices: 4.55 us -> none  [body(): lax.ppermute(group_pack, 'row', [(r, (r + shift) % rows) for r in range(r...]
    unnamed x40 -> x37, local copies, waits for them, and re-layouts: 4.61 us -> 5.04 us
  transfers between devices with their start and end apart: 8 -> 6, of which waited for: 1 -> 1; matrix products, arithmetic and copies ran while one was open for 12% -> 8% of each run, Pallas kernels for 42% -> 36%
where the time goes in v13:
time: 157 us; the launch traced here: 154 us
  Pallas kernels  65.7 us (42%)
  waiting for transfers between devices  35 us (22%)
  between operations  15.1 us (10%)
  starting transfers between devices  11.3 us (7%)
  matrix products  9.57 us (6%)
  local copies, waits for them, and re-layouts  9.14 us (6%)
  other arithmetic  8.61 us (5%)
    psum x1, waiting for transfers between devices, body(): every_group = lax.psum(slots, 'row')  34.9 us
    pallas_call x2, Pallas kernels, near_field(): pl.pallas_call(lambda *refs: near_kernel(leaf_of, halo, *refs), grid_spec...  32.2 us
    pallas_call x2, Pallas kernels, far_field(): pl.pallas_call(lambda *refs: far_kernel(leaf_of, halo, *refs), grid_spec=...  24.2 us
    pallas_call x1, Pallas kernels, final_field(): pl.pallas_call(final_kernel, grid_spec=pltpu.PrefetchScalarGridSpec(num_s...  9.35 us
    ppermute x2, starting transfers between devices, halos(): left = lax.ppermute(tail, FLAT, [(i, i + 1) for i in range(ends)])  8.41 us
    unnamed x37, local copies, waits for them, and re-layouts  5.04 us
    dot_general x1, matrix products, select_within(): jnp.einsum('bkp,bpc->bkc', onehot, table, preferred_element_type=jnp.floa...  3.23 us
    concatenate x2, other arithmetic, body(): own_rows = jnp.concatenate([leaf_coords, leaf_up], axis=-1)  3.2 us
  transfers between devices with their start and end apart: 6, of which 1 were waited for; matrix products, arithmetic and copies ran while one was open for 8% of the time, Pallas kernels for 36%

profile of v13, /device:TPU:0, one launch (start us, length us, event | category | flops | bytes accessed | tf_op | source)
XLA Modules:
  0.0 154.4 jit_solution(16299070101686820644)
XLA Ops:
  6.5 0.9 copy.28
  7.4 0.7 fusion.50
  9.5 3.2 %fusion.2 = (f32[24,128]{1,0:T(8,128)}, bf16[24,128,128]{2,1,0:T(8,128)(2,1)S(1)}) fusion(bf16[24,256,128]{2,1,0:T(8,128)(2,1)} %bitcast.89, s32[24,128]{1,0:T(8,128)} %param.19), kind=kOutput, calls=%fused_computation.14 | convolution fusion | flops 204469248 | bytes 2383872 | tf_op jit(solution)/shard_map/bkp,bpc->bkc/dot_general | solution.py:317
  12.7 0.6 multiply_reduce_fusion.2
  13.3 0.3 copy-done.2
  13.6 1.0 multiply_convert_fusion
  14.6 0.2 copy-done.6
  14.7 0.6 fusion.23
  15.4 0.7 pad_maximum_fusion.3
  16.1 1.8 %fusion.59 = (bf16[2048,256]{1,0:T(8,128)(2,1)S(1)}, bf16[2048,256]{1,0:T(8,128)(2,1)S(1)}) fusion(bf16[6144,256]{1,0:T(8,128)(2,1)} %param.16), kind=kLoop, calls=%fused_computation.97 | loop fusion | bytes 4194304 | tf_op jit(solution)/shard_map/slice | solution.py:16
  17.9 0.2 copy-done
  18.2 1.4 pad_maximum_fusion.1
  19.5 3.5 %collective-permute-start = (bf16[2048,384]{1,0:T(8,128)(2,1)}, bf16[2048,384]{1,0:T(8,128)(2,1)}, u32[]{:S(2)}, u32[]{:S(2)}) collective-permute-start(bf16[2048,384]{1,0:T(8,128)(2,1)} %pad_maximum_fusion.1), channel_id=1, source_target_pairs={{0,1},{1,2},{2,3},{3,4},{4,5},{5,6},{6,7},{7,8},{8,9},{9,10},{10,1... | collective-permute-start | bytes 4718600 | tf_op jit(solution)/shard_map/ppermute | solution.py:18
  23.1 1.3 pad_maximum_fusion.2
  24.4 1.4 collective-permute-start.1
  25.9 1.4 fusion.26
  27.3 4.9 %collective-permute-start.2 = (bf16[1024,384]{1,0:T(8,128)(2,1)}, bf16[1024,384]{1,0:T(8,128)(2,1)}, u32[]{:S(2)}, u32[]{:S(2)}) collective-permute-start(bf16[1024,384]{1,0:T(8,128)(2,1)} %bitcast.20), channel_id=1, source_target_pairs={{0,1},{1,2},{2,3},{3,4},{4,5},{5,6},{6,7},{7,8},{8,9},{9,10},{10,1... | collective-permute-start | bytes 2359304 | tf_op jit(solution)/shard_map/ppermute | solution.py:18
  32.1 1.5 collective-permute-start.3
  33.7 0.1 copy.34
  33.8 0.1 copy.35
  33.9 0.6 reshape.141.refs_0_
  34.5 0.1 copy.36
  34.6 0.6 reshape.142.refs_0_
  35.2 0.9 fusion
  36.1 0.6 reduce_sum.61.refs_4_
  36.7 11.4 %shard_map.145.refs_6_ = f32[24,256,256]{2,1,0:T(8,128)} custom-call(s32[120]{0:T(128)} %reshape.142.refs_0_, bf16[24,256,128]{2,1,0:T(8,128)(2,1)} %bitcast.90, bf16[24,256,128]{2,1,0:T(8,128)(2,1)} %bitcast.91, bf16[24,256,256]{2,1,0:T(8,128)(2,1)} %bitcast.94, f32[24,256]{1,0:T(8,128)} %reduce_sum.61.refs_4_), custom_call_target="tpu_custom_call" | custom-call | tf_op jit(solution)/shard_map/pallas_call | solution.py:186
  48.2 1.8 %pad_maximum_fusion.refs_2_.refs_3_ = bf16[24,128,384]{2,1,0:T(8,128)(2,1)} fusion(bf16[24,128,128]{2,1,0:T(8,128)(2,1)S(1)} %copy-done.4, bf16[24,128,256]{2,1,0:T(8,128)(2,1)S(1)} %multiply_convert_fusion), kind=kLoop, calls=%fused_computation.6 | loop fusion | flops 4718592 | bytes 4718592 | tf_op jit(solution)/shard_map/concatenate | solution.py:362
  49.9 8.9 %shard_map.147.refs_6_ = f32[24,128,256]{2,1,0:T(8,128)} custom-call(s32[96]{0:T(128)} %reshape.141.refs_0_, bf16[24,128,128]{2,1,0:T(8,128)(2,1)} %copy-done.2, bf16[24,128,384]{2,1,0:T(8,128)(2,1)} %pad_maximum_fusion.refs_2_.refs_3_, f32[24,128]{1,0:T(8,128)} %get-tuple-element.23.refs_3_), custom_call_target="tpu_custom_call" | custom-call | tf_op jit(solution)/shard_map/pallas_call | solution.py:242
  58.9 20.8 %shard_map.146.near_ref = f32[24,256,256]{2,1,0:T(8,128)} custom-call(s32[120]{0:T(128)} %reshape.142.refs_0_, bf16[24,256,128]{2,1,0:T(8,128)(2,1)} %bitcast.92, bf16[8,256,384]{2,1,0:T(8,128)(2,1)} %bitcast.18.refs_2_, bf16[24,256,128]{2,1,0:T(8,128)(2,1)} %bitcast.93, bf16[8,256,384]{2,1,0:T(8,128)(2,1)} %bitcast.19.refs_4_, ...), custom_call_target="tpu_custom_call", output_to_operand_aliasing={{}: (6, {})} | custom-call | tf_op jit(solution)/shard_map/pallas_call | solution.py:186
  79.8 1.5 copy.43
  81.4 0.3 copy.42
  81.7 0.2 copy.40
  82.0 0.4 multiply_reduce_fusion.3
  82.3 0.2 fusion.19
  82.6 0.1 select_bitcast_fusion
  82.7 1.0 copy.44
  83.8 0.3 fusion.10
  84.1 0.1 multiply_reduce_fusion
  84.2 0.3 copy.48
  84.6 15.2 %shard_map.148.far_ref = f32[24,128,256]{2,1,0:T(8,128)} custom-call(s32[96]{0:T(128)} %reshape.141.refs_0_, bf16[24,128,128]{2,1,0:T(8,128)(2,1)} %copy-done.2, bf16[8,128,384]{2,1,0:T(8,128)(2,1)} %bitcast.22.refs_2_, bf16[24,128,384]{2,1,0:T(8,128)(2,1)} %pad_maximum_fusion.refs_2_.refs_3_, ...), custom_call_target="tpu_custom_call", output_to_operand_aliasing={{}: (6, {})} | custom-call | tf_op jit(solution)/shard_map/pallas_call | solution.py:242
  99.8 0.4 convolution_convert_fusion.1
  100.2 0.4 convolution_bitcast_fusion
  100.6 34.9 %all-reduce.2.cloned.1.call-done = bf16[4,49152]{1,0:T(4,128)(2,1)} async-done(((bf16[4,49152]{1,0:T(4,128)(2,1)}), bf16[4,49152]{1,0:T(4,128)(2,1)}) %all-reduce.2.cloned.1.call-update) | async-done | bytes 393232 | tf_op jit(solution)/shard_map/psum | solution.py:432
  135.5 1.4 convolution_convert_fusion
  136.9 0.1 multiply_reduce_fusion.1
  137.0 0.2 fusion.20
  137.3 1.0 fusion.18.down_ref
  138.2 9.4 %shard_map.149 = bf16[24,256,256]{2,1,0:T(8,128)(2,1)} custom-call(s32[24]{0:T(128)} %rank_ref.1, bf16[24,128,128]{2,1,0:T(8,128)(2,1)} %bitcast.104, bf16[128,256]{1,0:T(8,128)(2,1)} %fusion.18.down_ref, f32[24,128,256]{2,1,0:T(8,128)} %shard_map.148.far_ref, bf16[24,256,128]{2,1,0:T(8,128)(2,1)} %bitcast.99, f32[24,256,256]{2,1,0:T(8,128)} %shard_map.146.near_ref), custom_call_target="tpu_custom_call" | custom-call | tf_op jit(solution)/shard_map/pallas_call | solution.py:285
  (46 shorter events, 0.4 us)
Async XLA Ops:
  6.5 73.2 %all-gather.3.cloned.1.call-start = ((), (), s32[]{:S(2)}) async-start(), calls=%async_computation.1 | async-start | bytes 1179648 | tf_op jit(solution)/shard_map/all_gather | solution.py:384
  6.5 6.2 %copy-start.11 = (s32[1,128]{1,0:T(1,128)S(1)}, s32[1,128]{1,0:T(1,128)}, u32[]{:S(2)}) copy-start(s32[1,128]{1,0:T(1,128)} %param.24) | copy-start | bytes 1540
  9.5 4.1 %copy-start.1 = (bf16[6144,256]{1,0:T(8,128)(2,1)S(1)}, bf16[6144,256]{1,0:T(8,128)(2,1)}, u32[]{:S(2)}) copy-start(bf16[6144,256]{1,0:T(8,128)(2,1)} %param.16) | copy-start | bytes 9437188
  9.5 4.1 %copy-start.5 = (bf16[6144,128]{1,0:T(8,128)(2,1)S(1)}, bf16[6144,128]{1,0:T(8,128)(2,1)}, u32[]{:S(2)}) copy-start(bf16[6144,128]{1,0:T(8,128)(2,1)} %param.17) | copy-start | bytes 4718596
  12.7 0.9 copy-start.2
  13.6 1.1 copy-start.6
  16.0 2.0 %copy-start = (bf16[6144,128]{1,0:T(8,128)(2,1)S(1)}, bf16[6144,128]{1,0:T(8,128)(2,1)}, u32[]{:S(2)}) copy-start(bf16[6144,128]{1,0:T(8,128)(2,1)} %param.15) | copy-start | bytes 4718596
  16.1 119.4 %all-reduce.2.cloned.1.call-start = ((), (), s32[]{:S(2)}) async-start(), calls=%async_computation | async-start | bytes 786432 | tf_op jit(solution)/shard_map/psum | solution.py:432
  19.5 39.4 %collective-permute-start = (bf16[2048,384]{1,0:T(8,128)(2,1)}, bf16[2048,384]{1,0:T(8,128)(2,1)}, u32[]{:S(2)}, u32[]{:S(2)}) collective-permute-start(bf16[2048,384]{1,0:T(8,128)(2,1)} %pad_maximum_fusion.1), channel_id=1, source_target_pairs={{0,1},{1,2},{2,3},{3,4},{4,5},{5,6},{6,7},{7,8},{8,9},{9,10},{10,1... | collective-permute-start | bytes 4718600 | tf_op jit(solution)/shard_map/ppermute | solution.py:18
  23.1 2.8 %copy-start.3 = (bf16[24,128,128]{2,1,0:T(8,128)(2,1)S(1)}, bf16[24,128,128]{2,1,0:T(8,128)(2,1)}, u32[]{:S(2)}) copy-start(bf16[24,128,128]{2,1,0:T(8,128)(2,1)} %copy-done.2) | copy-start | bytes 2359300
  24.4 9.2 %copy-start.9 = (s32[24,5]{0,1:T(8,128)S(1)}, s32[24,5]{0,1:T(8,128)}, u32[]{:S(2)}) copy-start(s32[24,5]{0,1:T(8,128)} %param.20) | copy-start | bytes 1444
  24.4 9.2 %copy-start.10 = (s32[24,4]{0,1:T(4,128)S(1)}, s32[24,4]{0,1:T(4,128)}, u32[]{:S(2)}) copy-start(s32[24,4]{0,1:T(4,128)} %param.21) | copy-start | bytes 1156
  24.4 34.5 %collective-permute-start.1 = (bf16[2048,384]{1,0:T(8,128)(2,1)}, bf16[2048,384]{1,0:T(8,128)(2,1)}, u32[]{:S(2)}, u32[]{:S(2)}) collective-permute-start(bf16[2048,384]{1,0:T(8,128)(2,1)} %pad_maximum_fusion.2), channel_id=1, source_target_pairs={{1,0},{2,1},{3,2},{4,3},{5,4},{6,5},{7,6},{8,7},{9,8},{10,9},{11,1... | collective-permute-start | bytes 4718600 | tf_op jit(solution)/shard_map/ppermute | solution.py:19
  27.3 52.4 %collective-permute-start.2 = (bf16[1024,384]{1,0:T(8,128)(2,1)}, bf16[1024,384]{1,0:T(8,128)(2,1)}, u32[]{:S(2)}, u32[]{:S(2)}) collective-permute-start(bf16[1024,384]{1,0:T(8,128)(2,1)} %bitcast.20), channel_id=1, source_target_pairs={{0,1},{1,2},{2,3},{3,4},{4,5},{5,6},{6,7},{7,8},{8,9},{9,10},{10,1... | collective-permute-start | bytes 2359304 | tf_op jit(solution)/shard_map/ppermute | solution.py:18
  32.1 47.6 %collective-permute-start.3 = (bf16[1024,384]{1,0:T(8,128)(2,1)}, bf16[1024,384]{1,0:T(8,128)(2,1)}, u32[]{:S(2)}, u32[]{:S(2)}) collective-permute-start(bf16[1024,384]{1,0:T(8,128)(2,1)} %bitcast.21), channel_id=1, source_target_pairs={{1,0},{2,1},{3,2},{4,3},{5,4},{6,5},{7,6},{8,7},{9,8},{10,9},{11,1... | collective-permute-start | bytes 2359304 | tf_op jit(solution)/shard_map/ppermute | solution.py:19
  36.7 11.4 %copy-start.4 = (bf16[24,128,128]{2,1,0:T(8,128)(2,1)S(1)}, bf16[24,128,128]{2,1,0:T(8,128)(2,1)}, u32[]{:S(2)}) copy-start(bf16[24,128,128]{2,1,0:T(8,128)(2,1)} %copy-done.2) | copy-start | bytes 2359300
  49.9 9.0 %copy-start.12 = (s32[1,4]{1,0:T(1,128)S(1)}, s32[1,4]{1,0:T(1,128)}, u32[]{:S(2)}) copy-start(s32[1,4]{1,0:T(1,128)} %param.25) | copy-start | bytes 52
  81.3 0.7 copy-start.13
  82.6 1.9 %copy-start.7 = (bf16[128,384]{1,0:T(8,128)(2,1)}, bf16[128,384]{1,0:T(8,128)(2,1)S(1)}, u32[]{:S(2)}) copy-start(bf16[128,384]{1,0:T(8,128)(2,1)S(1)} %pad_maximum_fusion.4.refs_5_) | copy-start | bytes 294916
  99.8 35.7 %copy-start.14 = (s32[1,2]{1,0:T(1,128)S(1)}, s32[1,2]{1,0:T(1,128)}, u32[]{:S(2)}) copy-start(s32[1,2]{1,0:T(1,128)} %param.29) | copy-start | bytes 28
  99.8 37.4 %copy-start.8 = (bf16[128,128]{1,0:T(8,128)(2,1)S(1)}, bf16[128,128]{1,0:T(8,128)(2,1)}, u32[]{:S(2)}) copy-start(bf16[128,128]{1,0:T(8,128)(2,1)} %param.26) | copy-start | bytes 98308
Sparse Core Ops, SparseCore 0:
  16.2 53.1 all-gather.2
  83.9 51.5 all-reduce.1

commit v14 on v12

--- a/solution.py
+++ b/solution.py
@@ -144,7 +144,7 @@
 
 
 def near_kernel(leaf_of, halo, index_ref, target_ref, *refs):
-    inputs = 6 if halo else 3
+    inputs = 5 if halo else 3
     out_ref = refs[inputs]
     point_buf, weight_buf, norm_buf, sems = refs[inputs + 1 :]
     count, size, dims = point_buf.shape[1], point_buf.shape[2], point_buf.shape[3]
@@ -169,7 +169,7 @@
     out_ref[0] = jnp.dot(kernel, values, preferred_element_type=jnp.float32)
 
 
-def near_field(local_points, local_weights, local_norms, near_local, halo_inputs=None, previous=None, after=None):
+def near_field(local_points, local_weights, local_norms, near_local, halo_inputs=None, previous=None):
     leaves, size, dims = local_points.shape
     rhs = local_weights.shape[-1]
     count = near_local.shape[1]
@@ -178,7 +178,7 @@
     anywhere = pl.BlockSpec(memory_space=pl.ANY)
     if halo:
         left_pairs, right_pairs = halo_inputs
-        inputs = (left_pairs, local_points, right_pairs, local_weights, after, previous)
+        inputs = (left_pairs, local_points, right_pairs, local_weights, previous)
     else:
         inputs = (local_points, local_weights, local_norms)
     aliases = {len(inputs) + 1: 0} if previous is not None else {}
@@ -204,7 +204,7 @@
 
 
 def far_kernel(leaf_of, halo, index_ref, target_ref, *refs):
-    inputs = 4 if halo else 2
+    inputs = 5 if halo else 2
     out_ref = refs[inputs]
     source_buf, norm_buf, sems = refs[inputs + 1 :]
     count, rank = source_buf.shape[1], source_buf.shape[2]
@@ -225,7 +225,7 @@
     out_ref[0] = jnp.dot(kernel, sources[:, dims:], preferred_element_type=jnp.float32)
 
 
-def far_field(leaf_coords, own_rows, own_norms, far_local, halo_inputs=None, previous=None):
+def far_field(leaf_coords, own_rows, own_norms, far_local, halo_inputs=None, previous=None, after=None):
     leaves, rank, dims = leaf_coords.shape
     width = own_rows.shape[-1]
     count = far_local.shape[1]
@@ -234,7 +234,7 @@
     anywhere = pl.BlockSpec(memory_space=pl.ANY)
     if halo:
         left_rows, right_rows = halo_inputs
-        inputs = (left_rows, own_rows, right_rows, previous)
+        inputs = (left_rows, own_rows, right_rows, after, previous)
     else:
         inputs = (own_rows, own_norms)
     aliases = {len(inputs) + 1: 0} if previous is not None else {}
@@ -383,7 +383,12 @@
     columns = lax.axis_size("col")
     source_columns = node_far[0] % columns
     node_pack = jnp.concatenate([node_coords, node_up, group_basis], axis=1)
-    gathered = lax.all_gather(node_pack[None], "col", axis=0, tiled=True)
+    received = [node_pack] + [
+        lax.ppermute(node_pack, "col", [(c, (c + shift) % columns) for c in range(columns)])
+        for shift in range(1, columns)
+    ]
+    origins = (lax.axis_index("col") - jnp.arange(columns, dtype=jnp.int32)) % columns
+    gathered = select_rows(jnp.stack(received), origins)
 
     near_local = near_list - offset
     local_norms = scaled_norms(local_points)
@@ -409,7 +414,6 @@
         near_local,
         (left_pairs, right_pairs),
         near_inner,
-        group_pack,
     )
     near_total, left_rows, right_rows = lax.optimization_barrier((near_total, left_rows, right_rows))
 
@@ -425,6 +429,7 @@
         far_local,
         (left_rows, right_rows),
         far_inner,
+        group_pack,
     )
     rows = lax.axis_size("row")
     received = [group_pack] + [

time: 136 us -> 155 us (1.14)
  the two profiles are of different devices: /device:TPU:0 before, /device:TPU:1 now
where the time goes in v14:
time: 155 us; the launch traced here: 152 us
  Pallas kernels  65.4 us (42%)
  starting transfers between devices  34.5 us (22%)
  local copies, waits for them, and re-layouts  25.6 us (17%)
  matrix products  13 us (8%)
  other arithmetic  11.9 us (8%)
  between operations  1.84 us (1%)
    pallas_call x2, Pallas kernels, near_field(): pl.pallas_call(lambda *refs: near_kernel(leaf_of, halo, *refs), grid_spec...  32 us
    pallas_call x2, Pallas kernels, far_field(): pl.pallas_call(lambda *refs: far_kernel(leaf_of, halo, *refs), grid_spec=...  24 us
    ppermute x2, starting transfers between devices, halos(): right = lax.ppermute(head, FLAT, [(i + 1, i) for i in range(ends)])  14.1 us
    unnamed x75, local copies, waits for them, and re-layouts  11.9 us
    pallas_call x1, Pallas kernels, final_field(): pl.pallas_call(final_kernel, grid_spec=pltpu.PrefetchScalarGridSpec(num_s...  9.37 us
    ppermute x7, starting transfers between devices, body(): lax.ppermute(node_pack, 'col', [(c, (c + shift) % columns) for c in range...  8.28 us
    ppermute x2, starting transfers between devices, halos(): left = lax.ppermute(tail, FLAT, [(i, i + 1) for i in range(ends)])  8.25 us
    another operation x1, local copies, waits for them, and re-layouts, body(): gathered = select_rows(jnp.stack(received), origins)  5.22 us
  transfers between devices with their start and end apart: 14, of which 1 were waited for; matrix products, arithmetic and copies ran while one was open for 25% of the time, Pallas kernels for 27%

profile of v14, /device:TPU:1, one launch (start us, length us, event | category | flops | bytes accessed | tf_op | source)
XLA Modules:
  0.0 152.4 jit_solution(1372892047833972989)
XLA Ops:
  0.0 0.9 copy.28
  0.9 0.7 fusion.55
  3.5 3.2 %fusion.2 = (f32[24,128]{1,0:T(8,128)}, bf16[24,128,128]{2,1,0:T(8,128)(2,1)S(1)}) fusion(bf16[24,256,128]{2,1,0:T(8,128)(2,1)} %bitcast.118, s32[24,128]{1,0:T(8,128)} %param.19), kind=kOutput, calls=%fused_computation.15 | convolution fusion | flops 204469248 | bytes 2383872 | tf_op jit(solution)/shard_map/bkp,bpc->bkc/dot_general | solution.py:317
  6.7 1.1 multiply_reduce_fusion.2
  7.9 1.0 multiply_convert_fusion
  9.6 2.6 %collective-permute-start = (bf16[128,512]{0,1:T(8,128)(2,1)S(1)}, bf16[128,512]{0,1:T(8,128)(2,1)}, u32[]{:S(2)}, u32[]{:S(2)}) collective-permute-start(bf16[128,512]{0,1:T(8,128)(2,1)S(1)} %pad_maximum_fusion.5), channel_id=1, source_target_pairs={{0,1},{1,2},{2,3},{3,4},{4,5},{5,6},{6,7},{7,0},{8,9},{9,10},{10,1... | collective-permute-start | bytes 393224 | tf_op jit(solution)/shard_map/ppermute | solution.py:387
  12.3 1.2 collective-permute-start.1
  14.1 2.4 %collective-permute-start.4 = (bf16[128,512]{0,1:T(8,128)(2,1)S(1)}, bf16[128,512]{0,1:T(8,128)(2,1)S(1)}, u32[]{:S(2)}, u32[]{:S(2)}) collective-permute-start(bf16[128,512]{0,1:T(8,128)(2,1)S(1)} %pad_maximum_fusion.5), channel_id=1, source_target_pairs={{0,5},{1,6},{2,7},{3,0},{4,1},{5,2},{6,3},{7,4},{8,13},{9,14},{10,... | collective-permute-start | bytes 393224 | tf_op jit(solution)/shard_map/ppermute | solution.py:387
  16.5 1.1 fusion.70
  17.6 0.7 copy-done
  18.3 0.9 fusion.71
  19.1 1.5 fusion
  21.2 1.1 and_select_fusion.1
  22.4 2.5 %pad_maximum_fusion.1 = bf16[2048,384]{1,0:T(8,128)(2,1)} fusion(bf16[2048,256]{1,0:T(8,128)(2,1)S(1)} %get-tuple-element.12, bf16[2048,128]{1,0:T(8,128)(2,1)} %get-tuple-element.16), kind=kLoop, calls=%fused_computation.16 | loop fusion | flops 3145728 | bytes 3145728 | tf_op jit(solution)/shard_map/concatenate | solution.py:17
  24.9 1.4 pad_maximum_fusion.2
  26.3 1.8 %pad_maximum_fusion.refs_2_.refs_3_ = bf16[24,128,384]{2,1,0:T(8,128)(2,1)} fusion(bf16[24,128,128]{2,1,0:T(8,128)(2,1)S(1)} %copy-done.3, bf16[24,128,256]{2,1,0:T(8,128)(2,1)S(1)} %multiply_convert_fusion), kind=kLoop, calls=%fused_computation.7 | loop fusion | flops 4718592 | bytes 4718592 | tf_op jit(solution)/shard_map/concatenate | solution.py:364
  28.1 1.5 collective-permute-start.5
  29.5 1.4 fusion.26
  31.1 0.7 copy.42
  32.1 0.7 reshape.194.refs_0_
  32.8 0.6 reshape.195.refs_0_
  34.1 11.2 %shard_map.145.refs_6_ = f32[24,256,256]{2,1,0:T(8,128)} custom-call(s32[120]{0:T(128)} %reshape.195.refs_0_, bf16[24,256,128]{2,1,0:T(8,128)(2,1)} %bitcast.119, bf16[24,256,128]{2,1,0:T(8,128)(2,1)} %bitcast.120, bf16[24,256,256]{2,1,0:T(8,128)(2,1)} %bitcast.123, f32[24,256]{1,0:T(8,128)} %reduce_sum.61.refs_4_), custom_call_target="tpu_custom_call" | custom-call | tf_op jit(solution)/shard_map/pallas_call | solution.py:186
  45.3 8.8 %shard_map.147.refs_6_ = f32[24,128,256]{2,1,0:T(8,128)} custom-call(s32[96]{0:T(128)} %reshape.194.refs_0_, bf16[24,128,128]{2,1,0:T(8,128)(2,1)} %copy-done.2, bf16[24,128,384]{2,1,0:T(8,128)(2,1)} %pad_maximum_fusion.refs_2_.refs_3_, f32[24,128]{1,0:T(8,128)} %get-tuple-element.25.refs_3_), custom_call_target="tpu_custom_call" | custom-call | tf_op jit(solution)/shard_map/pallas_call | solution.py:242
  54.1 1.0 copy.30
  55.4 1.0 copy.31
  56.6 3.6 %collective-permute-start.10 = (bf16[2048,384]{1,0:T(8,128)(2,1)}, bf16[2048,384]{1,0:T(8,128)(2,1)S(1)}, u32[]{:S(2)}, u32[]{:S(2)}) collective-permute-start(bf16[2048,384]{1,0:T(8,128)(2,1)} %pad_maximum_fusion.1), channel_id=1, source_target_pairs={{0,1},{1,2},{2,3},{3,4},{4,5},{5,6},{6,7},{7,8},{8,9},{9,10},{10,1... | collective-permute-start | bytes 4718600 | tf_op jit(solution)/shard_map/ppermute | solution.py:18
  60.3 1.0 copy.32
  61.3 0.9 copy.54
  62.2 1.9 %collective-permute-start.11 = (bf16[2048,384]{1,0:T(8,128)(2,1)}, bf16[2048,384]{1,0:T(8,128)(2,1)}, u32[]{:S(2)}, u32[]{:S(2)}) collective-permute-start(bf16[2048,384]{1,0:T(8,128)(2,1)} %pad_maximum_fusion.2), channel_id=1, source_target_pairs={{1,0},{2,1},{3,2},{4,3},{5,4},{6,5},{7,6},{8,7},{9,8},{10,9},{11,1... | collective-permute-start | bytes 4718600 | tf_op jit(solution)/shard_map/ppermute | solution.py:19
  64.2 0.9 copy.55
  65.2 0.9 copy.56
  66.3 0.9 copy.57
  67.3 0.9 copy.58
  68.2 5.2 %stack.50 = bf16[8,65536]{1,0:T(8,128)(2,1)S(1)} concatenate(bf16[1,65536]{1,0:T(2,128)(2,1)S(1)} %bitcast.136, bf16[1,65536]{1,0:T(2,128)(2,1)S(1)} %bitcast.137, bf16[1,65536]{1,0:T(2,128)(2,1)S(1)} %bitcast.138, bf16[1,65536]{1,0:T(2,128)(2,1)} %bitcast.139, bf16[1,65536]{1,0:T(2,128)(2,1)} %bitcast.140, bf16[1,65536]{1,0:T(2,128)(2,1)} %bitcast.141, ...), dimensions={0} | concatenate | bytes 2097152 | tf_op jit(solution)/shard_map/stack | solution.py:391
  74.9 0.9 multiply_reduce_fusion.3
  75.9 3.4 %collective-permute-start.9 = (bf16[128,384]{1,0:T(8,128)(2,1)S(1)}, bf16[128,384]{1,0:T(8,128)(2,1)S(1)}, u32[]{:S(2)}, u32[]{:S(2)}) collective-permute-start(bf16[128,384]{1,0:T(8,128)(2,1)S(1)} %get-tuple-element.20.refs_5_), channel_id=1, source_target_pairs={{0,24},{8,0},{16,8},{24,16},{1,25},{9,1},{17,9},{25,17},{2,26},{10... | collective-permute-start | bytes 294920 | tf_op jit(solution)/shard_map/ppermute | solution.py:436
  80.7 1.0 convolution_bitcast_fusion
  81.7 4.6 %collective-permute-start.12 = (bf16[1024,384]{1,0:T(8,128)(2,1)}, bf16[1024,384]{1,0:T(8,128)(2,1)S(1)}, u32[]{:S(2)}, u32[]{:S(2)}) collective-permute-start(bf16[1024,384]{1,0:T(8,128)(2,1)} %bitcast.21), channel_id=1, source_target_pairs={{0,1},{1,2},{2,3},{3,4},{4,5},{5,6},{6,7},{7,8},{8,9},{9,10},{10,1... | collective-permute-start | bytes 2359304 | tf_op jit(solution)/shard_map/ppermute | solution.py:18
  87.4 12.2 %collective-permute-start.13 = (bf16[1024,384]{1,0:T(8,128)(2,1)}, bf16[1024,384]{1,0:T(8,128)(2,1)S(1)}, u32[]{:S(2)}, u32[]{:S(2)}) collective-permute-start(bf16[1024,384]{1,0:T(8,128)(2,1)} %bitcast.149), channel_id=1, source_target_pairs={{1,0},{2,1},{3,2},{4,3},{5,4},{6,5},{7,6},{8,7},{9,8},{10,9},{11,1... | collective-permute-start | bytes 2359304 | tf_op jit(solution)/shard_map/ppermute | solution.py:19
  99.6 1.0 copy.61
  100.9 1.0 convolution_convert_fusion.1
  102.1 0.8 fusion.20
  102.9 1.8 %fusion.18.down_ref = bf16[128,256]{1,0:T(8,128)(2,1)} fusion(f32[128,256]{1,0:T(8,128)S(1)} %copy-done.11, bf16[128,128]{1,0:T(8,128)(2,1)S(1)} %copy-done.12, bf16[2,128,128]{2,1,0:T(8,128)(2,1)} %fusion.20, bf16[2,128,384]{2,1,0:T(8,128)(2,1)S(1)} %bitcast.148, f32[128]{0:T(128)S(1)} %get-tuple-element.28, f32[128]{0:T(128)S(1)} %copy-done.21), kind=kOutput, calls=%fused_computation.41 | convolution fusion | flops 25329664 | bytes 427008 | tf_op jit(solution)/shard_map/dot_general | solution.py:451
  104.7 1.1 copy-done.7
  105.9 20.8 %shard_map.146.near_ref = f32[24,256,256]{2,1,0:T(8,128)} custom-call(s32[120]{0:T(128)} %reshape.195.refs_0_, bf16[24,256,128]{2,1,0:T(8,128)(2,1)} %bitcast.121, bf16[8,256,384]{2,1,0:T(8,128)(2,1)} %bitcast.135, bf16[24,256,128]{2,1,0:T(8,128)(2,1)} %bitcast.122, bf16[8,256,384]{2,1,0:T(8,128)(2,1)} %bitcast.20.refs_4_, ...), custom_call_target="tpu_custom_call", output_to_operand_aliasing={{}: (6, {})} | custom-call | tf_op jit(solution)/shard_map/pallas_call | solution.py:186
  126.7 0.9 copy-done.8
  127.8 15.2 %shard_map.148.far_ref = f32[24,128,256]{2,1,0:T(8,128)} custom-call(s32[96]{0:T(128)} %reshape.194.refs_0_, bf16[24,128,128]{2,1,0:T(8,128)(2,1)} %copy-done.2, bf16[8,128,384]{2,1,0:T(8,128)(2,1)} %bitcast.144, bf16[24,128,384]{2,1,0:T(8,128)(2,1)} %pad_maximum_fusion.refs_2_.refs_3_, ...), custom_call_target="tpu_custom_call", output_to_operand_aliasing={{}: (6, {})} | custom-call | tf_op jit(solution)/shard_map/pallas_call | solution.py:242
  143.0 9.4 %shard_map.149 = bf16[24,256,256]{2,1,0:T(8,128)(2,1)} custom-call(s32[24]{0:T(128)} %rank_ref.1, bf16[24,128,128]{2,1,0:T(8,128)(2,1)} %bitcast.133, bf16[128,256]{1,0:T(8,128)(2,1)} %fusion.18.down_ref, f32[24,128,256]{2,1,0:T(8,128)} %shard_map.148.far_ref, bf16[24,256,128]{2,1,0:T(8,128)(2,1)} %bitcast.128, f32[24,256,256]{2,1,0:T(8,128)} %shard_map.146.near_ref), custom_call_target="tpu_custom_call" | custom-call | tf_op jit(solution)/shard_map/pallas_call | solution.py:285
  (108 shorter events, 9.0 us)
Async XLA Ops:
  0.0 6.7 %copy-start.24 = (s32[1,128]{1,0:T(1,128)S(1)}, s32[1,128]{1,0:T(1,128)}, u32[]{:S(2)}) copy-start(s32[1,128]{1,0:T(1,128)} %param.24) | copy-start | bytes 1540
  3.5 4.4 %copy-start.1 = (bf16[6144,256]{1,0:T(8,128)(2,1)S(1)}, bf16[6144,256]{1,0:T(8,128)(2,1)}, u32[]{:S(2)}) copy-start(bf16[6144,256]{1,0:T(8,128)(2,1)} %param.16) | copy-start | bytes 9437188
  3.5 4.4 %copy-start.4 = (bf16[6144,128]{1,0:T(8,128)(2,1)S(1)}, bf16[6144,128]{1,0:T(8,128)(2,1)}, u32[]{:S(2)}) copy-start(bf16[6144,128]{1,0:T(8,128)(2,1)} %param.17) | copy-start | bytes 4718596
  6.7 1.1 copy-start.2
  7.8 1.8 %copy-start.13 = (bf16[128,128]{0,1:T(8,128)(2,1)}, bf16[128,128]{0,1:T(8,128)(2,1)S(1)}, u32[]{:S(2)}) copy-start(bf16[128,128]{0,1:T(8,128)(2,1)S(1)} %get-tuple-element.22) | copy-start | bytes 98308
  7.9 1.1 copy-start.6
  9.6 18.4 %collective-permute-start = (bf16[128,512]{0,1:T(8,128)(2,1)S(1)}, bf16[128,512]{0,1:T(8,128)(2,1)}, u32[]{:S(2)}, u32[]{:S(2)}) collective-permute-start(bf16[128,512]{0,1:T(8,128)(2,1)S(1)} %pad_maximum_fusion.5), channel_id=1, source_target_pairs={{0,1},{1,2},{2,3},{3,4},{4,5},{5,6},{6,7},{7,0},{8,9},{9,10},{10,1... | collective-permute-start | bytes 393224 | tf_op jit(solution)/shard_map/ppermute | solution.py:387
  12.3 17.3 %collective-permute-start.1 = (bf16[128,512]{0,1:T(8,128)(2,1)S(1)}, bf16[128,512]{0,1:T(8,128)(2,1)}, u32[]{:S(2)}, u32[]{:S(2)}) collective-permute-start(bf16[128,512]{0,1:T(8,128)(2,1)S(1)} %pad_maximum_fusion.5), channel_id=1, source_target_pairs={{0,2},{1,3},{2,4},{3,5},{4,6},{5,7},{6,0},{7,1},{8,10},{9,11},{10,... | collective-permute-start | bytes 393224 | tf_op jit(solution)/shard_map/ppermute | solution.py:387
  13.5 43.1 %collective-permute-start.2 = (bf16[128,512]{0,1:T(8,128)(2,1)S(1)}, bf16[128,512]{0,1:T(8,128)(2,1)}, u32[]{:S(2)}, u32[]{:S(2)}) collective-permute-start(bf16[128,512]{0,1:T(8,128)(2,1)S(1)} %pad_maximum_fusion.5), channel_id=1, source_target_pairs={{0,3},{1,4},{2,5},{3,6},{4,7},{5,0},{6,1},{7,2},{8,11},{9,12},{10,... | collective-permute-start | bytes 393224 | tf_op jit(solution)/shard_map/ppermute | solution.py:387
  13.9 48.3 %collective-permute-start.3 = (bf16[128,512]{0,1:T(8,128)(2,1)S(1)}, bf16[128,512]{0,1:T(8,128)(2,1)S(1)}, u32[]{:S(2)}, u32[]{:S(2)}) collective-permute-start(bf16[128,512]{0,1:T(8,128)(2,1)S(1)} %pad_maximum_fusion.5), channel_id=1, source_target_pairs={{0,4},{1,5},{2,6},{3,7},{4,0},{5,1},{6,2},{7,3},{8,12},{9,13},{10,... | collective-permute-start | bytes 393224 | tf_op jit(solution)/shard_map/ppermute | solution.py:387
  14.1 51.0 %collective-permute-start.4 = (bf16[128,512]{0,1:T(8,128)(2,1)S(1)}, bf16[128,512]{0,1:T(8,128)(2,1)S(1)}, u32[]{:S(2)}, u32[]{:S(2)}) collective-permute-start(bf16[128,512]{0,1:T(8,128)(2,1)S(1)} %pad_maximum_fusion.5), channel_id=1, source_target_pairs={{0,5},{1,6},{2,7},{3,0},{4,1},{5,2},{6,3},{7,4},{8,13},{9,14},{10,... | collective-permute-start | bytes 393224 | tf_op jit(solution)/shard_map/ppermute | solution.py:387
  16.5 1.8 %copy-start = (bf16[6144,128]{1,0:T(8,128)(2,1)S(1)}, bf16[6144,128]{1,0:T(8,128)(2,1)}, u32[]{:S(2)}) copy-start(bf16[6144,128]{1,0:T(8,128)(2,1)} %param.15) | copy-start | bytes 4718596
  18.2 2.4 %copy-start.25 = (s32[1,4]{1,0:T(1,128)S(1)}, s32[1,4]{1,0:T(1,128)}, u32[]{:S(2)}) copy-start(s32[1,4]{1,0:T(1,128)} %param.25) | copy-start | bytes 52
  18.2 4.1 %copy-start.22 = (s32[24,4]{0,1:T(4,128)S(1)}, s32[24,4]{0,1:T(4,128)}, u32[]{:S(2)}) copy-start(s32[24,4]{0,1:T(4,128)} %param.21) | copy-start | bytes 1156
  18.3 4.1 %copy-start.20 = (s32[24,5]{0,1:T(8,128)S(1)}, s32[24,5]{0,1:T(8,128)}, u32[]{:S(2)}) copy-start(s32[24,5]{0,1:T(8,128)} %param.20) | copy-start | bytes 1444
  22.4 2.5 %copy-start.5 = (bf16[2048,256]{1,0:T(8,128)(2,1)S(1)}, bf16[2048,256]{1,0:T(8,128)(2,1)}, u32[]{:S(2)}) copy-start(bf16[2048,256]{1,0:T(8,128)(2,1)} %get-tuple-element.11) | copy-start | bytes 3145732
  24.9 1.4 copy-start.3
  28.1 3.0 %copy-start.14 = (bf16[128,128]{0,1:T(8,128)(2,1)S(1)}, bf16[128,128]{0,1:T(8,128)(2,1)}, u32[]{:S(2)}) copy-start(bf16[128,128]{0,1:T(8,128)(2,1)} %copy-done.13) | copy-start | bytes 98308
  28.1 5.4 %copy-start.16 = (f32[6144]{0:T(1024)S(1)}, f32[6144]{0:T(1024)}, u32[]{:S(2)}) copy-start(f32[6144]{0:T(1024)} %fusion) | copy-start | bytes 73732
  28.1 38.1 %collective-permute-start.5 = (bf16[128,512]{0,1:T(8,128)(2,1)S(1)}, bf16[128,512]{0,1:T(8,128)(2,1)S(1)}, u32[]{:S(2)}, u32[]{:S(2)}) collective-permute-start(bf16[128,512]{0,1:T(8,128)(2,1)S(1)} %pad_maximum_fusion.5), channel_id=1, source_target_pairs={{0,6},{1,7},{2,0},{3,1},{4,2},{5,3},{6,4},{7,5},{8,14},{9,15},{10,... | collective-permute-start | bytes 393224 | tf_op jit(solution)/shard_map/ppermute | solution.py:387
  29.5 37.6 %collective-permute-start.6 = (bf16[128,512]{0,1:T(8,128)(2,1)S(1)}, bf16[128,512]{0,1:T(8,128)(2,1)S(1)}, u32[]{:S(2)}, u32[]{:S(2)}) collective-permute-start(bf16[128,512]{0,1:T(8,128)(2,1)S(1)} %pad_maximum_fusion.5), channel_id=1, source_target_pairs={{0,7},{1,0},{2,1},{3,2},{4,3},{5,4},{6,5},{7,6},{8,15},{9,8},{10,9... | collective-permute-start | bytes 393224 | tf_op jit(solution)/shard_map/ppermute | solution.py:387
  56.6 48.1 %collective-permute-start.10 = (bf16[2048,384]{1,0:T(8,128)(2,1)}, bf16[2048,384]{1,0:T(8,128)(2,1)S(1)}, u32[]{:S(2)}, u32[]{:S(2)}) collective-permute-start(bf16[2048,384]{1,0:T(8,128)(2,1)} %pad_maximum_fusion.1), channel_id=1, source_target_pairs={{0,1},{1,2},{2,3},{3,4},{4,5},{5,6},{6,7},{7,8},{8,9},{9,10},{10,1... | collective-permute-start | bytes 4718600 | tf_op jit(solution)/shard_map/ppermute | solution.py:18
  62.2 42.5 %collective-permute-start.11 = (bf16[2048,384]{1,0:T(8,128)(2,1)}, bf16[2048,384]{1,0:T(8,128)(2,1)}, u32[]{:S(2)}, u32[]{:S(2)}) collective-permute-start(bf16[2048,384]{1,0:T(8,128)(2,1)} %pad_maximum_fusion.2), channel_id=1, source_target_pairs={{1,0},{2,1},{3,2},{4,3},{5,4},{6,5},{7,6},{8,7},{9,8},{10,9},{11,1... | collective-permute-start | bytes 4718600 | tf_op jit(solution)/shard_map/ppermute | solution.py:19
  73.9 0.7 copy-start.21
  73.9 1.0 copy-start.26
  74.0 5.9 %copy-start.23 = (s32[4]{0:T(128)S(1)}, s32[4]{0:T(128)}, u32[]{:S(2)}) copy-start(s32[4]{0:T(128)} %and_select_fusion) | copy-start | bytes 52
  74.6 6.1 %copy-start.19 = (bf16[128,128]{1,0:T(8,128)(2,1)S(1)}, bf16[128,128]{1,0:T(8,128)(2,1)}, u32[]{:S(2)}) copy-start(bf16[128,128]{1,0:T(8,128)(2,1)} %copy.42) | copy-start | bytes 98308
  74.6 6.1 %copy-start.29 = (f32[128]{0:T(128)S(1)}, f32[128]{0:T(128)}, u32[]{:S(2)}) copy-start(f32[128]{0:T(128)} %get-tuple-element.21) | copy-start | bytes 1540
  75.8 4.8 %copy-start.17 = (bf16[128,128]{1,0:T(8,128)(2,1)}, bf16[128,128]{1,0:T(8,128)(2,1)S(1)}, u32[]{:S(2)}) copy-start(bf16[128,128]{1,0:T(8,128)(2,1)S(1)} %get-tuple-element.24) | copy-start | bytes 98308
  75.9 25.0 %copy-start.10 = (bf16[128,384]{1,0:T(8,128)(2,1)}, bf16[128,384]{1,0:T(8,128)(2,1)S(1)}, u32[]{:S(2)}) copy-start(bf16[128,384]{1,0:T(8,128)(2,1)S(1)} %get-tuple-element.20.refs_5_) | copy-start | bytes 294916
  75.9 5.9 %collective-permute-start.9 = (bf16[128,384]{1,0:T(8,128)(2,1)S(1)}, bf16[128,384]{1,0:T(8,128)(2,1)S(1)}, u32[]{:S(2)}, u32[]{:S(2)}) collective-permute-start(bf16[128,384]{1,0:T(8,128)(2,1)S(1)} %get-tuple-element.20.refs_5_), channel_id=1, source_target_pairs={{0,24},{8,0},{16,8},{24,16},{1,25},{9,1},{17,9},{25,17},{2,26},{10... | collective-permute-start | bytes 294920 | tf_op jit(solution)/shard_map/ppermute | solution.py:436
  79.3 7.5 %collective-permute-start.8 = (bf16[128,384]{1,0:T(8,128)(2,1)S(1)}, bf16[128,384]{1,0:T(8,128)(2,1)S(1)}, u32[]{:S(2)}, u32[]{:S(2)}) collective-permute-start(bf16[128,384]{1,0:T(8,128)(2,1)S(1)} %get-tuple-element.20.refs_5_), channel_id=1, source_target_pairs={{0,16},{8,24},{16,0},{24,8},{1,17},{9,25},{17,1},{25,9},{2,18},{10... | collective-permute-start | bytes 294920 | tf_op jit(solution)/shard_map/ppermute | solution.py:436
  79.3 21.4 %collective-permute-start.7 = (bf16[128,384]{1,0:T(8,128)(2,1)S(1)}, bf16[128,384]{1,0:T(8,128)(2,1)S(1)}, u32[]{:S(2)}, u32[]{:S(2)}) collective-permute-start(bf16[128,384]{1,0:T(8,128)(2,1)S(1)} %get-tuple-element.20.refs_5_), channel_id=1, source_target_pairs={{0,8},{8,16},{16,24},{24,0},{1,9},{9,17},{17,25},{25,1},{2,10},{10... | collective-permute-start | bytes 294920 | tf_op jit(solution)/shard_map/ppermute | solution.py:436
  79.9 21.0 %copy-start.27 = (s32[2]{0:T(128)S(1)}, s32[2]{0:T(128)}, u32[]{:S(2)}) copy-start(s32[2]{0:T(128)} %and_select_fusion.1) | copy-start | bytes 28
  81.7 44.9 %collective-permute-start.12 = (bf16[1024,384]{1,0:T(8,128)(2,1)}, bf16[1024,384]{1,0:T(8,128)(2,1)S(1)}, u32[]{:S(2)}, u32[]{:S(2)}) collective-permute-start(bf16[1024,384]{1,0:T(8,128)(2,1)} %bitcast.21), channel_id=1, source_target_pairs={{0,1},{1,2},{2,3},{3,4},{4,5},{5,6},{6,7},{7,8},{8,9},{9,10},{10,1... | collective-permute-start | bytes 2359304 | tf_op jit(solution)/shard_map/ppermute | solution.py:18
  86.7 0.6 copy-start.15
  87.4 39.3 %collective-permute-start.13 = (bf16[1024,384]{1,0:T(8,128)(2,1)}, bf16[1024,384]{1,0:T(8,128)(2,1)S(1)}, u32[]{:S(2)}, u32[]{:S(2)}) collective-permute-start(bf16[1024,384]{1,0:T(8,128)(2,1)} %bitcast.149), channel_id=1, source_target_pairs={{1,0},{2,1},{3,2},{4,3},{5,4},{6,5},{7,6},{8,7},{9,8},{10,9},{11,1... | collective-permute-start | bytes 2359304 | tf_op jit(solution)/shard_map/ppermute | solution.py:19
  100.9 1.2 copy-start.18
  100.9 1.2 copy-start.28
  100.9 2.0 %copy-start.11 = (f32[128,256]{1,0:T(8,128)S(1)}, f32[128,256]{1,0:T(8,128)}, u32[]{:S(2)}) copy-start(f32[128,256]{1,0:T(8,128)} %convolution_bitcast_fusion) | copy-start | bytes 393220
  100.9 2.0 %copy-start.12 = (bf16[128,128]{1,0:T(8,128)(2,1)S(1)}, bf16[128,128]{1,0:T(8,128)(2,1)}, u32[]{:S(2)}) copy-start(bf16[128,128]{1,0:T(8,128)(2,1)} %param.26) | copy-start | bytes 98308
  104.7 1.1 copy-start.7
  126.7 0.9 copy-start.8
  126.7 1.1 copy-start.9

commit v15 on v14

--- a/solution.py
+++ b/solution.py
@@ -383,12 +383,7 @@
     columns = lax.axis_size("col")
     source_columns = node_far[0] % columns
     node_pack = jnp.concatenate([node_coords, node_up, group_basis], axis=1)
-    received = [node_pack] + [
-        lax.ppermute(node_pack, "col", [(c, (c + shift) % columns) for c in range(columns)])
-        for shift in range(1, columns)
-    ]
-    origins = (lax.axis_index("col") - jnp.arange(columns, dtype=jnp.int32)) % columns
-    gathered = select_rows(jnp.stack(received), origins)
+    gathered = lax.all_gather(node_pack[None], "col", axis=0, tiled=True)
 
     near_local = near_list - offset
     local_norms = scaled_norms(local_points)

time: 155 us -> 139 us (0.90)
  the two profiles are of different devices: /device:TPU:1 before, /device:TPU:13 now
where the time goes in v15:
time: 139 us; the launch traced here: 137 us
  Pallas kernels  65.8 us (47%)
  starting transfers between devices  16 us (12%)
  between operations  15.1 us (11%)
  waiting for transfers between devices  13.3 us (10%)
  matrix products  9.2 us (7%)
  local copies, waits for them, and re-layouts  8.75 us (6%)
  other arithmetic  8.52 us (6%)
    pallas_call x2, Pallas kernels, near_field(): pl.pallas_call(lambda *refs: near_kernel(leaf_of, halo, *refs), grid_spec...  32.2 us
    pallas_call x2, Pallas kernels, far_field(): pl.pallas_call(lambda *refs: far_kernel(leaf_of, halo, *refs), grid_spec=...  24.2 us
    ppermute x2, waiting for transfers between devices, halos(): right = lax.ppermute(head, FLAT, [(i + 1, i) for i in range(ends)])  13.3 us
    pallas_call x1, Pallas kernels, final_field(): pl.pallas_call(final_kernel, grid_spec=pltpu.PrefetchScalarGridSpec(num_s...  9.37 us
    ppermute x2, starting transfers between devices, halos(): left = lax.ppermute(tail, FLAT, [(i, i + 1) for i in range(ends)])  7.3 us
    ppermute x3, starting transfers between devices, body(): lax.ppermute(group_pack, 'row', [(r, (r + shift) % rows) for r in range(r...  4.72 us
    unnamed x40, local copies, waits for them, and re-layouts  4.65 us
    ppermute x2, starting transfers between devices, halos(): right = lax.ppermute(head, FLAT, [(i + 1, i) for i in range(ends)])  3.96 us
  transfers between devices with their start and end apart: 8, of which 1 were waited for; matrix products, arithmetic and copies ran while one was open for 9% of the time, Pallas kernels for 41%

profile of v15, /device:TPU:13, one launch (start us, length us, event | category | flops | bytes accessed | tf_op | source)
XLA Modules:
  0.0 136.7 jit_solution(12572044983344688886)
XLA Ops:
  6.5 0.9 copy.28
  7.4 0.7 fusion.55
  9.5 3.2 %fusion.2 = (f32[24,128]{1,0:T(8,128)}, bf16[24,128,128]{2,1,0:T(8,128)(2,1)S(1)}) fusion(bf16[24,256,128]{2,1,0:T(8,128)(2,1)} %bitcast.99, s32[24,128]{1,0:T(8,128)} %param.19), kind=kOutput, calls=%fused_computation.14 | convolution fusion | flops 204469248 | bytes 2383872 | tf_op jit(solution)/shard_map/bkp,bpc->bkc/dot_general | solution.py:317
  12.7 0.6 multiply_reduce_fusion.2
  13.3 0.3 copy-done.2
  13.6 1.0 multiply_convert_fusion
  14.6 0.2 copy-done.6
  14.8 0.6 fusion.23
  15.4 0.7 pad_maximum_fusion.5
  16.1 1.8 %fusion.67 = (bf16[2048,256]{1,0:T(8,128)(2,1)S(1)}, bf16[2048,256]{1,0:T(8,128)(2,1)S(1)}) fusion(bf16[6144,256]{1,0:T(8,128)(2,1)} %param.16), kind=kLoop, calls=%fused_computation.107 | loop fusion | bytes 4194304 | tf_op jit(solution)/shard_map/slice | solution.py:16
  17.9 0.2 copy-done
  18.2 1.4 %pad_maximum_fusion.1 = bf16[2048,384]{1,0:T(8,128)(2,1)} fusion(bf16[2048,256]{1,0:T(8,128)(2,1)S(1)} %get-tuple-element.12, bf16[2048,128]{1,0:T(8,128)(2,1)S(1)} %get-tuple-element.16), kind=kLoop, calls=%fused_computation.15 | loop fusion | flops 3145728 | bytes 3145728 | tf_op jit(solution)/shard_map/concatenate | solution.py:17
  19.6 3.7 %collective-permute-start.3 = (bf16[2048,384]{1,0:T(8,128)(2,1)}, bf16[2048,384]{1,0:T(8,128)(2,1)}, u32[]{:S(2)}, u32[]{:S(2)}) collective-permute-start(bf16[2048,384]{1,0:T(8,128)(2,1)} %pad_maximum_fusion.1), channel_id=1, source_target_pairs={{0,1},{1,2},{2,3},{3,4},{4,5},{5,6},{6,7},{7,8},{8,9},{9,10},{10,1... | collective-permute-start | bytes 4718600 | tf_op jit(solution)/shard_map/ppermute | solution.py:18
  23.2 1.4 pad_maximum_fusion.2
  24.6 2.0 %collective-permute-start.4 = (bf16[2048,384]{1,0:T(8,128)(2,1)}, bf16[2048,384]{1,0:T(8,128)(2,1)}, u32[]{:S(2)}, u32[]{:S(2)}) collective-permute-start(bf16[2048,384]{1,0:T(8,128)(2,1)} %pad_maximum_fusion.2), channel_id=1, source_target_pairs={{1,0},{2,1},{3,2},{4,3},{5,4},{6,5},{7,6},{8,7},{9,8},{10,9},{11,1... | collective-permute-start | bytes 4718600 | tf_op jit(solution)/shard_map/ppermute | solution.py:19
  26.7 1.4 %fusion.26 = (bf16[8,128,384]{2,1,0:T(8,128)(2,1)}, bf16[8,128,384]{2,1,0:T(8,128)(2,1)}) fusion(bf16[24,128,256]{2,1,0:T(8,128)(2,1)S(1)} %multiply_convert_fusion, bf16[24,128,128]{2,1,0:T(8,128)(2,1)S(1)} %copy-done.3), kind=kLoop, calls=%fused_computation.49 | loop fusion | flops 3145728 | bytes 3932160 | tf_op jit(solution)/shard_map/concatenate | solution.py:364
  28.1 3.6 %collective-permute-start.5 = (bf16[1024,384]{1,0:T(8,128)(2,1)}, bf16[1024,384]{1,0:T(8,128)(2,1)}, u32[]{:S(2)}, u32[]{:S(2)}) collective-permute-start(bf16[1024,384]{1,0:T(8,128)(2,1)} %bitcast.20), channel_id=1, source_target_pairs={{0,1},{1,2},{2,3},{3,4},{4,5},{5,6},{6,7},{7,8},{8,9},{9,10},{10,1... | collective-permute-start | bytes 2359304 | tf_op jit(solution)/shard_map/ppermute | solution.py:18
  31.7 1.9 %collective-permute-start.6 = (bf16[1024,384]{1,0:T(8,128)(2,1)}, bf16[1024,384]{1,0:T(8,128)(2,1)}, u32[]{:S(2)}, u32[]{:S(2)}) collective-permute-start(bf16[1024,384]{1,0:T(8,128)(2,1)} %bitcast.21), channel_id=1, source_target_pairs={{1,0},{2,1},{3,2},{4,3},{5,4},{6,5},{7,6},{8,7},{9,8},{10,9},{11,1... | collective-permute-start | bytes 2359304 | tf_op jit(solution)/shard_map/ppermute | solution.py:19
  33.9 0.7 reshape.158.refs_0_
  34.6 0.6 reshape.159.refs_0_
  35.2 0.9 fusion
  36.1 0.6 reduce_sum.61.refs_4_
  36.7 11.4 %shard_map.145.refs_6_ = f32[24,256,256]{2,1,0:T(8,128)} custom-call(s32[120]{0:T(128)} %reshape.159.refs_0_, bf16[24,256,128]{2,1,0:T(8,128)(2,1)} %bitcast.100, bf16[24,256,128]{2,1,0:T(8,128)(2,1)} %bitcast.101, bf16[24,256,256]{2,1,0:T(8,128)(2,1)} %bitcast.104, f32[24,256]{1,0:T(8,128)} %reduce_sum.61.refs_4_), custom_call_target="tpu_custom_call" | custom-call | tf_op jit(solution)/shard_map/pallas_call | solution.py:186
  48.2 1.8 %pad_maximum_fusion.refs_2_.refs_3_ = bf16[24,128,384]{2,1,0:T(8,128)(2,1)} fusion(bf16[24,128,128]{2,1,0:T(8,128)(2,1)S(1)} %copy-done.4, bf16[24,128,256]{2,1,0:T(8,128)(2,1)S(1)} %multiply_convert_fusion), kind=kLoop, calls=%fused_computation.6 | loop fusion | flops 4718592 | bytes 4718592 | tf_op jit(solution)/shard_map/concatenate | solution.py:364
  49.9 8.9 %shard_map.147.refs_6_ = f32[24,128,256]{2,1,0:T(8,128)} custom-call(s32[96]{0:T(128)} %reshape.158.refs_0_, bf16[24,128,128]{2,1,0:T(8,128)(2,1)} %copy-done.2, bf16[24,128,384]{2,1,0:T(8,128)(2,1)} %pad_maximum_fusion.refs_2_.refs_3_, f32[24,128]{1,0:T(8,128)} %get-tuple-element.25.refs_3_), custom_call_target="tpu_custom_call" | custom-call | tf_op jit(solution)/shard_map/pallas_call | solution.py:242
  59.0 13.3 %collective-permute-done.4 = bf16[2048,384]{1,0:T(8,128)(2,1)} collective-permute-done((bf16[2048,384]{1,0:T(8,128)(2,1)}, bf16[2048,384]{1,0:T(8,128)(2,1)}, u32[]{:S(2)}, u32[]{:S(2)}) %collective-permute-start.4) | collective-permute-done | bytes 1572896 | tf_op jit(solution)/shard_map/ppermute | solution.py:19
  72.2 20.8 %shard_map.146.near_ref = f32[24,256,256]{2,1,0:T(8,128)} custom-call(s32[120]{0:T(128)} %reshape.159.refs_0_, bf16[24,256,128]{2,1,0:T(8,128)(2,1)} %bitcast.102, bf16[8,256,384]{2,1,0:T(8,128)(2,1)} %bitcast.18.refs_2_, bf16[24,256,128]{2,1,0:T(8,128)(2,1)} %bitcast.103, bf16[8,256,384]{2,1,0:T(8,128)(2,1)} %bitcast.19.refs_4_, ...), custom_call_target="tpu_custom_call", output_to_operand_aliasing={{}: (6, {})} | custom-call | tf_op jit(solution)/shard_map/pallas_call | solution.py:186
  93.1 1.5 %copy.43 = bf16[64,8,8,128]{3,2,1,0:T(8,128)(2,1)S(1)} copy(bf16[64,8,8,128]{3,1,2,0:T(8,128)(2,1)} %bitcast.116) | data formatting | bytes 2097152
  94.7 0.3 copy.42
  95.0 0.2 copy.40
  95.3 0.4 multiply_reduce_fusion.3
  95.6 0.2 fusion.19
  96.0 2.5 %collective-permute-start.1 = (bf16[128,384]{1,0:T(8,128)(2,1)S(1)}, bf16[128,384]{1,0:T(8,128)(2,1)S(1)}, u32[]{:S(2)}, u32[]{:S(2)}) collective-permute-start(bf16[128,384]{1,0:T(8,128)(2,1)S(1)} %get-tuple-element.20.refs_5_), channel_id=1, source_target_pairs={{0,16},{8,24},{16,0},{24,8},{1,17},{9,25},{17,1},{25,9},{2,18},{10... | collective-permute-start | bytes 294920 | tf_op jit(solution)/shard_map/ppermute | solution.py:431
  98.4 2.2 %collective-permute-start = (bf16[128,384]{1,0:T(8,128)(2,1)S(1)}, bf16[128,384]{1,0:T(8,128)(2,1)S(1)}, u32[]{:S(2)}, u32[]{:S(2)}) collective-permute-start(bf16[128,384]{1,0:T(8,128)(2,1)S(1)} %get-tuple-element.20.refs_5_), channel_id=1, source_target_pairs={{0,8},{8,16},{16,24},{24,0},{1,9},{9,17},{17,25},{25,1},{2,10},{10... | collective-permute-start | bytes 294920 | tf_op jit(solution)/shard_map/ppermute | solution.py:431
  100.6 0.3 copy.51
  100.9 0.4 convolution_convert_fusion.1
  101.3 0.3 fusion.10
  101.6 0.1 multiply_reduce_fusion
  101.7 0.2 copy.44
  101.9 15.2 %shard_map.148.far_ref = f32[24,128,256]{2,1,0:T(8,128)} custom-call(s32[96]{0:T(128)} %reshape.158.refs_0_, bf16[24,128,128]{2,1,0:T(8,128)(2,1)} %copy-done.2, bf16[8,128,384]{2,1,0:T(8,128)(2,1)} %bitcast.22.refs_2_, bf16[24,128,384]{2,1,0:T(8,128)(2,1)} %pad_maximum_fusion.refs_2_.refs_3_, ...), custom_call_target="tpu_custom_call", output_to_operand_aliasing={{}: (6, {})} | custom-call | tf_op jit(solution)/shard_map/pallas_call | solution.py:242
  117.2 0.4 convolution_bitcast_fusion
  117.6 0.2 copy.47
  117.7 0.2 copy.46
  117.9 0.2 copy.45
  118.1 1.0 convolution_convert_fusion
  119.3 0.2 fusion.20
  119.5 1.0 fusion.18.down_ref
  120.4 9.4 %shard_map.149 = bf16[24,256,256]{2,1,0:T(8,128)(2,1)} custom-call(s32[24]{0:T(128)} %rank_ref.1, bf16[24,128,128]{2,1,0:T(8,128)(2,1)} %bitcast.114, bf16[128,256]{1,0:T(8,128)(2,1)} %fusion.18.down_ref, f32[24,128,256]{2,1,0:T(8,128)} %shard_map.148.far_ref, bf16[24,256,128]{2,1,0:T(8,128)(2,1)} %bitcast.109, f32[24,256,256]{2,1,0:T(8,128)} %shard_map.146.near_ref), custom_call_target="tpu_custom_call" | custom-call | tf_op jit(solution)/shard_map/pallas_call | solution.py:285
  (51 shorter events, 0.8 us)
Async XLA Ops:
  6.5 86.5 %all-gather.3.cloned.1.call-start = ((), (), s32[]{:S(2)}) async-start(), calls=%async_computation | async-start | bytes 1179648 | tf_op jit(solution)/shard_map/all_gather | solution.py:386
  6.5 6.2 %copy-start.11 = (s32[1,128]{1,0:T(1,128)S(1)}, s32[1,128]{1,0:T(1,128)}, u32[]{:S(2)}) copy-start(s32[1,128]{1,0:T(1,128)} %param.24) | copy-start | bytes 1540
  9.5 4.2 %copy-start.1 = (bf16[6144,256]{1,0:T(8,128)(2,1)S(1)}, bf16[6144,256]{1,0:T(8,128)(2,1)}, u32[]{:S(2)}) copy-start(bf16[6144,256]{1,0:T(8,128)(2,1)} %param.16) | copy-start | bytes 9437188
  9.5 4.1 %copy-start.5 = (bf16[6144,128]{1,0:T(8,128)(2,1)S(1)}, bf16[6144,128]{1,0:T(8,128)(2,1)}, u32[]{:S(2)}) copy-start(bf16[6144,128]{1,0:T(8,128)(2,1)} %param.17) | copy-start | bytes 4718596
  12.7 0.9 copy-start.2
  13.6 1.1 copy-start.6
  16.1 2.0 %copy-start = (bf16[6144,128]{1,0:T(8,128)(2,1)S(1)}, bf16[6144,128]{1,0:T(8,128)(2,1)}, u32[]{:S(2)}) copy-start(bf16[6144,128]{1,0:T(8,128)(2,1)} %param.15) | copy-start | bytes 4718596
  19.6 39.4 %collective-permute-start.3 = (bf16[2048,384]{1,0:T(8,128)(2,1)}, bf16[2048,384]{1,0:T(8,128)(2,1)}, u32[]{:S(2)}, u32[]{:S(2)}) collective-permute-start(bf16[2048,384]{1,0:T(8,128)(2,1)} %pad_maximum_fusion.1), channel_id=1, source_target_pairs={{0,1},{1,2},{2,3},{3,4},{4,5},{5,6},{6,7},{7,8},{8,9},{9,10},{10,1... | collective-permute-start | bytes 4718600 | tf_op jit(solution)/shard_map/ppermute | solution.py:18
  23.2 3.4 %copy-start.3 = (bf16[24,128,128]{2,1,0:T(8,128)(2,1)S(1)}, bf16[24,128,128]{2,1,0:T(8,128)(2,1)}, u32[]{:S(2)}) copy-start(bf16[24,128,128]{2,1,0:T(8,128)(2,1)} %copy-done.2) | copy-start | bytes 2359300
  24.6 9.2 %copy-start.10 = (s32[24,4]{0,1:T(4,128)S(1)}, s32[24,4]{0,1:T(4,128)}, u32[]{:S(2)}) copy-start(s32[24,4]{0,1:T(4,128)} %param.21) | copy-start | bytes 1156
  24.6 9.9 %copy-start.9 = (s32[24,5]{0,1:T(8,128)S(1)}, s32[24,5]{0,1:T(8,128)}, u32[]{:S(2)}) copy-start(s32[24,5]{0,1:T(8,128)} %param.20) | copy-start | bytes 1444
  24.6 47.6 %collective-permute-start.4 = (bf16[2048,384]{1,0:T(8,128)(2,1)}, bf16[2048,384]{1,0:T(8,128)(2,1)}, u32[]{:S(2)}, u32[]{:S(2)}) collective-permute-start(bf16[2048,384]{1,0:T(8,128)(2,1)} %pad_maximum_fusion.2), channel_id=1, source_target_pairs={{1,0},{2,1},{3,2},{4,3},{5,4},{6,5},{7,6},{8,7},{9,8},{10,9},{11,1... | collective-permute-start | bytes 4718600 | tf_op jit(solution)/shard_map/ppermute | solution.py:19
  28.1 65.0 %collective-permute-start.5 = (bf16[1024,384]{1,0:T(8,128)(2,1)}, bf16[1024,384]{1,0:T(8,128)(2,1)}, u32[]{:S(2)}, u32[]{:S(2)}) collective-permute-start(bf16[1024,384]{1,0:T(8,128)(2,1)} %bitcast.20), channel_id=1, source_target_pairs={{0,1},{1,2},{2,3},{3,4},{4,5},{5,6},{6,7},{7,8},{8,9},{9,10},{10,1... | collective-permute-start | bytes 2359304 | tf_op jit(solution)/shard_map/ppermute | solution.py:18
  31.7 61.3 %collective-permute-start.6 = (bf16[1024,384]{1,0:T(8,128)(2,1)}, bf16[1024,384]{1,0:T(8,128)(2,1)}, u32[]{:S(2)}, u32[]{:S(2)}) collective-permute-start(bf16[1024,384]{1,0:T(8,128)(2,1)} %bitcast.21), channel_id=1, source_target_pairs={{1,0},{2,1},{3,2},{4,3},{5,4},{6,5},{7,6},{8,7},{9,8},{10,9},{11,1... | collective-permute-start | bytes 2359304 | tf_op jit(solution)/shard_map/ppermute | solution.py:19
  36.7 11.4 %copy-start.4 = (bf16[24,128,128]{2,1,0:T(8,128)(2,1)S(1)}, bf16[24,128,128]{2,1,0:T(8,128)(2,1)}, u32[]{:S(2)}) copy-start(bf16[24,128,128]{2,1,0:T(8,128)(2,1)} %copy-done.2) | copy-start | bytes 2359300
  49.9 9.0 %copy-start.12 = (s32[1,4]{1,0:T(1,128)S(1)}, s32[1,4]{1,0:T(1,128)}, u32[]{:S(2)}) copy-start(s32[1,4]{1,0:T(1,128)} %param.25) | copy-start | bytes 52
  49.9 9.0 %copy-start.13 = (s32[1,2]{1,0:T(1,128)S(1)}, s32[1,2]{1,0:T(1,128)}, u32[]{:S(2)}) copy-start(s32[1,2]{1,0:T(1,128)} %param.29) | copy-start | bytes 28
  94.6 0.7 copy-start.14
  95.9 6.0 %copy-start.7 = (bf16[128,384]{1,0:T(8,128)(2,1)}, bf16[128,384]{1,0:T(8,128)(2,1)S(1)}, u32[]{:S(2)}) copy-start(bf16[128,384]{1,0:T(8,128)(2,1)S(1)} %get-tuple-element.20.refs_5_) | copy-start | bytes 294916
  95.9 21.6 %collective-permute-start.2 = (bf16[128,384]{1,0:T(8,128)(2,1)S(1)}, bf16[128,384]{1,0:T(8,128)(2,1)S(1)}, u32[]{:S(2)}, u32[]{:S(2)}) collective-permute-start(bf16[128,384]{1,0:T(8,128)(2,1)S(1)} %get-tuple-element.20.refs_5_), channel_id=1, source_target_pairs={{0,24},{8,0},{16,8},{24,16},{1,25},{9,1},{17,9},{25,17},{2,26},{10... | collective-permute-start | bytes 294920 | tf_op jit(solution)/shard_map/ppermute | solution.py:431
  96.0 21.8 %collective-permute-start.1 = (bf16[128,384]{1,0:T(8,128)(2,1)S(1)}, bf16[128,384]{1,0:T(8,128)(2,1)S(1)}, u32[]{:S(2)}, u32[]{:S(2)}) collective-permute-start(bf16[128,384]{1,0:T(8,128)(2,1)S(1)} %get-tuple-element.20.refs_5_), channel_id=1, source_target_pairs={{0,16},{8,24},{16,0},{24,8},{1,17},{9,25},{17,1},{25,9},{2,18},{10... | collective-permute-start | bytes 294920 | tf_op jit(solution)/shard_map/ppermute | solution.py:431
  98.4 19.5 %collective-permute-start = (bf16[128,384]{1,0:T(8,128)(2,1)S(1)}, bf16[128,384]{1,0:T(8,128)(2,1)S(1)}, u32[]{:S(2)}, u32[]{:S(2)}) collective-permute-start(bf16[128,384]{1,0:T(8,128)(2,1)S(1)} %get-tuple-element.20.refs_5_), channel_id=1, source_target_pairs={{0,8},{8,16},{16,24},{24,0},{1,9},{9,17},{17,25},{25,1},{2,10},{10... | collective-permute-start | bytes 294920 | tf_op jit(solution)/shard_map/ppermute | solution.py:431
  118.1 1.4 %copy-start.8 = (bf16[128,128]{1,0:T(8,128)(2,1)S(1)}, bf16[128,128]{1,0:T(8,128)(2,1)}, u32[]{:S(2)}) copy-start(bf16[128,128]{1,0:T(8,128)(2,1)} %param.26) | copy-start | bytes 98308
Sparse Core Ops, SparseCore 0:
  16.2 50.5 all-gather.2

commit v16 on v15

--- a/solution.py
+++ b/solution.py
@@ -8,6 +8,7 @@
 
 REACH = 8
 FLAT = ("row", "col")
+DEPTH = 4
 
 
 def halos(cells, width):
@@ -119,15 +120,21 @@
 def pipelined_sources(index_ref, count, parts, buffers, sems, leaf_of):
     step = pl.program_id(0)
     steps = pl.num_programs(0)
-    slot = step % 2
+    slot = step % DEPTH
 
     @pl.when(step == 0)
     def _():
-        fetch_sources(index_ref, leaf_of(0), count, parts, buffers, sems, 0)
-
-    @pl.when(step + 1 < steps)
+        for ahead in range(DEPTH - 1):
+
+            @pl.when(ahead < steps)
+            def _():
+                fetch_sources(index_ref, leaf_of(ahead), count, parts, buffers, sems, ahead)
+
+    @pl.when(step + DEPTH - 1 < steps)
     def _():
-        fetch_sources(index_ref, leaf_of(step + 1), count, parts, buffers, sems, 1 - slot)
+        fetch_sources(
+            index_ref, leaf_of(step + DEPTH - 1), count, parts, buffers, sems, (step + DEPTH - 1) % DEPTH
+        )
 
     wait_sources(count, parts, buffers, sems, slot)
     return slot
@@ -191,10 +198,10 @@
             in_specs=[pl.BlockSpec((1, size, dims), by_leaf)] + [anywhere] * len(inputs),
             out_specs=pl.BlockSpec((1, size, rhs), by_leaf),
             scratch_shapes=[
-                pltpu.VMEM((2, count, size, dims), local_points.dtype),
-                pltpu.VMEM((2, count, size, rhs), local_weights.dtype),
-                pltpu.VMEM((2, 1, count * size), jnp.float32),
-                pltpu.SemaphoreType.DMA((3, 2, count)),
+                pltpu.VMEM((DEPTH, count, size, dims), local_points.dtype),
+                pltpu.VMEM((DEPTH, count, size, rhs), local_weights.dtype),
+                pltpu.VMEM((DEPTH, 1, count * size), jnp.float32),
+                pltpu.SemaphoreType.DMA((3, DEPTH, count)),
             ],
         ),
         out_shape=jax.ShapeDtypeStruct((leaves, size, rhs), jnp.float32),
@@ -247,9 +254,9 @@
             in_specs=[pl.BlockSpec((1, rank, dims), by_leaf)] + [anywhere] * len(inputs),
             out_specs=pl.BlockSpec((1, rank, width - dims), by_leaf),
             scratch_shapes=[
-                pltpu.VMEM((2, count, rank, width), own_rows.dtype),
-                pltpu.VMEM((2, 1, count * rank), jnp.float32),
-                pltpu.SemaphoreType.DMA((2, 2, count)),
+                pltpu.VMEM((DEPTH, count, rank, width), own_rows.dtype),
+                pltpu.VMEM((DEPTH, 1, count * rank), jnp.float32),
+                pltpu.SemaphoreType.DMA((2, DEPTH, count)),
             ],
         ),
         out_shape=jax.ShapeDtypeStruct((leaves, rank, width - dims), jnp.float32),
@@ -353,9 +360,7 @@
     left_pairs = left_pairs.reshape(REACH, leaf_size, dim_count + rhs_count)
     right_pairs = right_pairs.reshape(REACH, leaf_size, dim_count + rhs_count)
 
-    leaf_mask = (
-        lax.broadcasted_iota(jnp.int32, (leaf_count, rank_count), 1) < leaf_rank[:, None]
-    ).astype(jnp.float32)
+    leaf_mask = (lax.broadcasted_iota(jnp.int32, (leaf_count, rank_count), 1) < leaf_rank[:, None]).astype(jnp.float32)
     leaf_up = (
         jnp.einsum("lpk,lpr->lkr", local_bases, local_weights, preferred_element_type=jnp.float32)
         * leaf_mask[:, :, None]
@@ -363,9 +368,7 @@
     leaf_coords = select_within(local_points, leaf_skeleton)
     own_rows = jnp.concatenate([leaf_coords, leaf_up], axis=-1)
     skeleton_width = dim_count + rhs_count
-    left_rows, right_rows = halos(
-        (own_rows.reshape(leaf_count * rank_count, skeleton_width),), REACH * rank_count
-    )
+    left_rows, right_rows = halos((own_rows.reshape(leaf_count * rank_count, skeleton_width),), REACH * rank_count)
 
     node_mask = (jnp.arange(node_width, dtype=jnp.int32) < node_rank[0]).astype(jnp.float32)
     node_up = (
@@ -417,15 +420,7 @@
     far_local = far_list - offset
     coord_norms = scaled_norms(leaf_coords)
     far_inner = far_field(leaf_coords, own_rows, coord_norms, far_local)
-    far_total = far_field(
-        leaf_coords,
-        own_rows,
-        coord_norms,
-        far_local,
-        (left_rows, right_rows),
-        far_inner,
-        group_pack,
-    )
+    far_total = far_field(leaf_coords, own_rows, coord_norms, far_local, (left_rows, right_rows), far_inner, group_pack)
     rows = lax.axis_size("row")
     received = [group_pack] + [
         lax.ppermute(group_pack, "row", [(r, (r + shift) % rows) for r in range(rows)])

time: 139 us -> 135 us (0.971)
  Pallas kernels: 65.8 us -> 59.8 us
  waiting for transfers between devices: 13.3 us -> 15.1 us
    pallas_call x2, Pallas kernels: 32.2 us -> 28.9 us  [near_field(): pl.pallas_call(lambda *refs: near_kernel(leaf_of, halo, *refs), grid_spec...]
    pallas_call x2, Pallas kernels: 24.2 us -> 21.6 us  [far_field(): pl.pallas_call(lambda *refs: far_kernel(leaf_of, halo, *refs), grid_spec=...]
    ppermute x2, waiting for transfers between devices: 13.3 us -> 15.1 us  [halos(): right = lax.ppermute(head, FLAT, [(i + 1, i) for i in range(ends)])]
  transfers between devices with their start and end apart: 8 -> 8, of which waited for: 1 -> 1; matrix products, arithmetic and copies ran while one was open for 9% -> 10% of each run, Pallas kernels for 41% -> 38%
where the time goes in v16:
time: 135 us; the launch traced here: 133 us
  Pallas kernels  59.8 us (44%)
  starting transfers between devices  16 us (12%)
  waiting for transfers between devices  15.1 us (11%)
  between operations  15.1 us (11%)
  matrix products  9.2 us (7%)
  local copies, waits for them, and re-layouts  8.75 us (6%)
  other arithmetic  8.52 us (6%)
    pallas_call x2, Pallas kernels, near_field(): pl.pallas_call(lambda *refs: near_kernel(leaf_of, halo, *refs), grid_spec...  28.9 us
    pallas_call x2, Pallas kernels, far_field(): pl.pallas_call(lambda *refs: far_kernel(leaf_of, halo, *refs), grid_spec=...  21.6 us
    ppermute x2, waiting for transfers between devices, halos(): right = lax.ppermute(head, FLAT, [(i + 1, i) for i in range(ends)])  15.1 us
    pallas_call x1, Pallas kernels, final_field(): pl.pallas_call(final_kernel, grid_spec=pltpu.PrefetchScalarGridSpec(num_s...  9.37 us
    ppermute x2, starting transfers between devices, halos(): left = lax.ppermute(tail, FLAT, [(i, i + 1) for i in range(ends)])  7.3 us
    ppermute x3, starting transfers between devices, body(): lax.ppermute(group_pack, 'row', [(r, (r + shift) % rows) for r in range(r...  4.72 us
    unnamed x40, local copies, waits for them, and re-layouts  4.65 us
    ppermute x2, starting transfers between devices, halos(): right = lax.ppermute(head, FLAT, [(i + 1, i) for i in range(ends)])  3.96 us
  transfers between devices with their start and end apart: 8, of which 1 were waited for; matrix products, arithmetic and copies ran while one was open for 10% of the time, Pallas kernels for 38%

profile of v16, /device:TPU:13, one launch (start us, length us, event | category | flops | bytes accessed | tf_op | source)
XLA Modules:
  0.0 132.5 jit_solution(3788724377043459926)
XLA Ops:
  6.5 0.9 copy.28
  7.4 0.7 fusion.55
  9.5 3.2 %fusion.2 = (f32[24,128]{1,0:T(8,128)}, bf16[24,128,128]{2,1,0:T(8,128)(2,1)S(1)}) fusion(bf16[24,256,128]{2,1,0:T(8,128)(2,1)} %bitcast.99, s32[24,128]{1,0:T(8,128)} %param.19), kind=kOutput, calls=%fused_computation.14 | convolution fusion | flops 204469248 | bytes 2383872 | tf_op jit(solution)/shard_map/bkp,bpc->bkc/dot_general | solution.py:324
  12.7 0.6 multiply_reduce_fusion.2
  13.3 0.3 copy-done.2
  13.6 1.0 multiply_convert_fusion
  14.6 0.2 copy-done.6
  14.8 0.6 fusion.23
  15.4 0.7 pad_maximum_fusion.5
  16.1 1.8 %fusion.67 = (bf16[2048,256]{1,0:T(8,128)(2,1)S(1)}, bf16[2048,256]{1,0:T(8,128)(2,1)S(1)}) fusion(bf16[6144,256]{1,0:T(8,128)(2,1)} %param.16), kind=kLoop, calls=%fused_computation.107 | loop fusion | bytes 4194304 | tf_op jit(solution)/shard_map/slice | solution.py:17
  17.9 0.2 copy-done
  18.2 1.4 %pad_maximum_fusion.1 = bf16[2048,384]{1,0:T(8,128)(2,1)} fusion(bf16[2048,256]{1,0:T(8,128)(2,1)S(1)} %get-tuple-element.12, bf16[2048,128]{1,0:T(8,128)(2,1)S(1)} %get-tuple-element.16), kind=kLoop, calls=%fused_computation.15 | loop fusion | flops 3145728 | bytes 3145728 | tf_op jit(solution)/shard_map/concatenate | solution.py:18
  19.6 3.7 %collective-permute-start.3 = (bf16[2048,384]{1,0:T(8,128)(2,1)}, bf16[2048,384]{1,0:T(8,128)(2,1)}, u32[]{:S(2)}, u32[]{:S(2)}) collective-permute-start(bf16[2048,384]{1,0:T(8,128)(2,1)} %pad_maximum_fusion.1), channel_id=1, source_target_pairs={{0,1},{1,2},{2,3},{3,4},{4,5},{5,6},{6,7},{7,8},{8,9},{9,10},{10,1... | collective-permute-start | bytes 4718600 | tf_op jit(solution)/shard_map/ppermute | solution.py:19
  23.2 1.4 %pad_maximum_fusion.2 = bf16[2048,384]{1,0:T(8,128)(2,1)} fusion(bf16[2048,256]{1,0:T(8,128)(2,1)S(1)} %get-tuple-element.11, bf16[2048,128]{1,0:T(8,128)(2,1)S(1)} %get-tuple-element.15), kind=kLoop, calls=%fused_computation.16 | loop fusion | flops 3145728 | bytes 3145728 | tf_op jit(solution)/shard_map/concatenate | solution.py:17
  24.6 2.0 %collective-permute-start.4 = (bf16[2048,384]{1,0:T(8,128)(2,1)}, bf16[2048,384]{1,0:T(8,128)(2,1)}, u32[]{:S(2)}, u32[]{:S(2)}) collective-permute-start(bf16[2048,384]{1,0:T(8,128)(2,1)} %pad_maximum_fusion.2), channel_id=1, source_target_pairs={{1,0},{2,1},{3,2},{4,3},{5,4},{6,5},{7,6},{8,7},{9,8},{10,9},{11,1... | collective-permute-start | bytes 4718600 | tf_op jit(solution)/shard_map/ppermute | solution.py:20
  26.7 1.4 %fusion.26 = (bf16[8,128,384]{2,1,0:T(8,128)(2,1)}, bf16[8,128,384]{2,1,0:T(8,128)(2,1)}) fusion(bf16[24,128,256]{2,1,0:T(8,128)(2,1)S(1)} %multiply_convert_fusion, bf16[24,128,128]{2,1,0:T(8,128)(2,1)S(1)} %copy-done.3), kind=kLoop, calls=%fused_computation.49 | loop fusion | flops 3145728 | bytes 3932160 | tf_op jit(solution)/shard_map/concatenate | solution.py:369
  28.1 3.6 %collective-permute-start.5 = (bf16[1024,384]{1,0:T(8,128)(2,1)}, bf16[1024,384]{1,0:T(8,128)(2,1)}, u32[]{:S(2)}, u32[]{:S(2)}) collective-permute-start(bf16[1024,384]{1,0:T(8,128)(2,1)} %bitcast.20), channel_id=1, source_target_pairs={{0,1},{1,2},{2,3},{3,4},{4,5},{5,6},{6,7},{7,8},{8,9},{9,10},{10,1... | collective-permute-start | bytes 2359304 | tf_op jit(solution)/shard_map/ppermute | solution.py:19
  31.7 1.9 %collective-permute-start.6 = (bf16[1024,384]{1,0:T(8,128)(2,1)}, bf16[1024,384]{1,0:T(8,128)(2,1)}, u32[]{:S(2)}, u32[]{:S(2)}) collective-permute-start(bf16[1024,384]{1,0:T(8,128)(2,1)} %bitcast.21), channel_id=1, source_target_pairs={{1,0},{2,1},{3,2},{4,3},{5,4},{6,5},{7,6},{8,7},{9,8},{10,9},{11,1... | collective-permute-start | bytes 2359304 | tf_op jit(solution)/shard_map/ppermute | solution.py:20
  33.9 0.7 reshape.158.refs_0_
  34.6 0.6 reshape.159.refs_0_
  35.2 0.9 fusion
  36.1 0.6 reduce_sum.61.refs_4_
  36.7 10.4 %shard_map.145.refs_6_ = f32[24,256,256]{2,1,0:T(8,128)} custom-call(s32[120]{0:T(128)} %reshape.159.refs_0_, bf16[24,256,128]{2,1,0:T(8,128)(2,1)} %bitcast.100, bf16[24,256,128]{2,1,0:T(8,128)(2,1)} %bitcast.101, bf16[24,256,256]{2,1,0:T(8,128)(2,1)} %bitcast.104, f32[24,256]{1,0:T(8,128)} %reduce_sum.61.refs_4_), custom_call_target="tpu_custom_call" | custom-call | tf_op jit(solution)/shard_map/pallas_call | solution.py:193
  47.1 1.8 %pad_maximum_fusion.refs_2_.refs_3_ = bf16[24,128,384]{2,1,0:T(8,128)(2,1)} fusion(bf16[24,128,128]{2,1,0:T(8,128)(2,1)S(1)} %copy-done.4, bf16[24,128,256]{2,1,0:T(8,128)(2,1)S(1)} %multiply_convert_fusion), kind=kLoop, calls=%fused_computation.6 | loop fusion | flops 4718592 | bytes 4718592 | tf_op jit(solution)/shard_map/concatenate | solution.py:369
  48.9 8.1 %shard_map.147.refs_6_ = f32[24,128,256]{2,1,0:T(8,128)} custom-call(s32[96]{0:T(128)} %reshape.158.refs_0_, bf16[24,128,128]{2,1,0:T(8,128)(2,1)} %copy-done.2, bf16[24,128,384]{2,1,0:T(8,128)(2,1)} %pad_maximum_fusion.refs_2_.refs_3_, f32[24,128]{1,0:T(8,128)} %get-tuple-element.25.refs_3_), custom_call_target="tpu_custom_call" | custom-call | tf_op jit(solution)/shard_map/pallas_call | solution.py:249
  57.1 15.1 %collective-permute-done.4 = bf16[2048,384]{1,0:T(8,128)(2,1)} collective-permute-done((bf16[2048,384]{1,0:T(8,128)(2,1)}, bf16[2048,384]{1,0:T(8,128)(2,1)}, u32[]{:S(2)}, u32[]{:S(2)}) %collective-permute-start.4) | collective-permute-done | bytes 1572896 | tf_op jit(solution)/shard_map/ppermute | solution.py:20
  72.2 18.5 %shard_map.146.near_ref = f32[24,256,256]{2,1,0:T(8,128)} custom-call(s32[120]{0:T(128)} %reshape.159.refs_0_, bf16[24,256,128]{2,1,0:T(8,128)(2,1)} %bitcast.102, bf16[8,256,384]{2,1,0:T(8,128)(2,1)} %bitcast.18.refs_2_, bf16[24,256,128]{2,1,0:T(8,128)(2,1)} %bitcast.103, bf16[8,256,384]{2,1,0:T(8,128)(2,1)} %bitcast.19.refs_4_, ...), custom_call_target="tpu_custom_call", output_to_operand_aliasing={{}: (6, {})} | custom-call | tf_op jit(solution)/shard_map/pallas_call | solution.py:193
  90.8 1.5 %copy.43 = bf16[64,8,8,128]{3,2,1,0:T(8,128)(2,1)S(1)} copy(bf16[64,8,8,128]{3,1,2,0:T(8,128)(2,1)} %bitcast.116) | data formatting | bytes 2097152
  92.4 0.3 copy.42
  92.7 0.2 copy.40
  93.0 0.4 multiply_reduce_fusion.3
  93.3 0.2 fusion.19
  93.7 2.5 %collective-permute-start.1 = (bf16[128,384]{1,0:T(8,128)(2,1)S(1)}, bf16[128,384]{1,0:T(8,128)(2,1)S(1)}, u32[]{:S(2)}, u32[]{:S(2)}) collective-permute-start(bf16[128,384]{1,0:T(8,128)(2,1)S(1)} %get-tuple-element.20.refs_5_), channel_id=1, source_target_pairs={{0,16},{8,24},{16,0},{24,8},{1,17},{9,25},{17,1},{25,9},{2,18},{10... | collective-permute-start | bytes 294920 | tf_op jit(solution)/shard_map/ppermute | solution.py:426
  96.1 2.2 %collective-permute-start = (bf16[128,384]{1,0:T(8,128)(2,1)S(1)}, bf16[128,384]{1,0:T(8,128)(2,1)S(1)}, u32[]{:S(2)}, u32[]{:S(2)}) collective-permute-start(bf16[128,384]{1,0:T(8,128)(2,1)S(1)} %get-tuple-element.20.refs_5_), channel_id=1, source_target_pairs={{0,8},{8,16},{16,24},{24,0},{1,9},{9,17},{17,25},{25,1},{2,10},{10... | collective-permute-start | bytes 294920 | tf_op jit(solution)/shard_map/ppermute | solution.py:426
  98.3 0.3 copy.51
  98.6 0.4 convolution_convert_fusion.1
  99.0 0.3 fusion.10
  99.3 0.1 multiply_reduce_fusion
  99.4 0.2 copy.44
  99.6 13.4 %shard_map.148.far_ref = f32[24,128,256]{2,1,0:T(8,128)} custom-call(s32[96]{0:T(128)} %reshape.158.refs_0_, bf16[24,128,128]{2,1,0:T(8,128)(2,1)} %copy-done.2, bf16[8,128,384]{2,1,0:T(8,128)(2,1)} %bitcast.22.refs_2_, bf16[24,128,384]{2,1,0:T(8,128)(2,1)} %pad_maximum_fusion.refs_2_.refs_3_, ...), custom_call_target="tpu_custom_call", output_to_operand_aliasing={{}: (6, {})} | custom-call | tf_op jit(solution)/shard_map/pallas_call | solution.py:249
  113.0 0.4 convolution_bitcast_fusion
  113.4 0.2 copy.47
  113.6 0.2 copy.46
  113.8 0.2 copy.45
  114.0 1.0 convolution_convert_fusion
  115.1 0.2 fusion.20
  115.3 1.0 fusion.18.down_ref
  116.3 9.4 %shard_map.149 = bf16[24,256,256]{2,1,0:T(8,128)(2,1)} custom-call(s32[24]{0:T(128)} %rank_ref.1, bf16[24,128,128]{2,1,0:T(8,128)(2,1)} %bitcast.114, bf16[128,256]{1,0:T(8,128)(2,1)} %fusion.18.down_ref, f32[24,128,256]{2,1,0:T(8,128)} %shard_map.148.far_ref, bf16[24,256,128]{2,1,0:T(8,128)(2,1)} %bitcast.109, f32[24,256,256]{2,1,0:T(8,128)} %shard_map.146.near_ref), custom_call_target="tpu_custom_call" | custom-call | tf_op jit(solution)/shard_map/pallas_call | solution.py:292
  (51 shorter events, 0.8 us)
Async XLA Ops:
  6.5 84.2 %all-gather.3.cloned.1.call-start = ((), (), s32[]{:S(2)}) async-start(), calls=%async_computation | async-start | bytes 1179648 | tf_op jit(solution)/shard_map/all_gather | solution.py:389
  6.5 6.2 %copy-start.11 = (s32[1,128]{1,0:T(1,128)S(1)}, s32[1,128]{1,0:T(1,128)}, u32[]{:S(2)}) copy-start(s32[1,128]{1,0:T(1,128)} %param.24) | copy-start | bytes 1540
  9.5 4.2 %copy-start.1 = (bf16[6144,256]{1,0:T(8,128)(2,1)S(1)}, bf16[6144,256]{1,0:T(8,128)(2,1)}, u32[]{:S(2)}) copy-start(bf16[6144,256]{1,0:T(8,128)(2,1)} %param.16) | copy-start | bytes 9437188
  9.5 4.1 %copy-start.5 = (bf16[6144,128]{1,0:T(8,128)(2,1)S(1)}, bf16[6144,128]{1,0:T(8,128)(2,1)}, u32[]{:S(2)}) copy-start(bf16[6144,128]{1,0:T(8,128)(2,1)} %param.17) | copy-start | bytes 4718596
  12.7 0.9 copy-start.2
  13.6 1.1 copy-start.6
  16.1 2.0 %copy-start = (bf16[6144,128]{1,0:T(8,128)(2,1)S(1)}, bf16[6144,128]{1,0:T(8,128)(2,1)}, u32[]{:S(2)}) copy-start(bf16[6144,128]{1,0:T(8,128)(2,1)} %param.15) | copy-start | bytes 4718596
  19.6 37.6 %collective-permute-start.3 = (bf16[2048,384]{1,0:T(8,128)(2,1)}, bf16[2048,384]{1,0:T(8,128)(2,1)}, u32[]{:S(2)}, u32[]{:S(2)}) collective-permute-start(bf16[2048,384]{1,0:T(8,128)(2,1)} %pad_maximum_fusion.1), channel_id=1, source_target_pairs={{0,1},{1,2},{2,3},{3,4},{4,5},{5,6},{6,7},{7,8},{8,9},{9,10},{10,1... | collective-permute-start | bytes 4718600 | tf_op jit(solution)/shard_map/ppermute | solution.py:19
  23.2 3.4 %copy-start.3 = (bf16[24,128,128]{2,1,0:T(8,128)(2,1)S(1)}, bf16[24,128,128]{2,1,0:T(8,128)(2,1)}, u32[]{:S(2)}) copy-start(bf16[24,128,128]{2,1,0:T(8,128)(2,1)} %copy-done.2) | copy-start | bytes 2359300
  24.6 9.2 %copy-start.10 = (s32[24,4]{0,1:T(4,128)S(1)}, s32[24,4]{0,1:T(4,128)}, u32[]{:S(2)}) copy-start(s32[24,4]{0,1:T(4,128)} %param.21) | copy-start | bytes 1156
  24.6 9.9 %copy-start.9 = (s32[24,5]{0,1:T(8,128)S(1)}, s32[24,5]{0,1:T(8,128)}, u32[]{:S(2)}) copy-start(s32[24,5]{0,1:T(8,128)} %param.20) | copy-start | bytes 1444
  24.6 47.6 %collective-permute-start.4 = (bf16[2048,384]{1,0:T(8,128)(2,1)}, bf16[2048,384]{1,0:T(8,128)(2,1)}, u32[]{:S(2)}, u32[]{:S(2)}) collective-permute-start(bf16[2048,384]{1,0:T(8,128)(2,1)} %pad_maximum_fusion.2), channel_id=1, source_target_pairs={{1,0},{2,1},{3,2},{4,3},{5,4},{6,5},{7,6},{8,7},{9,8},{10,9},{11,1... | collective-permute-start | bytes 4718600 | tf_op jit(solution)/shard_map/ppermute | solution.py:20
  28.1 62.7 %collective-permute-start.5 = (bf16[1024,384]{1,0:T(8,128)(2,1)}, bf16[1024,384]{1,0:T(8,128)(2,1)}, u32[]{:S(2)}, u32[]{:S(2)}) collective-permute-start(bf16[1024,384]{1,0:T(8,128)(2,1)} %bitcast.20), channel_id=1, source_target_pairs={{0,1},{1,2},{2,3},{3,4},{4,5},{5,6},{6,7},{7,8},{8,9},{9,10},{10,1... | collective-permute-start | bytes 2359304 | tf_op jit(solution)/shard_map/ppermute | solution.py:19
  31.7 59.0 %collective-permute-start.6 = (bf16[1024,384]{1,0:T(8,128)(2,1)}, bf16[1024,384]{1,0:T(8,128)(2,1)}, u32[]{:S(2)}, u32[]{:S(2)}) collective-permute-start(bf16[1024,384]{1,0:T(8,128)(2,1)} %bitcast.21), channel_id=1, source_target_pairs={{1,0},{2,1},{3,2},{4,3},{5,4},{6,5},{7,6},{8,7},{9,8},{10,9},{11,1... | collective-permute-start | bytes 2359304 | tf_op jit(solution)/shard_map/ppermute | solution.py:20
  36.7 10.4 %copy-start.4 = (bf16[24,128,128]{2,1,0:T(8,128)(2,1)S(1)}, bf16[24,128,128]{2,1,0:T(8,128)(2,1)}, u32[]{:S(2)}) copy-start(bf16[24,128,128]{2,1,0:T(8,128)(2,1)} %copy-done.2) | copy-start | bytes 2359300
  48.9 8.2 %copy-start.12 = (s32[1,4]{1,0:T(1,128)S(1)}, s32[1,4]{1,0:T(1,128)}, u32[]{:S(2)}) copy-start(s32[1,4]{1,0:T(1,128)} %param.25) | copy-start | bytes 52
  48.9 8.2 %copy-start.13 = (s32[1,2]{1,0:T(1,128)S(1)}, s32[1,2]{1,0:T(1,128)}, u32[]{:S(2)}) copy-start(s32[1,2]{1,0:T(1,128)} %param.29) | copy-start | bytes 28
  92.3 0.7 copy-start.14
  93.6 6.0 %copy-start.7 = (bf16[128,384]{1,0:T(8,128)(2,1)}, bf16[128,384]{1,0:T(8,128)(2,1)S(1)}, u32[]{:S(2)}) copy-start(bf16[128,384]{1,0:T(8,128)(2,1)S(1)} %get-tuple-element.20.refs_5_) | copy-start | bytes 294916
  93.6 19.8 %collective-permute-start.2 = (bf16[128,384]{1,0:T(8,128)(2,1)S(1)}, bf16[128,384]{1,0:T(8,128)(2,1)S(1)}, u32[]{:S(2)}, u32[]{:S(2)}) collective-permute-start(bf16[128,384]{1,0:T(8,128)(2,1)S(1)} %get-tuple-element.20.refs_5_), channel_id=1, source_target_pairs={{0,24},{8,0},{16,8},{24,16},{1,25},{9,1},{17,9},{25,17},{2,26},{10... | collective-permute-start | bytes 294920 | tf_op jit(solution)/shard_map/ppermute | solution.py:426
  93.7 19.9 %collective-permute-start.1 = (bf16[128,384]{1,0:T(8,128)(2,1)S(1)}, bf16[128,384]{1,0:T(8,128)(2,1)S(1)}, u32[]{:S(2)}, u32[]{:S(2)}) collective-permute-start(bf16[128,384]{1,0:T(8,128)(2,1)S(1)} %get-tuple-element.20.refs_5_), channel_id=1, source_target_pairs={{0,16},{8,24},{16,0},{24,8},{1,17},{9,25},{17,1},{25,9},{2,18},{10... | collective-permute-start | bytes 294920 | tf_op jit(solution)/shard_map/ppermute | solution.py:426
  96.1 17.6 %collective-permute-start = (bf16[128,384]{1,0:T(8,128)(2,1)S(1)}, bf16[128,384]{1,0:T(8,128)(2,1)S(1)}, u32[]{:S(2)}, u32[]{:S(2)}) collective-permute-start(bf16[128,384]{1,0:T(8,128)(2,1)S(1)} %get-tuple-element.20.refs_5_), channel_id=1, source_target_pairs={{0,8},{8,16},{16,24},{24,0},{1,9},{9,17},{17,25},{25,1},{2,10},{10... | collective-permute-start | bytes 294920 | tf_op jit(solution)/shard_map/ppermute | solution.py:426
  113.9 1.4 %copy-start.8 = (bf16[128,128]{1,0:T(8,128)(2,1)S(1)}, bf16[128,128]{1,0:T(8,128)(2,1)}, u32[]{:S(2)}) copy-start(bf16[128,128]{1,0:T(8,128)(2,1)} %param.26) | copy-start | bytes 98308
Sparse Core Ops, SparseCore 0:
  16.2 50.5 all-gather.2
